TPU v7x, 32 devices: a whole 2x2x4 slice. The times are simulated.
32 devices in a mesh: groups: 2 (over y), orient: 8 (over z, x), tile: 2 (over core).
Axes of the slice: x: 2, y: 2, z: 4, core: 2. Of those that a mesh axis runs over, the one named last changes fastest.
Arguments:
- micrograph: bfloat16 [2048, 256], P(('groups', 'orient'), 'tile'), parts along dimension 0, may hold values from -6 to 6
- templates: bfloat16 [8, 192, 192], P('orient'), may hold values from -0.03125 to 0.03125
- defocus: int32 [16], P(('groups', 'orient')), parts along dimension 0, may hold values from 0 to 7
- ctf: float32 [16, 320, 320], P('groups'), parts along dimension 0, may hold values from -1 to 1
- usable: int32 [16, 2], P(('groups', 'orient'), 'tile'), parts along dimension 0, may hold values from 1 to 4, as said below
Outputs:
- peak_map: float32 [2048, 256], P(('groups', 'orient'), 'tile'), parts along dimension 0
- mean_map: float32 [2048, 256], P(('groups', 'orient'), 'tile'), parts along dimension 0
- square_map: float32 [2048, 256], P(('groups', 'orient'), 'tile'), parts along dimension 0
There are 2 independent parts, one for each index of `groups`. A program takes and returns all parts, laid end to end along the dimension named above; an argument that names none is the same for every part. Nothing has to cross between parts.
Inputs may be any that keep to these rules, and one draw needn't show every extreme that they name: usable rows of each tile form its first usable x 32 rows; in every micrograph some tile has all 4 blocks usable.
All inputs are finite; a program needn't handle non-finite values.
Results may differ from a plain program's by a relative error of at most 0.0094.
Values may be sent and summed in bfloat16 or wider, within the bound.
No kernel may reach another device: no remote copies, remote signals or barrier semaphores. Data moves between devices by JAX's collectives and lax.ppermute only.
A program may use at most 128 MiB of HBM per device.

v0:
```python
import math

import jax
import jax.numpy as jnp
import ml_dtypes
import numpy as np
from jax import lax
from jax.sharding import PartitionSpec as P

RB = 32
CHUNK = 8


def extended(block, sides, width):
    for axis, dim in sides:
        count = lax.axis_size(axis)
        forward = [(i, i + 1) for i in range(count - 1)]
        backward = [(target, source) for source, target in forward]
        low = lax.ppermute(
            lax.slice_in_dim(block, block.shape[dim] - width, None, axis=dim), axis, forward
        )
        high = lax.ppermute(lax.slice_in_dim(block, 0, width, axis=dim), axis, backward)
        block = jnp.concatenate([low, block, high], axis=dim)
    return block


def twiddles(padded_size):
    position = np.arange(padded_size, dtype=np.int64)
    phase_index = (position[:, None] * position[None, :]) % padded_size
    angles = phase_index.astype(np.float32) * np.float32(2.0 * math.pi / padded_size)
    angles = angles.astype(np.float64)
    cosines = np.cos(angles).astype(np.float32).astype(ml_dtypes.bfloat16)
    sines = np.sin(angles).astype(np.float32).astype(ml_dtypes.bfloat16)
    return cosines, sines


def matmul(left, right):
    return jnp.dot(left, right, preferred_element_type=jnp.float32)


def body(micrograph, templates, defocus, ctf, usable):
    bf16 = jnp.bfloat16
    f32 = jnp.float32
    tile_width = micrograph.shape[0]
    padded_size = ctf.shape[1]
    box_size = templates.shape[1]
    margin = (padded_size - tile_width) // 2
    scaling = 1.0 / (padded_size * padded_size)
    n = padded_size
    cos_np, sin_np = twiddles(n)

    shifted = (np.arange(box_size) - box_size // 2) % n
    temp_rows = jnp.asarray(np.concatenate([cos_np[shifted, :], -sin_np[shifted, :]], axis=1))
    temp_cols = jnp.asarray(np.concatenate([cos_np[:, shifted], sin_np[:, shifted]], axis=0))
    half_mat = jnp.asarray(np.concatenate([cos_np, -sin_np], axis=1))
    spec_mat = jnp.asarray(np.concatenate([cos_np, sin_np], axis=0))
    row_mat = jnp.asarray(
        np.concatenate([cos_np[margin : margin + tile_width], sin_np[margin : margin + tile_width]], axis=0)
    )
    col_mat = jnp.asarray(
        np.concatenate([cos_np[:, margin : margin + tile_width], -sin_np[:, margin : margin + tile_width]], axis=0)
    )

    local_count = templates.shape[0]
    id_row = jnp.broadcast_to(defocus.astype(bf16)[:, None, None], (local_count, 1, box_size))
    packed = jnp.concatenate([templates, id_row], axis=1)
    gathered = lax.all_gather(packed, "orient", axis=0, tiled=True)
    all_templates = gathered[:, :box_size, :]
    all_ids = gathered[:, box_size, 0].astype(jnp.int32)
    total = all_templates.shape[0]

    padded = extended(micrograph, (("orient", 0), ("tile", 1)), margin)
    half = matmul(padded, half_mat).astype(bf16)
    spec_full = matmul(spec_mat, half)
    spec_real = (spec_full[:n, :n] + spec_full[n:, n:]).astype(bf16).astype(f32)
    spec_imag = (spec_full[:n, n:] - spec_full[n:, :n]).astype(bf16).astype(f32)

    def chunk_stats(chunk_templates, chunk_ids):
        count = chunk_templates.shape[0]
        part = jnp.einsum("okj,jv->kov", chunk_templates, temp_rows, preferred_element_type=f32).astype(bf16)
        full = jnp.einsum("pk,kov->pov", temp_cols, part, preferred_element_type=f32)
        full_real = full[:n, :, :n] + full[n:, :, n:]
        full_imag = full[:n, :, n:] - full[n:, :, :n]
        weight = jnp.take(ctf, chunk_ids, axis=0).transpose(1, 0, 2)
        w_real = (full_real * weight).astype(bf16).astype(f32)
        w_imag = (full_imag * weight).astype(bf16).astype(f32)
        s_real = spec_real[:, None, :]
        s_imag = spec_imag[:, None, :]
        prod_real = (s_real * w_real + s_imag * w_imag).astype(bf16)
        prod_imag = (s_imag * w_real - s_real * w_imag).astype(bf16)
        prod = jnp.stack([prod_real, prod_imag], axis=1).reshape(n, 2 * count * n)
        left = matmul(row_mat, prod).reshape(2 * tile_width, 2, count, n)
        left_real = (left[:tile_width, 0] - left[tile_width:, 1]).astype(bf16)
        left_imag = (left[:tile_width, 1] + left[tile_width:, 0]).astype(bf16)
        stacked = jnp.concatenate([left_real, left_imag], axis=-1).reshape(tile_width * count, 2 * n)
        corr = (matmul(stacked, col_mat) * scaling).reshape(tile_width, count, tile_width)
        return (jnp.max(corr, axis=1), jnp.sum(corr, axis=1), jnp.sum(corr * corr, axis=1))

    chunk = min(CHUNK, total)
    n_chunks = total // chunk
    if n_chunks == 1:
        peak_map, sum_map, squares = chunk_stats(all_templates, all_ids)
    else:

        def step(index, tallies):
            start = index * chunk
            part_templates = lax.dynamic_slice_in_dim(all_templates, start, chunk, 0)
            part_ids = lax.dynamic_slice_in_dim(all_ids, start, chunk, 0)
            peak_c, sum_c, sq_c = chunk_stats(part_templates, part_ids)
            return (jnp.maximum(tallies[0], peak_c), tallies[1] + sum_c, tallies[2] + sq_c)

        shape = (tile_width, tile_width)
        initial = (jnp.full(shape, -jnp.inf, f32), jnp.zeros(shape, f32), jnp.zeros(shape, f32))
        peak_map, sum_map, squares = lax.fori_loop(0, n_chunks, step, initial)

    live = usable[0, 0]
    row_mask = (jnp.arange(tile_width, dtype=jnp.int32) < RB * live)[:, None]
    orient_count = float(total)
    peak_out = jnp.where(row_mask, peak_map, 0.0)
    mean_out = jnp.where(row_mask, sum_map / orient_count, 0.0)
    square_out = jnp.where(row_mask, squares / orient_count, 0.0)
    return (peak_out, mean_out, square_out)


def solution(mesh):
    return jax.shard_map(
        body,
        mesh=mesh,
        in_specs=(
            P(("groups", "orient"), "tile"),
            P("orient", None, None),
            P(("groups", "orient")),
            P("groups", None, None),
            P(("groups", "orient"), "tile"),
        ),
        out_specs=(
            P(("groups", "orient"), "tile"),
            P(("groups", "orient"), "tile"),
            P(("groups", "orient"), "tile"),
        ),
        check_vma=False,
    )
```

profile of v0, /device:TPU:0, one launch (start us, length us, event | category | flops | bytes accessed | tf_op | source)
XLA Modules:
  0.0 86.4 jit_solution(17544548362719829288)
XLA Ops:
  0.6 0.8 fusion.36
  1.4 4.8 %collective-permute-start = (bf16[96,128]{1,0:T(8,128)(2,1)S(1)}, bf16[96,128]{1,0:T(8,128)(2,1)S(1)}, u32[]{:S(2)}, u32[]{:S(2)}) collective-permute-start(bf16[96,128]{1,0:T(8,128)(2,1)S(1)} %get-tuple-element.16), channel_id=1, source_target_pairs={{0,2},{2,4},{4,6},{6,8},{8,10},{10,12},{12,14},{1,3},{3,5},{5,7},{... | collective-permute-start | bytes 73736 | tf_op jit(solution)/shard_map/ppermute | solution.py:19
  6.3 1.3 %collective-permute-start.1 = (bf16[96,128]{1,0:T(8,128)(2,1)S(1)}, bf16[96,128]{1,0:T(8,128)(2,1)S(1)}, u32[]{:S(2)}, u32[]{:S(2)}) collective-permute-start(bf16[96,128]{1,0:T(8,128)(2,1)S(1)} %get-tuple-element.15), channel_id=1, source_target_pairs={{2,0},{4,2},{6,4},{8,6},{10,8},{12,10},{14,12},{3,1},{5,3},{7,5},{... | collective-permute-start | bytes 73736 | tf_op jit(solution)/shard_map/ppermute | solution.py:22
  7.6 1.0 %copy.27 = bf16[1,192,192]{1,2,0:T(8,128)(2,1)S(1)} copy(bf16[1,192,192]{2,1,0:T(8,128)(2,1)} %param.12) | data formatting | bytes 147456 | tf_op args[1]
  9.3 34.5 %all_gather.3 = bf16[8,193,192]{1,2,0:T(8,128)(2,1)S(1)} all-gather(bf16[1,193,192]{1,2,0:T(8,128)(2,1)S(1)} %concatenate.15), channel_id=1, replica_groups=mesh['groups'=2,'orient'=8,'tile'=2] {'orient'}, dimensions={0}, use_global_device_ids=true | all-gather | bytes 667008 | tf_op jit(solution)/shard_map/all_gather | solution.py:67
  43.7 0.3 fusion.31
  44.7 8.8 %fusion.10 = f32[640,8,640]{0,2,1:T(8,128)} fusion(bf16[640,192,1]{0,1,2:T(8,128)(2,1)} %constant.57, bf16[192,640,1]{1,0,2:T(8,128)(2,1)} %constant.58, bf16[8,193,192]{1,2,0:T(8,128)(2,1)S(1)} %all_gather.3), kind=kOutput, calls=%fused_computation.18 | convolution fusion | flops 1636761600 | bytes 14191616 | tf_op jit(solution)/shard_map/pk,kov->pov/dot_general | solution.py:81
  53.6 4.8 %gather_fusion = f32[8,320,320]{2,1,0:T(8,128)} fusion(f32[8,320,320]{2,1,0:T(8,128)} %param.14, s32[1024]{0:T(1024)S(1)} %pad_clamp_fusion), kind=kCustom, calls=%fused_computation | custom fusion | bytes 6553632 | tf_op jit(solution)/shard_map/jit(_take)/gather | solution.py:84
  58.3 5.5 %copy.29 = f32[8,320,320]{1,2,0:T(8,128)} copy(f32[8,320,320]{2,1,0:T(8,128)} %gather_fusion) | data formatting | bytes 6553600 | tf_op jit(solution)/shard_map/jit(_take)/gather | solution.py:84
  64.0 1.3 %collective-permute-start.3 = (bf16[320,96]{1,0:T(8,128)(2,1)S(1)}, bf16[320,96]{1,0:T(8,128)(2,1)S(1)}, u32[]{:S(2)}, u32[]{:S(2)}) collective-permute-start(bf16[320,96]{1,0:T(8,128)(2,1)S(1)} %get-tuple-element.14), channel_id=1, source_target_pairs={{1,0},{3,2},{5,4},{7,6},{9,8},{11,10},{13,12},{15,14},{17,16},{19,... | collective-permute-start | bytes 184328 | tf_op jit(solution)/shard_map/ppermute | solution.py:22
  65.3 3.2 %collective-permute-start.2 = (bf16[320,96]{1,0:T(8,128)(2,1)S(1)}, bf16[320,96]{1,0:T(8,128)(2,1)S(1)}, u32[]{:S(2)}, u32[]{:S(2)}) collective-permute-start(bf16[320,96]{1,0:T(8,128)(2,1)S(1)} %get-tuple-element.13), channel_id=1, source_target_pairs={{0,1},{2,3},{4,5},{6,7},{8,9},{10,11},{12,13},{14,15},{16,17},{18,... | collective-permute-start | bytes 184328 | tf_op jit(solution)/shard_map/ppermute | solution.py:19
  68.5 0.2 fusion.37
  69.3 1.9 %fusion.21 = f32[640,640]{1,0:T(8,128)S(1)} fusion(bf16[640,320]{1,0:T(8,128)(2,1)} %constant.44.clone, f32[320,640]{1,0:T(8,128)S(1)} %fusion.38, f32[320,640]{1,0:T(8,128)S(1)} %fusion.37, bf16[320,96]{1,0:T(8,128)(2,1)S(1)} %collective-permute-done.2, bf16[96,640]{1,0:T(8,128)(2,1)S(1)} %copy-done.3), kind=kOutput, calls=%fused_computation.32 | convolution fusion | flops 302080000 | bytes 3870720 | tf_op jit(solution)/shard_map/dot_general | solution.py:38
  71.1 0.3 fusion.29
  71.9 8.0 %fusion.9 = (bf16[320,1,8,320]{0,3,2,1:T(8,128)(2,1)S(1)}, bf16[320,8,320]{0,2,1:T(8,128)(2,1)S(1)}, bf16[320,8,320]{0,2,1:T(8,128)(2,1)S(1)}) fusion(f32[320,320]{0,1:T(8,128)S(1)} %copy.30, f32[320,320]{0,1:T(8,128)S(1)} %copy.26, f32[8,320,320]{1,2,0:T(8,128)} %copy.29, pred[8]{0:T(512)(128)(4,1)S(1)} %compare_and_fusion, f32[640,8,640]{0,2,1:T(8,128)} %fusion.10), kind=kLoop, calls=%fused_computation.17 | loop fusion | flops 10649600 | bytes 22118408 | tf_op jit(solution)/shard_map/stack | solution.py:91
  79.9 0.7 fusion.8
  80.7 0.8 pad_maximum_fusion
  81.6 1.5 %fusion.39 = f32[256,5120]{0,1:T(8,128)S(1)} fusion(bf16[256,320]{1,0:T(8,128)(2,1)S(1)} %copy-done, bf16[320,5120]{0,1:T(8,128)(2,1)S(1)} %bitcast.46), kind=kOutput, calls=%fused_computation.62 | convolution fusion | flops 838860800 | bytes 8683520 | tf_op jit(solution)/shard_map/dot_general | solution.py:38
  83.2 0.3 fusion.15
  83.5 0.5 copy.32
  84.0 0.5 copy.33
  84.6 0.4 fusion.25
  84.9 0.7 multiply_reduce_fusion
  85.6 0.8 multiply_select_fusion
  (30 shorter events, 1.2 us)
Async XLA Ops:
  1.4 62.4 %collective-permute-start = (bf16[96,128]{1,0:T(8,128)(2,1)S(1)}, bf16[96,128]{1,0:T(8,128)(2,1)S(1)}, u32[]{:S(2)}, u32[]{:S(2)}) collective-permute-start(bf16[96,128]{1,0:T(8,128)(2,1)S(1)} %get-tuple-element.16), channel_id=1, source_target_pairs={{0,2},{2,4},{4,6},{6,8},{8,10},{10,12},{12,14},{1,3},{3,5},{5,7},{... | collective-permute-start | bytes 73736 | tf_op jit(solution)/shard_map/ppermute | solution.py:19
  6.3 57.6 %collective-permute-start.1 = (bf16[96,128]{1,0:T(8,128)(2,1)S(1)}, bf16[96,128]{1,0:T(8,128)(2,1)S(1)}, u32[]{:S(2)}, u32[]{:S(2)}) collective-permute-start(bf16[96,128]{1,0:T(8,128)(2,1)S(1)} %get-tuple-element.15), channel_id=1, source_target_pairs={{2,0},{4,2},{6,4},{8,6},{10,8},{12,10},{14,12},{3,1},{5,3},{7,5},{... | collective-permute-start | bytes 73736 | tf_op jit(solution)/shard_map/ppermute | solution.py:22
  58.3 5.6 %copy-start.1 = (bf16[128,128]{1,0:T(8,128)(2,1)S(1)}, bf16[128,128]{1,0:T(8,128)(2,1)}, u32[]{:S(2)}) copy-start(bf16[128,128]{1,0:T(8,128)(2,1)} %param.11) | copy-start | bytes 98308
  58.3 10.2 %copy-start.2 = (bf16[128,640]{1,0:T(8,128)(2,1)S(1)}, bf16[128,640]{1,0:T(8,128)(2,1)}, u32[]{:S(2)}) copy-start(bf16[128,640]{1,0:T(8,128)(2,1)} %constant.53) | copy-start | bytes 491524
  58.3 10.5 %copy-start.4 = (bf16[96,640]{1,0:T(8,128)(2,1)S(1)}, bf16[96,640]{1,0:T(8,128)(2,1)}, u32[]{:S(2)}) copy-start(bf16[96,640]{1,0:T(8,128)(2,1)} %constant.54) | copy-start | bytes 368644
  58.3 10.9 %copy-start.3 = (bf16[96,640]{1,0:T(8,128)(2,1)S(1)}, bf16[96,640]{1,0:T(8,128)(2,1)}, u32[]{:S(2)}) copy-start(bf16[96,640]{1,0:T(8,128)(2,1)} %constant.52) | copy-start | bytes 368644
  64.0 4.8 %collective-permute-start.3 = (bf16[320,96]{1,0:T(8,128)(2,1)S(1)}, bf16[320,96]{1,0:T(8,128)(2,1)S(1)}, u32[]{:S(2)}, u32[]{:S(2)}) collective-permute-start(bf16[320,96]{1,0:T(8,128)(2,1)S(1)} %get-tuple-element.14), channel_id=1, source_target_pairs={{1,0},{3,2},{5,4},{7,6},{9,8},{11,10},{13,12},{15,14},{17,16},{19,... | collective-permute-start | bytes 184328 | tf_op jit(solution)/shard_map/ppermute | solution.py:22
  65.3 3.9 %collective-permute-start.2 = (bf16[320,96]{1,0:T(8,128)(2,1)S(1)}, bf16[320,96]{1,0:T(8,128)(2,1)S(1)}, u32[]{:S(2)}, u32[]{:S(2)}) collective-permute-start(bf16[320,96]{1,0:T(8,128)(2,1)S(1)} %get-tuple-element.13), channel_id=1, source_target_pairs={{0,1},{2,3},{4,5},{6,7},{8,9},{10,11},{12,13},{14,15},{16,17},{18,... | collective-permute-start | bytes 184328 | tf_op jit(solution)/shard_map/ppermute | solution.py:19
  80.7 0.9 %copy-start = (bf16[256,320]{1,0:T(8,128)(2,1)S(1)}, bf16[256,320]{1,0:T(8,128)(2,1)}, u32[]{:S(2)}) copy-start(bf16[256,320]{1,0:T(8,128)(2,1)} %constant.45.clone) | copy-start | bytes 491524
  83.1 1.4 %copy-start.5 = (bf16[320,128]{1,0:T(8,128)(2,1)S(1)}, bf16[320,128]{1,0:T(8,128)(2,1)}, u32[]{:S(2)}) copy-start(bf16[320,128]{1,0:T(8,128)(2,1)} %constant.55) | copy-start | bytes 245764
  83.2 1.8 %copy-start.6 = (bf16[320,128]{1,0:T(8,128)(2,1)S(1)}, bf16[320,128]{1,0:T(8,128)(2,1)}, u32[]{:S(2)}) copy-start(bf16[320,128]{1,0:T(8,128)(2,1)} %constant.56) | copy-start | bytes 245764
where the time goes:
time: 86.9 us; the launch traced here: 86.4 us
  blocking collectives  34.5 us (40%)
  local copies, waits for them, and re-layouts  13.9 us (16%)
  matrix products  13.7 us (16%)
  other arithmetic  11.3 us (13%)
  starting transfers between devices  10.6 us (12%)
  between operations  2.18 us (3%)
    all_gather x1, blocking collectives, body(): gathered = lax.all_gather(packed, 'orient', axis=0, tiled=True)  34.5 us
    gather x2, local copies, waits for them, and re-layouts, chunk_stats(): weight = jnp.take(ctf, chunk_ids, axis=0).transpose(1, 0, 2)  10.3 us
    another operation x3, other arithmetic, chunk_stats(): prod = jnp.stack([prod_real, prod_imag], axis=1).reshape(n, 2 * count * n)  9.55 us
    dot_general x1, matrix products, chunk_stats(): jnp.einsum('pk,kov->pov', temp_cols, part, preferred_element_type=f32)  8.81 us
    ppermute x2, starting transfers between devices, extended(): lax.ppermute(lax.slice_in_dim(block, block.shape[dim] - width, None, axis...  8.05 us
    dot_general x6, matrix products, matmul(): return jnp.dot(left, right, preferred_element_type=jnp.float32)  4.91 us
    ppermute x2, starting transfers between devices, extended(): lax.ppermute(lax.slice_in_dim(block, 0, width, axis=dim), axis, backward)  2.58 us
  transfers between devices with their start and end apart: 4, of which 1 were waited for; matrix products, arithmetic and copies ran while one was open for 24% of the time, Pallas kernels for 0%

commit v1 on v0

--- a/solution.py
+++ b/solution.py
@@ -38,6 +38,19 @@
     return jnp.dot(left, right, preferred_element_type=jnp.float32)
 
 
+def gather_orient(block):
+    size = lax.axis_size("orient")
+    index = lax.axis_index("orient")
+    step = 1
+    while step < size:
+        pairs = [(i, i ^ step) for i in range(size) if (i ^ step) < size]
+        other = lax.ppermute(block, "orient", pairs)
+        low_side = (index // step) % 2 == 0
+        block = jnp.where(low_side, jnp.concatenate([block, other], 0), jnp.concatenate([other, block], 0))
+        step *= 2
+    return block
+
+
 def body(micrograph, templates, defocus, ctf, usable):
     bf16 = jnp.bfloat16
     f32 = jnp.float32
@@ -50,51 +63,55 @@
     cos_np, sin_np = twiddles(n)
 
     shifted = (np.arange(box_size) - box_size // 2) % n
-    temp_rows = jnp.asarray(np.concatenate([cos_np[shifted, :], -sin_np[shifted, :]], axis=1))
-    temp_cols = jnp.asarray(np.concatenate([cos_np[:, shifted], sin_np[:, shifted]], axis=0))
-    half_mat = jnp.asarray(np.concatenate([cos_np, -sin_np], axis=1))
-    spec_mat = jnp.asarray(np.concatenate([cos_np, sin_np], axis=0))
-    row_mat = jnp.asarray(
-        np.concatenate([cos_np[margin : margin + tile_width], sin_np[margin : margin + tile_width]], axis=0)
-    )
-    col_mat = jnp.asarray(
-        np.concatenate([cos_np[:, margin : margin + tile_width], -sin_np[:, margin : margin + tile_width]], axis=0)
-    )
+    cos_full = jnp.asarray(cos_np)
+    sin_full = jnp.asarray(sin_np)
+    cos_rows = jnp.asarray(cos_np[shifted, :])
+    sin_rows = jnp.asarray(sin_np[shifted, :])
+    row_cos = jnp.asarray(cos_np[margin : margin + tile_width])
+    row_sin = jnp.asarray(sin_np[margin : margin + tile_width])
 
     local_count = templates.shape[0]
-    id_row = jnp.broadcast_to(defocus.astype(bf16)[:, None, None], (local_count, 1, box_size))
-    packed = jnp.concatenate([templates, id_row], axis=1)
-    gathered = lax.all_gather(packed, "orient", axis=0, tiled=True)
-    all_templates = gathered[:, :box_size, :]
-    all_ids = gathered[:, box_size, 0].astype(jnp.int32)
-    total = all_templates.shape[0]
+    flat_size = box_size * box_size
+    id_block = jnp.broadcast_to(defocus.astype(bf16)[:, None], (local_count, 128))
+    packed = jnp.concatenate([templates.reshape(local_count, flat_size), id_block], axis=1)
+    gathered = gather_orient(packed)
+    total = gathered.shape[0]
+    all_templates = gathered[:, :flat_size].reshape(total, box_size, box_size)
+    all_ids = gathered[:, flat_size].astype(jnp.int32)
 
     padded = extended(micrograph, (("orient", 0), ("tile", 1)), margin)
-    half = matmul(padded, half_mat).astype(bf16)
-    spec_full = matmul(spec_mat, half)
-    spec_real = (spec_full[:n, :n] + spec_full[n:, n:]).astype(bf16).astype(f32)
-    spec_imag = (spec_full[:n, n:] - spec_full[n:, :n]).astype(bf16).astype(f32)
+    half_real = matmul(padded, cos_full).astype(bf16)
+    half_imag = (-matmul(padded, sin_full)).astype(bf16)
+    spec_real = (matmul(cos_full, half_real) + matmul(sin_full, half_imag)).astype(bf16).astype(f32)
+    spec_imag = (matmul(cos_full, half_imag) - matmul(sin_full, half_real)).astype(bf16).astype(f32)
 
     def chunk_stats(chunk_templates, chunk_ids):
-        count = chunk_templates.shape[0]
-        part = jnp.einsum("okj,jv->kov", chunk_templates, temp_rows, preferred_element_type=f32).astype(bf16)
-        full = jnp.einsum("pk,kov->pov", temp_cols, part, preferred_element_type=f32)
-        full_real = full[:n, :, :n] + full[n:, :, n:]
-        full_imag = full[:n, :, n:] - full[n:, :, :n]
-        weight = jnp.take(ctf, chunk_ids, axis=0).transpose(1, 0, 2)
+        part_real = jnp.einsum("okj,jq->okq", chunk_templates, cos_rows, preferred_element_type=f32).astype(bf16)
+        part_imag = (-jnp.einsum("okj,jq->okq", chunk_templates, sin_rows, preferred_element_type=f32)).astype(bf16)
+        full_real = jnp.einsum("kp,okq->opq", cos_rows, part_real, preferred_element_type=f32) + jnp.einsum(
+            "kp,okq->opq", sin_rows, part_imag, preferred_element_type=f32
+        )
+        full_imag = jnp.einsum("kp,okq->opq", cos_rows, part_imag, preferred_element_type=f32) - jnp.einsum(
+            "kp,okq->opq", sin_rows, part_real, preferred_element_type=f32
+        )
+        weight = jnp.take(ctf, chunk_ids, axis=0)
         w_real = (full_real * weight).astype(bf16).astype(f32)
         w_imag = (full_imag * weight).astype(bf16).astype(f32)
-        s_real = spec_real[:, None, :]
-        s_imag = spec_imag[:, None, :]
-        prod_real = (s_real * w_real + s_imag * w_imag).astype(bf16)
-        prod_imag = (s_imag * w_real - s_real * w_imag).astype(bf16)
-        prod = jnp.stack([prod_real, prod_imag], axis=1).reshape(n, 2 * count * n)
-        left = matmul(row_mat, prod).reshape(2 * tile_width, 2, count, n)
-        left_real = (left[:tile_width, 0] - left[tile_width:, 1]).astype(bf16)
-        left_imag = (left[:tile_width, 1] + left[tile_width:, 0]).astype(bf16)
-        stacked = jnp.concatenate([left_real, left_imag], axis=-1).reshape(tile_width * count, 2 * n)
-        corr = (matmul(stacked, col_mat) * scaling).reshape(tile_width, count, tile_width)
-        return (jnp.max(corr, axis=1), jnp.sum(corr, axis=1), jnp.sum(corr * corr, axis=1))
+        prod_real = (spec_real * w_real + spec_imag * w_imag).astype(bf16)
+        prod_imag = (spec_imag * w_real - spec_real * w_imag).astype(bf16)
+        left_real = (
+            jnp.einsum("rp,opq->orq", row_cos, prod_real, preferred_element_type=f32)
+            - jnp.einsum("rp,opq->orq", row_sin, prod_imag, preferred_element_type=f32)
+        ).astype(bf16)
+        left_imag = (
+            jnp.einsum("rp,opq->orq", row_cos, prod_imag, preferred_element_type=f32)
+            + jnp.einsum("rp,opq->orq", row_sin, prod_real, preferred_element_type=f32)
+        ).astype(bf16)
+        corr = jnp.einsum("orq,cq->orc", left_real, row_cos, preferred_element_type=f32) - jnp.einsum(
+            "orq,cq->orc", left_imag, row_sin, preferred_element_type=f32
+        )
+        corr = corr * scaling
+        return (jnp.max(corr, axis=0), jnp.sum(corr, axis=0), jnp.sum(corr * corr, axis=0))
 
     chunk = min(CHUNK, total)
     n_chunks = total // chunk

time: 86.9 us -> 73.9 us (0.85)
  blocking collectives: 34.5 us -> 0 us
  waiting for transfers between devices: 0.2 us -> 16.9 us
  other arithmetic: 11.3 us -> 2.74 us
  matrix products: 13.7 us -> 20.9 us
  starting transfers between devices: 10.6 us -> 15 us
  local copies, waits for them, and re-layouts: 13.9 us -> 15.4 us
    all_gather x1 -> x0, blocking collectives: 34.5 us -> none  [body(): gathered = lax.all_gather(packed, 'orient', axis=0, tiled=True)]
    ppermute x0 -> x3, waiting for transfers between devices: none -> 13 us  [gather_orient(): other = lax.ppermute(block, 'orient', pairs)]
    another operation x3 -> x0, other arithmetic: 9.55 us -> none  [chunk_stats(): prod = jnp.stack([prod_real, prod_imag], axis=1).reshape(n, 2 * count * n)]
    dot_general x1 -> x10, matrix products: 8.81 us -> 17.4 us  [the longest x1 4.22 us: chunk_stats(): jnp.einsum('orq,cq->orc', left_real, row_cos, preferred_element_type=f32)]
    ppermute x0 -> x3, starting transfers between devices: none -> 7.3 us  [gather_orient(): other = lax.ppermute(block, 'orient', pairs)]
    ppermute x2, waiting for transfers between devices: 0.01 us -> 3.92 us  [extended(): lax.ppermute(lax.slice_in_dim(block, 0, width, axis=dim), axis, backward)]
    ppermute x2, starting transfers between devices: 8.05 us -> 4.94 us  [extended(): lax.ppermute(lax.slice_in_dim(block, block.shape[dim] - width, None, axis...]
    reshape x0 -> x2, local copies, waits for them, and re-layouts: none -> 1.99 us  [the longest x1 1.09 us: body(): templates.reshape(local_count, flat_size)]
  transfers between devices with their start and end apart: 4 -> 7, of which waited for: 1 -> 3; matrix products, arithmetic and copies ran while one was open for 24% -> 8% of each run, Pallas kernels for 0% -> 0%
where the time goes in v1:
time: 73.9 us; the launch traced here: 73.4 us
  matrix products  20.9 us (28%)
  waiting for transfers between devices  16.9 us (23%)
  local copies, waits for them, and re-layouts  15.4 us (21%)
  starting transfers between devices  15 us (20%)
  other arithmetic  2.74 us (4%)
  between operations  2.38 us (3%)
    ppermute x3, waiting for transfers between devices, gather_orient(): other = lax.ppermute(block, 'orient', pairs)  13 us
    gather x2, local copies, waits for them, and re-layouts, chunk_stats(): weight = jnp.take(ctf, chunk_ids, axis=0)  10.3 us
    ppermute x3, starting transfers between devices, gather_orient(): other = lax.ppermute(block, 'orient', pairs)  7.3 us
    ppermute x2, starting transfers between devices, extended(): lax.ppermute(lax.slice_in_dim(block, block.shape[dim] - width, None, axis...  4.94 us
    dot_general x1, matrix products, chunk_stats(): jnp.einsum('orq,cq->orc', left_real, row_cos, preferred_element_type=f32)  4.22 us
    ppermute x2, waiting for transfers between devices, extended(): lax.ppermute(lax.slice_in_dim(block, 0, width, axis=dim), axis, backward)  3.92 us
    dot_general x10, matrix products, matmul(): return jnp.dot(left, right, preferred_element_type=jnp.float32)  3.56 us
    dot_general x1, matrix products, chunk_stats(): jnp.einsum('orq,cq->orc', left_imag, row_sin, preferred_element_type=f32)  3.56 us
  transfers between devices with their start and end apart: 7, of which 3 were waited for; matrix products, arithmetic and copies ran while one was open for 8% of the time, Pallas kernels for 0%

profile of v1, /device:TPU:0, one launch (start us, length us, event | category | flops | bytes accessed | tf_op | source)
XLA Modules:
  0.0 73.4 jit_solution(8945686998190759338)
XLA Ops:
  0.7 1.1 %reshape.27 = bf16[1,36864]{1,0:T(2,128)(2,1)S(1)} reshape(bf16[1,192,192]{2,1,0:T(8,128)(2,1)} %param.12) | data formatting | bytes 147456 | tf_op jit(solution)/shard_map/reshape | solution.py:76
  2.6 3.0 %collective-permute-start.4 = (bf16[1,36992]{1,0:T(2,128)(2,1)S(1)}, bf16[1,36992]{1,0:T(2,128)(2,1)S(1)}, u32[]{:S(2)}, u32[]{:S(2)}) collective-permute-start(bf16[1,36992]{1,0:T(2,128)(2,1)S(1)} %concatenate.29), channel_id=1, source_target_pairs={{0,2},{2,0},{4,6},{6,4},{8,10},{10,8},{12,14},{14,12},{1,3},{3,1},... | collective-permute-start | bytes 221960 | tf_op jit(solution)/shard_map/ppermute | solution.py:47
  6.4 1.9 %collective-permute-start = (bf16[96,128]{1,0:T(8,128)(2,1)S(1)}, bf16[96,128]{1,0:T(8,128)(2,1)S(1)}, u32[]{:S(2)}, u32[]{:S(2)}) collective-permute-start(bf16[96,128]{1,0:T(8,128)(2,1)S(1)} %get-tuple-element.9), channel_id=1, source_target_pairs={{0,2},{2,4},{4,6},{6,8},{8,10},{10,12},{12,14},{1,3},{3,5},{5,7},{... | collective-permute-start | bytes 73736 | tf_op jit(solution)/shard_map/ppermute | solution.py:19
  8.3 1.3 %collective-permute-start.1 = (bf16[96,128]{1,0:T(8,128)(2,1)S(1)}, bf16[96,128]{1,0:T(8,128)(2,1)S(1)}, u32[]{:S(2)}, u32[]{:S(2)}) collective-permute-start(bf16[96,128]{1,0:T(8,128)(2,1)S(1)} %get-tuple-element.8), channel_id=1, source_target_pairs={{2,0},{4,2},{6,4},{8,6},{10,8},{12,10},{14,12},{3,1},{5,3},{7,5},{... | collective-permute-start | bytes 73736 | tf_op jit(solution)/shard_map/ppermute | solution.py:22
  11.1 3.9 %collective-permute-done.1 = bf16[96,128]{1,0:T(8,128)(2,1)S(1)} collective-permute-done((bf16[96,128]{1,0:T(8,128)(2,1)S(1)}, bf16[96,128]{1,0:T(8,128)(2,1)S(1)}, u32[]{:S(2)}, u32[]{:S(2)}) %collective-permute-start.1) | collective-permute-done | bytes 24608 | tf_op jit(solution)/shard_map/ppermute | solution.py:22
  15.2 1.4 %collective-permute-start.3 = (bf16[320,96]{1,0:T(8,128)(2,1)S(1)}, bf16[320,96]{1,0:T(8,128)(2,1)S(1)}, u32[]{:S(2)}, u32[]{:S(2)}) collective-permute-start(bf16[320,96]{1,0:T(8,128)(2,1)S(1)} %get-tuple-element.7), channel_id=1, source_target_pairs={{1,0},{3,2},{5,4},{7,6},{9,8},{11,10},{13,12},{15,14},{17,16},{19,... | collective-permute-start | bytes 184328 | tf_op jit(solution)/shard_map/ppermute | solution.py:22
  16.6 3.0 %collective-permute-start.2 = (bf16[320,96]{1,0:T(8,128)(2,1)S(1)}, bf16[320,96]{1,0:T(8,128)(2,1)S(1)}, u32[]{:S(2)}, u32[]{:S(2)}) collective-permute-start(bf16[320,96]{1,0:T(8,128)(2,1)S(1)} %get-tuple-element.6), channel_id=1, source_target_pairs={{0,1},{2,3},{4,5},{6,7},{8,9},{10,11},{12,13},{14,15},{16,17},{18,... | collective-permute-start | bytes 184328 | tf_op jit(solution)/shard_map/ppermute | solution.py:19
  19.6 1.1 %fusion.42 = f32[320,320]{1,0:T(8,128)S(1)} fusion(bf16[320,128]{1,0:T(8,128)(2,1)S(1)} %constant_dynamic-update-slice_fusion, bf16[128,320]{0,1:T(8,128)(2,1)} %constant.102.clone), kind=kOutput, calls=%fused_computation.62 | convolution fusion | flops 26214400 | bytes 573440 | tf_op jit(solution)/shard_map/dot_general | solution.py:38
  21.7 1.6 %collective-permute-start.5 = (bf16[2,36992]{1,0:T(2,128)(2,1)S(1)}, bf16[2,36992]{1,0:T(2,128)(2,1)S(1)}, u32[]{:S(2)}, u32[]{:S(2)}) collective-permute-start(bf16[2,36992]{1,0:T(2,128)(2,1)S(1)} %broadcast_select_fusion), channel_id=1, source_target_pairs={{0,4},{2,6},{4,0},{6,2},{8,12},{10,14},{12,8},{14,10},{1,5},{3,7},... | collective-permute-start | bytes 443912 | tf_op jit(solution)/shard_map/ppermute | solution.py:47
  25.0 1.9 %collective-permute-done.5 = bf16[2,36992]{1,0:T(2,128)(2,1)S(1)} collective-permute-done((bf16[2,36992]{1,0:T(2,128)(2,1)S(1)}, bf16[2,36992]{1,0:T(2,128)(2,1)S(1)}, u32[]{:S(2)}, u32[]{:S(2)}) %collective-permute-start.5) | collective-permute-done | bytes 148000 | tf_op jit(solution)/shard_map/ppermute | solution.py:47
  27.5 2.7 %collective-permute-start.6 = (bf16[4,36992]{1,0:T(4,128)(2,1)S(1)}, bf16[4,36992]{1,0:T(4,128)(2,1)S(1)}, u32[]{:S(2)}, u32[]{:S(2)}) collective-permute-start(bf16[4,36992]{1,0:T(4,128)(2,1)S(1)} %maximum_select_fusion.1), channel_id=1, source_target_pairs={{0,8},{2,10},{4,12},{6,14},{8,0},{10,2},{12,4},{14,6},{1,9},{3,11}... | collective-permute-start | bytes 887816 | tf_op jit(solution)/shard_map/ppermute | solution.py:47
  30.9 11.1 %collective-permute-done.6 = bf16[4,36992]{1,0:T(4,128)(2,1)S(1)} collective-permute-done((bf16[4,36992]{1,0:T(4,128)(2,1)S(1)}, bf16[4,36992]{1,0:T(4,128)(2,1)S(1)}, u32[]{:S(2)}, u32[]{:S(2)}) %collective-permute-start.6) | collective-permute-done | bytes 295968 | tf_op jit(solution)/shard_map/ppermute | solution.py:47
  42.8 4.8 %gather_fusion = f32[8,320,320]{2,1,0:T(8,128)} fusion(f32[8,320,320]{2,1,0:T(8,128)} %param.14, s32[1024]{0:T(1024)S(1)} %pad_clamp_fusion), kind=kCustom, calls=%fused_computation | custom fusion | bytes 6553632 | tf_op jit(solution)/shard_map/jit(_take)/gather | solution.py:97
  47.5 5.5 %copy.20 = f32[8,320,320]{1,2,0:T(8,128)} copy(f32[8,320,320]{2,1,0:T(8,128)} %gather_fusion) | data formatting | bytes 6553600 | tf_op jit(solution)/shard_map/jit(_take)/gather | solution.py:97
  53.0 0.9 %reshape.28 = bf16[8,192,192]{2,1,0:T(8,128)(2,1)S(1)} reshape(bf16[8,36864]{1,0:T(8,128)(2,1)S(1)} %slice.34) | data formatting | bytes 1179648 | tf_op jit(solution)/shard_map/reshape | solution.py:79
  55.1 0.9 %fusion.49 = f32[8,320,320]{2,1,0:T(8,128)S(1)} fusion(bf16[8,192,320]{2,1,0:T(8,128)(2,1)S(1)} %negate_convert_fusion, bf16[192,320,1]{1,0,2:T(8,128)(2,1)S(1)} %copy-done.2), kind=kOutput, calls=%fused_computation.69 | convolution fusion | flops 314572800 | bytes 4382720 | tf_op jit(solution)/shard_map/kp,okq->opq/dot_general | solution.py:94
  56.0 0.9 %fusion.47 = f32[8,320,320]{2,1,0:T(8,128)S(1)} fusion(bf16[8,192,320]{2,1,0:T(8,128)(2,1)S(1)} %convolution_convert_fusion, bf16[192,320,1]{1,0,2:T(8,128)(2,1)S(1)} %copy-done.2), kind=kOutput, calls=%fused_computation.67 | convolution fusion | flops 314572800 | bytes 4382720 | tf_op jit(solution)/shard_map/kp,okq->opq/dot_general | solution.py:91
  56.9 1.2 %copy-done = f32[8,320,320]{1,2,0:T(8,128)S(1)} copy-done((f32[8,320,320]{1,2,0:T(8,128)S(1)}, f32[8,320,320]{1,2,0:T(8,128)}, u32[]{:S(2)}) %copy-start) | copy-done | bytes 3276824
  58.1 1.3 %fusion.4 = bf16[8,320,320]{1,2,0:T(8,128)(2,1)S(1)} fusion(f32[8,320,320]{2,1,0:T(8,128)S(1)} %fusion.49, f32[8,320,320]{1,2,0:T(8,128)S(1)} %copy-done, bf16[8,192,320]{2,1,0:T(8,128)(2,1)S(1)} %convolution_convert_fusion, bf16[192,320,1]{1,0,2:T(8,128)(2,1)S(1)} %copy-done.3, pred[8]{0:T(512)(128)(4,1)S(1)} %fusion.29), kind=kOutput, calls=%fused_computation.10 | convolution fusion | flops 317849600 | bytes 9297928 | tf_op jit(solution)/shard_map/kp,okq->opq/dot_general | solution.py:94
  59.4 1.3 %fusion.5 = bf16[8,320,320]{1,2,0:T(8,128)(2,1)S(1)} fusion(f32[8,320,320]{2,1,0:T(8,128)S(1)} %fusion.47, f32[8,320,320]{1,2,0:T(8,128)S(1)} %copy-done, bf16[8,192,320]{2,1,0:T(8,128)(2,1)S(1)} %negate_convert_fusion, bf16[192,320,1]{1,0,2:T(8,128)(2,1)S(1)} %copy-done.3, pred[8]{0:T(512)(128)(4,1)S(1)} %fusion.29), kind=kOutput, calls=%fused_computation.12 | convolution fusion | flops 317849600 | bytes 9297928 | tf_op jit(solution)/shard_map/kp,okq->opq/dot_general | solution.py:91
  60.7 2.0 %fusion.30 = f32[8,320,128]{2,1,0:T(8,128)} fusion(bf16[128,320,1]{0,1,2:T(8,128)(2,1)S(1)} %copy-done.6, bf16[8,320,320]{1,2,0:T(8,128)(2,1)S(1)} %fusion.5, bf16[8,320,320]{1,2,0:T(8,128)(2,1)S(1)} %fusion.4, f32[320,320]{0,1:T(8,128)S(1)} %fusion.22, f32[320,320]{0,1:T(8,128)S(1)} %fusion.19), kind=kOutput, calls=%fused_computation.58 | convolution fusion | flops 214630400 | bytes 5488640 | tf_op jit(solution)/shard_map/rp,opq->orq/dot_general | solution.py:107
  62.8 2.0 %fusion.36 = f32[8,320,128]{2,1,0:T(8,128)} fusion(bf16[128,320,1]{0,1,2:T(8,128)(2,1)S(1)} %copy-done.6, bf16[8,320,320]{1,2,0:T(8,128)(2,1)S(1)} %fusion.5, bf16[8,320,320]{1,2,0:T(8,128)(2,1)S(1)} %fusion.4, f32[320,320]{0,1:T(8,128)S(1)} %fusion.22, f32[320,320]{0,1:T(8,128)S(1)} %fusion.19), kind=kOutput, calls=%fused_computation.59 | convolution fusion | flops 214630400 | bytes 5488640 | tf_op jit(solution)/shard_map/rp,opq->orq/dot_general | solution.py:103
  64.8 4.2 %fusion.10 = f32[8,128,128]{2,1,0:T(8,128)} fusion(bf16[128,320,1]{0,1,2:T(8,128)(2,1)S(1)} %copy-done.6, f32[8,320,128]{2,1,0:T(8,128)} %fusion.36, bf16[128,320,1]{0,1,2:T(8,128)(2,1)S(1)} %copy-done.8, bf16[8,320,320]{1,2,0:T(8,128)(2,1)} %copy-done.1, bf16[8,320,320]{1,2,0:T(8,128)(2,1)S(1)} %fusion.4, f32[320,320]{0,1:T(8,128)S(1)} %fusion.22, ...), kind=kOutput, calls=%fused_computation.21 | convolution fusion | flops 299171840 | bytes 6094848 | tf_op jit(solution)/shard_map/orq,cq->orc/dot_general | solution.py:110
  69.0 3.6 %multiply_reduce_fusion = (f32[128,128]{1,0:T(8,128)S(1)}, f32[128,128]{1,0:T(8,128)S(1)}, f32[128,128]{1,0:T(8,128)S(1)}) fusion(f32[8,128,128]{2,1,0:T(8,128)} %fusion.10, bf16[128,320,1]{0,1,2:T(8,128)(2,1)S(1)} %copy-done.8, f32[8,320,128]{2,1,0:T(8,128)} %fusion.30, bf16[8,320,320]{1,2,0:T(8,128)(2,1)} %copy-done.1, ...), kind=kOutput, calls=%fused_computation.41 | convolution fusion | flops 299909120 | bytes 6209536 | tf_op jit(solution)/shard_map/orq,cq->orc/dot_general | solution.py:110
  (55 shorter events, 8.3 us)
Async XLA Ops:
  0.6 20.1 %copy-start.7 = (bf16[128,320]{0,1:T(8,128)(2,1)S(1)}, bf16[128,320]{0,1:T(8,128)(2,1)}, u32[]{:S(2)}) copy-start(bf16[128,320]{0,1:T(8,128)(2,1)} %constant.103.clone) | copy-start | bytes 245764
  0.6 22.7 %copy-start.10 = (bf16[96,320]{1,0:T(8,128)(2,1)S(1)}, bf16[96,320]{1,0:T(8,128)(2,1)}, u32[]{:S(2)}) copy-start(bf16[96,320]{1,0:T(8,128)(2,1)} %constant.111) | copy-start | bytes 184324
  0.7 22.9 %copy-start.12 = (bf16[96,320]{1,0:T(8,128)(2,1)S(1)}, bf16[96,320]{1,0:T(8,128)(2,1)}, u32[]{:S(2)}) copy-start(bf16[96,320]{1,0:T(8,128)(2,1)} %constant.109) | copy-start | bytes 184324
  2.6 18.4 %collective-permute-start.4 = (bf16[1,36992]{1,0:T(2,128)(2,1)S(1)}, bf16[1,36992]{1,0:T(2,128)(2,1)S(1)}, u32[]{:S(2)}, u32[]{:S(2)}) collective-permute-start(bf16[1,36992]{1,0:T(2,128)(2,1)S(1)} %concatenate.29), channel_id=1, source_target_pairs={{0,2},{2,0},{4,6},{6,4},{8,10},{10,8},{12,14},{14,12},{1,3},{3,1},... | collective-permute-start | bytes 221960 | tf_op jit(solution)/shard_map/ppermute | solution.py:47
  6.4 3.9 %collective-permute-start = (bf16[96,128]{1,0:T(8,128)(2,1)S(1)}, bf16[96,128]{1,0:T(8,128)(2,1)S(1)}, u32[]{:S(2)}, u32[]{:S(2)}) collective-permute-start(bf16[96,128]{1,0:T(8,128)(2,1)S(1)} %get-tuple-element.9), channel_id=1, source_target_pairs={{0,2},{2,4},{4,6},{6,8},{8,10},{10,12},{12,14},{1,3},{3,5},{5,7},{... | collective-permute-start | bytes 73736 | tf_op jit(solution)/shard_map/ppermute | solution.py:19
  8.3 6.7 %collective-permute-start.1 = (bf16[96,128]{1,0:T(8,128)(2,1)S(1)}, bf16[96,128]{1,0:T(8,128)(2,1)S(1)}, u32[]{:S(2)}, u32[]{:S(2)}) collective-permute-start(bf16[96,128]{1,0:T(8,128)(2,1)S(1)} %get-tuple-element.8), channel_id=1, source_target_pairs={{2,0},{4,2},{6,4},{8,6},{10,8},{12,10},{14,12},{3,1},{5,3},{7,5},{... | collective-permute-start | bytes 73736 | tf_op jit(solution)/shard_map/ppermute | solution.py:22
  15.2 8.6 %copy-start.5 = (bf16[320,320]{1,0:T(8,128)(2,1)S(1)}, bf16[320,320]{1,0:T(8,128)(2,1)}, u32[]{:S(2)}) copy-start(bf16[320,320]{1,0:T(8,128)(2,1)} %constant.98.clone) | copy-start | bytes 614404
  15.2 8.2 %collective-permute-start.3 = (bf16[320,96]{1,0:T(8,128)(2,1)S(1)}, bf16[320,96]{1,0:T(8,128)(2,1)S(1)}, u32[]{:S(2)}, u32[]{:S(2)}) collective-permute-start(bf16[320,96]{1,0:T(8,128)(2,1)S(1)} %get-tuple-element.7), channel_id=1, source_target_pairs={{1,0},{3,2},{5,4},{7,6},{9,8},{11,10},{13,12},{15,14},{17,16},{19,... | collective-permute-start | bytes 184328 | tf_op jit(solution)/shard_map/ppermute | solution.py:22
  16.6 7.0 %collective-permute-start.2 = (bf16[320,96]{1,0:T(8,128)(2,1)S(1)}, bf16[320,96]{1,0:T(8,128)(2,1)S(1)}, u32[]{:S(2)}, u32[]{:S(2)}) collective-permute-start(bf16[320,96]{1,0:T(8,128)(2,1)S(1)} %get-tuple-element.6), channel_id=1, source_target_pairs={{0,1},{2,3},{4,5},{6,7},{8,9},{10,11},{12,13},{14,15},{16,17},{18,... | collective-permute-start | bytes 184328 | tf_op jit(solution)/shard_map/ppermute | solution.py:19
  20.8 3.4 %copy-start.9 = (bf16[96,320]{1,0:T(8,128)(2,1)S(1)}, bf16[96,320]{1,0:T(8,128)(2,1)}, u32[]{:S(2)}) copy-start(bf16[96,320]{1,0:T(8,128)(2,1)} %constant.114) | copy-start | bytes 184324
  21.0 3.4 %copy-start.11 = (bf16[96,320]{1,0:T(8,128)(2,1)S(1)}, bf16[96,320]{1,0:T(8,128)(2,1)}, u32[]{:S(2)}) copy-start(bf16[96,320]{1,0:T(8,128)(2,1)} %constant.112) | copy-start | bytes 184324
  21.7 5.2 %collective-permute-start.5 = (bf16[2,36992]{1,0:T(2,128)(2,1)S(1)}, bf16[2,36992]{1,0:T(2,128)(2,1)S(1)}, u32[]{:S(2)}, u32[]{:S(2)}) collective-permute-start(bf16[2,36992]{1,0:T(2,128)(2,1)S(1)} %broadcast_select_fusion), channel_id=1, source_target_pairs={{0,4},{2,6},{4,0},{6,2},{8,12},{10,14},{12,8},{14,10},{1,5},{3,7},... | collective-permute-start | bytes 443912 | tf_op jit(solution)/shard_map/ppermute | solution.py:47
  23.5 1.1 %copy-start.4 = (bf16[320,320]{1,0:T(8,128)(2,1)S(1)}, bf16[320,320]{1,0:T(8,128)(2,1)}, u32[]{:S(2)}) copy-start(bf16[320,320]{1,0:T(8,128)(2,1)} %constant.99.clone) | copy-start | bytes 614404
  27.5 14.5 %collective-permute-start.6 = (bf16[4,36992]{1,0:T(4,128)(2,1)S(1)}, bf16[4,36992]{1,0:T(4,128)(2,1)S(1)}, u32[]{:S(2)}, u32[]{:S(2)}) collective-permute-start(bf16[4,36992]{1,0:T(4,128)(2,1)S(1)} %maximum_select_fusion.1), channel_id=1, source_target_pairs={{0,8},{2,10},{4,12},{6,14},{8,0},{10,2},{12,4},{14,6},{1,9},{3,11}... | collective-permute-start | bytes 887816 | tf_op jit(solution)/shard_map/ppermute | solution.py:47
  47.5 6.4 %copy-start.3 = (bf16[192,320,1]{1,0,2:T(8,128)(2,1)S(1)}, bf16[192,320,1]{1,0,2:T(8,128)(2,1)}, u32[]{:S(2)}) copy-start(bf16[192,320,1]{1,0,2:T(8,128)(2,1)} %constant.116) | copy-start | bytes 368644
  53.0 1.5 %copy-start.2 = (bf16[192,320,1]{1,0,2:T(8,128)(2,1)S(1)}, bf16[192,320,1]{1,0,2:T(8,128)(2,1)}, u32[]{:S(2)}) copy-start(bf16[192,320,1]{1,0,2:T(8,128)(2,1)} %constant.115) | copy-start | bytes 368644
  56.0 2.1 %copy-start = (f32[8,320,320]{1,2,0:T(8,128)S(1)}, f32[8,320,320]{1,2,0:T(8,128)}, u32[]{:S(2)}) copy-start(f32[8,320,320]{1,2,0:T(8,128)} %copy.20) | copy-start | bytes 9830404
  59.4 1.3 %copy-start.6 = (bf16[128,320,1]{0,1,2:T(8,128)(2,1)S(1)}, bf16[128,320,1]{0,1,2:T(8,128)(2,1)}, u32[]{:S(2)}) copy-start(bf16[128,320,1]{0,1,2:T(8,128)(2,1)} %constant.117) | copy-start | bytes 245764
  60.7 2.1 %copy-start.1 = (bf16[8,320,320]{1,2,0:T(8,128)(2,1)}, bf16[8,320,320]{1,2,0:T(8,128)(2,1)S(1)}, u32[]{:S(2)}) copy-start(bf16[8,320,320]{1,2,0:T(8,128)(2,1)S(1)} %fusion.5) | copy-start | bytes 4915204
  62.8 2.1 %copy-start.8 = (bf16[128,320,1]{0,1,2:T(8,128)(2,1)S(1)}, bf16[128,320,1]{0,1,2:T(8,128)(2,1)}, u32[]{:S(2)}) copy-start(bf16[128,320,1]{0,1,2:T(8,128)(2,1)} %constant.118) | copy-start | bytes 245764

commit v2 on v1

v2 whole, which is shorter than its diff:
```python
import math

import jax
import jax.numpy as jnp
import ml_dtypes
import numpy as np
from jax import lax
from jax.sharding import PartitionSpec as P

RB = 32
CHUNK = 8


def twiddles(padded_size):
    position = np.arange(padded_size, dtype=np.int64)
    phase_index = (position[:, None] * position[None, :]) % padded_size
    angles = phase_index.astype(np.float32) * np.float32(2.0 * math.pi / padded_size)
    angles = angles.astype(np.float64)
    cosines = np.cos(angles).astype(np.float32).astype(ml_dtypes.bfloat16)
    sines = np.sin(angles).astype(np.float32).astype(ml_dtypes.bfloat16)
    return cosines, sines


def matmul(left, right):
    return jnp.dot(left, right, preferred_element_type=jnp.float32)


def halo_window(block, width):
    rows, cols = block.shape
    count_o = lax.axis_size("orient")
    count_t = lax.axis_size("tile")
    axes = ("orient", "tile")
    row_part = {-1: slice(rows - width, rows), 0: slice(0, rows), 1: slice(0, width)}
    col_part = {-1: slice(cols - width, cols), 0: slice(0, cols), 1: slice(0, width)}
    grid = []
    for d_o in (-1, 0, 1):
        line = []
        for d_t in (-1, 0, 1):
            piece = block[row_part[d_o], col_part[d_t]]
            if d_o or d_t:
                pairs = []
                for o in range(count_o):
                    for t in range(count_t):
                        so, st = o + d_o, t + d_t
                        if 0 <= so < count_o and 0 <= st < count_t:
                            pairs.append((so * count_t + st, o * count_t + t))
                piece = lax.ppermute(piece, axes, pairs)
            line.append(piece)
        grid.append(jnp.concatenate(line, axis=1))
    return jnp.concatenate(grid, axis=0)


def exchange_orient(block):
    size = lax.axis_size("orient")
    if size <= 8:
        pieces = [block]
        for shift in range(1, size):
            pieces.append(lax.ppermute(block, "orient", [(i, (i + shift) % size) for i in range(size)]))
        return jnp.concatenate(pieces, axis=0)
    step = 1
    while step < size:
        other = lax.ppermute(block, "orient", [(i, i ^ step) for i in range(size)])
        block = jnp.concatenate([block, other], axis=0)
        step *= 2
    return block


def body(micrograph, templates, defocus, ctf, usable):
    bf16 = jnp.bfloat16
    f32 = jnp.float32
    tile_width = micrograph.shape[0]
    padded_size = ctf.shape[1]
    box_size = templates.shape[1]
    margin = (padded_size - tile_width) // 2
    scaling = 1.0 / (padded_size * padded_size)
    n = padded_size
    cos_np, sin_np = twiddles(n)

    cos_full, sin_full = lax.optimization_barrier((jnp.asarray(cos_np), jnp.asarray(sin_np)))
    low = n - box_size // 2
    cos_rows = jnp.concatenate([cos_full[low:], cos_full[: box_size - (n - low)]], axis=0)
    sin_rows = jnp.concatenate([sin_full[low:], sin_full[: box_size - (n - low)]], axis=0)
    cos_cols = cos_rows.T
    sin_cols = sin_rows.T
    row_cos = cos_full[margin : margin + tile_width]
    row_sin = sin_full[margin : margin + tile_width]
    col_cos = row_cos.T
    col_sin = row_sin.T

    local_count = templates.shape[0]
    flat_size = box_size * box_size
    id_block = jnp.broadcast_to(defocus.astype(bf16)[:, None], (local_count, 128))
    packed = jnp.concatenate([templates.reshape(local_count, flat_size), id_block], axis=1)
    gathered = exchange_orient(packed)
    total = gathered.shape[0]
    all_templates = gathered[:, :flat_size].reshape(total, box_size, box_size)
    all_ids = gathered[:, flat_size].astype(jnp.int32)

    padded = halo_window(micrograph, margin)
    half_real = matmul(padded, cos_full).astype(bf16)
    half_imag = (-matmul(padded, sin_full)).astype(bf16)
    spec_real = (matmul(cos_full, half_real) + matmul(sin_full, half_imag)).astype(bf16).astype(f32)
    spec_imag = (matmul(cos_full, half_imag) - matmul(sin_full, half_real)).astype(bf16).astype(f32)
    spec_real = spec_real[:, None, :]
    spec_imag = spec_imag[:, None, :]

    def chunk_stats(chunk_templates, chunk_ids):
        count = chunk_templates.shape[0]
        stacked = jnp.transpose(chunk_templates, (1, 0, 2)).reshape(box_size * count, box_size)
        part_real = matmul(stacked, cos_rows).astype(bf16).reshape(box_size, count * n)
        part_imag = (-matmul(stacked, sin_rows)).astype(bf16).reshape(box_size, count * n)
        full_real = (matmul(cos_cols, part_real) + matmul(sin_cols, part_imag)).reshape(n, count, n)
        full_imag = (matmul(cos_cols, part_imag) - matmul(sin_cols, part_real)).reshape(n, count, n)
        weight = jnp.stack(
            [lax.dynamic_index_in_dim(ctf, chunk_ids[o], 0, keepdims=False) for o in range(count)], axis=1
        )
        w_real = (full_real * weight).astype(bf16).astype(f32)
        w_imag = (full_imag * weight).astype(bf16).astype(f32)
        prod_real = (spec_real * w_real + spec_imag * w_imag).astype(bf16).reshape(n, count * n)
        prod_imag = (spec_imag * w_real - spec_real * w_imag).astype(bf16).reshape(n, count * n)
        left_real = (matmul(row_cos, prod_real) - matmul(row_sin, prod_imag)).astype(bf16)
        left_imag = (matmul(row_cos, prod_imag) + matmul(row_sin, prod_real)).astype(bf16)
        left_real = left_real.reshape(tile_width * count, n)
        left_imag = left_imag.reshape(tile_width * count, n)
        corr = (matmul(left_real, col_cos) - matmul(left_imag, col_sin)) * scaling
        corr = corr.reshape(tile_width, count, tile_width)
        return (jnp.max(corr, axis=1), jnp.sum(corr, axis=1), jnp.sum(corr * corr, axis=1))

    chunk = min(CHUNK, total)
    n_chunks = total // chunk
    if n_chunks == 1:
        peak_map, sum_map, squares = chunk_stats(all_templates, all_ids)
    else:

        def step(index, tallies):
            start = index * chunk
            part_templates = lax.dynamic_slice_in_dim(all_templates, start, chunk, 0)
            part_ids = lax.dynamic_slice_in_dim(all_ids, start, chunk, 0)
            peak_c, sum_c, sq_c = chunk_stats(part_templates, part_ids)
            return (jnp.maximum(tallies[0], peak_c), tallies[1] + sum_c, tallies[2] + sq_c)

        shape = (tile_width, tile_width)
        initial = (jnp.full(shape, -jnp.inf, f32), jnp.zeros(shape, f32), jnp.zeros(shape, f32))
        peak_map, sum_map, squares = lax.fori_loop(0, n_chunks, step, initial)

    live = usable[0, 0]
    row_mask = (jnp.arange(tile_width, dtype=jnp.int32) < RB * live)[:, None]
    orient_count = float(total)
    peak_out = jnp.where(row_mask, peak_map, 0.0)
    mean_out = jnp.where(row_mask, sum_map / orient_count, 0.0)
    square_out = jnp.where(row_mask, squares / orient_count, 0.0)
    return (peak_out, mean_out, square_out)


def solution(mesh):
    return jax.shard_map(
        body,
        mesh=mesh,
        in_specs=(
            P(("groups", "orient"), "tile"),
            P("orient", None, None),
            P(("groups", "orient")),
            P("groups", None, None),
            P(("groups", "orient"), "tile"),
        ),
        out_specs=(
            P(("groups", "orient"), "tile"),
            P(("groups", "orient"), "tile"),
            P(("groups", "orient"), "tile"),
        ),
        check_vma=False,
    )
```

time: 73.9 us -> 154 us (2.08)
  the two profiles are of different devices: /device:TPU:0 before, /device:TPU:29 now
where the time goes in v2:
time: 154 us; the launch traced here: 152 us
  local copies, waits for them, and re-layouts  68.7 us (45%)
  starting transfers between devices  38.5 us (25%)
  matrix products  23.1 us (15%)
  between operations  17.7 us (11%)
  waiting for transfers between devices  3.27 us (2%)
    dot_general x18, matrix products, matmul(): return jnp.dot(left, right, preferred_element_type=jnp.float32)  23.1 us
    ppermute x7, starting transfers between devices, exchange_orient(): lax.ppermute(block, 'orient', [(i, (i + shift) % size) for i in range(siz...  21.3 us
    another operation x10, local copies, waits for them, and re-layouts, chunk_stats(): jnp.stack([lax.dynamic_index_in_dim(ctf, chunk_ids[o], 0, keepdims=False)...  18.8 us
    ppermute x8, starting transfers between devices, halo_window(): piece = lax.ppermute(piece, axes, pairs)  17.2 us
    mul x2, local copies, waits for them, and re-layouts, chunk_stats(): spec_real * w_real + spec_imag * w_imag  7.15 us
    mul x2, local copies, waits for them, and re-layouts, chunk_stats(): spec_imag * w_imag  7.02 us
    concatenate x1, local copies, waits for them, and re-layouts, exchange_orient(): return jnp.concatenate(pieces, axis=0)  5 us
    unnamed x32, local copies, waits for them, and re-layouts  3.6 us
  transfers between devices with their start and end apart: 15, of which 1 were waited for; matrix products, arithmetic and copies ran while one was open for 14% of the time, Pallas kernels for 0%

profile of v2, /device:TPU:29, one launch (start us, length us, event | category | flops | bytes accessed | tf_op | source)
XLA Modules:
  0.0 152.0 jit_solution(17981523044697591458)
XLA Ops:
  1.6 3.7 %collective-permute-start.7 = (bf16[96,96]{1,0:T(8,128)(2,1)S(1)}, bf16[96,96]{1,0:T(8,128)(2,1)S(1)}, u32[]{:S(2)}, u32[]{:S(2)}) collective-permute-start(bf16[96,96]{1,0:T(8,128)(2,1)S(1)} %get-tuple-element.27), channel_id=1, source_target_pairs={{3,0},{5,2},{7,4},{9,6},{11,8},{13,10},{15,12},{19,16},{21,18},{23... | collective-permute-start | bytes 55304 | tf_op jit(solution)/shard_map/ppermute | solution.py:47
  6.1 2.2 %collective-permute-start.6 = (bf16[96,128]{1,0:T(8,128)(2,1)S(1)}, bf16[96,128]{1,0:T(8,128)(2,1)S(1)}, u32[]{:S(2)}, u32[]{:S(2)}) collective-permute-start(bf16[96,128]{1,0:T(8,128)(2,1)S(1)} %get-tuple-element.29), channel_id=1, source_target_pairs={{2,0},{3,1},{4,2},{5,3},{6,4},{7,5},{8,6},{9,7},{10,8},{11,9},{12,... | collective-permute-start | bytes 73736 | tf_op jit(solution)/shard_map/ppermute | solution.py:47
  10.5 4.0 %collective-permute-start.4 = (bf16[128,96]{1,0:T(8,128)(2,1)S(1)}, bf16[128,96]{1,0:T(8,128)(2,1)S(1)}, u32[]{:S(2)}, u32[]{:S(2)}) collective-permute-start(bf16[128,96]{1,0:T(8,128)(2,1)S(1)} %get-tuple-element.31), channel_id=1, source_target_pairs={{1,0},{3,2},{5,4},{7,6},{9,8},{11,10},{13,12},{15,14},{17,16},{19,... | collective-permute-start | bytes 73736 | tf_op jit(solution)/shard_map/ppermute | solution.py:47
  24.9 3.2 %collective-permute-done = bf16[96,96]{1,0:T(8,128)(2,1)S(1)} collective-permute-done((bf16[96,96]{1,0:T(8,128)(2,1)S(1)}, bf16[96,96]{1,0:T(8,128)(2,1)S(1)}, u32[]{:S(2)}, u32[]{:S(2)}) %collective-permute-start) | collective-permute-done | bytes 18464 | tf_op jit(solution)/shard_map/ppermute | solution.py:47
  29.3 4.0 %collective-permute-start.10 = (bf16[1,36992]{1,0:T(2,128)(2,1)S(1)}, bf16[1,36992]{1,0:T(2,128)(2,1)S(1)}, u32[]{:S(2)}, u32[]{:S(2)}) collective-permute-start(bf16[1,36992]{1,0:T(2,128)(2,1)S(1)} %concatenate.29), channel_id=1, source_target_pairs={{0,6},{2,8},{4,10},{6,12},{8,14},{10,0},{12,2},{14,4},{1,7},{3,9},... | collective-permute-start | bytes 221960 | tf_op jit(solution)/shard_map/ppermute | solution.py:58
  37.6 14.7 %collective-permute-start.14 = (bf16[1,36992]{1,0:T(2,128)(2,1)S(1)}, bf16[1,36992]{1,0:T(2,128)(2,1)S(1)}, u32[]{:S(2)}, u32[]{:S(2)}) collective-permute-start(bf16[1,36992]{1,0:T(2,128)(2,1)S(1)} %concatenate.29), channel_id=1, source_target_pairs={{0,14},{2,0},{4,2},{6,4},{8,6},{10,8},{12,10},{14,12},{1,15},{3,1}... | collective-permute-start | bytes 221960 | tf_op jit(solution)/shard_map/ppermute | solution.py:58
  52.7 2.1 %mul.59 = f32[320,8,320]{2,1,0:T(8,128)} broadcast(f32[320,320]{1,0:T(8,128)S(1)} %fusion.17), dimensions={0,2} | broadcast | bytes 3686400 | tf_op jit(solution)/shard_map/mul | solution.py:119
  54.8 4.9 %mul.60 = f32[320,2560]{1,0:T(8,128)} reshape(f32[320,8,320]{2,1,0:T(8,128)} %mul.59) | data formatting | bytes 6553600 | tf_op jit(solution)/shard_map/mul | solution.py:119
  59.7 2.2 %mul.55 = f32[320,8,320]{2,1,0:T(8,128)} broadcast(f32[320,320]{1,0:T(8,128)S(1)} %fusion.15), dimensions={0,2} | broadcast | bytes 3686400 | tf_op jit(solution)/shard_map/mul | solution.py:119
  61.9 4.9 %mul.56 = f32[320,2560]{1,0:T(8,128)} reshape(f32[320,8,320]{2,1,0:T(8,128)} %mul.55) | data formatting | bytes 6553600 | tf_op jit(solution)/shard_map/mul | solution.py:119
  66.9 5.0 %concatenate.30 = bf16[8,36992]{1,0:T(8,128)(2,1)S(1)} concatenate(bf16[1,36992]{1,0:T(2,128)(2,1)S(1)} %concatenate.29, bf16[1,36992]{1,0:T(2,128)(2,1)S(1)} %collective-permute-done.8, bf16[1,36992]{1,0:T(2,128)(2,1)S(1)} %collective-permute-done.9, bf16[1,36992]{1,0:T(2,128)(2,1)S(1)} %collective-permute-done.10, bf16[1,36992]{1,0:T(2,128)(2,1)S(1)} %collective-permute-done.11, ...), dimensions={0} | concatenate | bytes 1183744 | tf_op jit(solution)/shard_map/concatenate | solution.py:59
  88.6 2.7 %constant_dynamic-slice_fusion = (f32[1,320,320]{2,1,0:T(8,128)S(1)}, f32[1,320,320]{2,1,0:T(8,128)S(1)}, f32[1,320,320]{2,1,0:T(8,128)S(1)}, f32[1,320,320]{2,1...) fusion(f32[8,320,320]{2,1,0:T(8,128)} %param.10, ...), kind=kLoop, calls=%fused_computation.56 | loop fusion | bytes 6553632 | tf_op jit(solution)/shard_map/jit(dynamic_index_in_dim)/dynamic_slice | solution.py:115
  95.7 11.3 %stack.37 = f32[320,8,320]{2,1,0:T(8,128)} concatenate(f32[320,1,320]{2,1,0:T(1,128)S(1)} %stack.29, f32[320,1,320]{2,1,0:T(1,128)S(1)} %stack.30, f32[320,1,320]{2,1,0:T(1,128)S(1)} %stack.31, f32[320,1,320]{2,1,0:T(1,128)S(1)} %stack.32, f32[320,1,320]{2,1,0:T(1,128)S(1)} %stack.33, f32[320,1,320]{2,1,0:T(1,128)S(1)} %stack.34, f32[320,1,320]{2,1,0:T(1,128)} %stack.35, ...), dimensions={1} | concatenate | bytes 6553600 | tf_op jit(solution)/shard_map/stack | solution.py:114
  107.0 3.2 %stack.38 = f32[320,2560]{1,0:T(8,128)S(1)} reshape(f32[320,8,320]{2,1,0:T(8,128)} %stack.37) | data formatting | bytes 6553600 | tf_op jit(solution)/shard_map/stack | solution.py:114
  110.3 2.9 %reshape.77 = bf16[8,192,192]{2,1,0:T(8,128)(2,1)} reshape(bf16[8,36864]{1,0:T(8,128)(2,1)} %slice.104) | data formatting | bytes 1179648 | tf_op jit(solution)/shard_map/reshape | solution.py:96
  113.2 2.8 %fusion.10 = bf16[1536,320]{0,1:T(8,128)(2,1)} fusion(bf16[192,8,192]{2,0,1:T(8,128)(2,1)} %bitcast.38, bf16[96,320]{1,0:T(8,128)(2,1)} %get-tuple-element.21, bf16[96,320]{1,0:T(8,128)(2,1)} %get-tuple-element.20), kind=kOutput, calls=%fused_computation.19 | convolution fusion | flops 189972480 | bytes 1695744 | tf_op jit(solution)/shard_map/dot_general | solution.py:25
  116.0 2.3 %copy.14 = bf16[1536,320]{1,0:T(8,128)(2,1)} copy(bf16[1536,320]{0,1:T(8,128)(2,1)} %fusion.10) | data formatting | bytes 1966080 | tf_op jit(solution)/shard_map/convert_element_type | solution.py:111
  118.4 2.7 %reshape.80 = bf16[192,2560]{1,0:T(8,128)(2,1)} reshape(bf16[1536,320]{1,0:T(8,128)(2,1)} %copy.14) | data formatting | bytes 1966080 | tf_op jit(solution)/shard_map/reshape | solution.py:111
  121.1 2.9 %convolution_convert_fusion = bf16[1536,320]{0,1:T(8,128)(2,1)} fusion(bf16[192,8,192]{2,0,1:T(8,128)(2,1)} %bitcast.39, bf16[96,320]{1,0:T(8,128)(2,1)} %get-tuple-element.43, bf16[96,320]{1,0:T(8,128)(2,1)} %get-tuple-element.44), kind=kOutput, calls=%fused_computation.20 | convolution fusion | flops 189480960 | bytes 1695744 | tf_op jit(solution)/shard_map/dot_general | solution.py:25
  124.0 2.4 %fusion.31 = f32[320,2560]{1,0:T(8,128)} fusion(bf16[192,2560]{1,0:T(8,128)(2,1)S(1)} %copy-done.5, bf16[96,320]{1,0:T(8,128)(2,1)S(1)} %copy-done.12, bf16[96,320]{1,0:T(8,128)(2,1)S(1)} %copy-done.13), kind=kOutput, calls=%fused_computation.52 | convolution fusion | flops 314818560 | bytes 4382720 | tf_op jit(solution)/shard_map/dot_general | solution.py:25
  126.4 2.4 %copy.13 = bf16[1536,320]{1,0:T(8,128)(2,1)} copy(bf16[1536,320]{0,1:T(8,128)(2,1)} %convolution_convert_fusion) | data formatting | bytes 1966080 | tf_op jit(solution)/shard_map/convert_element_type | solution.py:110
  128.8 2.7 %reshape.79 = bf16[192,2560]{1,0:T(8,128)(2,1)} reshape(bf16[1536,320]{1,0:T(8,128)(2,1)} %copy.13) | data formatting | bytes 1966080 | tf_op jit(solution)/shard_map/reshape | solution.py:110
  141.6 2.5 %reshape.81 = bf16[1024,320]{1,0:T(8,128)(2,1)} reshape(bf16[128,2560]{1,0:T(8,128)(2,1)} %fusion.4) | data formatting | bytes 1310720 | tf_op jit(solution)/shard_map/reshape | solution.py:123
  144.1 2.3 %fusion.27 = f32[1024,128]{1,0:T(8,128)} fusion(bf16[1024,320]{1,0:T(8,128)(2,1)} %reshape.81, bf16[320,320]{1,0:T(8,128)(2,1)S(1)} %copy-done.8), kind=kOutput, calls=%fused_computation.46 | convolution fusion | flops 83886080 | bytes 1277952 | tf_op jit(solution)/shard_map/dot_general | solution.py:25
  (90 shorter events, 40.0 us)
Async XLA Ops:
  1.6 34.2 %copy-start.8 = (bf16[320,320]{1,0:T(8,128)(2,1)S(1)}, bf16[320,320]{1,0:T(8,128)(2,1)}, u32[]{:S(2)}) copy-start(bf16[320,320]{1,0:T(8,128)(2,1)} %constant.37.clone) | copy-start | bytes 614404
  1.6 16.8 %collective-permute-start.7 = (bf16[96,96]{1,0:T(8,128)(2,1)S(1)}, bf16[96,96]{1,0:T(8,128)(2,1)S(1)}, u32[]{:S(2)}, u32[]{:S(2)}) collective-permute-start(bf16[96,96]{1,0:T(8,128)(2,1)S(1)} %get-tuple-element.27), channel_id=1, source_target_pairs={{3,0},{5,2},{7,4},{9,6},{11,8},{13,10},{15,12},{19,16},{21,18},{23... | collective-permute-start | bytes 55304 | tf_op jit(solution)/shard_map/ppermute | solution.py:47
  6.1 22.0 %collective-permute-start.6 = (bf16[96,128]{1,0:T(8,128)(2,1)S(1)}, bf16[96,128]{1,0:T(8,128)(2,1)S(1)}, u32[]{:S(2)}, u32[]{:S(2)}) collective-permute-start(bf16[96,128]{1,0:T(8,128)(2,1)S(1)} %get-tuple-element.29), channel_id=1, source_target_pairs={{2,0},{3,1},{4,2},{5,3},{6,4},{7,5},{8,6},{9,7},{10,8},{11,9},{12,... | collective-permute-start | bytes 73736 | tf_op jit(solution)/shard_map/ppermute | solution.py:47
  8.3 11.5 %collective-permute-start.5 = (bf16[96,96]{1,0:T(8,128)(2,1)S(1)}, bf16[96,96]{1,0:T(8,128)(2,1)S(1)}, u32[]{:S(2)}, u32[]{:S(2)}) collective-permute-start(bf16[96,96]{1,0:T(8,128)(2,1)S(1)} %get-tuple-element.25), channel_id=1, source_target_pairs={{2,1},{4,3},{6,5},{8,7},{10,9},{12,11},{14,13},{18,17},{20,19},{22... | collective-permute-start | bytes 55304 | tf_op jit(solution)/shard_map/ppermute | solution.py:47
  10.5 18.8 %collective-permute-start.4 = (bf16[128,96]{1,0:T(8,128)(2,1)S(1)}, bf16[128,96]{1,0:T(8,128)(2,1)S(1)}, u32[]{:S(2)}, u32[]{:S(2)}) collective-permute-start(bf16[128,96]{1,0:T(8,128)(2,1)S(1)} %get-tuple-element.31), channel_id=1, source_target_pairs={{1,0},{3,2},{5,4},{7,6},{9,8},{11,10},{13,12},{15,14},{17,16},{19,... | collective-permute-start | bytes 73736 | tf_op jit(solution)/shard_map/ppermute | solution.py:47
  14.5 7.2 %collective-permute-start.2 = (bf16[96,96]{1,0:T(8,128)(2,1)S(1)}, bf16[96,96]{1,0:T(8,128)(2,1)S(1)}, u32[]{:S(2)}, u32[]{:S(2)}) collective-permute-start(bf16[96,96]{1,0:T(8,128)(2,1)S(1)} %get-tuple-element.26), channel_id=1, source_target_pairs={{1,2},{3,4},{5,6},{7,8},{9,10},{11,12},{13,14},{17,18},{19,20},{21... | collective-permute-start | bytes 55304 | tf_op jit(solution)/shard_map/ppermute | solution.py:47
  18.5 14.8 %collective-permute-start.3 = (bf16[128,96]{1,0:T(8,128)(2,1)S(1)}, bf16[128,96]{1,0:T(8,128)(2,1)S(1)}, u32[]{:S(2)}, u32[]{:S(2)}) collective-permute-start(bf16[128,96]{1,0:T(8,128)(2,1)S(1)} %get-tuple-element.30), channel_id=1, source_target_pairs={{0,1},{2,3},{4,5},{6,7},{8,9},{10,11},{12,13},{14,15},{16,17},{18,... | collective-permute-start | bytes 73736 | tf_op jit(solution)/shard_map/ppermute | solution.py:47
  19.8 13.5 %collective-permute-start.1 = (bf16[96,128]{1,0:T(8,128)(2,1)S(1)}, bf16[96,128]{1,0:T(8,128)(2,1)S(1)}, u32[]{:S(2)}, u32[]{:S(2)}) collective-permute-start(bf16[96,128]{1,0:T(8,128)(2,1)S(1)} %get-tuple-element.28), channel_id=1, source_target_pairs={{0,2},{1,3},{2,4},{3,5},{4,6},{5,7},{6,8},{7,9},{8,10},{9,11},{10,... | collective-permute-start | bytes 73736 | tf_op jit(solution)/shard_map/ppermute | solution.py:47
  21.7 6.4 %collective-permute-start = (bf16[96,96]{1,0:T(8,128)(2,1)S(1)}, bf16[96,96]{1,0:T(8,128)(2,1)S(1)}, u32[]{:S(2)}, u32[]{:S(2)}) collective-permute-start(bf16[96,96]{1,0:T(8,128)(2,1)S(1)} %get-tuple-element.24), channel_id=1, source_target_pairs={{0,3},{2,5},{4,7},{6,9},{8,11},{10,13},{12,15},{16,19},{18,21},{20... | collective-permute-start | bytes 55304 | tf_op jit(solution)/shard_map/ppermute | solution.py:47
  24.1 12.1 %copy-start.11 = (bf16[128,128]{1,0:T(8,128)(2,1)S(1)}, bf16[128,128]{1,0:T(8,128)(2,1)}, u32[]{:S(2)}) copy-start(bf16[128,128]{1,0:T(8,128)(2,1)} %param.7) | copy-start | bytes 98308
  28.1 9.3 %collective-permute-start.8 = (bf16[1,36992]{1,0:T(2,128)(2,1)S(1)}, bf16[1,36992]{1,0:T(2,128)(2,1)S(1)}, u32[]{:S(2)}, u32[]{:S(2)}) collective-permute-start(bf16[1,36992]{1,0:T(2,128)(2,1)S(1)} %concatenate.29), channel_id=1, source_target_pairs={{0,2},{2,4},{4,6},{6,8},{8,10},{10,12},{12,14},{14,0},{1,3},{3,5},... | collective-permute-start | bytes 221960 | tf_op jit(solution)/shard_map/ppermute | solution.py:58
  28.2 9.5 %collective-permute-start.9 = (bf16[1,36992]{1,0:T(2,128)(2,1)S(1)}, bf16[1,36992]{1,0:T(2,128)(2,1)S(1)}, u32[]{:S(2)}, u32[]{:S(2)}) collective-permute-start(bf16[1,36992]{1,0:T(2,128)(2,1)S(1)} %concatenate.29), channel_id=1, source_target_pairs={{0,4},{2,6},{4,8},{6,10},{8,12},{10,14},{12,0},{14,2},{1,5},{3,7},... | collective-permute-start | bytes 221960 | tf_op jit(solution)/shard_map/ppermute | solution.py:58
  29.3 37.5 %collective-permute-start.10 = (bf16[1,36992]{1,0:T(2,128)(2,1)S(1)}, bf16[1,36992]{1,0:T(2,128)(2,1)S(1)}, u32[]{:S(2)}, u32[]{:S(2)}) collective-permute-start(bf16[1,36992]{1,0:T(2,128)(2,1)S(1)} %concatenate.29), channel_id=1, source_target_pairs={{0,6},{2,8},{4,10},{6,12},{8,14},{10,0},{12,2},{14,4},{1,7},{3,9},... | collective-permute-start | bytes 221960 | tf_op jit(solution)/shard_map/ppermute | solution.py:58
  33.3 33.5 %collective-permute-start.11 = (bf16[1,36992]{1,0:T(2,128)(2,1)S(1)}, bf16[1,36992]{1,0:T(2,128)(2,1)S(1)}, u32[]{:S(2)}, u32[]{:S(2)}) collective-permute-start(bf16[1,36992]{1,0:T(2,128)(2,1)S(1)} %concatenate.29), channel_id=1, source_target_pairs={{0,8},{2,10},{4,12},{6,14},{8,0},{10,2},{12,4},{14,6},{1,9},{3,11}... | collective-permute-start | bytes 221960 | tf_op jit(solution)/shard_map/ppermute | solution.py:58
  33.3 33.5 %collective-permute-start.12 = (bf16[1,36992]{1,0:T(2,128)(2,1)S(1)}, bf16[1,36992]{1,0:T(2,128)(2,1)S(1)}, u32[]{:S(2)}, u32[]{:S(2)}) collective-permute-start(bf16[1,36992]{1,0:T(2,128)(2,1)S(1)} %concatenate.29), channel_id=1, source_target_pairs={{0,10},{2,12},{4,14},{6,0},{8,2},{10,4},{12,6},{14,8},{1,11},{3,13... | collective-permute-start | bytes 221960 | tf_op jit(solution)/shard_map/ppermute | solution.py:58
  37.4 29.4 %collective-permute-start.13 = (bf16[1,36992]{1,0:T(2,128)(2,1)S(1)}, bf16[1,36992]{1,0:T(2,128)(2,1)S(1)}, u32[]{:S(2)}, u32[]{:S(2)}) collective-permute-start(bf16[1,36992]{1,0:T(2,128)(2,1)S(1)} %concatenate.29), channel_id=1, source_target_pairs={{0,12},{2,14},{4,0},{6,2},{8,4},{10,6},{12,8},{14,10},{1,13},{3,15... | collective-permute-start | bytes 221960 | tf_op jit(solution)/shard_map/ppermute | solution.py:58
  37.6 29.2 %collective-permute-start.14 = (bf16[1,36992]{1,0:T(2,128)(2,1)S(1)}, bf16[1,36992]{1,0:T(2,128)(2,1)S(1)}, u32[]{:S(2)}, u32[]{:S(2)}) collective-permute-start(bf16[1,36992]{1,0:T(2,128)(2,1)S(1)} %concatenate.29), channel_id=1, source_target_pairs={{0,14},{2,0},{4,2},{6,4},{8,6},{10,8},{12,10},{14,12},{1,15},{3,1}... | collective-permute-start | bytes 221960 | tf_op jit(solution)/shard_map/ppermute | solution.py:58
  121.1 2.9 %copy-start.5 = (bf16[192,2560]{1,0:T(8,128)(2,1)S(1)}, bf16[192,2560]{1,0:T(8,128)(2,1)}, u32[]{:S(2)}) copy-start(bf16[192,2560]{1,0:T(8,128)(2,1)} %reshape.80) | copy-start | bytes 2949124
  121.1 2.9 %copy-start.12 = (bf16[96,320]{1,0:T(8,128)(2,1)S(1)}, bf16[96,320]{1,0:T(8,128)(2,1)}, u32[]{:S(2)}) copy-start(bf16[96,320]{1,0:T(8,128)(2,1)} %get-tuple-element.43) | copy-start | bytes 184324
  121.1 2.9 %copy-start.13 = (bf16[96,320]{1,0:T(8,128)(2,1)S(1)}, bf16[96,320]{1,0:T(8,128)(2,1)}, u32[]{:S(2)}) copy-start(bf16[96,320]{1,0:T(8,128)(2,1)} %get-tuple-element.44) | copy-start | bytes 184324
  131.5 2.6 %copy-start.14 = (bf16[96,320]{1,0:T(8,128)(2,1)S(1)}, bf16[96,320]{1,0:T(8,128)(2,1)}, u32[]{:S(2)}) copy-start(bf16[96,320]{1,0:T(8,128)(2,1)} %get-tuple-element.20) | copy-start | bytes 184324
  134.1 2.9 %copy-start.4 = (f32[320,2560]{1,0:T(8,128)S(1)}, f32[320,2560]{1,0:T(8,128)}, u32[]{:S(2)}) copy-start(f32[320,2560]{1,0:T(8,128)} %mul.56) | copy-start | bytes 9830404
  134.1 3.1 %copy-start.6 = (bf16[192,2560]{1,0:T(8,128)(2,1)S(1)}, bf16[192,2560]{1,0:T(8,128)(2,1)}, u32[]{:S(2)}) copy-start(bf16[192,2560]{1,0:T(8,128)(2,1)} %reshape.80) | copy-start | bytes 2949124
  141.6 4.8 %copy-start.2 = (bf16[320,2560]{1,0:T(8,128)(2,1)S(1)}, bf16[320,2560]{1,0:T(8,128)(2,1)}, u32[]{:S(2)}) copy-start(bf16[320,2560]{1,0:T(8,128)(2,1)} %copy-done.1) | copy-start | bytes 4915204
  (7 other events, 12.5 us)

commit v3 on v1

v3 whole, which is shorter than its diff:
```python
import math

import jax
import jax.numpy as jnp
import ml_dtypes
import numpy as np
from jax import lax
from jax.sharding import PartitionSpec as P

RB = 32
CHUNK = 8


def extended(block, sides, width):
    for axis, dim in sides:
        count = lax.axis_size(axis)
        forward = [(i, i + 1) for i in range(count - 1)]
        backward = [(target, source) for source, target in forward]
        low = lax.ppermute(
            lax.slice_in_dim(block, block.shape[dim] - width, None, axis=dim), axis, forward
        )
        high = lax.ppermute(lax.slice_in_dim(block, 0, width, axis=dim), axis, backward)
        block = jnp.concatenate([low, block, high], axis=dim)
    return block


def twiddles(padded_size):
    position = np.arange(padded_size, dtype=np.int64)
    phase_index = (position[:, None] * position[None, :]) % padded_size
    angles = phase_index.astype(np.float32) * np.float32(2.0 * math.pi / padded_size)
    angles = angles.astype(np.float64)
    cosines = np.cos(angles).astype(np.float32).astype(ml_dtypes.bfloat16)
    sines = np.sin(angles).astype(np.float32).astype(ml_dtypes.bfloat16)
    return cosines, sines


def matmul(left, right):
    return jnp.dot(left, right, preferred_element_type=jnp.float32)


def exchange_rounds(block):
    size = lax.axis_size("orient")
    rounds = [block]
    step = 1
    while step * 2 < size:
        step *= 2
    held = block
    while step >= 1:
        other = lax.ppermute(held, "orient", [(i, i ^ step) for i in range(size)])
        rounds.append(other)
        held = jnp.concatenate([held, other], axis=0)
        step //= 2
    return rounds


def body(micrograph, templates, defocus, ctf, usable):
    bf16 = jnp.bfloat16
    f32 = jnp.float32
    tile_width = micrograph.shape[0]
    padded_size = ctf.shape[1]
    box_size = templates.shape[1]
    margin = (padded_size - tile_width) // 2
    scaling = 1.0 / (padded_size * padded_size)
    n = padded_size
    cos_np, sin_np = twiddles(n)

    cos_full, sin_full = lax.optimization_barrier((jnp.asarray(cos_np), jnp.asarray(sin_np)))
    low = n - box_size // 2
    cos_rows = jnp.concatenate([cos_full[low:], cos_full[: box_size - (n - low)]], axis=0)
    sin_rows = jnp.concatenate([sin_full[low:], sin_full[: box_size - (n - low)]], axis=0)
    cos_cols = cos_rows.T
    sin_cols = sin_rows.T
    row_cos = cos_full[margin : margin + tile_width]
    row_sin = sin_full[margin : margin + tile_width]
    col_cos = row_cos.T
    col_sin = row_sin.T

    local_count = templates.shape[0]
    flat_size = box_size * box_size
    id_block = jnp.broadcast_to(defocus.astype(bf16)[:, None], (local_count, 128))
    packed = jnp.concatenate([templates.reshape(local_count, flat_size), id_block], axis=1)
    arrivals = exchange_rounds(packed)
    total = sum(piece.shape[0] for piece in arrivals)

    padded = extended(micrograph, (("orient", 0), ("tile", 1)), margin)
    half_real = matmul(padded, cos_full).astype(bf16)
    half_imag = (-matmul(padded, sin_full)).astype(bf16)
    spec_real = (matmul(cos_full, half_real) + matmul(sin_full, half_imag)).astype(bf16).astype(f32)
    spec_imag = (matmul(cos_full, half_imag) - matmul(sin_full, half_real)).astype(bf16).astype(f32)

    def batched(shared, count):
        return jnp.broadcast_to(shared[None], (count,) + shared.shape)

    def chunk_stats(chunk):
        count = chunk.shape[0]
        chunk_templates = chunk[:, :flat_size].reshape(count, box_size, box_size)
        chunk_ids = chunk[:, flat_size].astype(jnp.int32)
        part_real = jnp.einsum("okj,jq->okq", chunk_templates, cos_rows, preferred_element_type=f32).astype(bf16)
        part_imag = (-jnp.einsum("okj,jq->okq", chunk_templates, sin_rows, preferred_element_type=f32)).astype(bf16)
        left_c = batched(cos_cols, count)
        left_s = batched(sin_cols, count)
        full_real = jnp.einsum("opk,okq->opq", left_c, part_real, preferred_element_type=f32) + jnp.einsum(
            "opk,okq->opq", left_s, part_imag, preferred_element_type=f32
        )
        full_imag = jnp.einsum("opk,okq->opq", left_c, part_imag, preferred_element_type=f32) - jnp.einsum(
            "opk,okq->opq", left_s, part_real, preferred_element_type=f32
        )
        weight = jnp.stack([lax.dynamic_index_in_dim(ctf, chunk_ids[o], 0, keepdims=False) for o in range(count)])
        w_real = (full_real * weight).astype(bf16).astype(f32)
        w_imag = (full_imag * weight).astype(bf16).astype(f32)
        prod_real = (spec_real * w_real + spec_imag * w_imag).astype(bf16)
        prod_imag = (spec_imag * w_real - spec_real * w_imag).astype(bf16)
        rc = batched(row_cos, count)
        rs = batched(row_sin, count)
        left_real = (
            jnp.einsum("orp,opq->orq", rc, prod_real, preferred_element_type=f32)
            - jnp.einsum("orp,opq->orq", rs, prod_imag, preferred_element_type=f32)
        ).astype(bf16)
        left_imag = (
            jnp.einsum("orp,opq->orq", rc, prod_imag, preferred_element_type=f32)
            + jnp.einsum("orp,opq->orq", rs, prod_real, preferred_element_type=f32)
        ).astype(bf16)
        corr = jnp.einsum("orq,qc->orc", left_real, col_cos, preferred_element_type=f32) - jnp.einsum(
            "orq,qc->orc", left_imag, col_sin, preferred_element_type=f32
        )
        corr = corr * scaling
        return (jnp.max(corr, axis=0), jnp.sum(corr, axis=0), jnp.sum(corr * corr, axis=0))

    peak_map = sum_map = squares = None
    for piece in arrivals:
        for start in range(0, piece.shape[0], CHUNK):
            stats = chunk_stats(piece[start : start + CHUNK])
            if peak_map is None:
                peak_map, sum_map, squares = stats
            else:
                peak_map = jnp.maximum(peak_map, stats[0])
                sum_map = sum_map + stats[1]
                squares = squares + stats[2]

    live = usable[0, 0]
    row_mask = (jnp.arange(tile_width, dtype=jnp.int32) < RB * live)[:, None]
    orient_count = float(total)
    peak_out = jnp.where(row_mask, peak_map, 0.0)
    mean_out = jnp.where(row_mask, sum_map / orient_count, 0.0)
    square_out = jnp.where(row_mask, squares / orient_count, 0.0)
    return (peak_out, mean_out, square_out)


def solution(mesh):
    return jax.shard_map(
        body,
        mesh=mesh,
        in_specs=(
            P(("groups", "orient"), "tile"),
            P("orient", None, None),
            P(("groups", "orient")),
            P("groups", None, None),
            P(("groups", "orient"), "tile"),
        ),
        out_specs=(
            P(("groups", "orient"), "tile"),
            P(("groups", "orient"), "tile"),
            P(("groups", "orient"), "tile"),
        ),
        check_vma=False,
    )
```

time: 73.9 us -> 104 us (1.41)
  matrix products: 20.9 us -> 52.4 us
  waiting for transfers between devices: 16.9 us -> 0.02 us
  between operations: 2.38 us -> 14.6 us
  starting transfers between devices: 15 us -> 17.3 us
  other arithmetic: 2.74 us -> 4.54 us
  local copies, waits for them, and re-layouts: 15.4 us -> 13.9 us
    dot_general x8 -> x32, matrix products: 16.2 us -> 46.3 us  [the longest x4 8.55 us: chunk_stats(): jnp.einsum('orq,qc->orc', left_real, col_cos, preferred_element_type=f32)]
    ppermute x3, waiting for transfers between devices: 13 us -> 0.01 us  [exchange_rounds(): other = lax.ppermute(held, 'orient', [(i, i ^ step) for i in range(size)])]
    gather x2 -> x0, local copies, waits for them, and re-layouts: 10.3 us -> none  [chunk_stats(): weight = jnp.take(ctf, chunk_ids, axis=0)]
    slice x1 -> x9, local copies, waits for them, and re-layouts: 0.04 us -> 4.78 us  [the longest x3 1.53 us: chunk_stats(): chunk_templates = chunk[:, :flat_size].reshape(count, box_size, box_size)]
    ppermute x2, waiting for transfers between devices: 3.92 us -> 0.01 us  [extended(): lax.ppermute(lax.slice_in_dim(block, 0, width, axis=dim), axis, backward)]
    concatenate x0 -> x2, other arithmetic: none -> 3.22 us  [exchange_rounds(): held = jnp.concatenate([held, other], axis=0)]
    dot_general x1 -> x4, matrix products: 0.56 us -> 3.17 us  [chunk_stats(): jnp.einsum('okj,jq->okq', chunk_templates, sin_rows, preferred_element_ty...]
    select_n x5 -> x0, other arithmetic: 2.6 us -> none  [the longest x3 1.72 us: gather_orient(): jnp.where(low_side, jnp.concatenate([block, other], 0), jnp.concatenate([...]
  transfers between devices with their start and end apart: 7 -> 7, of which waited for: 3 -> 0; matrix products, arithmetic and copies ran while one was open for 8% -> 29% of each run, Pallas kernels for 0% -> 0%
where the time goes in v3:
time: 104 us; the launch traced here: 103 us
  matrix products  52.4 us (50%)
  starting transfers between devices  17.3 us (17%)
  between operations  14.6 us (14%)
  local copies, waits for them, and re-layouts  13.9 us (13%)
  other arithmetic  4.54 us (4%)
    dot_general x4, matrix products, chunk_stats(): jnp.einsum('orq,qc->orc', left_real, col_cos, preferred_element_type=f32)  8.55 us
    ppermute x3, starting transfers between devices, exchange_rounds(): other = lax.ppermute(held, 'orient', [(i, i ^ step) for i in range(size)])  8.32 us
    dot_general x4, matrix products, chunk_stats(): jnp.einsum('orq,qc->orc', left_imag, col_sin, preferred_element_type=f32)  8.14 us
    dot_general x4, matrix products, chunk_stats(): jnp.einsum('opk,okq->opq', left_s, part_real, preferred_element_type=f32)  6.79 us
    ppermute x2, starting transfers between devices, extended(): lax.ppermute(lax.slice_in_dim(block, block.shape[dim] - width, None, axis...  6.42 us
    dot_general x4, matrix products, chunk_stats(): jnp.einsum('orp,opq->orq', rc, prod_imag, preferred_element_type=f32)  5.59 us
    dot_general x4, matrix products, chunk_stats(): jnp.einsum('opk,okq->opq', left_c, part_imag, preferred_element_type=f32)  4.59 us
    dot_general x4, matrix products, chunk_stats(): jnp.einsum('opk,okq->opq', left_s, part_imag, preferred_element_type=f32)  4.42 us
  transfers between devices with their start and end apart: 7, of which 0 were waited for; matrix products, arithmetic and copies ran while one was open for 29% of the time, Pallas kernels for 0%

profile of v3, /device:TPU:0, one launch (start us, length us, event | category | flops | bytes accessed | tf_op | source)
XLA Modules:
  0.0 102.8 jit_solution(15617460384036052316)
XLA Ops:
  2.6 4.1 %collective-permute-start.4 = (bf16[1,36992]{1,0:T(2,128)(2,1)S(1)}, bf16[1,36992]{1,0:T(2,128)(2,1)S(1)}, u32[]{:S(2)}, u32[]{:S(2)}) collective-permute-start(bf16[1,36992]{1,0:T(2,128)(2,1)S(1)} %concatenate.26), channel_id=1, source_target_pairs={{0,8},{2,10},{4,12},{6,14},{8,0},{10,2},{12,4},{14,6},{1,9},{3,11}... | collective-permute-start | bytes 221960 | tf_op jit(solution)/shard_map/ppermute | solution.py:49
  7.5 3.4 %collective-permute-start = (bf16[96,128]{1,0:T(8,128)(2,1)S(1)}, bf16[96,128]{1,0:T(8,128)(2,1)S(1)}, u32[]{:S(2)}, u32[]{:S(2)}) collective-permute-start(bf16[96,128]{1,0:T(8,128)(2,1)S(1)} %get-tuple-element.37), channel_id=1, source_target_pairs={{0,2},{2,4},{4,6},{6,8},{8,10},{10,12},{12,14},{1,3},{3,5},{5,7},{... | collective-permute-start | bytes 73736 | tf_op jit(solution)/shard_map/ppermute | solution.py:19
  15.3 2.2 %fusion.29 = f32[1,320,320]{2,1,0:T(8,128)} fusion(f32[320,320]{1,0:T(8,128)S(1)} %fusion.135, bf16[320,192]{0,1:T(8,128)(2,1)S(1)} %convolution_convert_fusion.3, f32[8,320,320]{2,1,0:T(8,128)} %param.10, s32[]{:T(128)S(6)} %select_n.35, bf16[96,320]{1,0:T(8,128)(2,1)S(1)} %get-tuple-element.28, bf16[96,320]{1,0:T(8,128)(2,1)S(1)} %get-tuple-element.27), kind=kOutput, calls=%fused_computation.52 | convolution fusion | flops 39976960 | bytes 1474564 | tf_op jit(solution)/shard_map/opk,okq->opq/dot_general | solution.py:105
  17.4 2.1 %fusion.30 = f32[1,320,320]{2,1,0:T(8,128)} fusion(f32[320,320]{1,0:T(8,128)S(1)} %fusion.136, bf16[320,192]{0,1:T(8,128)(2,1)S(1)} %fusion.42, f32[8,320,320]{2,1,0:T(8,128)} %param.10, s32[]{:T(128)S(6)} %select_n.35, bf16[96,320]{1,0:T(8,128)(2,1)S(1)} %get-tuple-element.28, bf16[96,320]{1,0:T(8,128)(2,1)S(1)} %get-tuple-element.27), kind=kOutput, calls=%fused_computation.53 | convolution fusion | flops 39976960 | bytes 1474564 | tf_op jit(solution)/shard_map/opk,okq->opq/dot_general | solution.py:102
  22.3 3.0 %collective-permute-start.2 = (bf16[320,96]{1,0:T(8,128)(2,1)S(1)}, bf16[320,96]{1,0:T(8,128)(2,1)S(1)}, u32[]{:S(2)}, u32[]{:S(2)}) collective-permute-start(bf16[320,96]{1,0:T(8,128)(2,1)S(1)} %get-tuple-element.34), channel_id=1, source_target_pairs={{0,1},{2,3},{4,5},{6,7},{8,9},{10,11},{12,13},{14,15},{16,17},{18,... | collective-permute-start | bytes 184328 | tf_op jit(solution)/shard_map/ppermute | solution.py:19
  28.5 3.6 %collective-permute-start.5 = (bf16[2,36992]{1,0:T(2,128)(2,1)}, bf16[2,36992]{1,0:T(2,128)(2,1)}, u32[]{:S(2)}, u32[]{:S(2)}) collective-permute-start(bf16[2,36992]{1,0:T(2,128)(2,1)} %pad_maximum_fusion.4), channel_id=1, source_target_pairs={{0,4},{2,6},{4,0},{6,2},{8,12},{10,14},{12,8},{14,10},{1,5},{3,7},... | collective-permute-start | bytes 443912 | tf_op jit(solution)/shard_map/ppermute | solution.py:49
  42.6 1.9 %fusion.56 = f32[128,128]{1,0:T(8,128)} fusion(f32[128,128]{1,0:T(8,128)S(1)} %fusion.53, f32[128,320]{1,0:T(8,128)} %fusion.129, bf16[320,320]{1,0:T(8,128)(2,1)S(1)} %get-tuple-element.25, bf16[320,320]{1,0:T(8,128)(2,1)S(1)} %copy-done.3, bf16[320,320]{1,0:T(8,128)(2,1)S(1)} %copy-done), kind=kOutput, calls=%fused_computation.89 | convolution fusion | flops 36814848 | bytes 737280 | tf_op jit(solution)/shard_map/orq,qc->orc/dot_general | solution.py:123
  44.5 1.9 %fusion.51 = f32[128,128]{1,0:T(8,128)} fusion(f32[128,320]{1,0:T(8,128)} %fusion.121, bf16[320,320]{1,0:T(8,128)(2,1)S(1)} %get-tuple-element.21, bf16[320,320]{1,0:T(8,128)(2,1)S(1)} %copy-done.3), kind=kOutput, calls=%fused_computation.84 | convolution fusion | flops 36782080 | bytes 671744 | tf_op jit(solution)/shard_map/orq,qc->orc/dot_general | solution.py:123
  49.0 2.2 %pad_maximum_fusion.2 = bf16[4,36992]{1,0:T(4,128)(2,1)} fusion(bf16[2,36992]{1,0:T(2,128)(2,1)} %collective-permute-done.5, bf16[1,36992]{1,0:T(2,128)(2,1)S(1)} %copy-done.20, bf16[1,36992]{1,0:T(2,128)(2,1)S(1)} %concatenate.26), kind=kLoop, calls=%fused_computation.111 | loop fusion | flops 887808 | bytes 591872 | tf_op jit(solution)/shard_map/concatenate | solution.py:51
  51.9 1.4 %fusion.93 = f32[2,320,320]{2,1,0:T(8,128)} fusion(bf16[2,192,320]{2,1,0:T(8,128)(2,1)S(1)} %convolution_convert_fusion.1, bf16[320,192]{0,1:T(8,128)(2,1)S(1)} %fusion.132), kind=kOutput, calls=%fused_computation.142 | convolution fusion | flops 78643200 | bytes 1187840 | tf_op jit(solution)/shard_map/opk,okq->opq/dot_general | solution.py:102
  62.1 1.6 %fusion.6 = bf16[4,192,320]{2,1,0:T(8,128)(2,1)S(1)} fusion(bf16[4,192,192]{2,1,0:T(8,128)(2,1)} %copy-done.18, bf16[96,320]{1,0:T(8,128)(2,1)S(1)} %get-tuple-element.28, bf16[96,320]{1,0:T(8,128)(2,1)S(1)} %get-tuple-element.27), kind=kOutput, calls=%fused_computation.16 | convolution fusion | flops 95109120 | bytes 909312 | tf_op jit(solution)/shard_map/okj,jq->okq/dot_general | solution.py:99
  69.9 1.9 %fusion.71 = f32[4,320,320]{2,1,0:T(8,128)} fusion(bf16[4,192,320]{2,1,0:T(8,128)(2,1)S(1)} %convolution_convert_fusion, bf16[320,192]{0,1:T(8,128)(2,1)S(1)} %fusion.132), kind=kOutput, calls=%fused_computation.116 | convolution fusion | flops 157286400 | bytes 2252800 | tf_op jit(solution)/shard_map/opk,okq->opq/dot_general | solution.py:102
  71.8 1.8 %fusion.69 = f32[4,320,320]{2,1,0:T(8,128)} fusion(bf16[4,192,320]{2,1,0:T(8,128)(2,1)S(1)} %fusion.6, bf16[320,192]{0,1:T(8,128)(2,1)S(1)} %fusion.132), kind=kOutput, calls=%fused_computation.114 | convolution fusion | flops 157286400 | bytes 2252800 | tf_op jit(solution)/shard_map/opk,okq->opq/dot_general | solution.py:105
  76.1 2.1 %constant_dynamic-slice_fusion.5 = (f32[1,320,320]{2,1,0:T(8,128)S(1)}, f32[1,320,320]{2,1,0:T(8,128)S(1)}, f32[1,320,320]{2,1,0:T(8,128)S(1)}, f32[1,320,320]{2...) fusion(f32[8,320,320]{2,1,0:T(8,128)} %param.10, s32[]{:T(128)S(6)} %select_n.37, ...), kind=kLoop, calls=%fused_computation.168 | loop fusion | bytes 4915224 | tf_op jit(solution)/shard_map/jit(dynamic_index_in_dim)/dynamic_slice | solution.py:108
  80.2 1.6 %multiply_convert_fusion = bf16[4,320,320]{2,1,0:T(8,128)(2,1)S(1)} fusion(f32[4,320,320]{2,1,0:T(8,128)S(1)} %copy-done.1, bf16[4,192,320]{2,1,0:T(8,128)(2,1)S(1)} %copy-done.5, f32[1,320,320]{2,1,0:T(8,128)S(1)} %get-tuple-element.17, f32[1,320,320]{2,1,0:T(8,128)S(1)} %get-tuple-element.18, f32[1,320,320]{2,1,0:T(8,128)S(1)} %get-tuple-element.14, ...), kind=kOutput, calls=%fused_computation.9 | convolution fusion | flops 159744000 | bytes 4710400 | tf_op jit(solution)/shard_map/opk,okq->opq/dot_general | solution.py:105
  81.8 1.5 %fusion.81 = f32[4,128,320]{1,2,0:T(8,128)} fusion(bf16[128,320]{1,0:T(8,128)(2,1)S(1)} %copy-done.13, bf16[4,320,320]{2,1,0:T(8,128)(2,1)S(1)} %multiply_convert_fusion.1, bf16[4,320,320]{2,1,0:T(8,128)(2,1)S(1)} %multiply_convert_fusion, f32[320,320]{1,0:T(8,128)S(1)} %fusion.34, f32[320,320]{1,0:T(8,128)S(1)} %fusion.32), kind=kOutput, calls=%fused_computation.126 | convolution fusion | flops 107315200 | bytes 3194880 | tf_op jit(solution)/shard_map/orp,opq->orq/dot_general | solution.py:120
  83.3 1.5 %fusion.83 = f32[4,128,320]{1,2,0:T(8,128)} fusion(bf16[128,320]{1,0:T(8,128)(2,1)S(1)} %copy-done.13, bf16[4,320,320]{2,1,0:T(8,128)(2,1)S(1)} %multiply_convert_fusion.1, bf16[4,320,320]{2,1,0:T(8,128)(2,1)S(1)} %multiply_convert_fusion, f32[320,320]{1,0:T(8,128)S(1)} %fusion.34, f32[320,320]{1,0:T(8,128)S(1)} %fusion.32), kind=kOutput, calls=%fused_computation.128 | convolution fusion | flops 107315200 | bytes 3194880 | tf_op jit(solution)/shard_map/orp,opq->orq/dot_general | solution.py:116
  86.1 1.6 %add_convert_fusion = (bf16[2,320,320]{2,1,0:T(8,128)(2,1)S(1)}, bf16[2,320,320]{2,1,0:T(8,128)(2,1)}) fusion(f32[2,320,320]{2,1,0:T(8,128)S(1)} %fusion.10, f32[320,320]{1,0:T(8,128)S(1)} %fusion.34, f32[320,320]{1,0:T(8,128)S(1)} %fusion.32, f32[1,320,320]{2,1,0:T(8,128)S(1)} %get-tuple-element.16, f32[1,320,320]{2,1,0:T(8,128)S(1)} %get-tuple-element.13, ...), kind=kOutput, calls=%fused_computation.94 | convolution fusion | flops 81305600 | bytes 4464640 | tf_op jit(solution)/shard_map/opk,okq->opq/dot_general | solution.py:105
  87.7 2.3 %fusion.105 = f32[2,128,320]{1,2,0:T(8,128)} fusion(bf16[2,320,320]{2,1,0:T(8,128)(2,1)} %get-tuple-element.20, bf16[128,320]{1,0:T(8,128)(2,1)S(1)} %copy-done.13), kind=kOutput, calls=%fused_computation.153 | convolution fusion | flops 52428800 | bytes 819200 | tf_op jit(solution)/shard_map/orp,opq->orq/dot_general | solution.py:120
  91.2 2.7 %fusion.35 = f32[4,128,128]{2,1,0:T(8,128)} fusion(f32[4,128,320]{1,2,0:T(8,128)} %fusion.81, bf16[128,320]{1,0:T(8,128)(2,1)S(1)} %slice.82, bf16[4,320,320]{2,1,0:T(8,128)(2,1)S(1)} %multiply_convert_fusion.1, bf16[4,320,320]{2,1,0:T(8,128)(2,1)S(1)} %multiply_convert_fusion, f32[320,320]{1,0:T(8,128)S(1)} %fusion.34, f32[320,320]{1,0:T(8,128)S(1)} %fusion.32), kind=kOutput, calls=%fused_computation.58 | convolution fusion | flops 149585920 | bytes 3457024 | tf_op jit(solution)/shard_map/orq,qc->orc/dot_general | solution.py:123
  93.8 2.3 %fusion.43 = f32[2,128,128]{2,1,0:T(8,128)} fusion(f32[2,128,320]{1,2,0:T(8,128)} %fusion.105, bf16[2,320,320]{2,1,0:T(8,128)(2,1)} %copy-done.6, bf16[128,320]{1,0:T(8,128)(2,1)S(1)} %slice.82), kind=kOutput, calls=%fused_computation.76 | convolution fusion | flops 73564160 | bytes 950272 | tf_op jit(solution)/shard_map/orq,qc->orc/dot_general | solution.py:123
  96.2 2.7 %multiply_reduce_fusion = (f32[128,128]{1,0:T(8,128)}, f32[128,128]{1,0:T(8,128)}, f32[128,128]{1,0:T(8,128)}) fusion(f32[4,128,128]{2,1,0:T(8,128)} %fusion.35, bf16[320,320]{1,0:T(8,128)(2,1)S(1)} %copy-done, f32[4,128,320]{1,2,0:T(8,128)} %fusion.83, bf16[128,320]{1,0:T(8,128)(2,1)S(1)} %slice.82, bf16[4,320,320]{2,1,0:T(8,128)(2,1)S(1)} %multiply_convert_fusion.1, ...), kind=kOutput, calls=%fused_computation.118 | convolution fusion | flops 149929984 | bytes 4259840 | tf_op jit(solution)/shard_map/orq,qc->orc/dot_general | solution.py:123
  98.9 1.7 %multiply_reduce_fusion.1 = (f32[128,128]{1,0:T(8,128)S(1)}, f32[128,128]{1,0:T(8,128)S(1)}, f32[128,128]{1,0:T(8,128)S(1)}) fusion(f32[2,128,128]{2,1,0:T(8,128)} %fusion.43, bf16[320,320]{1,0:T(8,128)(2,1)S(1)} %copy-done, f32[2,128,320]{1,2,0:T(8,128)} %fusion.107, bf16[2,320,320]{2,1,0:T(8,128)(2,1)} %get-tuple-element.20, bf16[128,320]{1,0:T(8,128)(2,1)S(1)} %slice.82), kind=kOutput, calls=%fused_computation.144 | convolution fusion | flops 73711616 | bytes 1261568 | tf_op jit(solution)/shard_map/orq,qc->orc/dot_general | solution.py:123
  100.6 2.2 %multiply_select_fusion = (f32[128,128]{1,0:T(8,128)}, f32[128,128]{1,0:T(8,128)}, f32[128,128]{1,0:T(8,128)}) fusion(f32[128,128]{1,0:T(8,128)} %get-tuple-element.7, f32[128,128]{1,0:T(8,128)S(1)} %get-tuple-element.10, f32[128,128]{1,0:T(8,128)} %fusion.56, pred[128]{0:T(512)(128)(4,1)S(1)} %iota_compare_fusion, f32[128,128]{1,0:T(8,128)} %get-tuple-element.8, ...), kind=kOutput, calls=%fused_computation.157 | convolution fusion | flops 37076992 | bytes 1286656 | tf_op jit(solution)/shard_map/orq,qc->orc/dot_general | solution.py:123
  (119 shorter events, 34.7 us)
Async XLA Ops:
  0.6 13.8 %copy-start.25 = (bf16[1,192,192]{2,1,0:T(8,128)(2,1)S(1)}, bf16[1,192,192]{2,1,0:T(8,128)(2,1)}, u32[]{:S(2)}) copy-start(bf16[1,192,192]{2,1,0:T(8,128)(2,1)} %param.8) | copy-start | bytes 221188
  2.6 22.8 %collective-permute-start.4 = (bf16[1,36992]{1,0:T(2,128)(2,1)S(1)}, bf16[1,36992]{1,0:T(2,128)(2,1)S(1)}, u32[]{:S(2)}, u32[]{:S(2)}) collective-permute-start(bf16[1,36992]{1,0:T(2,128)(2,1)S(1)} %concatenate.26), channel_id=1, source_target_pairs={{0,8},{2,10},{4,12},{6,14},{8,0},{10,2},{12,4},{14,6},{1,9},{3,11}... | collective-permute-start | bytes 221960 | tf_op jit(solution)/shard_map/ppermute | solution.py:49
  7.5 13.4 %collective-permute-start = (bf16[96,128]{1,0:T(8,128)(2,1)S(1)}, bf16[96,128]{1,0:T(8,128)(2,1)S(1)}, u32[]{:S(2)}, u32[]{:S(2)}) collective-permute-start(bf16[96,128]{1,0:T(8,128)(2,1)S(1)} %get-tuple-element.37), channel_id=1, source_target_pairs={{0,2},{2,4},{4,6},{6,8},{8,10},{10,12},{12,14},{1,3},{3,5},{5,7},{... | collective-permute-start | bytes 73736 | tf_op jit(solution)/shard_map/ppermute | solution.py:19
  10.9 10.0 %collective-permute-start.1 = (bf16[96,128]{1,0:T(8,128)(2,1)S(1)}, bf16[96,128]{1,0:T(8,128)(2,1)S(1)}, u32[]{:S(2)}, u32[]{:S(2)}) collective-permute-start(bf16[96,128]{1,0:T(8,128)(2,1)S(1)} %get-tuple-element.36), channel_id=1, source_target_pairs={{2,0},{4,2},{6,4},{8,6},{10,8},{12,10},{14,12},{3,1},{5,3},{7,5},{... | collective-permute-start | bytes 73736 | tf_op jit(solution)/shard_map/ppermute | solution.py:22
  13.2 65.0 %copy-start.9 = (bf16[320,192]{0,1:T(8,128)(2,1)}, bf16[320,192]{0,1:T(8,128)(2,1)S(1)}, u32[]{:S(2)}) copy-start(bf16[320,192]{0,1:T(8,128)(2,1)S(1)} %fusion.131) | copy-start | bytes 368644
  15.2 5.0 %copy-start = (bf16[320,320]{1,0:T(8,128)(2,1)S(1)}, bf16[320,320]{1,0:T(8,128)(2,1)}, u32[]{:S(2)}) copy-start(bf16[320,320]{1,0:T(8,128)(2,1)} %constant.39.clone) | copy-start | bytes 614404
  15.2 5.6 %copy-start.3 = (bf16[320,320]{1,0:T(8,128)(2,1)S(1)}, bf16[320,320]{1,0:T(8,128)(2,1)}, u32[]{:S(2)}) copy-start(bf16[320,320]{1,0:T(8,128)(2,1)} %constant.40.clone) | copy-start | bytes 614404
  15.3 5.6 %copy-start.27 = (bf16[128,128]{1,0:T(8,128)(2,1)S(1)}, bf16[128,128]{1,0:T(8,128)(2,1)}, u32[]{:S(2)}) copy-start(bf16[128,128]{1,0:T(8,128)(2,1)} %param.7) | copy-start | bytes 98308
  21.0 13.8 %collective-permute-start.3 = (bf16[320,96]{1,0:T(8,128)(2,1)S(1)}, bf16[320,96]{1,0:T(8,128)(2,1)S(1)}, u32[]{:S(2)}, u32[]{:S(2)}) collective-permute-start(bf16[320,96]{1,0:T(8,128)(2,1)S(1)} %get-tuple-element.35), channel_id=1, source_target_pairs={{1,0},{3,2},{5,4},{7,6},{9,8},{11,10},{13,12},{15,14},{17,16},{19,... | collective-permute-start | bytes 184328 | tf_op jit(solution)/shard_map/ppermute | solution.py:22
  22.3 12.5 %collective-permute-start.2 = (bf16[320,96]{1,0:T(8,128)(2,1)S(1)}, bf16[320,96]{1,0:T(8,128)(2,1)S(1)}, u32[]{:S(2)}, u32[]{:S(2)}) collective-permute-start(bf16[320,96]{1,0:T(8,128)(2,1)S(1)} %get-tuple-element.34), channel_id=1, source_target_pairs={{0,1},{2,3},{4,5},{6,7},{8,9},{10,11},{12,13},{14,15},{16,17},{18,... | collective-permute-start | bytes 184328 | tf_op jit(solution)/shard_map/ppermute | solution.py:19
  25.4 9.4 %copy-start.19 = (bf16[1,36992]{1,0:T(2,128)(2,1)}, bf16[1,36992]{1,0:T(2,128)(2,1)S(1)}, u32[]{:S(2)}) copy-start(bf16[1,36992]{1,0:T(2,128)(2,1)S(1)} %collective-permute-done.4) | copy-start | bytes 221956
  26.1 8.7 %copy-start.21 = (bf16[192,320]{1,0:T(8,128)(2,1)}, bf16[192,320]{1,0:T(8,128)(2,1)S(1)}, u32[]{:S(2)}) copy-start(bf16[192,320]{1,0:T(8,128)(2,1)S(1)} %convolution_convert_fusion.4) | copy-start | bytes 368644
  28.5 18.7 %collective-permute-start.5 = (bf16[2,36992]{1,0:T(2,128)(2,1)}, bf16[2,36992]{1,0:T(2,128)(2,1)}, u32[]{:S(2)}, u32[]{:S(2)}) collective-permute-start(bf16[2,36992]{1,0:T(2,128)(2,1)} %pad_maximum_fusion.4), channel_id=1, source_target_pairs={{0,4},{2,6},{4,0},{6,2},{8,12},{10,14},{12,8},{14,10},{1,5},{3,7},... | collective-permute-start | bytes 443912 | tf_op jit(solution)/shard_map/ppermute | solution.py:49
  38.7 8.6 %copy-start.14 = (bf16[320,320]{1,0:T(8,128)(2,1)}, bf16[320,320]{1,0:T(8,128)(2,1)S(1)}, u32[]{:S(2)}) copy-start(bf16[320,320]{1,0:T(8,128)(2,1)S(1)} %get-tuple-element.22) | copy-start | bytes 614404
  42.6 6.4 %copy-start.20 = (bf16[1,36992]{1,0:T(2,128)(2,1)S(1)}, bf16[1,36992]{1,0:T(2,128)(2,1)}, u32[]{:S(2)}) copy-start(bf16[1,36992]{1,0:T(2,128)(2,1)} %copy-done.19) | copy-start | bytes 221956
  48.7 11.0 %copy-start.11 = (bf16[2,192,320]{2,1,0:T(8,128)(2,1)}, bf16[2,192,320]{2,1,0:T(8,128)(2,1)S(1)}, u32[]{:S(2)}) copy-start(bf16[2,192,320]{2,1,0:T(8,128)(2,1)S(1)} %convolution_convert_fusion.1) | copy-start | bytes 737284
  49.0 11.5 %copy-start.23 = (bf16[2,192,320]{2,1,0:T(8,128)(2,1)}, bf16[2,192,320]{2,1,0:T(8,128)(2,1)S(1)}, u32[]{:S(2)}) copy-start(bf16[2,192,320]{2,1,0:T(8,128)(2,1)S(1)} %fusion.21) | copy-start | bytes 737284
  51.3 8.5 %collective-permute-start.6 = (bf16[4,36992]{1,0:T(4,128)(2,1)}, bf16[4,36992]{1,0:T(4,128)(2,1)S(1)}, u32[]{:S(2)}, u32[]{:S(2)}) collective-permute-start(bf16[4,36992]{1,0:T(4,128)(2,1)} %pad_maximum_fusion.2), channel_id=1, source_target_pairs={{0,2},{2,0},{4,6},{6,4},{8,10},{10,8},{12,14},{14,12},{1,3},{3,1},... | collective-permute-start | bytes 887816 | tf_op jit(solution)/shard_map/ppermute | solution.py:49
  62.1 11.5 %copy-start.4 = (bf16[4,192,320]{2,1,0:T(8,128)(2,1)}, bf16[4,192,320]{2,1,0:T(8,128)(2,1)S(1)}, u32[]{:S(2)}) copy-start(bf16[4,192,320]{2,1,0:T(8,128)(2,1)S(1)} %convolution_convert_fusion) | copy-start | bytes 1474564
  76.1 2.4 %copy-start.2 = (f32[4,320,320]{2,1,0:T(8,128)S(1)}, f32[4,320,320]{2,1,0:T(8,128)}, u32[]{:S(2)}) copy-start(f32[4,320,320]{2,1,0:T(8,128)} %fusion.71) | copy-start | bytes 4915204
  78.6 1.5 %copy-start.1 = (f32[4,320,320]{2,1,0:T(8,128)S(1)}, f32[4,320,320]{2,1,0:T(8,128)}, u32[]{:S(2)}) copy-start(f32[4,320,320]{2,1,0:T(8,128)} %fusion.69) | copy-start | bytes 4915204
  78.6 1.7 %copy-start.5 = (bf16[4,192,320]{2,1,0:T(8,128)(2,1)S(1)}, bf16[4,192,320]{2,1,0:T(8,128)(2,1)}, u32[]{:S(2)}) copy-start(bf16[4,192,320]{2,1,0:T(8,128)(2,1)} %copy-done.4) | copy-start | bytes 1474564
  80.2 1.6 %copy-start.13 = (bf16[128,320]{1,0:T(8,128)(2,1)S(1)}, bf16[128,320]{1,0:T(8,128)(2,1)}, u32[]{:S(2)}) copy-start(bf16[128,320]{1,0:T(8,128)(2,1)} %slice.73) | copy-start | bytes 245764
  87.7 2.3 %copy-start.6 = (bf16[2,320,320]{2,1,0:T(8,128)(2,1)}, bf16[2,320,320]{2,1,0:T(8,128)(2,1)S(1)}, u32[]{:S(2)}) copy-start(bf16[2,320,320]{2,1,0:T(8,128)(2,1)S(1)} %get-tuple-element.19) | copy-start | bytes 1228804
  (11 other events, 13.4 us)

commit v4 on v3

--- a/solution.py
+++ b/solution.py
@@ -40,13 +40,15 @@
 
 def exchange_rounds(block):
     size = lax.axis_size("orient")
-    rounds = [block]
     step = 1
     while step * 2 < size:
         step *= 2
+    rounds = [block]
     held = block
     while step >= 1:
         other = lax.ppermute(held, "orient", [(i, i ^ step) for i in range(size)])
+        if step > 1:
+            other, rounds[-1] = lax.optimization_barrier((other, rounds[-1]))
         rounds.append(other)
         held = jnp.concatenate([held, other], axis=0)
         step //= 2

time: 104 us -> 105 us (level)
  other arithmetic: 4.54 us -> 2.96 us
    unnamed x58 -> x50, local copies, waits for them, and re-layouts: 4.1 us -> 2.98 us
  transfers between devices with their start and end apart: 7 -> 7, of which waited for: 0 -> 1; matrix products, arithmetic and copies ran while one was open for 29% -> 29% of each run, Pallas kernels for 0% -> 0%
where the time goes in v4:
time: 105 us; the launch traced here: 103 us
  matrix products  53.1 us (51%)
  starting transfers between devices  16.4 us (16%)
  between operations  15.2 us (14%)
  local copies, waits for them, and re-layouts  14.8 us (14%)
  other arithmetic  2.96 us (3%)
    dot_general x4, matrix products, chunk_stats(): jnp.einsum('orq,qc->orc', left_imag, col_sin, preferred_element_type=f32)  8.81 us
    dot_general x4, matrix products, chunk_stats(): jnp.einsum('orq,qc->orc', left_real, col_cos, preferred_element_type=f32)  7.6 us
    ppermute x3, starting transfers between devices, exchange_rounds(): other = lax.ppermute(held, 'orient', [(i, i ^ step) for i in range(size)])  7.41 us
    dot_general x4, matrix products, chunk_stats(): jnp.einsum('opk,okq->opq', left_s, part_real, preferred_element_type=f32)  6.67 us
    ppermute x2, starting transfers between devices, extended(): lax.ppermute(lax.slice_in_dim(block, block.shape[dim] - width, None, axis...  6.42 us
    dot_general x4, matrix products, chunk_stats(): jnp.einsum('orp,opq->orq', rc, prod_imag, preferred_element_type=f32)  5.8 us
    dot_general x4, matrix products, chunk_stats(): jnp.einsum('opk,okq->opq', left_c, part_imag, preferred_element_type=f32)  5.56 us
    dot_general x4, matrix products, chunk_stats(): jnp.einsum('opk,okq->opq', left_c, part_real, preferred_element_type=f32)  4.6 us
  transfers between devices with their start and end apart: 7, of which 1 were waited for; matrix products, arithmetic and copies ran while one was open for 29% of the time, Pallas kernels for 0%

profile of v4, /device:TPU:0, one launch (start us, length us, event | category | flops | bytes accessed | tf_op | source)
XLA Modules:
  0.0 103.4 jit_solution(7819010672600314931)
XLA Ops:
  2.6 4.1 %collective-permute-start.4 = (bf16[1,36992]{1,0:T(2,128)(2,1)S(1)}, bf16[1,36992]{1,0:T(2,128)(2,1)S(1)}, u32[]{:S(2)}, u32[]{:S(2)}) collective-permute-start(bf16[1,36992]{1,0:T(2,128)(2,1)S(1)} %concatenate.25), channel_id=1, source_target_pairs={{0,8},{2,10},{4,12},{6,14},{8,0},{10,2},{12,4},{14,6},{1,9},{3,11}... | collective-permute-start | bytes 221960 | tf_op jit(solution)/shard_map/ppermute | solution.py:49
  7.5 3.4 %collective-permute-start = (bf16[96,128]{1,0:T(8,128)(2,1)S(1)}, bf16[96,128]{1,0:T(8,128)(2,1)S(1)}, u32[]{:S(2)}, u32[]{:S(2)}) collective-permute-start(bf16[96,128]{1,0:T(8,128)(2,1)S(1)} %get-tuple-element.45), channel_id=1, source_target_pairs={{0,2},{2,4},{4,6},{6,8},{8,10},{10,12},{12,14},{1,3},{3,5},{5,7},{... | collective-permute-start | bytes 73736 | tf_op jit(solution)/shard_map/ppermute | solution.py:19
  13.9 1.6 %slice.78 = bf16[128,320]{1,0:T(8,128)(2,1)} slice(bf16[320,320]{1,0:T(8,128)(2,1)} %constant.39.clone), slice={[96:224], [0:320]} | slice | bytes 163840 | tf_op jit(solution)/shard_map/slice | solution.py:75
  18.0 3.0 %collective-permute-start.2 = (bf16[320,96]{1,0:T(8,128)(2,1)S(1)}, bf16[320,96]{1,0:T(8,128)(2,1)S(1)}, u32[]{:S(2)}, u32[]{:S(2)}) collective-permute-start(bf16[320,96]{1,0:T(8,128)(2,1)S(1)} %get-tuple-element.42), channel_id=1, source_target_pairs={{0,1},{2,3},{4,5},{6,7},{8,9},{10,11},{12,13},{14,15},{16,17},{18,... | collective-permute-start | bytes 184328 | tf_op jit(solution)/shard_map/ppermute | solution.py:19
  23.5 2.7 %collective-permute-start.5 = (bf16[2,36992]{1,0:T(2,128)(2,1)}, bf16[2,36992]{1,0:T(2,128)(2,1)S(1)}, u32[]{:S(2)}, u32[]{:S(2)}) collective-permute-start(bf16[2,36992]{1,0:T(2,128)(2,1)} %pad_maximum_fusion.4), channel_id=1, source_target_pairs={{0,4},{2,6},{4,0},{6,2},{8,12},{10,14},{12,8},{14,10},{1,5},{3,7},... | collective-permute-start | bytes 443912 | tf_op jit(solution)/shard_map/ppermute | solution.py:49
  28.2 2.1 %fusion.29 = f32[1,320,320]{2,1,0:T(8,128)} fusion(f32[320,320]{1,0:T(8,128)S(1)} %fusion.133, bf16[192,320]{1,0:T(8,128)(2,1)S(1)} %convolution_convert_fusion.4, f32[8,320,320]{2,1,0:T(8,128)} %param.10, s32[]{:T(128)S(6)} %select_n.35, bf16[96,320]{1,0:T(8,128)(2,1)S(1)} %get-tuple-element.36, bf16[96,320]{1,0:T(8,128)(2,1)S(1)} %get-tuple-element.35), kind=kOutput, calls=%fused_computation.52 | convolution fusion | flops 39976960 | bytes 1474564 | tf_op jit(solution)/shard_map/opk,okq->opq/dot_general | solution.py:107
  39.3 1.5 %fusion.27 = f32[1,320,320]{2,1,0:T(8,128)S(1)} fusion(f32[320,320]{1,0:T(8,128)} %fusion.131, bf16[192,320]{1,0:T(8,128)(2,1)S(1)} %convolution_convert_fusion.3, f32[8,320,320]{2,1,0:T(8,128)} %param.10, s32[]{:T(128)S(6)} %select_n.36, bf16[96,320]{1,0:T(8,128)(2,1)S(1)} %get-tuple-element.36, bf16[96,320]{1,0:T(8,128)(2,1)S(1)} %get-tuple-element.35), kind=kOutput, calls=%fused_computation.50 | convolution fusion | flops 39976960 | bytes 1474564 | tf_op jit(solution)/shard_map/opk,okq->opq/dot_general | solution.py:107
  45.4 1.9 %fusion.53 = f32[128,128]{1,0:T(8,128)} fusion(f32[128,320]{1,0:T(8,128)} %fusion.124, bf16[320,320]{1,0:T(8,128)(2,1)S(1)} %get-tuple-element.34, bf16[320,320]{1,0:T(8,128)(2,1)S(1)} %copy-done.3), kind=kOutput, calls=%fused_computation.86 | convolution fusion | flops 36782080 | bytes 671744 | tf_op jit(solution)/shard_map/orq,qc->orc/dot_general | solution.py:125
  49.1 1.9 %fusion.51 = f32[128,128]{1,0:T(8,128)} fusion(f32[128,320]{1,0:T(8,128)} %fusion.119, bf16[320,320]{1,0:T(8,128)(2,1)S(1)} %get-tuple-element.29, bf16[320,320]{1,0:T(8,128)(2,1)S(1)} %copy-done.3), kind=kOutput, calls=%fused_computation.84 | convolution fusion | flops 36782080 | bytes 671744 | tf_op jit(solution)/shard_map/orq,qc->orc/dot_general | solution.py:125
  57.8 2.4 %fusion.91 = f32[2,320,320]{2,1,0:T(8,128)} fusion(bf16[2,192,320]{2,1,0:T(8,128)(2,1)} %fusion.21, bf16[320,192]{0,1:T(8,128)(2,1)S(1)} %fusion.130), kind=kOutput, calls=%fused_computation.139 | convolution fusion | flops 78643200 | bytes 1187840 | tf_op jit(solution)/shard_map/opk,okq->opq/dot_general | solution.py:107
  62.8 1.6 %fusion.6 = bf16[4,192,320]{2,1,0:T(8,128)(2,1)S(1)} fusion(bf16[4,192,192]{2,1,0:T(8,128)(2,1)} %copy-done.17, bf16[96,320]{1,0:T(8,128)(2,1)S(1)} %get-tuple-element.36, bf16[96,320]{1,0:T(8,128)(2,1)S(1)} %get-tuple-element.35), kind=kOutput, calls=%fused_computation.16 | convolution fusion | flops 95109120 | bytes 909312 | tf_op jit(solution)/shard_map/okj,jq->okq/dot_general | solution.py:101
  70.6 1.9 %fusion.71 = f32[4,320,320]{2,1,0:T(8,128)} fusion(bf16[4,192,320]{2,1,0:T(8,128)(2,1)S(1)} %convolution_convert_fusion, bf16[320,192]{0,1:T(8,128)(2,1)S(1)} %fusion.130), kind=kOutput, calls=%fused_computation.116 | convolution fusion | flops 157286400 | bytes 2252800 | tf_op jit(solution)/shard_map/opk,okq->opq/dot_general | solution.py:104
  72.4 1.8 %fusion.69 = f32[4,320,320]{2,1,0:T(8,128)} fusion(bf16[4,192,320]{2,1,0:T(8,128)(2,1)S(1)} %fusion.6, bf16[320,192]{0,1:T(8,128)(2,1)S(1)} %fusion.130), kind=kOutput, calls=%fused_computation.114 | convolution fusion | flops 157286400 | bytes 2252800 | tf_op jit(solution)/shard_map/opk,okq->opq/dot_general | solution.py:107
  76.8 2.1 %constant_dynamic-slice_fusion.5 = (f32[1,320,320]{2,1,0:T(8,128)S(1)}, f32[1,320,320]{2,1,0:T(8,128)S(1)}, f32[1,320,320]{2,1,0:T(8,128)S(1)}, f32[1,320,320]{2...) fusion(f32[8,320,320]{2,1,0:T(8,128)} %param.10, s32[]{:T(128)S(6)} %select_n.37, ...), kind=kLoop, calls=%fused_computation.167 | loop fusion | bytes 4915224 | tf_op jit(solution)/shard_map/jit(dynamic_index_in_dim)/dynamic_slice | solution.py:110
  80.8 1.6 %multiply_convert_fusion = bf16[4,320,320]{2,1,0:T(8,128)(2,1)S(1)} fusion(f32[4,320,320]{2,1,0:T(8,128)S(1)} %copy-done.1, bf16[4,192,320]{2,1,0:T(8,128)(2,1)S(1)} %copy-done.5, f32[1,320,320]{2,1,0:T(8,128)S(1)} %get-tuple-element.25, f32[1,320,320]{2,1,0:T(8,128)S(1)} %get-tuple-element.26, f32[1,320,320]{2,1,0:T(8,128)S(1)} %get-tuple-element.22, ...), kind=kOutput, calls=%fused_computation.9 | convolution fusion | flops 159744000 | bytes 4710400 | tf_op jit(solution)/shard_map/opk,okq->opq/dot_general | solution.py:107
  82.4 1.7 %fusion.81 = f32[4,128,320]{1,2,0:T(8,128)} fusion(bf16[128,320]{1,0:T(8,128)(2,1)S(1)} %copy-done.13, bf16[4,320,320]{2,1,0:T(8,128)(2,1)S(1)} %multiply_convert_fusion.1, bf16[4,320,320]{2,1,0:T(8,128)(2,1)S(1)} %multiply_convert_fusion, f32[320,320]{1,0:T(8,128)S(1)} %fusion.34, f32[320,320]{1,0:T(8,128)S(1)} %fusion.32), kind=kOutput, calls=%fused_computation.126 | convolution fusion | flops 107315200 | bytes 3194880 | tf_op jit(solution)/shard_map/orp,opq->orq/dot_general | solution.py:122
  84.1 1.5 %fusion.83 = f32[4,128,320]{1,2,0:T(8,128)} fusion(bf16[128,320]{1,0:T(8,128)(2,1)S(1)} %copy-done.13, bf16[4,320,320]{2,1,0:T(8,128)(2,1)S(1)} %multiply_convert_fusion.1, bf16[4,320,320]{2,1,0:T(8,128)(2,1)S(1)} %multiply_convert_fusion, f32[320,320]{1,0:T(8,128)S(1)} %fusion.34, f32[320,320]{1,0:T(8,128)S(1)} %fusion.32), kind=kOutput, calls=%fused_computation.128 | convolution fusion | flops 107315200 | bytes 3194880 | tf_op jit(solution)/shard_map/orp,opq->orq/dot_general | solution.py:118
  86.9 1.5 %add_convert_fusion = (bf16[2,320,320]{2,1,0:T(8,128)(2,1)S(1)}, bf16[2,320,320]{2,1,0:T(8,128)(2,1)}) fusion(f32[2,320,320]{2,1,0:T(8,128)S(1)} %fusion.10, f32[320,320]{1,0:T(8,128)S(1)} %fusion.34, f32[320,320]{1,0:T(8,128)S(1)} %fusion.32, f32[1,320,320]{2,1,0:T(8,128)S(1)} %get-tuple-element.24, f32[1,320,320]{2,1,0:T(8,128)S(1)} %get-tuple-element.21, ...), kind=kOutput, calls=%fused_computation.94 | convolution fusion | flops 81305600 | bytes 4464640 | tf_op jit(solution)/shard_map/opk,okq->opq/dot_general | solution.py:107
  88.4 2.3 %fusion.103 = f32[2,128,320]{1,2,0:T(8,128)} fusion(bf16[2,320,320]{2,1,0:T(8,128)(2,1)} %get-tuple-element.28, bf16[128,320]{1,0:T(8,128)(2,1)S(1)} %copy-done.13), kind=kOutput, calls=%fused_computation.152 | convolution fusion | flops 52428800 | bytes 819200 | tf_op jit(solution)/shard_map/orp,opq->orq/dot_general | solution.py:122
  91.8 2.7 %fusion.35 = f32[4,128,128]{2,1,0:T(8,128)} fusion(f32[4,128,320]{1,2,0:T(8,128)} %fusion.81, bf16[128,320]{1,0:T(8,128)(2,1)S(1)} %slice.89, bf16[4,320,320]{2,1,0:T(8,128)(2,1)S(1)} %multiply_convert_fusion.1, bf16[4,320,320]{2,1,0:T(8,128)(2,1)S(1)} %multiply_convert_fusion, f32[320,320]{1,0:T(8,128)S(1)} %fusion.34, f32[320,320]{1,0:T(8,128)S(1)} %fusion.32), kind=kOutput, calls=%fused_computation.58 | convolution fusion | flops 149585920 | bytes 3457024 | tf_op jit(solution)/shard_map/orq,qc->orc/dot_general | solution.py:125
  94.4 2.3 %fusion.43 = f32[2,128,128]{2,1,0:T(8,128)} fusion(f32[2,128,320]{1,2,0:T(8,128)} %fusion.103, bf16[2,320,320]{2,1,0:T(8,128)(2,1)} %copy-done.6, bf16[128,320]{1,0:T(8,128)(2,1)S(1)} %slice.89), kind=kOutput, calls=%fused_computation.76 | convolution fusion | flops 73564160 | bytes 950272 | tf_op jit(solution)/shard_map/orq,qc->orc/dot_general | solution.py:125
  96.8 2.7 %multiply_reduce_fusion = (f32[128,128]{1,0:T(8,128)}, f32[128,128]{1,0:T(8,128)}, f32[128,128]{1,0:T(8,128)}) fusion(f32[4,128,128]{2,1,0:T(8,128)} %fusion.35, bf16[320,320]{1,0:T(8,128)(2,1)S(1)} %copy-done, f32[4,128,320]{1,2,0:T(8,128)} %fusion.83, bf16[128,320]{1,0:T(8,128)(2,1)S(1)} %slice.89, bf16[4,320,320]{2,1,0:T(8,128)(2,1)S(1)} %multiply_convert_fusion.1, ...), kind=kOutput, calls=%fused_computation.118 | convolution fusion | flops 149929984 | bytes 4259840 | tf_op jit(solution)/shard_map/orq,qc->orc/dot_general | solution.py:125
  99.5 1.7 %multiply_reduce_fusion.1 = (f32[128,128]{1,0:T(8,128)S(1)}, f32[128,128]{1,0:T(8,128)S(1)}, f32[128,128]{1,0:T(8,128)S(1)}) fusion(f32[2,128,128]{2,1,0:T(8,128)} %fusion.43, bf16[320,320]{1,0:T(8,128)(2,1)S(1)} %copy-done, f32[2,128,320]{1,2,0:T(8,128)} %fusion.105, bf16[2,320,320]{2,1,0:T(8,128)(2,1)} %get-tuple-element.28, bf16[128,320]{1,0:T(8,128)(2,1)S(1)} %slice.89), kind=kOutput, calls=%fused_computation.145 | convolution fusion | flops 73711616 | bytes 1261568 | tf_op jit(solution)/shard_map/orq,qc->orc/dot_general | solution.py:125
  101.2 2.2 %multiply_select_fusion = (f32[128,128]{1,0:T(8,128)}, f32[128,128]{1,0:T(8,128)}, f32[128,128]{1,0:T(8,128)}) fusion(f32[128,128]{1,0:T(8,128)} %get-tuple-element.15, f32[128,128]{1,0:T(8,128)S(1)} %get-tuple-element.18, f32[128,128]{1,0:T(8,128)} %fusion.56, pred[128]{0:T(512)(128)(4,1)S(1)} %iota_compare_fusion, f32[128,128]{1,0:T(8,128)} %get-tuple-element.16, ...), kind=kOutput, calls=%fused_computation.156 | convolution fusion | flops 37076992 | bytes 1286656 | tf_op jit(solution)/shard_map/orq,qc->orc/dot_general | solution.py:125
  (114 shorter events, 36.1 us)
Async XLA Ops:
  0.6 14.9 %copy-start.3 = (bf16[320,320]{1,0:T(8,128)(2,1)S(1)}, bf16[320,320]{1,0:T(8,128)(2,1)}, u32[]{:S(2)}) copy-start(bf16[320,320]{1,0:T(8,128)(2,1)} %constant.40.clone) | copy-start | bytes 614404
  0.6 14.9 %copy-start.23 = (bf16[128,128]{1,0:T(8,128)(2,1)S(1)}, bf16[128,128]{1,0:T(8,128)(2,1)}, u32[]{:S(2)}) copy-start(bf16[128,128]{1,0:T(8,128)(2,1)} %param.7) | copy-start | bytes 98308
  2.6 18.5 %collective-permute-start.4 = (bf16[1,36992]{1,0:T(2,128)(2,1)S(1)}, bf16[1,36992]{1,0:T(2,128)(2,1)S(1)}, u32[]{:S(2)}, u32[]{:S(2)}) collective-permute-start(bf16[1,36992]{1,0:T(2,128)(2,1)S(1)} %concatenate.25), channel_id=1, source_target_pairs={{0,8},{2,10},{4,12},{6,14},{8,0},{10,2},{12,4},{14,6},{1,9},{3,11}... | collective-permute-start | bytes 221960 | tf_op jit(solution)/shard_map/ppermute | solution.py:49
  7.5 8.1 %collective-permute-start = (bf16[96,128]{1,0:T(8,128)(2,1)S(1)}, bf16[96,128]{1,0:T(8,128)(2,1)S(1)}, u32[]{:S(2)}, u32[]{:S(2)}) collective-permute-start(bf16[96,128]{1,0:T(8,128)(2,1)S(1)} %get-tuple-element.45), channel_id=1, source_target_pairs={{0,2},{2,4},{4,6},{6,8},{8,10},{10,12},{12,14},{1,3},{3,5},{5,7},{... | collective-permute-start | bytes 73736 | tf_op jit(solution)/shard_map/ppermute | solution.py:19
  10.9 5.7 %collective-permute-start.1 = (bf16[96,128]{1,0:T(8,128)(2,1)S(1)}, bf16[96,128]{1,0:T(8,128)(2,1)S(1)}, u32[]{:S(2)}, u32[]{:S(2)}) collective-permute-start(bf16[96,128]{1,0:T(8,128)(2,1)S(1)} %get-tuple-element.44), channel_id=1, source_target_pairs={{2,0},{4,2},{6,4},{8,6},{10,8},{12,10},{14,12},{3,1},{5,3},{7,5},{... | collective-permute-start | bytes 73736 | tf_op jit(solution)/shard_map/ppermute | solution.py:22
  13.9 65.0 %copy-start.9 = (bf16[320,192]{0,1:T(8,128)(2,1)}, bf16[320,192]{0,1:T(8,128)(2,1)S(1)}, u32[]{:S(2)}) copy-start(bf16[320,192]{0,1:T(8,128)(2,1)S(1)} %fusion.129) | copy-start | bytes 368644
  16.7 13.6 %collective-permute-start.3 = (bf16[320,96]{1,0:T(8,128)(2,1)S(1)}, bf16[320,96]{1,0:T(8,128)(2,1)S(1)}, u32[]{:S(2)}, u32[]{:S(2)}) collective-permute-start(bf16[320,96]{1,0:T(8,128)(2,1)S(1)} %get-tuple-element.43), channel_id=1, source_target_pairs={{1,0},{3,2},{5,4},{7,6},{9,8},{11,10},{13,12},{15,14},{17,16},{19,... | collective-permute-start | bytes 184328 | tf_op jit(solution)/shard_map/ppermute | solution.py:22
  18.0 12.3 %collective-permute-start.2 = (bf16[320,96]{1,0:T(8,128)(2,1)S(1)}, bf16[320,96]{1,0:T(8,128)(2,1)S(1)}, u32[]{:S(2)}, u32[]{:S(2)}) collective-permute-start(bf16[320,96]{1,0:T(8,128)(2,1)S(1)} %get-tuple-element.42), channel_id=1, source_target_pairs={{0,1},{2,3},{4,5},{6,7},{8,9},{10,11},{12,13},{14,15},{16,17},{18,... | collective-permute-start | bytes 184328 | tf_op jit(solution)/shard_map/ppermute | solution.py:19
  21.8 8.5 %copy-start.20 = (bf16[192,320]{1,0:T(8,128)(2,1)}, bf16[192,320]{1,0:T(8,128)(2,1)S(1)}, u32[]{:S(2)}) copy-start(bf16[192,320]{1,0:T(8,128)(2,1)S(1)} %fusion.41) | copy-start | bytes 368644
  23.5 8.8 %collective-permute-start.5 = (bf16[2,36992]{1,0:T(2,128)(2,1)}, bf16[2,36992]{1,0:T(2,128)(2,1)S(1)}, u32[]{:S(2)}, u32[]{:S(2)}) collective-permute-start(bf16[2,36992]{1,0:T(2,128)(2,1)} %pad_maximum_fusion.4), channel_id=1, source_target_pairs={{0,4},{2,6},{4,0},{6,2},{8,12},{10,14},{12,8},{14,10},{1,5},{3,7},... | collective-permute-start | bytes 443912 | tf_op jit(solution)/shard_map/ppermute | solution.py:49
  26.4 4.3 %copy-start = (bf16[320,320]{1,0:T(8,128)(2,1)S(1)}, bf16[320,320]{1,0:T(8,128)(2,1)}, u32[]{:S(2)}) copy-start(bf16[320,320]{1,0:T(8,128)(2,1)} %constant.39.clone) | copy-start | bytes 614404
  34.1 16.9 %copy-start.11 = (bf16[2,192,320]{2,1,0:T(8,128)(2,1)}, bf16[2,192,320]{2,1,0:T(8,128)(2,1)S(1)}, u32[]{:S(2)}) copy-start(bf16[2,192,320]{2,1,0:T(8,128)(2,1)S(1)} %convolution_convert_fusion.1) | copy-start | bytes 737284
  37.3 22.9 %collective-permute-start.6 = (bf16[4,36992]{1,0:T(4,128)(2,1)}, bf16[4,36992]{1,0:T(4,128)(2,1)}, u32[]{:S(2)}, u32[]{:S(2)}) collective-permute-start(bf16[4,36992]{1,0:T(4,128)(2,1)} %pad_maximum_fusion.2), channel_id=1, source_target_pairs={{0,2},{2,0},{4,6},{6,4},{8,10},{10,8},{12,14},{14,12},{1,3},{3,1},... | collective-permute-start | bytes 887816 | tf_op jit(solution)/shard_map/ppermute | solution.py:49
  39.3 2.9 %copy-start.15 = (f32[320,320]{1,0:T(8,128)S(1)}, f32[320,320]{1,0:T(8,128)}, u32[]{:S(2)}) copy-start(f32[320,320]{1,0:T(8,128)} %fusion.134) | copy-start | bytes 1228804
  39.3 2.9 %copy-start.16 = (f32[1,320,320]{2,1,0:T(8,128)S(1)}, f32[1,320,320]{2,1,0:T(8,128)}, u32[]{:S(2)}) copy-start(f32[1,320,320]{2,1,0:T(8,128)} %fusion.29) | copy-start | bytes 1228804
  39.3 2.9 %copy-start.21 = (bf16[192,320]{1,0:T(8,128)(2,1)S(1)}, bf16[192,320]{1,0:T(8,128)(2,1)}, u32[]{:S(2)}) copy-start(bf16[192,320]{1,0:T(8,128)(2,1)} %copy-done.20) | copy-start | bytes 368644
  43.7 8.8 %copy-start.14 = (bf16[320,320]{1,0:T(8,128)(2,1)}, bf16[320,320]{1,0:T(8,128)(2,1)S(1)}, u32[]{:S(2)}) copy-start(bf16[320,320]{1,0:T(8,128)(2,1)S(1)} %get-tuple-element.30) | copy-start | bytes 614404
  47.3 5.1 %copy-start.19 = (f32[128,320]{1,0:T(8,128)S(1)}, f32[128,320]{1,0:T(8,128)}, u32[]{:S(2)}) copy-start(f32[128,320]{1,0:T(8,128)} %fusion.127) | copy-start | bytes 491524
  47.3 5.1 %copy-start.22 = (f32[128,128]{1,0:T(8,128)S(1)}, f32[128,128]{1,0:T(8,128)}, u32[]{:S(2)}) copy-start(f32[128,128]{1,0:T(8,128)} %fusion.53) | copy-start | bytes 196612
  62.8 11.5 %copy-start.4 = (bf16[4,192,320]{2,1,0:T(8,128)(2,1)}, bf16[4,192,320]{2,1,0:T(8,128)(2,1)S(1)}, u32[]{:S(2)}) copy-start(bf16[4,192,320]{2,1,0:T(8,128)(2,1)S(1)} %convolution_convert_fusion) | copy-start | bytes 1474564
  76.7 2.4 %copy-start.2 = (f32[4,320,320]{2,1,0:T(8,128)S(1)}, f32[4,320,320]{2,1,0:T(8,128)}, u32[]{:S(2)}) copy-start(f32[4,320,320]{2,1,0:T(8,128)} %fusion.71) | copy-start | bytes 4915204
  79.2 1.7 %copy-start.5 = (bf16[4,192,320]{2,1,0:T(8,128)(2,1)S(1)}, bf16[4,192,320]{2,1,0:T(8,128)(2,1)}, u32[]{:S(2)}) copy-start(bf16[4,192,320]{2,1,0:T(8,128)(2,1)} %copy-done.4) | copy-start | bytes 1474564
  80.8 1.6 %copy-start.13 = (bf16[128,320]{1,0:T(8,128)(2,1)S(1)}, bf16[128,320]{1,0:T(8,128)(2,1)}, u32[]{:S(2)}) copy-start(bf16[128,320]{1,0:T(8,128)(2,1)} %slice.78) | copy-start | bytes 245764
  88.4 2.3 %copy-start.6 = (bf16[2,320,320]{2,1,0:T(8,128)(2,1)}, bf16[2,320,320]{2,1,0:T(8,128)(2,1)S(1)}, u32[]{:S(2)}) copy-start(bf16[2,320,320]{2,1,0:T(8,128)(2,1)S(1)} %get-tuple-element.27) | copy-start | bytes 1228804
  (7 other events, 9.3 us)

commit v5 on v1

v5 whole, which is shorter than its diff:
```python
import functools
import math

import jax
import jax.numpy as jnp
import ml_dtypes
import numpy as np
from jax import lax
from jax.experimental import pallas as pl
from jax.experimental.pallas import tpu as pltpu
from jax.sharding import PartitionSpec as P

RB = 32
CHUNK = 8


def extended(block, sides, width):
    for axis, dim in sides:
        count = lax.axis_size(axis)
        forward = [(i, i + 1) for i in range(count - 1)]
        backward = [(target, source) for source, target in forward]
        low = lax.ppermute(
            lax.slice_in_dim(block, block.shape[dim] - width, None, axis=dim), axis, forward
        )
        high = lax.ppermute(lax.slice_in_dim(block, 0, width, axis=dim), axis, backward)
        block = jnp.concatenate([low, block, high], axis=dim)
    return block


def twiddles(padded_size):
    position = np.arange(padded_size, dtype=np.int64)
    phase_index = (position[:, None] * position[None, :]) % padded_size
    angles = phase_index.astype(np.float32) * np.float32(2.0 * math.pi / padded_size)
    angles = angles.astype(np.float64)
    cosines = np.cos(angles).astype(np.float32).astype(ml_dtypes.bfloat16)
    sines = np.sin(angles).astype(np.float32).astype(ml_dtypes.bfloat16)
    return cosines, sines


def matmul(left, right):
    return jnp.dot(left, right, preferred_element_type=jnp.float32)


def gather_orient(block):
    size = lax.axis_size("orient")
    index = lax.axis_index("orient")
    step = 1
    while step < size:
        pairs = [(i, i ^ step) for i in range(size) if (i ^ step) < size]
        other = lax.ppermute(block, "orient", pairs)
        low_side = (index // step) % 2 == 0
        block = jnp.where(low_side, jnp.concatenate([block, other], 0), jnp.concatenate([other, block], 0))
        step *= 2
    return block


def correlate_kernel(ids_ref, tmpl_ref, ctf_ref, spec_r_ref, spec_i_ref, cos_rows_ref, sin_rows_ref,
                     cos_cols_ref, sin_cols_ref, row_cos_ref, row_sin_ref, col_cos_ref, col_sin_ref,
                     peak_ref, sum_ref, sq_ref, *, scaling):
    bf16 = jnp.bfloat16
    f32 = jnp.float32
    o = pl.program_id(0)

    def mm(a, b):
        return jnp.dot(a, b, preferred_element_type=f32)

    template = tmpl_ref[0]
    part_real = mm(template, cos_rows_ref[...]).astype(bf16)
    part_imag = (-mm(template, sin_rows_ref[...])).astype(bf16)
    cos_cols = cos_cols_ref[...]
    sin_cols = sin_cols_ref[...]
    full_real = mm(cos_cols, part_real) + mm(sin_cols, part_imag)
    full_imag = mm(cos_cols, part_imag) - mm(sin_cols, part_real)
    weight = ctf_ref[0]
    w_real = (full_real * weight).astype(bf16).astype(f32)
    w_imag = (full_imag * weight).astype(bf16).astype(f32)
    spec_real = spec_r_ref[...]
    spec_imag = spec_i_ref[...]
    prod_real = (spec_real * w_real + spec_imag * w_imag).astype(bf16)
    prod_imag = (spec_imag * w_real - spec_real * w_imag).astype(bf16)
    row_cos = row_cos_ref[...]
    row_sin = row_sin_ref[...]
    left_real = (mm(row_cos, prod_real) - mm(row_sin, prod_imag)).astype(bf16)
    left_imag = (mm(row_cos, prod_imag) + mm(row_sin, prod_real)).astype(bf16)
    corr = (mm(left_real, col_cos_ref[...]) - mm(left_imag, col_sin_ref[...])) * scaling

    @pl.when(o == 0)
    def _():
        peak_ref[...] = corr
        sum_ref[...] = corr
        sq_ref[...] = corr * corr

    @pl.when(o > 0)
    def _():
        peak_ref[...] = jnp.maximum(peak_ref[...], corr)
        sum_ref[...] = sum_ref[...] + corr
        sq_ref[...] = sq_ref[...] + corr * corr


def correlate(ids, all_templates, ctf, spec_real, spec_imag, tables, scaling):
    count, box, _ = all_templates.shape
    n = ctf.shape[1]
    tile = tables[4].shape[0]
    full = lambda shape: pl.BlockSpec(shape, lambda o, ids: (0,) * len(shape))
    in_specs = [
        pl.BlockSpec((1, box, box), lambda o, ids: (o, 0, 0)),
        pl.BlockSpec((1, n, n), lambda o, ids: (ids[o], 0, 0)),
        full((n, n)),
        full((n, n)),
    ] + [full(t.shape) for t in tables]
    out_block = full((tile, tile))
    grid_spec = pltpu.PrefetchScalarGridSpec(
        num_scalar_prefetch=1,
        grid=(count,),
        in_specs=in_specs,
        out_specs=[out_block, out_block, out_block],
    )
    out_shape = [jax.ShapeDtypeStruct((tile, tile), jnp.float32)] * 3
    return pl.pallas_call(
        functools.partial(correlate_kernel, scaling=scaling),
        grid_spec=grid_spec,
        out_shape=out_shape,
        compiler_params=pltpu.CompilerParams(dimension_semantics=("arbitrary",)),
    )(ids, all_templates, ctf, spec_real, spec_imag, *tables)


def body(micrograph, templates, defocus, ctf, usable):
    bf16 = jnp.bfloat16
    f32 = jnp.float32
    tile_width = micrograph.shape[0]
    padded_size = ctf.shape[1]
    box_size = templates.shape[1]
    margin = (padded_size - tile_width) // 2
    scaling = 1.0 / (padded_size * padded_size)
    n = padded_size
    cos_np, sin_np = twiddles(n)

    cos_full, sin_full = lax.optimization_barrier((jnp.asarray(cos_np), jnp.asarray(sin_np)))
    low = n - box_size // 2
    cos_rows = jnp.concatenate([cos_full[low:], cos_full[: box_size - (n - low)]], axis=0)
    sin_rows = jnp.concatenate([sin_full[low:], sin_full[: box_size - (n - low)]], axis=0)
    cos_cols = cos_rows.T
    sin_cols = sin_rows.T
    row_cos = cos_full[margin : margin + tile_width]
    row_sin = sin_full[margin : margin + tile_width]
    col_cos = row_cos.T
    col_sin = row_sin.T

    local_count = templates.shape[0]
    flat_size = box_size * box_size
    id_block = jnp.broadcast_to(defocus.astype(bf16)[:, None], (local_count, 128))
    packed = jnp.concatenate([templates.reshape(local_count, flat_size), id_block], axis=1)
    gathered = gather_orient(packed)
    total = gathered.shape[0]
    all_templates = gathered[:, :flat_size].reshape(total, box_size, box_size)
    all_ids = gathered[:, flat_size].astype(jnp.int32)

    padded = extended(micrograph, (("orient", 0), ("tile", 1)), margin)
    half_real = matmul(padded, cos_full).astype(bf16)
    half_imag = (-matmul(padded, sin_full)).astype(bf16)
    spec_real = (matmul(cos_full, half_real) + matmul(sin_full, half_imag)).astype(bf16).astype(f32)
    spec_imag = (matmul(cos_full, half_imag) - matmul(sin_full, half_real)).astype(bf16).astype(f32)

    tables = (cos_rows, sin_rows, cos_cols, sin_cols, row_cos, row_sin, col_cos, col_sin)
    peak_map, sum_map, squares = correlate(all_ids, all_templates, ctf, spec_real, spec_imag, tables, scaling)

    live = usable[0, 0]
    row_mask = (jnp.arange(tile_width, dtype=jnp.int32) < RB * live)[:, None]
    orient_count = float(total)
    peak_out = jnp.where(row_mask, peak_map, 0.0)
    mean_out = jnp.where(row_mask, sum_map / orient_count, 0.0)
    square_out = jnp.where(row_mask, squares / orient_count, 0.0)
    return (peak_out, mean_out, square_out)


def solution(mesh):
    return jax.shard_map(
        body,
        mesh=mesh,
        in_specs=(
            P(("groups", "orient"), "tile"),
            P("orient", None, None),
            P(("groups", "orient")),
            P("groups", None, None),
            P(("groups", "orient"), "tile"),
        ),
        out_specs=(
            P(("groups", "orient"), "tile"),
            P(("groups", "orient"), "tile"),
            P(("groups", "orient"), "tile"),
        ),
        check_vma=False,
    )
```

time: 73.9 us -> 66.5 us (0.90)
  matrix products: 20.9 us -> 3.7 us
  Pallas kernels: 0 us -> 14 us
  local copies, waits for them, and re-layouts: 15.4 us -> 9.07 us
  other arithmetic: 2.74 us -> 5.64 us
  waiting for transfers between devices: 16.9 us -> 14.3 us
  starting transfers between devices: 15 us -> 17.3 us
    dot_general x10 -> x0, matrix products: 17.4 us -> none  [the longest x1 4.22 us: chunk_stats(): jnp.einsum('orq,cq->orc', left_real, row_cos, preferred_element_type=f32)]
    pallas_call x0 -> x1, Pallas kernels: none -> 14 us  [correlate(): pl.pallas_call(functools.partial(correlate_kernel, scaling=scaling), grid...]
    gather x2 -> x0, local copies, waits for them, and re-layouts: 10.3 us -> none  [chunk_stats(): weight = jnp.take(ctf, chunk_ids, axis=0)]
    ppermute x3, starting transfers between devices: 7.3 us -> 11.3 us  [gather_orient(): other = lax.ppermute(block, 'orient', pairs)]
    ppermute x2, waiting for transfers between devices: 3.92 us -> 0.01 us  [extended(): lax.ppermute(lax.slice_in_dim(block, 0, width, axis=dim), axis, backward)]
    slice x0 -> x3, local copies, waits for them, and re-layouts: none -> 2.68 us  [the longest x1 1.19 us: body(): sin_full[low:]]
    unnamed x28 -> x8, local copies, waits for them, and re-layouts: 2.06 us -> 0.03 us
    ppermute x2, starting transfers between devices: 4.94 us -> 3.37 us  [extended(): lax.ppermute(lax.slice_in_dim(block, block.shape[dim] - width, None, axis...]
  transfers between devices with their start and end apart: 7 -> 7, of which waited for: 3 -> 2; matrix products, arithmetic and copies ran while one was open for 8% -> 18% of each run, Pallas kernels for 0% -> 0%
where the time goes in v5:
time: 66.5 us; the launch traced here: 66.1 us
  starting transfers between devices  17.3 us (26%)
  waiting for transfers between devices  14.3 us (22%)
  Pallas kernels  14 us (21%)
  local copies, waits for them, and re-layouts  9.07 us (14%)
  other arithmetic  5.64 us (8%)
  matrix products  3.7 us (6%)
  between operations  2.11 us (3%)
    ppermute x3, waiting for transfers between devices, gather_orient(): other = lax.ppermute(block, 'orient', pairs)  14.3 us
    pallas_call x1, Pallas kernels, correlate(): pl.pallas_call(functools.partial(correlate_kernel, scaling=scaling), grid...  14 us
    ppermute x3, starting transfers between devices, gather_orient(): other = lax.ppermute(block, 'orient', pairs)  11.3 us
    dot_general x6, matrix products, matmul(): return jnp.dot(left, right, preferred_element_type=jnp.float32)  3.7 us
    ppermute x2, starting transfers between devices, extended(): lax.ppermute(lax.slice_in_dim(block, block.shape[dim] - width, None, axis...  3.37 us
    ppermute x2, starting transfers between devices, extended(): lax.ppermute(lax.slice_in_dim(block, 0, width, axis=dim), axis, backward)  2.58 us
    reshape x1, local copies, waits for them, and re-layouts, body(): all_templates = gathered[:, :flat_size].reshape(total, box_size, box_size)  1.81 us
    select_n x3, other arithmetic, gather_orient(): jnp.where(low_side, jnp.concatenate([block, other], 0), jnp.concatenate([...  1.72 us
  transfers between devices with their start and end apart: 7, of which 2 were waited for; matrix products, arithmetic and copies ran while one was open for 18% of the time, Pallas kernels for 0%

profile of v5, /device:TPU:0, one launch (start us, length us, event | category | flops | bytes accessed | tf_op | source)
XLA Modules:
  0.0 66.1 jit_solution(18155346235607101025)
XLA Ops:
  0.7 1.1 %reshape.23 = bf16[1,36864]{1,0:T(2,128)(2,1)S(1)} reshape(bf16[1,192,192]{2,1,0:T(8,128)(2,1)} %param.8) | data formatting | bytes 147456 | tf_op jit(solution)/shard_map/reshape | solution.py:152
  2.6 3.0 %collective-permute-start = (bf16[1,36992]{1,0:T(2,128)(2,1)S(1)}, bf16[1,36992]{1,0:T(2,128)(2,1)S(1)}, u32[]{:S(2)}, u32[]{:S(2)}) collective-permute-start(bf16[1,36992]{1,0:T(2,128)(2,1)S(1)} %concatenate.33), channel_id=1, source_target_pairs={{0,2},{2,0},{4,6},{6,4},{8,10},{10,8},{12,14},{14,12},{1,3},{3,1},... | collective-permute-start | bytes 221960 | tf_op jit(solution)/shard_map/ppermute | solution.py:50
  5.6 0.8 %fusion.12 = (bf16[96,128]{1,0:T(8,128)(2,1)S(1)}, bf16[96,128]{1,0:T(8,128)(2,1)S(1)}) fusion(bf16[128,128]{1,0:T(8,128)(2,1)} %param.7), kind=kLoop, calls=%fused_computation.32 | loop fusion | bytes 98304 | tf_op jit(solution)/shard_map/slice | solution.py:25
  6.4 1.9 %collective-permute-start.3 = (bf16[96,128]{1,0:T(8,128)(2,1)S(1)}, bf16[96,128]{1,0:T(8,128)(2,1)S(1)}, u32[]{:S(2)}, u32[]{:S(2)}) collective-permute-start(bf16[96,128]{1,0:T(8,128)(2,1)S(1)} %get-tuple-element.28), channel_id=1, source_target_pairs={{0,2},{2,4},{4,6},{6,8},{8,10},{10,12},{12,14},{1,3},{3,5},{5,7},{... | collective-permute-start | bytes 73736 | tf_op jit(solution)/shard_map/ppermute | solution.py:22
  8.3 1.3 %collective-permute-start.4 = (bf16[96,128]{1,0:T(8,128)(2,1)S(1)}, bf16[96,128]{1,0:T(8,128)(2,1)S(1)}, u32[]{:S(2)}, u32[]{:S(2)}) collective-permute-start(bf16[96,128]{1,0:T(8,128)(2,1)S(1)} %get-tuple-element.27), channel_id=1, source_target_pairs={{2,0},{4,2},{6,4},{8,6},{10,8},{12,10},{14,12},{3,1},{5,3},{7,5},{... | collective-permute-start | bytes 73736 | tf_op jit(solution)/shard_map/ppermute | solution.py:25
  9.6 1.2 %fusion.9 = (bf16[96,320]{0,1:T(8,128)(2,1)S(1)}, bf16[96,320]{0,1:T(8,128)(2,1)S(1)}, bf16[96,320]{0,1:T(8,128)(2,1)S(1)}, bf16[96,320]{0,1:T(8,128)(2,1)S(1)}) fusion(bf16[320,320]{0,1:T(8,128)(2,1)} %constant.72.clone, bf16[320,320]{0,1:T(8,128)(2,1)} %constant.71.clone), kind=kLoop, calls=%fused_computation.29 | loop fusion | bytes 491520 | tf_op jit(solution)/shard_map/slice | solution.py:141
  10.8 0.8 %slice_bitcast_fusion = (bf16[320,128]{1,0:T(8,128)(2,1)}, bf16[128,320]{0,1:T(8,128)(2,1)S(1)}, bf16[128,320]{0,1:T(8,128)(2,1)S(1)}, bf16[320,128]{1,0:T(8,128)(2,1)}) fusion(bf16[320,320]{0,1:T(8,128)(2,1)S(1)} %copy-done, bf16[320,320]{0,1:T(8,128)(2,1)S(1)} %copy-done.1), kind=kLoop, calls=%fused_computation.25 | loop fusion | bytes 491520 | tf_op jit(solution)/shard_map/transpose | solution.py:147
  12.3 0.8 %fusion.8 = (bf16[320,192]{1,0:T(8,128)(2,1)}, bf16[192,320]{0,1:T(8,128)(2,1)S(1)}) fusion(bf16[96,320]{0,1:T(8,128)(2,1)S(1)} %get-tuple-element.34, bf16[96,320]{0,1:T(8,128)(2,1)S(1)} %get-tuple-element.35), kind=kLoop, calls=%fused_computation.28 | loop fusion | flops 245760 | bytes 368640 | tf_op jit(solution)/shard_map/transpose | solution.py:142
  13.0 0.8 %fusion.7 = (bf16[320,192]{1,0:T(8,128)(2,1)}, bf16[192,320]{0,1:T(8,128)(2,1)S(1)}) fusion(bf16[96,320]{0,1:T(8,128)(2,1)S(1)} %get-tuple-element.18, bf16[96,320]{0,1:T(8,128)(2,1)S(1)} %get-tuple-element.17), kind=kLoop, calls=%fused_computation.27 | loop fusion | flops 245760 | bytes 368640 | tf_op jit(solution)/shard_map/transpose | solution.py:143
  13.8 0.8 %copy.20.cos_rows_ref = bf16[192,320]{1,0:T(8,128)(2,1)} copy(bf16[192,320]{0,1:T(8,128)(2,1)S(1)} %get-tuple-element.24) | data formatting | bytes 245760 | tf_op jit(solution)/shard_map/concatenate | solution.py:140
  14.6 0.8 %copy.21.sin_rows_ref = bf16[192,320]{1,0:T(8,128)(2,1)} copy(bf16[192,320]{0,1:T(8,128)(2,1)S(1)} %get-tuple-element.22) | data formatting | bytes 245760 | tf_op jit(solution)/shard_map/concatenate | solution.py:141
  15.4 0.7 %copy.22.row_cos_ref = bf16[128,320]{1,0:T(8,128)(2,1)} copy(bf16[128,320]{0,1:T(8,128)(2,1)S(1)} %get-tuple-element.32) | data formatting | bytes 163840 | tf_op jit(solution)/shard_map/slice | solution.py:144
  16.1 0.7 %copy.23.row_sin_ref = bf16[128,320]{1,0:T(8,128)(2,1)} copy(bf16[128,320]{0,1:T(8,128)(2,1)S(1)} %get-tuple-element.14) | data formatting | bytes 163840 | tf_op jit(solution)/shard_map/slice | solution.py:145
  17.0 1.5 %collective-permute-start.5 = (bf16[320,96]{1,0:T(8,128)(2,1)S(1)}, bf16[320,96]{1,0:T(8,128)(2,1)S(1)}, u32[]{:S(2)}, u32[]{:S(2)}) collective-permute-start(bf16[320,96]{1,0:T(8,128)(2,1)S(1)} %get-tuple-element.25), channel_id=1, source_target_pairs={{0,1},{2,3},{4,5},{6,7},{8,9},{10,11},{12,13},{14,15},{16,17},{18,... | collective-permute-start | bytes 184328 | tf_op jit(solution)/shard_map/ppermute | solution.py:22
  18.5 1.3 %collective-permute-start.6 = (bf16[320,96]{1,0:T(8,128)(2,1)S(1)}, bf16[320,96]{1,0:T(8,128)(2,1)S(1)}, u32[]{:S(2)}, u32[]{:S(2)}) collective-permute-start(bf16[320,96]{1,0:T(8,128)(2,1)S(1)} %get-tuple-element.26), channel_id=1, source_target_pairs={{1,0},{3,2},{5,4},{7,6},{9,8},{11,10},{13,12},{15,14},{17,16},{19,... | collective-permute-start | bytes 184328 | tf_op jit(solution)/shard_map/ppermute | solution.py:25
  20.5 5.0 %collective-permute-start.1 = (bf16[2,36992]{1,0:T(2,128)(2,1)S(1)}, bf16[2,36992]{1,0:T(2,128)(2,1)S(1)}, u32[]{:S(2)}, u32[]{:S(2)}) collective-permute-start(bf16[2,36992]{1,0:T(2,128)(2,1)S(1)} %broadcast_select_fusion), channel_id=1, source_target_pairs={{0,4},{2,6},{4,0},{6,2},{8,12},{10,14},{12,8},{14,10},{1,5},{3,7},... | collective-permute-start | bytes 443912 | tf_op jit(solution)/shard_map/ppermute | solution.py:50
  26.6 1.1 %fusion.2.spec_r_ref = f32[320,320]{1,0:T(8,128)} fusion(f32[320,320]{1,0:T(8,128)S(1)} %fusion.13, bf16[320,320]{0,1:T(8,128)(2,1)S(1)} %copy-done, bf16[320,320]{1,0:T(8,128)(2,1)S(1)} %fusion), kind=kOutput, calls=%fused_computation.6 | convolution fusion | flops 65843200 | bytes 1228800 | tf_op jit(solution)/shard_map/dot_general | solution.py:41
  27.8 2.1 %collective-permute-done.1 = bf16[2,36992]{1,0:T(2,128)(2,1)S(1)} collective-permute-done((bf16[2,36992]{1,0:T(2,128)(2,1)S(1)}, bf16[2,36992]{1,0:T(2,128)(2,1)S(1)}, u32[]{:S(2)}, u32[]{:S(2)}) %collective-permute-start.1) | collective-permute-done | bytes 148000 | tf_op jit(solution)/shard_map/ppermute | solution.py:50
  30.4 3.3 %collective-permute-start.2 = (bf16[4,36992]{1,0:T(4,128)(2,1)S(1)}, bf16[4,36992]{1,0:T(4,128)(2,1)S(1)}, u32[]{:S(2)}, u32[]{:S(2)}) collective-permute-start(bf16[4,36992]{1,0:T(4,128)(2,1)S(1)} %maximum_select_fusion.1), channel_id=1, source_target_pairs={{0,8},{2,10},{4,12},{6,14},{8,0},{10,2},{12,4},{14,6},{1,9},{3,11}... | collective-permute-start | bytes 887816 | tf_op jit(solution)/shard_map/ppermute | solution.py:50
  34.0 1.1 %fusion.4.spec_i_ref = f32[320,320]{1,0:T(8,128)} fusion(f32[320,320]{1,0:T(8,128)S(1)} %fusion.14, bf16[320,320]{0,1:T(8,128)(2,1)S(1)} %copy-done, bf16[320,320]{1,0:T(8,128)(2,1)S(1)} %convolution_convert_fusion), kind=kOutput, calls=%fused_computation.8 | convolution fusion | flops 65843200 | bytes 1228800 | tf_op jit(solution)/shard_map/dot_general | solution.py:41
  35.2 12.2 %collective-permute-done.2 = bf16[4,36992]{1,0:T(4,128)(2,1)S(1)} collective-permute-done((bf16[4,36992]{1,0:T(4,128)(2,1)S(1)}, bf16[4,36992]{1,0:T(4,128)(2,1)S(1)}, u32[]{:S(2)}, u32[]{:S(2)}) %collective-permute-start.2) | collective-permute-done | bytes 295968 | tf_op jit(solution)/shard_map/ppermute | solution.py:50
  48.6 1.8 %reshape.24.tmpl_ref = bf16[8,192,192]{2,1,0:T(8,128)(2,1)} reshape(bf16[8,36864]{1,0:T(8,128)(2,1)S(1)} %slice.49) | data formatting | bytes 1179648 | tf_op jit(solution)/shard_map/reshape | solution.py:155
  50.4 14.0 %shard_map.94 = (f32[128,128]{1,0:T(8,128)}, f32[128,128]{1,0:T(8,128)}, f32[128,128]{1,0:T(8,128)}) custom-call(s32[8]{0:T(128)} %convert_reduce_fusion.ids_ref, bf16[8,192,192]{2,1,0:T(8,128)(2,1)} %reshape.24.tmpl_ref, f32[8,320,320]{2,1,0:T(8,128)} %ctf_ref.1, f32[320,320]{1,0:T(8,128)} %fusion.2.spec_r_ref, f32[320,320]{1,0:T(8,128)} %fusion.4.spec_i_ref, ...), custom_call_target="tpu_custom_call" | custom-call | tf_op jit(solution)/shard_map/pallas_call | solution.py:119
  64.4 1.7 %multiply_select_fusion = (f32[128,128]{1,0:T(8,128)}, f32[128,128]{1,0:T(8,128)}, f32[128,128]{1,0:T(8,128)}) fusion(f32[128,128]{1,0:T(8,128)} %get-tuple-element.12, pred[128]{0:T(512)(128)(4,1)S(1)} %iota_compare_fusion, f32[128,128]{1,0:T(8,128)} %get-tuple-element.11, f32[128,128]{1,0:T(8,128)} %get-tuple-element.10), kind=kLoop, calls=%fused_computation.15 | loop fusion | flops 81920 | bytes 393344 | tf_op jit(solution)/shard_map/jit(_where)/select_n | solution.py:172
  (26 shorter events, 4.2 us)
Async XLA Ops:
  0.6 10.2 %copy-start.1 = (bf16[320,320]{0,1:T(8,128)(2,1)S(1)}, bf16[320,320]{0,1:T(8,128)(2,1)}, u32[]{:S(2)}) copy-start(bf16[320,320]{0,1:T(8,128)(2,1)} %constant.71.clone) | copy-start | bytes 614404
  0.6 10.2 %copy-start = (bf16[320,320]{0,1:T(8,128)(2,1)S(1)}, bf16[320,320]{0,1:T(8,128)(2,1)}, u32[]{:S(2)}) copy-start(bf16[320,320]{0,1:T(8,128)(2,1)} %constant.72.clone) | copy-start | bytes 614404
  2.6 17.2 %collective-permute-start = (bf16[1,36992]{1,0:T(2,128)(2,1)S(1)}, bf16[1,36992]{1,0:T(2,128)(2,1)S(1)}, u32[]{:S(2)}, u32[]{:S(2)}) collective-permute-start(bf16[1,36992]{1,0:T(2,128)(2,1)S(1)} %concatenate.33), channel_id=1, source_target_pairs={{0,2},{2,0},{4,6},{6,4},{8,10},{10,8},{12,14},{14,12},{1,3},{3,1},... | collective-permute-start | bytes 221960 | tf_op jit(solution)/shard_map/ppermute | solution.py:50
  6.4 10.5 %collective-permute-start.3 = (bf16[96,128]{1,0:T(8,128)(2,1)S(1)}, bf16[96,128]{1,0:T(8,128)(2,1)S(1)}, u32[]{:S(2)}, u32[]{:S(2)}) collective-permute-start(bf16[96,128]{1,0:T(8,128)(2,1)S(1)} %get-tuple-element.28), channel_id=1, source_target_pairs={{0,2},{2,4},{4,6},{6,8},{8,10},{10,12},{12,14},{1,3},{3,5},{5,7},{... | collective-permute-start | bytes 73736 | tf_op jit(solution)/shard_map/ppermute | solution.py:22
  8.3 8.6 %collective-permute-start.4 = (bf16[96,128]{1,0:T(8,128)(2,1)S(1)}, bf16[96,128]{1,0:T(8,128)(2,1)S(1)}, u32[]{:S(2)}, u32[]{:S(2)}) collective-permute-start(bf16[96,128]{1,0:T(8,128)(2,1)S(1)} %get-tuple-element.27), channel_id=1, source_target_pairs={{2,0},{4,2},{6,4},{8,6},{10,8},{12,10},{14,12},{3,1},{5,3},{7,5},{... | collective-permute-start | bytes 73736 | tf_op jit(solution)/shard_map/ppermute | solution.py:25
  11.6 5.3 %copy-start.2 = (bf16[128,128]{1,0:T(8,128)(2,1)S(1)}, bf16[128,128]{1,0:T(8,128)(2,1)}, u32[]{:S(2)}) copy-start(bf16[128,128]{1,0:T(8,128)(2,1)} %param.7) | copy-start | bytes 98308
  17.0 8.5 %collective-permute-start.5 = (bf16[320,96]{1,0:T(8,128)(2,1)S(1)}, bf16[320,96]{1,0:T(8,128)(2,1)S(1)}, u32[]{:S(2)}, u32[]{:S(2)}) collective-permute-start(bf16[320,96]{1,0:T(8,128)(2,1)S(1)} %get-tuple-element.25), channel_id=1, source_target_pairs={{0,1},{2,3},{4,5},{6,7},{8,9},{10,11},{12,13},{14,15},{16,17},{18,... | collective-permute-start | bytes 184328 | tf_op jit(solution)/shard_map/ppermute | solution.py:22
  18.5 7.0 %collective-permute-start.6 = (bf16[320,96]{1,0:T(8,128)(2,1)S(1)}, bf16[320,96]{1,0:T(8,128)(2,1)S(1)}, u32[]{:S(2)}, u32[]{:S(2)}) collective-permute-start(bf16[320,96]{1,0:T(8,128)(2,1)S(1)} %get-tuple-element.26), channel_id=1, source_target_pairs={{1,0},{3,2},{5,4},{7,6},{9,8},{11,10},{13,12},{15,14},{17,16},{19,... | collective-permute-start | bytes 184328 | tf_op jit(solution)/shard_map/ppermute | solution.py:25
  20.5 9.4 %collective-permute-start.1 = (bf16[2,36992]{1,0:T(2,128)(2,1)S(1)}, bf16[2,36992]{1,0:T(2,128)(2,1)S(1)}, u32[]{:S(2)}, u32[]{:S(2)}) collective-permute-start(bf16[2,36992]{1,0:T(2,128)(2,1)S(1)} %broadcast_select_fusion), channel_id=1, source_target_pairs={{0,4},{2,6},{4,0},{6,2},{8,12},{10,14},{12,8},{14,10},{1,5},{3,7},... | collective-permute-start | bytes 443912 | tf_op jit(solution)/shard_map/ppermute | solution.py:50
  30.4 16.9 %collective-permute-start.2 = (bf16[4,36992]{1,0:T(4,128)(2,1)S(1)}, bf16[4,36992]{1,0:T(4,128)(2,1)S(1)}, u32[]{:S(2)}, u32[]{:S(2)}) collective-permute-start(bf16[4,36992]{1,0:T(4,128)(2,1)S(1)} %maximum_select_fusion.1), channel_id=1, source_target_pairs={{0,8},{2,10},{4,12},{6,14},{8,0},{10,2},{12,4},{14,6},{1,9},{3,11}... | collective-permute-start | bytes 887816 | tf_op jit(solution)/shard_map/ppermute | solution.py:50

commit v6 on v5

--- a/solution.py
+++ b/solution.py
@@ -41,22 +41,26 @@
     return jnp.dot(left, right, preferred_element_type=jnp.float32)
 
 
-def gather_orient(block):
+def exchange_rounds(block):
     size = lax.axis_size("orient")
-    index = lax.axis_index("orient")
     step = 1
-    while step < size:
-        pairs = [(i, i ^ step) for i in range(size) if (i ^ step) < size]
-        other = lax.ppermute(block, "orient", pairs)
-        low_side = (index // step) % 2 == 0
-        block = jnp.where(low_side, jnp.concatenate([block, other], 0), jnp.concatenate([other, block], 0))
+    while step * 2 < size:
         step *= 2
-    return block
+    rounds = [block]
+    held = block
+    while step >= 1:
+        other = lax.ppermute(held, "orient", [(i, i ^ step) for i in range(size)])
+        if len(rounds) > 1:
+            other, rounds[-1] = lax.optimization_barrier((other, rounds[-1]))
+        rounds.append(other)
+        held = jnp.concatenate([held, other], axis=0)
+        step //= 2
+    return rounds
 
 
 def correlate_kernel(ids_ref, tmpl_ref, ctf_ref, spec_r_ref, spec_i_ref, cos_rows_ref, sin_rows_ref,
                      cos_cols_ref, sin_cols_ref, row_cos_ref, row_sin_ref, col_cos_ref, col_sin_ref,
-                     peak_ref, sum_ref, sq_ref, *, scaling):
+                     prev_peak_ref, prev_sum_ref, prev_sq_ref, peak_ref, sum_ref, sq_ref, *, scaling):
     bf16 = jnp.bfloat16
     f32 = jnp.float32
     o = pl.program_id(0)
@@ -86,9 +90,9 @@
 
     @pl.when(o == 0)
     def _():
-        peak_ref[...] = corr
-        sum_ref[...] = corr
-        sq_ref[...] = corr * corr
+        peak_ref[...] = jnp.maximum(prev_peak_ref[...], corr)
+        sum_ref[...] = prev_sum_ref[...] + corr
+        sq_ref[...] = prev_sq_ref[...] + corr * corr
 
     @pl.when(o > 0)
     def _():
@@ -97,7 +101,7 @@
         sq_ref[...] = sq_ref[...] + corr * corr
 
 
-def correlate(ids, all_templates, ctf, spec_real, spec_imag, tables, scaling):
+def correlate(ids, all_templates, ctf, spec_real, spec_imag, tables, scaling, previous):
     count, box, _ = all_templates.shape
     n = ctf.shape[1]
     tile = tables[4].shape[0]
@@ -107,7 +111,7 @@
         pl.BlockSpec((1, n, n), lambda o, ids: (ids[o], 0, 0)),
         full((n, n)),
         full((n, n)),
-    ] + [full(t.shape) for t in tables]
+    ] + [full(t.shape) for t in tables] + [full((tile, tile))] * 3
     out_block = full((tile, tile))
     grid_spec = pltpu.PrefetchScalarGridSpec(
         num_scalar_prefetch=1,
@@ -121,7 +125,8 @@
         grid_spec=grid_spec,
         out_shape=out_shape,
         compiler_params=pltpu.CompilerParams(dimension_semantics=("arbitrary",)),
-    )(ids, all_templates, ctf, spec_real, spec_imag, *tables)
+        input_output_aliases={5 + len(tables): 0, 6 + len(tables): 1, 7 + len(tables): 2},
+    )(ids, all_templates, ctf, spec_real, spec_imag, *tables, *previous)
 
 
 def body(micrograph, templates, defocus, ctf, usable):
@@ -150,10 +155,8 @@
     flat_size = box_size * box_size
     id_block = jnp.broadcast_to(defocus.astype(bf16)[:, None], (local_count, 128))
     packed = jnp.concatenate([templates.reshape(local_count, flat_size), id_block], axis=1)
-    gathered = gather_orient(packed)
-    total = gathered.shape[0]
-    all_templates = gathered[:, :flat_size].reshape(total, box_size, box_size)
-    all_ids = gathered[:, flat_size].astype(jnp.int32)
+    arrivals = exchange_rounds(packed)
+    total = sum(piece.shape[0] for piece in arrivals)
 
     padded = extended(micrograph, (("orient", 0), ("tile", 1)), margin)
     half_real = matmul(padded, cos_full).astype(bf16)
@@ -162,7 +165,14 @@
     spec_imag = (matmul(cos_full, half_imag) - matmul(sin_full, half_real)).astype(bf16).astype(f32)
 
     tables = (cos_rows, sin_rows, cos_cols, sin_cols, row_cos, row_sin, col_cos, col_sin)
-    peak_map, sum_map, squares = correlate(all_ids, all_templates, ctf, spec_real, spec_imag, tables, scaling)
+    shape = (tile_width, tile_width)
+    stats = (jnp.full(shape, -jnp.inf, f32), jnp.zeros(shape, f32), jnp.zeros(shape, f32))
+    for piece in arrivals:
+        count = piece.shape[0]
+        piece_templates = piece[:, :flat_size].reshape(count, box_size, box_size)
+        piece_ids = piece[:, flat_size].astype(jnp.int32)
+        stats = correlate(piece_ids, piece_templates, ctf, spec_real, spec_imag, tables, scaling, stats)
+    peak_map, sum_map, squares = stats
 
     live = usable[0, 0]
     row_mask = (jnp.arange(tile_width, dtype=jnp.int32) < RB * live)[:, None]

time: 66.5 us -> 67.4 us (1.014)
  waiting for transfers between devices: 14.3 us -> 0.81 us
  Pallas kernels: 14 us -> 21.7 us
  local copies, waits for them, and re-layouts: 9.07 us -> 14.9 us
    ppermute x3, waiting for transfers between devices: 14.3 us -> 0.8 us  [exchange_rounds(): other = lax.ppermute(held, 'orient', [(i, i ^ step) for i in range(size)])]
    pallas_call x1 -> x4, Pallas kernels: 14 us -> 21.7 us  [correlate(): pl.pallas_call(functools.partial(correlate_kernel, scaling=scaling), grid...]
    ppermute x2, starting transfers between devices: 3.37 us -> 6.42 us  [extended(): lax.ppermute(lax.slice_in_dim(block, block.shape[dim] - width, None, axis...]
    ppermute x3, starting transfers between devices: 11.3 us -> 8.62 us  [exchange_rounds(): other = lax.ppermute(held, 'orient', [(i, i ^ step) for i in range(size)])]
    select_n x3 -> x0, other arithmetic: 1.72 us -> none  [gather_orient(): jnp.where(low_side, jnp.concatenate([block, other], 0), jnp.concatenate([...]
    another operation x0 -> x2, local copies, waits for them, and re-layouts: none -> 1.27 us
    slice x1 -> x4, local copies, waits for them, and re-layouts: 0.04 us -> 1.19 us  [the longest x3 0.62 us: body(): piece_templates = piece[:, :flat_size].reshape(count, box_size, box_size)]
    reshape x1 -> x3, local copies, waits for them, and re-layouts: 1.81 us -> 2.83 us  [body(): piece_templates = piece[:, :flat_size].reshape(count, box_size, box_size)]
  transfers between devices with their start and end apart: 7 -> 7, of which waited for: 2 -> 1; matrix products, arithmetic and copies ran while one was open for 18% -> 25% of each run, Pallas kernels for 0% -> 11%
where the time goes in v6:
time: 67.4 us; the launch traced here: 66.8 us
  Pallas kernels  21.7 us (32%)
  starting transfers between devices  17.6 us (26%)
  local copies, waits for them, and re-layouts  14.9 us (22%)
  other arithmetic  5.4 us (8%)
  matrix products  3.69 us (5%)
  between operations  2.71 us (4%)
  waiting for transfers between devices  0.81 us (1%)
    pallas_call x4, Pallas kernels, correlate(): pl.pallas_call(functools.partial(correlate_kernel, scaling=scaling), grid...  21.7 us
    ppermute x3, starting transfers between devices, exchange_rounds(): other = lax.ppermute(held, 'orient', [(i, i ^ step) for i in range(size)])  8.62 us
    ppermute x2, starting transfers between devices, extended(): lax.ppermute(lax.slice_in_dim(block, block.shape[dim] - width, None, axis...  6.42 us
    dot_general x6, matrix products, matmul(): return jnp.dot(left, right, preferred_element_type=jnp.float32)  3.69 us
    reshape x3, local copies, waits for them, and re-layouts, body(): piece_templates = piece[:, :flat_size].reshape(count, box_size, box_size)  2.83 us
    ppermute x2, starting transfers between devices, extended(): lax.ppermute(lax.slice_in_dim(block, 0, width, axis=dim), axis, backward)  2.58 us
    transpose x1, local copies, waits for them, and re-layouts, body(): col_sin = row_sin.T  1.77 us
    select_n x1, other arithmetic, body(): square_out = jnp.where(row_mask, squares / orient_count, 0.0)  1.66 us
  transfers between devices with their start and end apart: 7, of which 1 were waited for; matrix products, arithmetic and copies ran while one was open for 25% of the time, Pallas kernels for 11%

profile of v6, /device:TPU:0, one launch (start us, length us, event | category | flops | bytes accessed | tf_op | source)
XLA Modules:
  0.0 66.8 jit_solution(3311200816102123289)
XLA Ops:
  0.7 1.1 %reshape.35 = bf16[1,36864]{1,0:T(2,128)(2,1)S(1)} reshape(bf16[1,192,192]{2,1,0:T(8,128)(2,1)} %tmpl_ref.1) | data formatting | bytes 147456 | tf_op jit(solution)/shard_map/reshape | solution.py:157
  2.6 4.1 %collective-permute-start = (bf16[1,36992]{1,0:T(2,128)(2,1)S(1)}, bf16[1,36992]{1,0:T(2,128)(2,1)S(1)}, u32[]{:S(2)}, u32[]{:S(2)}) collective-permute-start(bf16[1,36992]{1,0:T(2,128)(2,1)S(1)} %concatenate.22), channel_id=1, source_target_pairs={{0,8},{2,10},{4,12},{6,14},{8,0},{10,2},{12,4},{14,6},{1,9},{3,11}... | collective-permute-start | bytes 221960 | tf_op jit(solution)/shard_map/ppermute | solution.py:52
  6.7 0.8 %fusion.12 = (bf16[96,128]{1,0:T(8,128)(2,1)S(1)}, bf16[96,128]{1,0:T(8,128)(2,1)S(1)}) fusion(bf16[128,128]{1,0:T(8,128)(2,1)} %param.7), kind=kLoop, calls=%fused_computation.33 | loop fusion | bytes 98304 | tf_op jit(solution)/shard_map/slice | solution.py:25
  7.5 3.4 %collective-permute-start.3 = (bf16[96,128]{1,0:T(8,128)(2,1)S(1)}, bf16[96,128]{1,0:T(8,128)(2,1)S(1)}, u32[]{:S(2)}, u32[]{:S(2)}) collective-permute-start(bf16[96,128]{1,0:T(8,128)(2,1)S(1)} %get-tuple-element.54), channel_id=1, source_target_pairs={{0,2},{2,4},{4,6},{6,8},{8,10},{10,12},{12,14},{1,3},{3,5},{5,7},{... | collective-permute-start | bytes 73736 | tf_op jit(solution)/shard_map/ppermute | solution.py:22
  10.9 1.3 %collective-permute-start.4 = (bf16[96,128]{1,0:T(8,128)(2,1)S(1)}, bf16[96,128]{1,0:T(8,128)(2,1)S(1)}, u32[]{:S(2)}, u32[]{:S(2)}) collective-permute-start(bf16[96,128]{1,0:T(8,128)(2,1)S(1)} %get-tuple-element.53), channel_id=1, source_target_pairs={{2,0},{4,2},{6,4},{8,6},{10,8},{12,10},{14,12},{3,1},{5,3},{7,5},{... | collective-permute-start | bytes 73736 | tf_op jit(solution)/shard_map/ppermute | solution.py:25
  12.2 1.2 %fusion.9 = (bf16[96,320]{0,1:T(8,128)(2,1)S(1)}, bf16[96,320]{0,1:T(8,128)(2,1)S(1)}, bf16[96,320]{0,1:T(8,128)(2,1)S(1)}, bf16[96,320]{0,1:T(8,128)(2,1)S(1)}) fusion(bf16[320,320]{0,1:T(8,128)(2,1)} %constant.17.clone, bf16[320,320]{0,1:T(8,128)(2,1)} %constant.16.clone), kind=kLoop, calls=%fused_computation.30 | loop fusion | bytes 491520 | tf_op jit(solution)/shard_map/slice | solution.py:146
  13.4 1.8 %slice_bitcast_fusion = (bf16[320,128]{1,0:T(8,128)(2,1)}, bf16[128,320]{0,1:T(8,128)(2,1)S(1)}, bf16[128,320]{0,1:T(8,128)(2,1)S(1)}, bf16[320,128]{1,0:T(8,128)(2,1)}) fusion(bf16[320,320]{0,1:T(8,128)(2,1)} %constant.17.clone, bf16[320,320]{0,1:T(8,128)(2,1)} %constant.16.clone), kind=kLoop, calls=%fused_computation.26 | loop fusion | bytes 491520 | tf_op jit(solution)/shard_map/transpose | solution.py:152
  16.6 0.8 %fusion.7 = (bf16[320,192]{1,0:T(8,128)(2,1)}, bf16[192,320]{0,1:T(8,128)(2,1)S(1)}) fusion(bf16[96,320]{0,1:T(8,128)(2,1)S(1)} %get-tuple-element.44, bf16[96,320]{0,1:T(8,128)(2,1)S(1)} %get-tuple-element.43), kind=kLoop, calls=%fused_computation.28 | loop fusion | flops 245760 | bytes 368640 | tf_op jit(solution)/shard_map/transpose | solution.py:148
  17.4 0.8 %copy.69.cos_rows_ref = bf16[192,320]{1,0:T(8,128)(2,1)} copy(bf16[192,320]{0,1:T(8,128)(2,1)S(1)} %get-tuple-element.50) | data formatting | bytes 245760 | tf_op jit(solution)/shard_map/concatenate | solution.py:145
  18.2 0.8 %copy.70.sin_rows_ref = bf16[192,320]{1,0:T(8,128)(2,1)} copy(bf16[192,320]{0,1:T(8,128)(2,1)S(1)} %get-tuple-element.48) | data formatting | bytes 245760 | tf_op jit(solution)/shard_map/concatenate | solution.py:146
  21.3 1.3 %collective-permute-start.6 = (bf16[320,96]{1,0:T(8,128)(2,1)S(1)}, bf16[320,96]{1,0:T(8,128)(2,1)S(1)}, u32[]{:S(2)}, u32[]{:S(2)}) collective-permute-start(bf16[320,96]{1,0:T(8,128)(2,1)S(1)} %get-tuple-element.52), channel_id=1, source_target_pairs={{1,0},{3,2},{5,4},{7,6},{9,8},{11,10},{13,12},{15,14},{17,16},{19,... | collective-permute-start | bytes 184328 | tf_op jit(solution)/shard_map/ppermute | solution.py:25
  22.6 3.0 %collective-permute-start.5 = (bf16[320,96]{1,0:T(8,128)(2,1)S(1)}, bf16[320,96]{1,0:T(8,128)(2,1)S(1)}, u32[]{:S(2)}, u32[]{:S(2)}) collective-permute-start(bf16[320,96]{1,0:T(8,128)(2,1)S(1)} %get-tuple-element.51), channel_id=1, source_target_pairs={{0,1},{2,3},{4,5},{6,7},{8,9},{10,11},{12,13},{14,15},{16,17},{18,... | collective-permute-start | bytes 184328 | tf_op jit(solution)/shard_map/ppermute | solution.py:22
  26.0 3.7 %collective-permute-start.1 = (bf16[2,36992]{1,0:T(2,128)(2,1)S(1)}, bf16[2,36992]{1,0:T(2,128)(2,1)S(1)}, u32[]{:S(2)}, u32[]{:S(2)}) collective-permute-start(bf16[2,36992]{1,0:T(2,128)(2,1)S(1)} %pad_maximum_fusion.4), channel_id=1, source_target_pairs={{0,4},{2,6},{4,0},{6,2},{8,12},{10,14},{12,8},{14,10},{1,5},{3,7},... | collective-permute-start | bytes 443912 | tf_op jit(solution)/shard_map/ppermute | solution.py:52
  30.9 1.1 %fusion.2.spec_r_ref = f32[320,320]{1,0:T(8,128)} fusion(f32[320,320]{1,0:T(8,128)S(1)} %fusion.13, bf16[320,320]{0,1:T(8,128)(2,1)S(1)} %copy-done, bf16[320,320]{1,0:T(8,128)(2,1)S(1)} %fusion), kind=kOutput, calls=%fused_computation.6 | convolution fusion | flops 65843200 | bytes 1228800 | tf_op jit(solution)/shard_map/dot_general | solution.py:41
  32.3 0.8 %collective-permute-done.1 = bf16[2,36992]{1,0:T(2,128)(2,1)S(1)} collective-permute-done((bf16[2,36992]{1,0:T(2,128)(2,1)S(1)}, bf16[2,36992]{1,0:T(2,128)(2,1)S(1)}, u32[]{:S(2)}, u32[]{:S(2)}) %collective-permute-start.1) | collective-permute-done | bytes 148000 | tf_op jit(solution)/shard_map/ppermute | solution.py:52
  33.6 0.8 %collective-permute-start.2 = (bf16[4,36992]{1,0:T(4,128)(2,1)S(1)}, bf16[4,36992]{1,0:T(4,128)(2,1)S(1)}, u32[]{:S(2)}, u32[]{:S(2)}) collective-permute-start(bf16[4,36992]{1,0:T(4,128)(2,1)S(1)} %pad_maximum_fusion), channel_id=1, source_target_pairs={{0,2},{2,0},{4,6},{6,4},{8,10},{10,8},{12,14},{14,12},{1,3},{3,1},... | collective-permute-start | bytes 887816 | tf_op jit(solution)/shard_map/ppermute | solution.py:52
  34.4 1.1 %fusion.4.spec_i_ref = f32[320,320]{1,0:T(8,128)} fusion(f32[320,320]{1,0:T(8,128)S(1)} %fusion.14, bf16[320,320]{0,1:T(8,128)(2,1)S(1)} %copy-done, bf16[320,320]{1,0:T(8,128)(2,1)S(1)} %convolution_convert_fusion), kind=kOutput, calls=%fused_computation.8 | convolution fusion | flops 65843200 | bytes 1228800 | tf_op jit(solution)/shard_map/dot_general | solution.py:41
  37.5 3.6 %shard_map.94 = (f32[128,128]{1,0:T(8,128)}, f32[128,128]{1,0:T(8,128)}, f32[128,128]{1,0:T(8,128)}) custom-call(s32[1]{0:T(128)S(6)} %convert_element_type.52.ids_ref, bf16[1,192,192]{2,1,0:T(8,128)(2,1)} %tmpl_ref.1, f32[8,320,320]{2,1,0:T(8,128)} %ctf_ref.7, ...), custom_call_target="tpu_custom_call", output_to_operand_aliasing={{0}: (13, {}), {1}: (14, {}), {2}: (15, {})} | custom-call | tf_op jit(solution)/shard_map/pallas_call | solution.py:123
  43.5 3.6 %shard_map.95 = (f32[128,128]{1,0:T(8,128)}, f32[128,128]{1,0:T(8,128)}, f32[128,128]{1,0:T(8,128)}) custom-call(s32[1]{0:T(128)S(6)} %convert.3.ids_ref, bf16[1,192,192]{2,1,0:T(8,128)(2,1)} %reshape.38.tmpl_ref, f32[8,320,320]{2,1,0:T(8,128)} %ctf_ref.7, ...), custom_call_target="tpu_custom_call", output_to_operand_aliasing={{0}: (13, {}), {1}: (14, {}), {2}: (15, {})} | custom-call | tf_op jit(solution)/shard_map/pallas_call | solution.py:123
  48.7 1.2 %reshape.36.tmpl_ref = bf16[4,192,192]{2,1,0:T(8,128)(2,1)} reshape(bf16[4,36864]{1,0:T(4,128)(2,1)S(1)} %slice.50) | data formatting | bytes 589824 | tf_op jit(solution)/shard_map/reshape | solution.py:172
  49.9 0.9 %reshape.37.tmpl_ref = bf16[2,192,192]{2,1,0:T(8,128)(2,1)} reshape(bf16[2,36864]{1,0:T(2,128)(2,1)S(1)} %slice.62) | data formatting | bytes 294912 | tf_op jit(solution)/shard_map/reshape | solution.py:172
  50.8 5.8 %shard_map.96 = (f32[128,128]{1,0:T(8,128)}, f32[128,128]{1,0:T(8,128)}, f32[128,128]{1,0:T(8,128)}) custom-call(s32[2]{0:T(128)} %convert_reduce_fusion.1.ids_ref, bf16[2,192,192]{2,1,0:T(8,128)(2,1)} %reshape.37.tmpl_ref, f32[8,320,320]{2,1,0:T(8,128)} %ctf_ref.7, ...), custom_call_target="tpu_custom_call", output_to_operand_aliasing={{0}: (13, {}), {1}: (14, {}), {2}: (15, {})} | custom-call | tf_op jit(solution)/shard_map/pallas_call | solution.py:123
  56.5 8.6 %shard_map.97 = (f32[128,128]{1,0:T(8,128)}, f32[128,128]{1,0:T(8,128)}, f32[128,128]{1,0:T(8,128)}) custom-call(s32[4]{0:T(128)} %convert_reduce_fusion.ids_ref, bf16[4,192,192]{2,1,0:T(8,128)(2,1)} %reshape.36.tmpl_ref, f32[8,320,320]{2,1,0:T(8,128)} %ctf_ref.7, ...), custom_call_target="tpu_custom_call", output_to_operand_aliasing={{0}: (13, {}), {1}: (14, {}), {2}: (15, {})} | custom-call | tf_op jit(solution)/shard_map/pallas_call | solution.py:123
  65.1 1.7 %multiply_select_fusion = (f32[128,128]{1,0:T(8,128)}, f32[128,128]{1,0:T(8,128)}, f32[128,128]{1,0:T(8,128)}) fusion(f32[128,128]{1,0:T(8,128)} %get-tuple-element.38, pred[128]{0:T(512)(128)(4,1)S(1)} %iota_compare_fusion, f32[128,128]{1,0:T(8,128)} %get-tuple-element.37, f32[128,128]{1,0:T(8,128)} %get-tuple-element.36), kind=kLoop, calls=%fused_computation.15 | loop fusion | flops 81920 | bytes 393344 | tf_op jit(solution)/shard_map/jit(_where)/select_n | solution.py:182
  (35 shorter events, 10.8 us)
Async XLA Ops:
  0.6 29.1 %copy-start.1 = (bf16[320,320]{0,1:T(8,128)(2,1)S(1)}, bf16[320,320]{0,1:T(8,128)(2,1)}, u32[]{:S(2)}) copy-start(bf16[320,320]{0,1:T(8,128)(2,1)} %constant.16.clone) | copy-start | bytes 614404
  0.6 29.8 %copy-start = (bf16[320,320]{0,1:T(8,128)(2,1)S(1)}, bf16[320,320]{0,1:T(8,128)(2,1)}, u32[]{:S(2)}) copy-start(bf16[320,320]{0,1:T(8,128)(2,1)} %constant.17.clone) | copy-start | bytes 614404
  2.6 23.1 %collective-permute-start = (bf16[1,36992]{1,0:T(2,128)(2,1)S(1)}, bf16[1,36992]{1,0:T(2,128)(2,1)S(1)}, u32[]{:S(2)}, u32[]{:S(2)}) collective-permute-start(bf16[1,36992]{1,0:T(2,128)(2,1)S(1)} %concatenate.22), channel_id=1, source_target_pairs={{0,8},{2,10},{4,12},{6,14},{8,0},{10,2},{12,4},{14,6},{1,9},{3,11}... | collective-permute-start | bytes 221960 | tf_op jit(solution)/shard_map/ppermute | solution.py:52
  7.5 12.9 %collective-permute-start.3 = (bf16[96,128]{1,0:T(8,128)(2,1)S(1)}, bf16[96,128]{1,0:T(8,128)(2,1)S(1)}, u32[]{:S(2)}, u32[]{:S(2)}) collective-permute-start(bf16[96,128]{1,0:T(8,128)(2,1)S(1)} %get-tuple-element.54), channel_id=1, source_target_pairs={{0,2},{2,4},{4,6},{6,8},{8,10},{10,12},{12,14},{1,3},{3,5},{5,7},{... | collective-permute-start | bytes 73736 | tf_op jit(solution)/shard_map/ppermute | solution.py:22
  10.9 10.3 %collective-permute-start.4 = (bf16[96,128]{1,0:T(8,128)(2,1)S(1)}, bf16[96,128]{1,0:T(8,128)(2,1)S(1)}, u32[]{:S(2)}, u32[]{:S(2)}) collective-permute-start(bf16[96,128]{1,0:T(8,128)(2,1)S(1)} %get-tuple-element.53), channel_id=1, source_target_pairs={{2,0},{4,2},{6,4},{8,6},{10,8},{12,10},{14,12},{3,1},{5,3},{7,5},{... | collective-permute-start | bytes 73736 | tf_op jit(solution)/shard_map/ppermute | solution.py:25
  21.3 8.4 %collective-permute-start.6 = (bf16[320,96]{1,0:T(8,128)(2,1)S(1)}, bf16[320,96]{1,0:T(8,128)(2,1)S(1)}, u32[]{:S(2)}, u32[]{:S(2)}) collective-permute-start(bf16[320,96]{1,0:T(8,128)(2,1)S(1)} %get-tuple-element.52), channel_id=1, source_target_pairs={{1,0},{3,2},{5,4},{7,6},{9,8},{11,10},{13,12},{15,14},{17,16},{19,... | collective-permute-start | bytes 184328 | tf_op jit(solution)/shard_map/ppermute | solution.py:25
  22.6 7.1 %collective-permute-start.5 = (bf16[320,96]{1,0:T(8,128)(2,1)S(1)}, bf16[320,96]{1,0:T(8,128)(2,1)S(1)}, u32[]{:S(2)}, u32[]{:S(2)}) collective-permute-start(bf16[320,96]{1,0:T(8,128)(2,1)S(1)} %get-tuple-element.51), channel_id=1, source_target_pairs={{0,1},{2,3},{4,5},{6,7},{8,9},{10,11},{12,13},{14,15},{16,17},{18,... | collective-permute-start | bytes 184328 | tf_op jit(solution)/shard_map/ppermute | solution.py:22
  26.0 7.1 %collective-permute-start.1 = (bf16[2,36992]{1,0:T(2,128)(2,1)S(1)}, bf16[2,36992]{1,0:T(2,128)(2,1)S(1)}, u32[]{:S(2)}, u32[]{:S(2)}) collective-permute-start(bf16[2,36992]{1,0:T(2,128)(2,1)S(1)} %pad_maximum_fusion.4), channel_id=1, source_target_pairs={{0,4},{2,6},{4,0},{6,2},{8,12},{10,14},{12,8},{14,10},{1,5},{3,7},... | collective-permute-start | bytes 443912 | tf_op jit(solution)/shard_map/ppermute | solution.py:52
  33.6 13.5 %collective-permute-start.2 = (bf16[4,36992]{1,0:T(4,128)(2,1)S(1)}, bf16[4,36992]{1,0:T(4,128)(2,1)S(1)}, u32[]{:S(2)}, u32[]{:S(2)}) collective-permute-start(bf16[4,36992]{1,0:T(4,128)(2,1)S(1)} %pad_maximum_fusion), channel_id=1, source_target_pairs={{0,2},{2,0},{4,6},{6,4},{8,10},{10,8},{12,14},{14,12},{1,3},{3,1},... | collective-permute-start | bytes 887816 | tf_op jit(solution)/shard_map/ppermute | solution.py:52

commit v7 on v6

--- a/solution.py
+++ b/solution.py
@@ -56,6 +56,38 @@
         held = jnp.concatenate([held, other], axis=0)
         step //= 2
     return rounds
+
+
+def swap(payload, pairs):
+    return lax.ppermute(payload, "orient", [(a, b) for a, b in pairs] + [(b, a) for a, b in pairs])
+
+
+def exchange_with_rows(block, tile, width):
+    size = lax.axis_size("orient")
+    index = lax.axis_index("orient")
+    odd = index % 2 == 1
+    low_rows = tile[tile.shape[0] - width :]
+    high_rows = tile[:width]
+    flat = block.shape[1]
+    rows_size = width * tile.shape[1]
+
+    def send(held, rows, pairs):
+        payload = jnp.concatenate([held.reshape(-1), rows.reshape(-1)])
+        got = swap(payload, pairs)
+        count = held.shape[0]
+        return got[: count * flat].reshape(count, flat), got[count * flat :].reshape(width, tile.shape[1])
+
+    first, rows_one = send(block, jnp.where(odd, high_rows, low_rows), [(2 * i, 2 * i + 1) for i in range(size // 2)])
+    held = jnp.concatenate([block, first], axis=0)
+    second_pairs = [(2 * i + 1, 2 * i + 2) for i in range(size // 2 - 1)] + [(0, size - 1)]
+    second, rows_two = send(held, jnp.where(odd, low_rows, high_rows), second_pairs)
+    held = jnp.concatenate([held, second], axis=0)
+    third_pairs = [(0, size // 2), (size - 1, size // 2 - 1), (1, size // 2 + 1), (2, size // 2 + 2)]
+    third = swap(held, third_pairs)
+    zero = jnp.zeros_like(rows_one)
+    top = jnp.where(odd, rows_one, jnp.where(index == 0, zero, rows_two))
+    bottom = jnp.where(odd, jnp.where(index == size - 1, zero, rows_two), rows_one)
+    return [held, third], jnp.concatenate([top, tile, bottom], axis=0)
 
 
 def correlate_kernel(ids_ref, tmpl_ref, ctf_ref, spec_r_ref, spec_i_ref, cos_rows_ref, sin_rows_ref,
@@ -155,10 +187,14 @@
     flat_size = box_size * box_size
     id_block = jnp.broadcast_to(defocus.astype(bf16)[:, None], (local_count, 128))
     packed = jnp.concatenate([templates.reshape(local_count, flat_size), id_block], axis=1)
-    arrivals = exchange_rounds(packed)
+    if lax.axis_size("orient") == 8 and local_count == 1:
+        arrivals, row_padded = exchange_with_rows(packed, micrograph, margin)
+        padded = extended(row_padded, (("tile", 1),), margin)
+    else:
+        arrivals = exchange_rounds(packed)
+        padded = extended(micrograph, (("orient", 0), ("tile", 1)), margin)
     total = sum(piece.shape[0] for piece in arrivals)
 
-    padded = extended(micrograph, (("orient", 0), ("tile", 1)), margin)
     half_real = matmul(padded, cos_full).astype(bf16)
     half_imag = (-matmul(padded, sin_full)).astype(bf16)
     spec_real = (matmul(cos_full, half_real) + matmul(sin_full, half_imag)).astype(bf16).astype(f32)

time: 67.4 us -> 53.6 us (0.80)
  the two profiles are of different devices: /device:TPU:0 before, /device:TPU:11 now
where the time goes in v7:
time: 53.6 us; the launch traced here: 53.2 us
  Pallas kernels  17.2 us (32%)
  local copies, waits for them, and re-layouts  12.7 us (24%)
  starting transfers between devices  11.3 us (21%)
  other arithmetic  6.25 us (12%)
  matrix products  3.69 us (7%)
  between operations  2.15 us (4%)
    pallas_call x2, Pallas kernels, correlate(): pl.pallas_call(functools.partial(correlate_kernel, scaling=scaling), grid...  17.2 us
    ppermute x3, starting transfers between devices, swap(): lax.ppermute(payload, 'orient', [(a, b) for a, b in pairs] + [(b, a) for...  5.54 us
    ppermute x1, starting transfers between devices, extended(): lax.ppermute(lax.slice_in_dim(block, 0, width, axis=dim), axis, backward)  4.42 us
    dot_general x6, matrix products, matmul(): return jnp.dot(left, right, preferred_element_type=jnp.float32)  3.69 us
    reshape x2, local copies, waits for them, and re-layouts, body(): piece_templates = piece[:, :flat_size].reshape(count, box_size, box_size)  2.39 us
    transpose x1, local copies, waits for them, and re-layouts, body(): col_sin = row_sin.T  1.78 us
    select_n x1, other arithmetic, body(): square_out = jnp.where(row_mask, squares / orient_count, 0.0)  1.66 us
    convert_element_type x2, other arithmetic, body(): piece_ids = piece[:, flat_size].astype(jnp.int32)  1.3 us
  transfers between devices with their start and end apart: 5, of which 0 were waited for; matrix products, arithmetic and copies ran while one was open for 28% of the time, Pallas kernels for 16%

profile of v7, /device:TPU:11, one launch (start us, length us, event | category | flops | bytes accessed | tf_op | source)
XLA Modules:
  0.0 53.2 jit_solution(14304454212469808357)
XLA Ops:
  0.7 1.0 %reshape.74 = bf16[1,36864]{1,0:T(2,128)(2,1)S(1)} reshape(bf16[1,192,192]{2,1,0:T(8,128)(2,1)} %param.8) | data formatting | bytes 147456 | tf_op jit(solution)/shard_map/reshape | solution.py:189
  2.4 0.8 %select_bitcast_fusion.3 = (bf16[12288]{0:T(1024)(128)(2,1)S(1)}, bf16[12288]{0:T(1024)(128)(2,1)S(1)}) fusion(pred[]{:T(512)S(6)} %eq.11, bf16[128,128]{1,0:T(8,128)(2,1)} %param.7), kind=kLoop, calls=%fused_computation.23 | loop fusion | flops 24576 | bytes 98305 | tf_op jit(solution)/shard_map/reshape | solution.py:75
  4.0 1.2 %fusion.7 = (bf16[96,320]{0,1:T(8,128)(2,1)S(1)}, bf16[96,320]{0,1:T(8,128)(2,1)S(1)}, bf16[96,320]{0,1:T(8,128)(2,1)S(1)}, bf16[96,320]{0,1:T(8,128)(2,1)S(1)}) fusion(bf16[320,320]{0,1:T(8,128)(2,1)} %constant.42.clone, bf16[320,320]{0,1:T(8,128)(2,1)} %constant.41.clone), kind=kLoop, calls=%fused_computation.32 | loop fusion | bytes 491520 | tf_op jit(solution)/shard_map/slice | solution.py:178
  5.2 1.8 %slice_bitcast_fusion = (bf16[320,128]{1,0:T(8,128)(2,1)}, bf16[128,320]{0,1:T(8,128)(2,1)S(1)}, bf16[128,320]{0,1:T(8,128)(2,1)S(1)}, bf16[320,128]{1,0:T(8,128)(2,1)}) fusion(bf16[320,320]{0,1:T(8,128)(2,1)} %constant.42.clone, bf16[320,320]{0,1:T(8,128)(2,1)} %constant.41.clone), kind=kLoop, calls=%fused_computation.27 | loop fusion | bytes 491520 | tf_op jit(solution)/shard_map/transpose | solution.py:184
  7.0 0.8 %fusion.6 = (bf16[320,192]{1,0:T(8,128)(2,1)}, bf16[192,320]{0,1:T(8,128)(2,1)S(1)}) fusion(bf16[96,320]{0,1:T(8,128)(2,1)S(1)} %get-tuple-element.44, bf16[96,320]{0,1:T(8,128)(2,1)S(1)} %get-tuple-element.45), kind=kLoop, calls=%fused_computation.30 | loop fusion | flops 245760 | bytes 368640 | tf_op jit(solution)/shard_map/transpose | solution.py:179
  8.5 2.3 %collective-permute-start.1 = (bf16[86272]{0:T(1024)(128)(2,1)S(1)}, bf16[86272]{0:T(1024)(128)(2,1)S(1)}, u32[]{:S(2)}, u32[]{:S(2)}) collective-permute-start(bf16[86272]{0:T(1024)(128)(2,1)S(1)} %pad_maximum_fusion.2), channel_id=1, source_target_pairs={{2,4},{6,8},{10,12},{0,14},{4,2},{8,6},{12,10},{14,0},{3,5},{7,9},... | collective-permute-start | bytes 517640 | tf_op jit(solution)/shard_map/ppermute | solution.py:62
  10.8 0.8 %fusion.5 = (bf16[320,192]{1,0:T(8,128)(2,1)}, bf16[192,320]{0,1:T(8,128)(2,1)S(1)}) fusion(bf16[96,320]{0,1:T(8,128)(2,1)S(1)} %get-tuple-element.26, bf16[96,320]{0,1:T(8,128)(2,1)S(1)} %get-tuple-element.25), kind=kLoop, calls=%fused_computation.29 | loop fusion | flops 245760 | bytes 368640 | tf_op jit(solution)/shard_map/transpose | solution.py:180
  11.6 0.8 %copy.39.cos_rows_ref = bf16[192,320]{1,0:T(8,128)(2,1)} copy(bf16[192,320]{0,1:T(8,128)(2,1)S(1)} %get-tuple-element.32) | data formatting | bytes 245760 | tf_op jit(solution)/shard_map/concatenate | solution.py:177
  12.3 0.8 %copy.40.sin_rows_ref = bf16[192,320]{1,0:T(8,128)(2,1)} copy(bf16[192,320]{0,1:T(8,128)(2,1)S(1)} %get-tuple-element.30) | data formatting | bytes 245760 | tf_op jit(solution)/shard_map/concatenate | solution.py:178
  13.1 0.7 %copy.41.row_cos_ref = bf16[128,320]{1,0:T(8,128)(2,1)} copy(bf16[128,320]{0,1:T(8,128)(2,1)S(1)} %get-tuple-element.42) | data formatting | bytes 163840 | tf_op jit(solution)/shard_map/slice | solution.py:181
  13.9 0.7 %copy.42.row_sin_ref = bf16[128,320]{1,0:T(8,128)(2,1)} copy(bf16[128,320]{0,1:T(8,128)(2,1)S(1)} %get-tuple-element.22) | data formatting | bytes 163840 | tf_op jit(solution)/shard_map/slice | solution.py:182
  16.1 2.9 %collective-permute-start.2 = (bf16[4,36992]{1,0:T(4,128)(2,1)S(1)}, bf16[4,36992]{1,0:T(4,128)(2,1)S(1)}, u32[]{:S(2)}, u32[]{:S(2)}) collective-permute-start(bf16[4,36992]{1,0:T(4,128)(2,1)S(1)} %pad_maximum_fusion), channel_id=1, source_target_pairs={{0,8},{14,6},{2,10},{4,12},{8,0},{6,14},{10,2},{12,4},{1,9},{15,7}... | collective-permute-start | bytes 887816 | tf_op jit(solution)/shard_map/ppermute | solution.py:62
  19.2 1.3 %collective-permute-start.3 = (bf16[320,96]{1,0:T(8,128)(2,1)S(1)}, bf16[320,96]{1,0:T(8,128)(2,1)S(1)}, u32[]{:S(2)}, u32[]{:S(2)}) collective-permute-start(bf16[320,96]{1,0:T(8,128)(2,1)S(1)} %get-tuple-element.35), channel_id=1, source_target_pairs={{0,1},{2,3},{4,5},{6,7},{8,9},{10,11},{12,13},{14,15},{16,17},{18,... | collective-permute-start | bytes 184328 | tf_op jit(solution)/shard_map/ppermute | solution.py:22
  20.5 4.4 %collective-permute-start.4 = (bf16[320,96]{1,0:T(8,128)(2,1)S(1)}, bf16[320,96]{1,0:T(8,128)(2,1)S(1)}, u32[]{:S(2)}, u32[]{:S(2)}) collective-permute-start(bf16[320,96]{1,0:T(8,128)(2,1)S(1)} %get-tuple-element.36), channel_id=1, source_target_pairs={{1,0},{3,2},{5,4},{7,6},{9,8},{11,10},{13,12},{15,14},{17,16},{19,... | collective-permute-start | bytes 184328 | tf_op jit(solution)/shard_map/ppermute | solution.py:25
  24.9 1.2 %reshape.82.tmpl_ref = bf16[4,192,192]{2,1,0:T(8,128)(2,1)} reshape(bf16[4,36864]{1,0:T(4,128)(2,1)S(1)} %slice.97) | data formatting | bytes 589824 | tf_op jit(solution)/shard_map/reshape | solution.py:208
  26.1 0.7 %convert_reduce_fusion.ids_ref = s32[4]{0:T(128)} fusion(bf16[4,36992]{1,0:T(4,128)(2,1)S(1)} %pad_maximum_fusion), kind=kLoop, calls=%fused_computation.24 | loop fusion | flops 4 | bytes 24 | tf_op jit(solution)/shard_map/convert_element_type | solution.py:209
  27.9 1.1 %fusion.4.spec_i_ref = f32[320,320]{1,0:T(8,128)} fusion(f32[320,320]{1,0:T(8,128)S(1)} %fusion.12, bf16[320,320]{0,1:T(8,128)(2,1)S(1)} %copy-done, bf16[320,320]{1,0:T(8,128)(2,1)S(1)} %convolution_convert_fusion), kind=kOutput, calls=%fused_computation.8 | convolution fusion | flops 65843200 | bytes 1228800 | tf_op jit(solution)/shard_map/dot_general | solution.py:41
  29.4 1.1 %fusion.2.spec_r_ref = f32[320,320]{1,0:T(8,128)} fusion(f32[320,320]{1,0:T(8,128)S(1)} %fusion.11, bf16[320,320]{0,1:T(8,128)(2,1)S(1)} %copy-done, bf16[320,320]{1,0:T(8,128)(2,1)S(1)} %fusion), kind=kOutput, calls=%fused_computation.6 | convolution fusion | flops 65843200 | bytes 1228800 | tf_op jit(solution)/shard_map/dot_general | solution.py:41
  31.8 0.6 %broadcast_in_dim.34.prev_peak_ref = f32[128,128]{1,0:T(8,128)} broadcast(f32[]{:T(128)} %constant.38.clone.1), dimensions={} | broadcast | bytes 65540 | tf_op jit(solution)/shard_map/broadcast_in_dim | solution.py:205
  32.4 8.6 %shard_map.94 = (f32[128,128]{1,0:T(8,128)}, f32[128,128]{1,0:T(8,128)}, f32[128,128]{1,0:T(8,128)}) custom-call(s32[4]{0:T(128)} %convert_reduce_fusion.ids_ref, bf16[4,192,192]{2,1,0:T(8,128)(2,1)} %reshape.82.tmpl_ref, f32[8,320,320]{2,1,0:T(8,128)} %ctf_ref.3, ...), custom_call_target="tpu_custom_call", output_to_operand_aliasing={{0}: (13, {}), {1}: (14, {}), {2}: (15, {})} | custom-call | tf_op jit(solution)/shard_map/pallas_call | solution.py:155
  41.1 1.2 %reshape.81.tmpl_ref = bf16[4,192,192]{2,1,0:T(8,128)(2,1)} reshape(bf16[4,36864]{1,0:T(4,128)(2,1)S(1)} %slice.91) | data formatting | bytes 589824 | tf_op jit(solution)/shard_map/reshape | solution.py:208
  42.3 0.7 %convert_reduce_fusion.1.ids_ref = s32[4]{0:T(128)} fusion(bf16[4,36992]{1,0:T(4,128)(2,1)S(1)} %collective-permute-done.2), kind=kLoop, calls=%fused_computation.25 | loop fusion | flops 4 | bytes 24 | tf_op jit(solution)/shard_map/convert_element_type | solution.py:209
  43.0 8.6 %shard_map.95 = (f32[128,128]{1,0:T(8,128)}, f32[128,128]{1,0:T(8,128)}, f32[128,128]{1,0:T(8,128)}) custom-call(s32[4]{0:T(128)} %convert_reduce_fusion.1.ids_ref, bf16[4,192,192]{2,1,0:T(8,128)(2,1)} %reshape.81.tmpl_ref, f32[8,320,320]{2,1,0:T(8,128)} %ctf_ref.3, ...), custom_call_target="tpu_custom_call", output_to_operand_aliasing={{0}: (13, {}), {1}: (14, {}), {2}: (15, {})} | custom-call | tf_op jit(solution)/shard_map/pallas_call | solution.py:155
  51.5 1.7 %multiply_select_fusion = (f32[128,128]{1,0:T(8,128)}, f32[128,128]{1,0:T(8,128)}, f32[128,128]{1,0:T(8,128)}) fusion(f32[128,128]{1,0:T(8,128)} %get-tuple-element.18, pred[128]{0:T(512)(128)(4,1)S(1)} %iota_compare_fusion, f32[128,128]{1,0:T(8,128)} %get-tuple-element.17, f32[128,128]{1,0:T(8,128)} %get-tuple-element.16), kind=kLoop, calls=%fused_computation.17 | loop fusion | flops 81920 | bytes 393344 | tf_op jit(solution)/shard_map/jit(_where)/select_n | solution.py:218
  (34 shorter events, 5.3 us)
Async XLA Ops:
  0.6 18.4 %copy-start.2 = (bf16[128,128]{1,0:T(8,128)(2,1)S(1)}, bf16[128,128]{1,0:T(8,128)(2,1)}, u32[]{:S(2)}) copy-start(bf16[128,128]{1,0:T(8,128)(2,1)} %param.7) | copy-start | bytes 98308
  3.7 23.1 %copy-start = (bf16[320,320]{0,1:T(8,128)(2,1)S(1)}, bf16[320,320]{0,1:T(8,128)(2,1)}, u32[]{:S(2)}) copy-start(bf16[320,320]{0,1:T(8,128)(2,1)} %constant.42.clone) | copy-start | bytes 614404
  3.7 4.1 %collective-permute-start = (bf16[49280]{0:T(1024)(128)(2,1)S(1)}, bf16[49280]{0:T(1024)(128)(2,1)S(1)}, u32[]{:S(2)}, u32[]{:S(2)}) collective-permute-start(bf16[49280]{0:T(1024)(128)(2,1)S(1)} %pad_maximum_fusion.6), channel_id=1, source_target_pairs={{0,2},{4,6},{8,10},{12,14},{2,0},{6,4},{10,8},{14,12},{1,3},{5,7},... | collective-permute-start | bytes 295688 | tf_op jit(solution)/shard_map/ppermute | solution.py:62
  7.7 19.4 %copy-start.1 = (bf16[320,320]{0,1:T(8,128)(2,1)S(1)}, bf16[320,320]{0,1:T(8,128)(2,1)}, u32[]{:S(2)}) copy-start(bf16[320,320]{0,1:T(8,128)(2,1)} %constant.41.clone) | copy-start | bytes 614404
  8.5 6.8 %collective-permute-start.1 = (bf16[86272]{0:T(1024)(128)(2,1)S(1)}, bf16[86272]{0:T(1024)(128)(2,1)S(1)}, u32[]{:S(2)}, u32[]{:S(2)}) collective-permute-start(bf16[86272]{0:T(1024)(128)(2,1)S(1)} %pad_maximum_fusion.2), channel_id=1, source_target_pairs={{2,4},{6,8},{10,12},{0,14},{4,2},{8,6},{12,10},{14,0},{3,5},{7,9},... | collective-permute-start | bytes 517640 | tf_op jit(solution)/shard_map/ppermute | solution.py:62
  16.1 24.9 %collective-permute-start.2 = (bf16[4,36992]{1,0:T(4,128)(2,1)S(1)}, bf16[4,36992]{1,0:T(4,128)(2,1)S(1)}, u32[]{:S(2)}, u32[]{:S(2)}) collective-permute-start(bf16[4,36992]{1,0:T(4,128)(2,1)S(1)} %pad_maximum_fusion), channel_id=1, source_target_pairs={{0,8},{14,6},{2,10},{4,12},{8,0},{6,14},{10,2},{12,4},{1,9},{15,7}... | collective-permute-start | bytes 887816 | tf_op jit(solution)/shard_map/ppermute | solution.py:62
  19.2 7.6 %collective-permute-start.3 = (bf16[320,96]{1,0:T(8,128)(2,1)S(1)}, bf16[320,96]{1,0:T(8,128)(2,1)S(1)}, u32[]{:S(2)}, u32[]{:S(2)}) collective-permute-start(bf16[320,96]{1,0:T(8,128)(2,1)S(1)} %get-tuple-element.35), channel_id=1, source_target_pairs={{0,1},{2,3},{4,5},{6,7},{8,9},{10,11},{12,13},{14,15},{16,17},{18,... | collective-permute-start | bytes 184328 | tf_op jit(solution)/shard_map/ppermute | solution.py:22
  20.5 6.3 %collective-permute-start.4 = (bf16[320,96]{1,0:T(8,128)(2,1)S(1)}, bf16[320,96]{1,0:T(8,128)(2,1)S(1)}, u32[]{:S(2)}, u32[]{:S(2)}) collective-permute-start(bf16[320,96]{1,0:T(8,128)(2,1)S(1)} %get-tuple-element.36), channel_id=1, source_target_pairs={{1,0},{3,2},{5,4},{7,6},{9,8},{11,10},{13,12},{15,14},{17,16},{19,... | collective-permute-start | bytes 184328 | tf_op jit(solution)/shard_map/ppermute | solution.py:25

commit v8 on v7

--- a/solution.py
+++ b/solution.py
@@ -68,14 +68,13 @@
     odd = index % 2 == 1
     low_rows = tile[tile.shape[0] - width :]
     high_rows = tile[:width]
-    flat = block.shape[1]
-    rows_size = width * tile.shape[1]
+    lanes = block.shape[1]
+    carried = width * tile.shape[1] // lanes
 
     def send(held, rows, pairs):
-        payload = jnp.concatenate([held.reshape(-1), rows.reshape(-1)])
+        payload = jnp.concatenate([held, rows.reshape(carried, lanes)], axis=0)
         got = swap(payload, pairs)
-        count = held.shape[0]
-        return got[: count * flat].reshape(count, flat), got[count * flat :].reshape(width, tile.shape[1])
+        return got[: held.shape[0]], got[held.shape[0] :].reshape(width, tile.shape[1])
 
     first, rows_one = send(block, jnp.where(odd, high_rows, low_rows), [(2 * i, 2 * i + 1) for i in range(size // 2)])
     held = jnp.concatenate([block, first], axis=0)
@@ -91,7 +90,7 @@
 
 
 def correlate_kernel(ids_ref, tmpl_ref, ctf_ref, spec_r_ref, spec_i_ref, cos_rows_ref, sin_rows_ref,
-                     cos_cols_ref, sin_cols_ref, row_cos_ref, row_sin_ref, col_cos_ref, col_sin_ref,
+                     cols_ref, rows_ref, col_cos_ref, col_sin_ref,
                      prev_peak_ref, prev_sum_ref, prev_sq_ref, peak_ref, sum_ref, sq_ref, *, scaling):
     bf16 = jnp.bfloat16
     f32 = jnp.float32
@@ -103,21 +102,25 @@
     template = tmpl_ref[0]
     part_real = mm(template, cos_rows_ref[...]).astype(bf16)
     part_imag = (-mm(template, sin_rows_ref[...])).astype(bf16)
-    cos_cols = cos_cols_ref[...]
-    sin_cols = sin_cols_ref[...]
-    full_real = mm(cos_cols, part_real) + mm(sin_cols, part_imag)
-    full_imag = mm(cos_cols, part_imag) - mm(sin_cols, part_real)
+    cols = cols_ref[...]
+    n = cols.shape[0] // 2
+    from_real = mm(cols, part_real)
+    from_imag = mm(cols, part_imag)
+    full_real = from_real[:n] + from_imag[n:]
+    full_imag = from_imag[:n] - from_real[n:]
     weight = ctf_ref[0]
     w_real = (full_real * weight).astype(bf16).astype(f32)
     w_imag = (full_imag * weight).astype(bf16).astype(f32)
-    spec_real = spec_r_ref[...]
-    spec_imag = spec_i_ref[...]
+    spec_real = spec_r_ref[...].astype(f32)
+    spec_imag = spec_i_ref[...].astype(f32)
     prod_real = (spec_real * w_real + spec_imag * w_imag).astype(bf16)
     prod_imag = (spec_imag * w_real - spec_real * w_imag).astype(bf16)
-    row_cos = row_cos_ref[...]
-    row_sin = row_sin_ref[...]
-    left_real = (mm(row_cos, prod_real) - mm(row_sin, prod_imag)).astype(bf16)
-    left_imag = (mm(row_cos, prod_imag) + mm(row_sin, prod_real)).astype(bf16)
+    rows = rows_ref[...]
+    tile = rows.shape[0] // 2
+    left_from_real = mm(rows, prod_real)
+    left_from_imag = mm(rows, prod_imag)
+    left_real = (left_from_real[:tile] - left_from_imag[tile:]).astype(bf16)
+    left_imag = (left_from_imag[:tile] + left_from_real[tile:]).astype(bf16)
     corr = (mm(left_real, col_cos_ref[...]) - mm(left_imag, col_sin_ref[...])) * scaling
 
     @pl.when(o == 0)
@@ -134,9 +137,10 @@
 
 
 def correlate(ids, all_templates, ctf, spec_real, spec_imag, tables, scaling, previous):
-    count, box, _ = all_templates.shape
+    count = all_templates.shape[0]
+    box = all_templates.shape[2]
     n = ctf.shape[1]
-    tile = tables[4].shape[0]
+    tile = tables[4].shape[1]
     full = lambda shape: pl.BlockSpec(shape, lambda o, ids: (0,) * len(shape))
     in_specs = [
         pl.BlockSpec((1, box, box), lambda o, ids: (o, 0, 0)),
@@ -184,30 +188,37 @@
     col_sin = row_sin.T
 
     local_count = templates.shape[0]
-    flat_size = box_size * box_size
-    id_block = jnp.broadcast_to(defocus.astype(bf16)[:, None], (local_count, 128))
-    packed = jnp.concatenate([templates.reshape(local_count, flat_size), id_block], axis=1)
-    if lax.axis_size("orient") == 8 and local_count == 1:
+    id_rows = jnp.broadcast_to(defocus.astype(bf16)[:, None, None], (local_count, 8, box_size))
+    block_rows = box_size + 8
+    packed = jnp.concatenate([templates, id_rows], axis=1).reshape(local_count * block_rows, box_size)
+    if lax.axis_size("orient") == 8 and local_count == 1 and (margin * tile_width) % box_size == 0:
         arrivals, row_padded = exchange_with_rows(packed, micrograph, margin)
         padded = extended(row_padded, (("tile", 1),), margin)
     else:
         arrivals = exchange_rounds(packed)
         padded = extended(micrograph, (("orient", 0), ("tile", 1)), margin)
-    total = sum(piece.shape[0] for piece in arrivals)
+    total = sum(piece.shape[0] for piece in arrivals) // block_rows
 
     half_real = matmul(padded, cos_full).astype(bf16)
     half_imag = (-matmul(padded, sin_full)).astype(bf16)
-    spec_real = (matmul(cos_full, half_real) + matmul(sin_full, half_imag)).astype(bf16).astype(f32)
-    spec_imag = (matmul(cos_full, half_imag) - matmul(sin_full, half_real)).astype(bf16).astype(f32)
-
-    tables = (cos_rows, sin_rows, cos_cols, sin_cols, row_cos, row_sin, col_cos, col_sin)
+    spec_real = (matmul(cos_full, half_real) + matmul(sin_full, half_imag)).astype(bf16)
+    spec_imag = (matmul(cos_full, half_imag) - matmul(sin_full, half_real)).astype(bf16)
+
+    tables = (
+        cos_rows,
+        sin_rows,
+        jnp.concatenate([cos_cols, sin_cols], axis=0),
+        jnp.concatenate([row_cos, row_sin], axis=0),
+        col_cos,
+        col_sin,
+    )
     shape = (tile_width, tile_width)
     stats = (jnp.full(shape, -jnp.inf, f32), jnp.zeros(shape, f32), jnp.zeros(shape, f32))
     for piece in arrivals:
-        count = piece.shape[0]
-        piece_templates = piece[:, :flat_size].reshape(count, box_size, box_size)
-        piece_ids = piece[:, flat_size].astype(jnp.int32)
-        stats = correlate(piece_ids, piece_templates, ctf, spec_real, spec_imag, tables, scaling, stats)
+        count = piece.shape[0] // block_rows
+        piece = piece.reshape(count, block_rows, box_size)
+        piece_ids = piece[:, box_size, 0].astype(jnp.int32)
+        stats = correlate(piece_ids, piece, ctf, spec_real, spec_imag, tables, scaling, stats)
     peak_map, sum_map, squares = stats
 
     live = usable[0, 0]

time: 53.6 us -> 58.4 us (1.090)
  the two profiles are of different devices: /device:TPU:11 before, /device:TPU:0 now
where the time goes in v8:
time: 58.4 us; the launch traced here: 58 us
  Pallas kernels  17.1 us (29%)
  waiting for transfers between devices  11.3 us (19%)
  starting transfers between devices  10.1 us (17%)
  local copies, waits for them, and re-layouts  8.75 us (15%)
  other arithmetic  5.07 us (9%)
  matrix products  3.51 us (6%)
  between operations  2.16 us (4%)
    pallas_call x2, Pallas kernels, correlate(): pl.pallas_call(functools.partial(correlate_kernel, scaling=scaling), grid...  17.1 us
    ppermute x3, waiting for transfers between devices, swap(): lax.ppermute(payload, 'orient', [(a, b) for a, b in pairs] + [(b, a) for...  11.1 us
    ppermute x3, starting transfers between devices, swap(): lax.ppermute(payload, 'orient', [(a, b) for a, b in pairs] + [(b, a) for...  7.5 us
    dot_general x6, matrix products, matmul(): return jnp.dot(left, right, preferred_element_type=jnp.float32)  3.51 us
    transpose x1, local copies, waits for them, and re-layouts, body(): col_sin = row_sin.T  1.77 us
    select_n x1, other arithmetic, body(): square_out = jnp.where(row_mask, squares / orient_count, 0.0)  1.66 us
    convert_element_type x2, other arithmetic, body(): piece_ids = piece[:, box_size, 0].astype(jnp.int32)  1.41 us
    ppermute x1, starting transfers between devices, extended(): lax.ppermute(lax.slice_in_dim(block, block.shape[dim] - width, None, axis...  1.29 us
  transfers between devices with their start and end apart: 5, of which 3 were waited for; matrix products, arithmetic and copies ran while one was open for 22% of the time, Pallas kernels for 15%

profile of v8, /device:TPU:0, one launch (start us, length us, event | category | flops | bytes accessed | tf_op | source)
XLA Modules:
  0.0 58.0 jit_solution(6206149003505283519)
XLA Ops:
  0.7 0.8 %broadcast_select_fusion.2 = (bf16[96,128]{1,0:T(8,128)(2,1)S(1)}, bf16[96,128]{1,0:T(8,128)(2,1)S(1)}) fusion(pred[]{:T(512)S(6)} %eq.11, bf16[128,128]{1,0:T(8,128)(2,1)} %param.7), kind=kLoop, calls=%fused_computation.22 | loop fusion | flops 24576 | bytes 98305 | tf_op jit(solution)/shard_map/jit(_where)/select_n | solution.py:79
  2.2 0.9 %pad_bitcast_fusion = bf16[200,192]{1,0:T(8,128)(2,1)S(1)} fusion(bf16[1,192,192]{2,1,0:T(8,128)(2,1)} %param.8, bf16[]{:T(256)} %bitcast.1), kind=kLoop, calls=%fused_computation.15 | loop fusion | bytes 150530 | tf_op jit(solution)/shard_map/reshape | solution.py:193
  3.2 3.0 %collective-permute-start = (bf16[264,192]{1,0:T(8,128)(2,1)S(1)}, bf16[264,192]{1,0:T(8,128)(2,1)S(1)}, u32[]{:S(2)}, u32[]{:S(2)}) collective-permute-start(bf16[264,192]{1,0:T(8,128)(2,1)S(1)} %pad_maximum_fusion.7), channel_id=1, source_target_pairs={{0,2},{4,6},{8,10},{12,14},{2,0},{6,4},{10,8},{14,12},{1,3},{5,7},... | collective-permute-start | bytes 304136 | tf_op jit(solution)/shard_map/ppermute | solution.py:62
  6.2 1.2 %fusion.9 = (bf16[96,320]{0,1:T(8,128)(2,1)S(1)}, bf16[96,320]{0,1:T(8,128)(2,1)S(1)}, bf16[96,320]{0,1:T(8,128)(2,1)S(1)}, bf16[96,320]{0,1:T(8,128)(2,1)S(1)}) fusion(bf16[320,320]{0,1:T(8,128)(2,1)} %constant.42.clone, bf16[320,320]{0,1:T(8,128)(2,1)} %constant.41.clone), kind=kLoop, calls=%fused_computation.37 | loop fusion | bytes 491520 | tf_op jit(solution)/shard_map/slice | solution.py:182
  7.4 1.8 %slice_bitcast_fusion = (bf16[320,128]{1,0:T(8,128)(2,1)}, bf16[128,320]{0,1:T(8,128)(2,1)S(1)}, bf16[128,320]{0,1:T(8,128)(2,1)S(1)}, bf16[320,128]{1,0:T(8,128)(2,1)}) fusion(bf16[320,320]{0,1:T(8,128)(2,1)} %constant.42.clone, bf16[320,320]{0,1:T(8,128)(2,1)} %constant.41.clone), kind=kLoop, calls=%fused_computation.33 | loop fusion | bytes 491520 | tf_op jit(solution)/shard_map/transpose | solution.py:188
  9.4 0.8 %copy.25.cos_rows_ref = bf16[192,320]{1,0:T(8,128)(2,1)} copy(bf16[192,320]{0,1:T(8,128)(2,1)S(1)} %get-tuple-element.30) | data formatting | bytes 245760 | tf_op jit(solution)/shard_map/concatenate | solution.py:181
  10.3 0.8 %copy.26.sin_rows_ref = bf16[192,320]{1,0:T(8,128)(2,1)} copy(bf16[192,320]{0,1:T(8,128)(2,1)S(1)} %get-tuple-element.32) | data formatting | bytes 245760 | tf_op jit(solution)/shard_map/concatenate | solution.py:182
  11.1 0.8 %copy.27.rows_ref = bf16[256,320]{1,0:T(8,128)(2,1)} copy(bf16[256,320]{0,1:T(8,128)(2,1)S(1)} %pad_maximum_fusion.6) | data formatting | bytes 327680 | tf_op jit(solution)/shard_map/concatenate | solution.py:211
  12.7 3.6 %collective-permute-start.1 = (bf16[464,192]{1,0:T(8,128)(2,1)S(1)}, bf16[464,192]{1,0:T(8,128)(2,1)S(1)}, u32[]{:S(2)}, u32[]{:S(2)}) collective-permute-start(bf16[464,192]{1,0:T(8,128)(2,1)S(1)} %pad_maximum_fusion.3), channel_id=1, source_target_pairs={{2,4},{6,8},{10,12},{0,14},{4,2},{8,6},{12,10},{14,0},{3,5},{7,9},... | collective-permute-start | bytes 534536 | tf_op jit(solution)/shard_map/ppermute | solution.py:62
  16.3 0.8 %pad_maximum_fusion.1.cols_ref = bf16[640,192]{1,0:T(8,128)(2,1)} fusion(bf16[320,192]{1,0:T(8,128)(2,1)S(1)} %get-tuple-element.31, bf16[320,192]{1,0:T(8,128)(2,1)S(1)} %get-tuple-element.29), kind=kLoop, calls=%fused_computation.8 | loop fusion | flops 491520 | bytes 491520 | tf_op jit(solution)/shard_map/concatenate | solution.py:210
  17.1 5.6 %collective-permute-done.1 = bf16[464,192]{1,0:T(8,128)(2,1)S(1)} collective-permute-done((bf16[464,192]{1,0:T(8,128)(2,1)S(1)}, bf16[464,192]{1,0:T(8,128)(2,1)S(1)}, u32[]{:S(2)}, u32[]{:S(2)}) %collective-permute-start.1) | collective-permute-done | bytes 178208 | tf_op jit(solution)/shard_map/ppermute | solution.py:62
  23.0 1.3 %collective-permute-start.3 = (bf16[320,96]{1,0:T(8,128)(2,1)S(1)}, bf16[320,96]{1,0:T(8,128)(2,1)S(1)}, u32[]{:S(2)}, u32[]{:S(2)}) collective-permute-start(bf16[320,96]{1,0:T(8,128)(2,1)S(1)} %get-tuple-element.33), channel_id=1, source_target_pairs={{0,1},{2,3},{4,5},{6,7},{8,9},{10,11},{12,13},{14,15},{16,17},{18,... | collective-permute-start | bytes 184328 | tf_op jit(solution)/shard_map/ppermute | solution.py:22
  24.3 1.3 %collective-permute-start.4 = (bf16[320,96]{1,0:T(8,128)(2,1)S(1)}, bf16[320,96]{1,0:T(8,128)(2,1)S(1)}, u32[]{:S(2)}, u32[]{:S(2)}) collective-permute-start(bf16[320,96]{1,0:T(8,128)(2,1)S(1)} %get-tuple-element.34), channel_id=1, source_target_pairs={{1,0},{3,2},{5,4},{7,6},{9,8},{11,10},{13,12},{15,14},{17,16},{19,... | collective-permute-start | bytes 184328 | tf_op jit(solution)/shard_map/ppermute | solution.py:25
  25.7 0.9 %collective-permute-start.2 = (bf16[800,192]{1,0:T(8,128)(2,1)S(1)}, bf16[800,192]{1,0:T(8,128)(2,1)S(1)}, u32[]{:S(2)}, u32[]{:S(2)}) collective-permute-start(bf16[800,192]{1,0:T(8,128)(2,1)S(1)} %pad_maximum_fusion), channel_id=1, source_target_pairs={{0,8},{14,6},{2,10},{4,12},{8,0},{6,14},{10,2},{12,4},{1,9},{15,7}... | collective-permute-start | bytes 921608 | tf_op jit(solution)/shard_map/ppermute | solution.py:62
  26.6 0.7 %fusion.3.ids_ref = s32[4]{0:T(128)} fusion(bf16[4,200,192]{2,1,0:T(8,128)(2,1)S(1)} %bitcast.24), kind=kLoop, calls=%fused_computation.27 | loop fusion | flops 4 | bytes 24 | tf_op jit(solution)/shard_map/convert_element_type | solution.py:220
  28.6 1.1 %fusion.2.spec_i_ref = bf16[320,320]{1,0:T(8,128)(2,1)} fusion(f32[320,320]{1,0:T(8,128)S(1)} %fusion.13, bf16[320,320]{0,1:T(8,128)(2,1)S(1)} %copy-done, bf16[320,320]{1,0:T(8,128)(2,1)S(1)} %convolution_convert_fusion), kind=kOutput, calls=%fused_computation.6 | convolution fusion | flops 65740800 | bytes 1024000 | tf_op jit(solution)/shard_map/dot_general | solution.py:41
  30.0 1.0 %fusion.1.spec_r_ref = bf16[320,320]{1,0:T(8,128)(2,1)} fusion(f32[320,320]{1,0:T(8,128)S(1)} %fusion.12, bf16[320,320]{0,1:T(8,128)(2,1)S(1)} %copy-done, bf16[320,320]{1,0:T(8,128)(2,1)S(1)} %fusion), kind=kOutput, calls=%fused_computation.5 | convolution fusion | flops 65740800 | bytes 1024000 | tf_op jit(solution)/shard_map/dot_general | solution.py:41
  31.1 0.6 %broadcast_3_prev_sum_ref_prev_sq_ref.2.prev_sum_ref = f32[128,128]{1,0:T(8,128)} broadcast(f32[]{:T(128)} %constant.39.clone.1), dimensions={} | broadcast | bytes 65540 | tf_op jit(solution)/shard_map/broadcast.3.prev_sum_ref.prev_sq_ref
  31.7 0.6 %broadcast_3_prev_sum_ref_prev_sq_ref.2.clone.prev_sq_ref = f32[128,128]{1,0:T(8,128)} broadcast(f32[]{:T(128)} %constant.39.clone.1), dimensions={} | broadcast | bytes 65540 | tf_op jit(solution)/shard_map/broadcast.3.prev_sum_ref.prev_sq_ref
  33.0 8.5 %shard_map.94 = (f32[128,128]{1,0:T(8,128)}, f32[128,128]{1,0:T(8,128)}, f32[128,128]{1,0:T(8,128)}) custom-call(s32[4]{0:T(128)} %fusion.3.ids_ref, bf16[4,200,192]{2,1,0:T(8,128)(2,1)} %bitcast.25, f32[8,320,320]{2,1,0:T(8,128)} %ctf_ref.3, bf16[320,320]{1,0:T(8,128)(2,1)} %fusion.1.spec_r_ref, ...), custom_call_target="tpu_custom_call", output_to_operand_aliasing={{0}: (11, {}), {1}: (12, {}), {2}: (13, {})} | custom-call | tf_op jit(solution)/shard_map/pallas_call | solution.py:159
  41.5 5.5 %collective-permute-done.2 = bf16[800,192]{1,0:T(8,128)(2,1)S(1)} collective-permute-done((bf16[800,192]{1,0:T(8,128)(2,1)S(1)}, bf16[800,192]{1,0:T(8,128)(2,1)S(1)}, u32[]{:S(2)}, u32[]{:S(2)}) %collective-permute-start.2) | collective-permute-done | bytes 307232 | tf_op jit(solution)/shard_map/ppermute | solution.py:62
  47.0 0.7 %fusion.4.ids_ref = s32[4]{0:T(128)} fusion(bf16[4,200,192]{2,1,0:T(8,128)(2,1)S(1)} %bitcast.26), kind=kLoop, calls=%fused_computation.29 | loop fusion | flops 4 | bytes 24 | tf_op jit(solution)/shard_map/convert_element_type | solution.py:220
  47.8 8.5 %shard_map.95 = (f32[128,128]{1,0:T(8,128)}, f32[128,128]{1,0:T(8,128)}, f32[128,128]{1,0:T(8,128)}) custom-call(s32[4]{0:T(128)} %fusion.4.ids_ref, bf16[4,200,192]{2,1,0:T(8,128)(2,1)} %bitcast.27, f32[8,320,320]{2,1,0:T(8,128)} %ctf_ref.3, bf16[320,320]{1,0:T(8,128)(2,1)} %fusion.1.spec_r_ref, ...), custom_call_target="tpu_custom_call", output_to_operand_aliasing={{0}: (11, {}), {1}: (12, {}), {2}: (13, {})} | custom-call | tf_op jit(solution)/shard_map/pallas_call | solution.py:159
  56.3 1.7 %multiply_select_fusion = (f32[128,128]{1,0:T(8,128)}, f32[128,128]{1,0:T(8,128)}, f32[128,128]{1,0:T(8,128)}) fusion(f32[128,128]{1,0:T(8,128)} %get-tuple-element.18, pred[128]{0:T(512)(128)(4,1)S(1)} %iota_compare_fusion, f32[128,128]{1,0:T(8,128)} %get-tuple-element.17, f32[128,128]{1,0:T(8,128)} %get-tuple-element.16), kind=kLoop, calls=%fused_computation.16 | loop fusion | flops 81920 | bytes 393344 | tf_op jit(solution)/shard_map/jit(_where)/select_n | solution.py:229
  (36 shorter events, 3.2 us)
Async XLA Ops:
  0.6 26.9 %copy-start = (bf16[320,320]{0,1:T(8,128)(2,1)S(1)}, bf16[320,320]{0,1:T(8,128)(2,1)}, u32[]{:S(2)}) copy-start(bf16[320,320]{0,1:T(8,128)(2,1)} %constant.42.clone) | copy-start | bytes 614404
  0.6 22.1 %copy-start.4 = (bf16[128,128]{1,0:T(8,128)(2,1)S(1)}, bf16[128,128]{1,0:T(8,128)(2,1)}, u32[]{:S(2)}) copy-start(bf16[128,128]{1,0:T(8,128)(2,1)} %param.7) | copy-start | bytes 98308
  3.2 9.4 %collective-permute-start = (bf16[264,192]{1,0:T(8,128)(2,1)S(1)}, bf16[264,192]{1,0:T(8,128)(2,1)S(1)}, u32[]{:S(2)}, u32[]{:S(2)}) collective-permute-start(bf16[264,192]{1,0:T(8,128)(2,1)S(1)} %pad_maximum_fusion.7), channel_id=1, source_target_pairs={{0,2},{4,6},{8,10},{12,14},{2,0},{6,4},{10,8},{14,12},{1,3},{5,7},... | collective-permute-start | bytes 304136 | tf_op jit(solution)/shard_map/ppermute | solution.py:62
  6.2 21.7 %copy-start.1 = (bf16[320,320]{0,1:T(8,128)(2,1)S(1)}, bf16[320,320]{0,1:T(8,128)(2,1)}, u32[]{:S(2)}) copy-start(bf16[320,320]{0,1:T(8,128)(2,1)} %constant.41.clone) | copy-start | bytes 614404
  12.7 10.0 %collective-permute-start.1 = (bf16[464,192]{1,0:T(8,128)(2,1)S(1)}, bf16[464,192]{1,0:T(8,128)(2,1)S(1)}, u32[]{:S(2)}, u32[]{:S(2)}) collective-permute-start(bf16[464,192]{1,0:T(8,128)(2,1)S(1)} %pad_maximum_fusion.3), channel_id=1, source_target_pairs={{2,4},{6,8},{10,12},{0,14},{4,2},{8,6},{12,10},{14,0},{3,5},{7,9},... | collective-permute-start | bytes 534536 | tf_op jit(solution)/shard_map/ppermute | solution.py:62
  23.0 4.3 %collective-permute-start.3 = (bf16[320,96]{1,0:T(8,128)(2,1)S(1)}, bf16[320,96]{1,0:T(8,128)(2,1)S(1)}, u32[]{:S(2)}, u32[]{:S(2)}) collective-permute-start(bf16[320,96]{1,0:T(8,128)(2,1)S(1)} %get-tuple-element.33), channel_id=1, source_target_pairs={{0,1},{2,3},{4,5},{6,7},{8,9},{10,11},{12,13},{14,15},{16,17},{18,... | collective-permute-start | bytes 184328 | tf_op jit(solution)/shard_map/ppermute | solution.py:22
  24.3 3.2 %collective-permute-start.4 = (bf16[320,96]{1,0:T(8,128)(2,1)S(1)}, bf16[320,96]{1,0:T(8,128)(2,1)S(1)}, u32[]{:S(2)}, u32[]{:S(2)}) collective-permute-start(bf16[320,96]{1,0:T(8,128)(2,1)S(1)} %get-tuple-element.34), channel_id=1, source_target_pairs={{1,0},{3,2},{5,4},{7,6},{9,8},{11,10},{13,12},{15,14},{17,16},{19,... | collective-permute-start | bytes 184328 | tf_op jit(solution)/shard_map/ppermute | solution.py:25
  25.7 7.2 %copy-start.2 = (bf16[800,192]{1,0:T(8,128)(2,1)}, bf16[800,192]{1,0:T(8,128)(2,1)S(1)}, u32[]{:S(2)}) copy-start(bf16[800,192]{1,0:T(8,128)(2,1)S(1)} %pad_maximum_fusion) | copy-start | bytes 921604
  25.7 21.3 %collective-permute-start.2 = (bf16[800,192]{1,0:T(8,128)(2,1)S(1)}, bf16[800,192]{1,0:T(8,128)(2,1)S(1)}, u32[]{:S(2)}, u32[]{:S(2)}) collective-permute-start(bf16[800,192]{1,0:T(8,128)(2,1)S(1)} %pad_maximum_fusion), channel_id=1, source_target_pairs={{0,8},{14,6},{2,10},{4,12},{8,0},{6,14},{10,2},{12,4},{1,9},{15,7}... | collective-permute-start | bytes 921608 | tf_op jit(solution)/shard_map/ppermute | solution.py:62
  47.0 0.8 %copy-start.3 = (bf16[800,192]{1,0:T(8,128)(2,1)}, bf16[800,192]{1,0:T(8,128)(2,1)S(1)}, u32[]{:S(2)}) copy-start(bf16[800,192]{1,0:T(8,128)(2,1)S(1)} %collective-permute-done.2) | copy-start | bytes 921604

commit v9 on v8

--- a/solution.py
+++ b/solution.py
@@ -82,11 +82,16 @@
     second, rows_two = send(held, jnp.where(odd, low_rows, high_rows), second_pairs)
     held = jnp.concatenate([held, second], axis=0)
     third_pairs = [(0, size // 2), (size - 1, size // 2 - 1), (1, size // 2 + 1), (2, size // 2 + 2)]
-    third = swap(held, third_pairs)
+    cores = lax.axis_size("tile")
+    share = held.shape[0] // cores
+    core = lax.axis_index("tile")
+    mine = lax.dynamic_slice_in_dim(held, core * share, share, 0)
+    third = swap(mine, third_pairs)
+    arrivals = [held, third]
     zero = jnp.zeros_like(rows_one)
     top = jnp.where(odd, rows_one, jnp.where(index == 0, zero, rows_two))
     bottom = jnp.where(odd, jnp.where(index == size - 1, zero, rows_two), rows_one)
-    return [held, third], jnp.concatenate([top, tile, bottom], axis=0)
+    return arrivals, jnp.concatenate([top, tile, bottom], axis=0)
 
 
 def correlate_kernel(ids_ref, tmpl_ref, ctf_ref, spec_r_ref, spec_i_ref, cos_rows_ref, sin_rows_ref,
@@ -191,7 +196,9 @@
     id_rows = jnp.broadcast_to(defocus.astype(bf16)[:, None, None], (local_count, 8, box_size))
     block_rows = box_size + 8
     packed = jnp.concatenate([templates, id_rows], axis=1).reshape(local_count * block_rows, box_size)
-    if lax.axis_size("orient") == 8 and local_count == 1 and (margin * tile_width) % box_size == 0:
+    split_last = lax.axis_size("orient") == 8 and lax.axis_size("tile") == 2
+    split_last = split_last and local_count == 1 and (margin * tile_width) % box_size == 0
+    if split_last:
         arrivals, row_padded = exchange_with_rows(packed, micrograph, margin)
         padded = extended(row_padded, (("tile", 1),), margin)
     else:
@@ -214,11 +221,22 @@
     )
     shape = (tile_width, tile_width)
     stats = (jnp.full(shape, -jnp.inf, f32), jnp.zeros(shape, f32), jnp.zeros(shape, f32))
-    for piece in arrivals:
+    def run(piece, stats):
         count = piece.shape[0] // block_rows
         piece = piece.reshape(count, block_rows, box_size)
         piece_ids = piece[:, box_size, 0].astype(jnp.int32)
-        stats = correlate(piece_ids, piece, ctf, spec_real, spec_imag, tables, scaling, stats)
+        return correlate(piece_ids, piece, ctf, spec_real, spec_imag, tables, scaling, stats)
+
+    if split_last:
+        stats = run(arrivals[0], stats)
+        half, stats = lax.optimization_barrier((arrivals[1], stats))
+        other_half = lax.ppermute(half, "tile", [(0, 1), (1, 0)])
+        stats = run(half, stats)
+        stats = run(other_half, stats)
+        total = (arrivals[0].shape[0] + 2 * half.shape[0]) // block_rows
+    else:
+        for piece in arrivals:
+            stats = run(piece, stats)
     peak_map, sum_map, squares = stats
 
     live = usable[0, 0]

time: 58.4 us -> 54.6 us (0.935)
  waiting for transfers between devices: 11.3 us -> 1.59 us
  Pallas kernels: 17.1 us -> 20 us
  starting transfers between devices: 10.1 us -> 12 us
  other arithmetic: 5.07 us -> 5.74 us
    ppermute x3, waiting for transfers between devices: 11.1 us -> 1.36 us  [swap(): lax.ppermute(payload, 'orient', [(a, b) for a, b in pairs] + [(b, a) for...]
    pallas_call x2 -> x3, Pallas kernels: 17.1 us -> 20 us  [correlate(): pl.pallas_call(functools.partial(correlate_kernel, scaling=scaling), grid...]
    ppermute x3, starting transfers between devices: 7.5 us -> 8.7 us  [swap(): lax.ppermute(payload, 'orient', [(a, b) for a, b in pairs] + [(b, a) for...]
    ppermute x0 -> x1, starting transfers between devices: none -> 0.69 us  [body(): other_half = lax.ppermute(half, 'tile', [(0, 1), (1, 0)])]
    convert_element_type x2 -> x3, other arithmetic: 1.41 us -> 2.06 us  [run(): piece_ids = piece[:, box_size, 0].astype(jnp.int32)]
  transfers between devices with their start and end apart: 5 -> 6, of which waited for: 3 -> 3; matrix products, arithmetic and copies ran while one was open for 22% -> 25% of each run, Pallas kernels for 15% -> 27%
where the time goes in v9:
time: 54.6 us; the launch traced here: 53.7 us
  Pallas kernels  20 us (37%)
  starting transfers between devices  12 us (22%)
  local copies, waits for them, and re-layouts  8.75 us (16%)
  other arithmetic  5.74 us (11%)
  matrix products  3.51 us (6%)
  between operations  2.19 us (4%)
  waiting for transfers between devices  1.59 us (3%)
    pallas_call x3, Pallas kernels, correlate(): pl.pallas_call(functools.partial(correlate_kernel, scaling=scaling), grid...  20 us
    ppermute x3, starting transfers between devices, swap(): lax.ppermute(payload, 'orient', [(a, b) for a, b in pairs] + [(b, a) for...  8.7 us
    dot_general x6, matrix products, matmul(): return jnp.dot(left, right, preferred_element_type=jnp.float32)  3.51 us
    convert_element_type x3, other arithmetic, run(): piece_ids = piece[:, box_size, 0].astype(jnp.int32)  2.06 us
    transpose x1, local copies, waits for them, and re-layouts, body(): col_sin = row_sin.T  1.81 us
    select_n x1, other arithmetic, body(): square_out = jnp.where(row_mask, squares / orient_count, 0.0)  1.66 us
    ppermute x3, waiting for transfers between devices, swap(): lax.ppermute(payload, 'orient', [(a, b) for a, b in pairs] + [(b, a) for...  1.36 us
    ppermute x1, starting transfers between devices, extended(): lax.ppermute(lax.slice_in_dim(block, block.shape[dim] - width, None, axis...  1.29 us
  transfers between devices with their start and end apart: 6, of which 3 were waited for; matrix products, arithmetic and copies ran while one was open for 25% of the time, Pallas kernels for 27%

profile of v9, /device:TPU:0, one launch (start us, length us, event | category | flops | bytes accessed | tf_op | source)
XLA Modules:
  0.0 53.7 jit_solution(3337611632583717972)
XLA Ops:
  0.7 0.9 %broadcast_select_fusion.2 = (bf16[96,128]{1,0:T(8,128)(2,1)S(1)}, bf16[96,128]{1,0:T(8,128)(2,1)S(1)}) fusion(pred[]{:T(512)S(6)} %eq.11, bf16[128,128]{1,0:T(8,128)(2,1)} %param.7), kind=kLoop, calls=%fused_computation.22 | loop fusion | flops 24576 | bytes 98305 | tf_op jit(solution)/shard_map/jit(_where)/select_n | solution.py:79
  2.3 0.9 %pad_bitcast_fusion = bf16[200,192]{1,0:T(8,128)(2,1)S(1)} fusion(bf16[1,192,192]{2,1,0:T(8,128)(2,1)} %param.8, bf16[]{:T(256)} %bitcast.1), kind=kLoop, calls=%fused_computation.15 | loop fusion | bytes 150530 | tf_op jit(solution)/shard_map/reshape | solution.py:198
  3.2 3.0 %collective-permute-start = (bf16[264,192]{1,0:T(8,128)(2,1)S(1)}, bf16[264,192]{1,0:T(8,128)(2,1)S(1)}, u32[]{:S(2)}, u32[]{:S(2)}) collective-permute-start(bf16[264,192]{1,0:T(8,128)(2,1)S(1)} %pad_maximum_fusion.7), channel_id=1, source_target_pairs={{0,2},{4,6},{8,10},{12,14},{2,0},{6,4},{10,8},{14,12},{1,3},{5,7},... | collective-permute-start | bytes 304136 | tf_op jit(solution)/shard_map/ppermute | solution.py:62
  6.2 1.2 %fusion.10 = (bf16[96,320]{0,1:T(8,128)(2,1)S(1)}, bf16[96,320]{0,1:T(8,128)(2,1)S(1)}, bf16[96,320]{0,1:T(8,128)(2,1)S(1)}, bf16[96,320]{0,1:T(8,128)(2,1)S(1)}) fusion(bf16[320,320]{0,1:T(8,128)(2,1)} %constant.48.clone, bf16[320,320]{0,1:T(8,128)(2,1)} %constant.47.clone), kind=kLoop, calls=%fused_computation.40 | loop fusion | bytes 491520 | tf_op jit(solution)/shard_map/slice | solution.py:187
  7.4 1.8 %slice_bitcast_fusion = (bf16[320,128]{1,0:T(8,128)(2,1)}, bf16[128,320]{0,1:T(8,128)(2,1)S(1)}, bf16[128,320]{0,1:T(8,128)(2,1)S(1)}, bf16[320,128]{1,0:T(8,128)(2,1)}) fusion(bf16[320,320]{0,1:T(8,128)(2,1)} %constant.48.clone, bf16[320,320]{0,1:T(8,128)(2,1)} %constant.47.clone), kind=kLoop, calls=%fused_computation.36 | loop fusion | bytes 491520 | tf_op jit(solution)/shard_map/transpose | solution.py:193
  9.9 4.8 %collective-permute-start.1 = (bf16[464,192]{1,0:T(8,128)(2,1)S(1)}, bf16[464,192]{1,0:T(8,128)(2,1)S(1)}, u32[]{:S(2)}, u32[]{:S(2)}) collective-permute-start(bf16[464,192]{1,0:T(8,128)(2,1)S(1)} %pad_maximum_fusion.3), channel_id=1, source_target_pairs={{2,4},{6,8},{10,12},{0,14},{4,2},{8,6},{12,10},{14,0},{3,5},{7,9},... | collective-permute-start | bytes 534536 | tf_op jit(solution)/shard_map/ppermute | solution.py:62
  14.7 0.8 %copy.28.cos_rows_ref = bf16[192,320]{1,0:T(8,128)(2,1)} copy(bf16[192,320]{0,1:T(8,128)(2,1)S(1)} %get-tuple-element.44) | data formatting | bytes 245760 | tf_op jit(solution)/shard_map/concatenate | solution.py:186
  15.5 0.8 %copy.29.sin_rows_ref = bf16[192,320]{1,0:T(8,128)(2,1)} copy(bf16[192,320]{0,1:T(8,128)(2,1)S(1)} %get-tuple-element.46) | data formatting | bytes 245760 | tf_op jit(solution)/shard_map/concatenate | solution.py:187
  16.3 0.8 %copy.30.rows_ref = bf16[256,320]{1,0:T(8,128)(2,1)} copy(bf16[256,320]{0,1:T(8,128)(2,1)S(1)} %pad_maximum_fusion.6) | data formatting | bytes 327680 | tf_op jit(solution)/shard_map/concatenate | solution.py:218
  17.7 0.8 %pad_maximum_fusion.1.cols_ref = bf16[640,192]{1,0:T(8,128)(2,1)} fusion(bf16[320,192]{1,0:T(8,128)(2,1)S(1)} %get-tuple-element.45, bf16[320,192]{1,0:T(8,128)(2,1)S(1)} %get-tuple-element.43), kind=kLoop, calls=%fused_computation.8 | loop fusion | flops 491520 | bytes 491520 | tf_op jit(solution)/shard_map/concatenate | solution.py:217
  18.5 1.1 %collective-permute-done.1 = bf16[464,192]{1,0:T(8,128)(2,1)S(1)} collective-permute-done((bf16[464,192]{1,0:T(8,128)(2,1)S(1)}, bf16[464,192]{1,0:T(8,128)(2,1)S(1)}, u32[]{:S(2)}, u32[]{:S(2)}) %collective-permute-start.1) | collective-permute-done | bytes 178208 | tf_op jit(solution)/shard_map/ppermute | solution.py:62
  20.0 1.3 %collective-permute-start.3 = (bf16[320,96]{1,0:T(8,128)(2,1)S(1)}, bf16[320,96]{1,0:T(8,128)(2,1)S(1)}, u32[]{:S(2)}, u32[]{:S(2)}) collective-permute-start(bf16[320,96]{1,0:T(8,128)(2,1)S(1)} %get-tuple-element.47), channel_id=1, source_target_pairs={{0,1},{2,3},{4,5},{6,7},{8,9},{10,11},{12,13},{14,15},{16,17},{18,... | collective-permute-start | bytes 184328 | tf_op jit(solution)/shard_map/ppermute | solution.py:22
  21.3 1.3 %collective-permute-start.4 = (bf16[320,96]{1,0:T(8,128)(2,1)S(1)}, bf16[320,96]{1,0:T(8,128)(2,1)S(1)}, u32[]{:S(2)}, u32[]{:S(2)}) collective-permute-start(bf16[320,96]{1,0:T(8,128)(2,1)S(1)} %get-tuple-element.48), channel_id=1, source_target_pairs={{1,0},{3,2},{5,4},{7,6},{9,8},{11,10},{13,12},{15,14},{17,16},{19,... | collective-permute-start | bytes 184328 | tf_op jit(solution)/shard_map/ppermute | solution.py:25
  22.8 0.9 %collective-permute-start.2 = (bf16[400,192]{1,0:T(8,128)(2,1)S(1)}, bf16[400,192]{1,0:T(8,128)(2,1)S(1)}, u32[]{:S(2)}, u32[]{:S(2)}) collective-permute-start(bf16[400,192]{1,0:T(8,128)(2,1)S(1)} %constant_dynamic-slice_fusion), channel_id=1, source_target_pairs={{0,8},{14,6},{2,10},{4,12},{8,0},{6,14},{10,2},{12,4},{1,9},{15,7}... | collective-permute-start | bytes 460808 | tf_op jit(solution)/shard_map/ppermute | solution.py:62
  23.6 0.6 %fusion.3.ids_ref = s32[4]{0:T(128)} fusion(bf16[4,200,192]{2,1,0:T(8,128)(2,1)S(1)} %bitcast.25), kind=kLoop, calls=%fused_computation.27 | loop fusion | flops 4 | bytes 24 | tf_op jit(solution)/shard_map/convert_element_type | solution.py:227
  26.0 1.1 %fusion.2.spec_i_ref = bf16[320,320]{1,0:T(8,128)(2,1)} fusion(f32[320,320]{1,0:T(8,128)S(1)} %fusion.14, bf16[320,320]{0,1:T(8,128)(2,1)S(1)} %copy-done.1, bf16[320,320]{1,0:T(8,128)(2,1)S(1)} %convolution_convert_fusion), kind=kOutput, calls=%fused_computation.6 | convolution fusion | flops 65740800 | bytes 1024000 | tf_op jit(solution)/shard_map/dot_general | solution.py:41
  27.0 1.0 %fusion.1.spec_r_ref = bf16[320,320]{1,0:T(8,128)(2,1)} fusion(f32[320,320]{1,0:T(8,128)S(1)} %fusion.13, bf16[320,320]{0,1:T(8,128)(2,1)S(1)} %copy-done.1, bf16[320,320]{1,0:T(8,128)(2,1)S(1)} %fusion), kind=kOutput, calls=%fused_computation.5 | convolution fusion | flops 65740800 | bytes 1024000 | tf_op jit(solution)/shard_map/dot_general | solution.py:41
  30.0 8.5 %shard_map.94 = (f32[128,128]{1,0:T(8,128)}, f32[128,128]{1,0:T(8,128)}, f32[128,128]{1,0:T(8,128)}) custom-call(s32[4]{0:T(128)} %fusion.3.ids_ref, bf16[4,200,192]{2,1,0:T(8,128)(2,1)} %bitcast.26, f32[8,320,320]{2,1,0:T(8,128)} %ctf_ref.5, bf16[320,320]{1,0:T(8,128)(2,1)} %fusion.1.spec_r_ref, ...), custom_call_target="tpu_custom_call", output_to_operand_aliasing={{0}: (11, {}), {1}: (12, {}), {2}: (13, {})} | custom-call | tf_op jit(solution)/shard_map/pallas_call | solution.py:164
  38.5 0.7 %collective-permute-start.5 = (bf16[400,192]{1,0:T(8,128)(2,1)S(1)}, bf16[400,192]{1,0:T(8,128)(2,1)S(1)}, u32[]{:S(2)}, u32[]{:S(2)}) collective-permute-start(bf16[400,192]{1,0:T(8,128)(2,1)S(1)} %collective-permute-done.2), channel_id=1, source_target_pairs={{0,1},{1,0},{2,3},{3,2},{4,5},{5,4},{6,7},{7,6},{8,9},{9,8},{10,11... | collective-permute-start | bytes 460808 | tf_op jit(solution)/shard_map/ppermute | solution.py:233
  39.2 0.7 %fusion.4.ids_ref = s32[2]{0:T(128)} fusion(bf16[2,200,192]{2,1,0:T(8,128)(2,1)S(1)} %bitcast.27), kind=kLoop, calls=%fused_computation.29 | loop fusion | flops 2 | bytes 12 | tf_op jit(solution)/shard_map/convert_element_type | solution.py:227
  39.9 5.7 %shard_map.95 = (f32[128,128]{1,0:T(8,128)}, f32[128,128]{1,0:T(8,128)}, f32[128,128]{1,0:T(8,128)}) custom-call(s32[2]{0:T(128)} %fusion.4.ids_ref, bf16[2,200,192]{2,1,0:T(8,128)(2,1)} %bitcast.28, f32[8,320,320]{2,1,0:T(8,128)} %ctf_ref.5, bf16[320,320]{1,0:T(8,128)(2,1)} %fusion.1.spec_r_ref, ...), custom_call_target="tpu_custom_call", output_to_operand_aliasing={{0}: (11, {}), {1}: (12, {}), {2}: (13, {})} | custom-call | tf_op jit(solution)/shard_map/pallas_call | solution.py:164
  45.7 0.7 %fusion.5.ids_ref = s32[2]{0:T(128)} fusion(bf16[2,200,192]{2,1,0:T(8,128)(2,1)S(1)} %bitcast.29), kind=kLoop, calls=%fused_computation.31 | loop fusion | flops 2 | bytes 12 | tf_op jit(solution)/shard_map/convert_element_type | solution.py:227
  46.4 5.7 %shard_map.96 = (f32[128,128]{1,0:T(8,128)}, f32[128,128]{1,0:T(8,128)}, f32[128,128]{1,0:T(8,128)}) custom-call(s32[2]{0:T(128)} %fusion.5.ids_ref, bf16[2,200,192]{2,1,0:T(8,128)(2,1)} %bitcast.30, f32[8,320,320]{2,1,0:T(8,128)} %ctf_ref.5, bf16[320,320]{1,0:T(8,128)(2,1)} %fusion.1.spec_r_ref, ...), custom_call_target="tpu_custom_call", output_to_operand_aliasing={{0}: (11, {}), {1}: (12, {}), {2}: (13, {})} | custom-call | tf_op jit(solution)/shard_map/pallas_call | solution.py:164
  52.1 1.7 %multiply_select_fusion = (f32[128,128]{1,0:T(8,128)}, f32[128,128]{1,0:T(8,128)}, f32[128,128]{1,0:T(8,128)}) fusion(f32[128,128]{1,0:T(8,128)} %get-tuple-element.32, pred[128]{0:T(512)(128)(4,1)S(1)} %iota_compare_fusion, f32[128,128]{1,0:T(8,128)} %get-tuple-element.31, f32[128,128]{1,0:T(8,128)} %get-tuple-element.30), kind=kLoop, calls=%fused_computation.16 | loop fusion | flops 81920 | bytes 393344 | tf_op jit(solution)/shard_map/jit(_where)/select_n | solution.py:247
  (43 shorter events, 4.8 us)
Async XLA Ops:
  0.6 19.2 %copy-start.3 = (bf16[128,128]{1,0:T(8,128)(2,1)S(1)}, bf16[128,128]{1,0:T(8,128)(2,1)}, u32[]{:S(2)}) copy-start(bf16[128,128]{1,0:T(8,128)(2,1)} %param.7) | copy-start | bytes 98308
  0.7 23.8 %copy-start.1 = (bf16[320,320]{0,1:T(8,128)(2,1)S(1)}, bf16[320,320]{0,1:T(8,128)(2,1)}, u32[]{:S(2)}) copy-start(bf16[320,320]{0,1:T(8,128)(2,1)} %constant.48.clone) | copy-start | bytes 614404
  3.2 6.6 %collective-permute-start = (bf16[264,192]{1,0:T(8,128)(2,1)S(1)}, bf16[264,192]{1,0:T(8,128)(2,1)S(1)}, u32[]{:S(2)}, u32[]{:S(2)}) collective-permute-start(bf16[264,192]{1,0:T(8,128)(2,1)S(1)} %pad_maximum_fusion.7), channel_id=1, source_target_pairs={{0,2},{4,6},{8,10},{12,14},{2,0},{6,4},{10,8},{14,12},{1,3},{5,7},... | collective-permute-start | bytes 304136 | tf_op jit(solution)/shard_map/ppermute | solution.py:62
  7.4 17.5 %copy-start.2 = (bf16[320,320]{0,1:T(8,128)(2,1)S(1)}, bf16[320,320]{0,1:T(8,128)(2,1)}, u32[]{:S(2)}) copy-start(bf16[320,320]{0,1:T(8,128)(2,1)} %constant.47.clone) | copy-start | bytes 614404
  9.9 9.8 %collective-permute-start.1 = (bf16[464,192]{1,0:T(8,128)(2,1)S(1)}, bf16[464,192]{1,0:T(8,128)(2,1)S(1)}, u32[]{:S(2)}, u32[]{:S(2)}) collective-permute-start(bf16[464,192]{1,0:T(8,128)(2,1)S(1)} %pad_maximum_fusion.3), channel_id=1, source_target_pairs={{2,4},{6,8},{10,12},{0,14},{4,2},{8,6},{12,10},{14,0},{3,5},{7,9},... | collective-permute-start | bytes 534536 | tf_op jit(solution)/shard_map/ppermute | solution.py:62
  20.0 4.2 %collective-permute-start.3 = (bf16[320,96]{1,0:T(8,128)(2,1)S(1)}, bf16[320,96]{1,0:T(8,128)(2,1)S(1)}, u32[]{:S(2)}, u32[]{:S(2)}) collective-permute-start(bf16[320,96]{1,0:T(8,128)(2,1)S(1)} %get-tuple-element.47), channel_id=1, source_target_pairs={{0,1},{2,3},{4,5},{6,7},{8,9},{10,11},{12,13},{14,15},{16,17},{18,... | collective-permute-start | bytes 184328 | tf_op jit(solution)/shard_map/ppermute | solution.py:22
  21.3 3.2 %collective-permute-start.4 = (bf16[320,96]{1,0:T(8,128)(2,1)S(1)}, bf16[320,96]{1,0:T(8,128)(2,1)S(1)}, u32[]{:S(2)}, u32[]{:S(2)}) collective-permute-start(bf16[320,96]{1,0:T(8,128)(2,1)S(1)} %get-tuple-element.48), channel_id=1, source_target_pairs={{1,0},{3,2},{5,4},{7,6},{9,8},{11,10},{13,12},{15,14},{17,16},{19,... | collective-permute-start | bytes 184328 | tf_op jit(solution)/shard_map/ppermute | solution.py:25
  22.7 7.2 %copy-start = (bf16[800,192]{1,0:T(8,128)(2,1)}, bf16[800,192]{1,0:T(8,128)(2,1)S(1)}, u32[]{:S(2)}) copy-start(bf16[800,192]{1,0:T(8,128)(2,1)S(1)} %pad_maximum_fusion) | copy-start | bytes 921604
  22.8 15.7 %collective-permute-start.2 = (bf16[400,192]{1,0:T(8,128)(2,1)S(1)}, bf16[400,192]{1,0:T(8,128)(2,1)S(1)}, u32[]{:S(2)}, u32[]{:S(2)}) collective-permute-start(bf16[400,192]{1,0:T(8,128)(2,1)S(1)} %constant_dynamic-slice_fusion), channel_id=1, source_target_pairs={{0,8},{14,6},{2,10},{4,12},{8,0},{6,14},{10,2},{12,4},{1,9},{15,7}... | collective-permute-start | bytes 460808 | tf_op jit(solution)/shard_map/ppermute | solution.py:62
  38.5 1.4 %copy-start.4 = (bf16[400,192]{1,0:T(8,128)(2,1)}, bf16[400,192]{1,0:T(8,128)(2,1)S(1)}, u32[]{:S(2)}) copy-start(bf16[400,192]{1,0:T(8,128)(2,1)S(1)} %collective-permute-done.2) | copy-start | bytes 460804
  38.5 7.1 %collective-permute-start.5 = (bf16[400,192]{1,0:T(8,128)(2,1)S(1)}, bf16[400,192]{1,0:T(8,128)(2,1)S(1)}, u32[]{:S(2)}, u32[]{:S(2)}) collective-permute-start(bf16[400,192]{1,0:T(8,128)(2,1)S(1)} %collective-permute-done.2), channel_id=1, source_target_pairs={{0,1},{1,0},{2,3},{3,2},{4,5},{5,4},{6,7},{7,6},{8,9},{9,8},{10,11... | collective-permute-start | bytes 460808 | tf_op jit(solution)/shard_map/ppermute | solution.py:233
  45.6 0.7 %copy-start.5 = (bf16[400,192]{1,0:T(8,128)(2,1)}, bf16[400,192]{1,0:T(8,128)(2,1)S(1)}, u32[]{:S(2)}) copy-start(bf16[400,192]{1,0:T(8,128)(2,1)S(1)} %collective-permute-done.5) | copy-start | bytes 460804

commit v10 on v9

--- a/solution.py
+++ b/solution.py
@@ -95,8 +95,11 @@
 
 
 def correlate_kernel(ids_ref, tmpl_ref, ctf_ref, spec_r_ref, spec_i_ref, cos_rows_ref, sin_rows_ref,
-                     cols_ref, rows_ref, col_cos_ref, col_sin_ref,
-                     prev_peak_ref, prev_sum_ref, prev_sq_ref, peak_ref, sum_ref, sq_ref, *, scaling):
+                     cols_ref, rows_ref, col_cos_ref, col_sin_ref, *refs, scaling):
+    if len(refs) == 6:
+        prev_peak_ref, prev_sum_ref, prev_sq_ref, peak_ref, sum_ref, sq_ref = refs
+    else:
+        peak_ref, sum_ref, sq_ref = refs
     bf16 = jnp.bfloat16
     f32 = jnp.float32
     o = pl.program_id(0)
@@ -130,9 +133,14 @@
 
     @pl.when(o == 0)
     def _():
-        peak_ref[...] = jnp.maximum(prev_peak_ref[...], corr)
-        sum_ref[...] = prev_sum_ref[...] + corr
-        sq_ref[...] = prev_sq_ref[...] + corr * corr
+        if len(refs) == 6:
+            peak_ref[...] = jnp.maximum(prev_peak_ref[...], corr)
+            sum_ref[...] = prev_sum_ref[...] + corr
+            sq_ref[...] = prev_sq_ref[...] + corr * corr
+        else:
+            peak_ref[...] = corr
+            sum_ref[...] = corr
+            sq_ref[...] = corr * corr
 
     @pl.when(o > 0)
     def _():
@@ -152,7 +160,7 @@
         pl.BlockSpec((1, n, n), lambda o, ids: (ids[o], 0, 0)),
         full((n, n)),
         full((n, n)),
-    ] + [full(t.shape) for t in tables] + [full((tile, tile))] * 3
+    ] + [full(t.shape) for t in tables] + [full((tile, tile))] * len(previous)
     out_block = full((tile, tile))
     grid_spec = pltpu.PrefetchScalarGridSpec(
         num_scalar_prefetch=1,
@@ -166,7 +174,7 @@
         grid_spec=grid_spec,
         out_shape=out_shape,
         compiler_params=pltpu.CompilerParams(dimension_semantics=("arbitrary",)),
-        input_output_aliases={5 + len(tables): 0, 6 + len(tables): 1, 7 + len(tables): 2},
+        input_output_aliases={5 + len(tables) + i: i for i in range(len(previous))},
     )(ids, all_templates, ctf, spec_real, spec_imag, *tables, *previous)
 
 
@@ -220,7 +228,7 @@
         col_sin,
     )
     shape = (tile_width, tile_width)
-    stats = (jnp.full(shape, -jnp.inf, f32), jnp.zeros(shape, f32), jnp.zeros(shape, f32))
+    stats = ()
     def run(piece, stats):
         count = piece.shape[0] // block_rows
         piece = piece.reshape(count, block_rows, box_size)
@@ -231,8 +239,7 @@
         stats = run(arrivals[0], stats)
         half, stats = lax.optimization_barrier((arrivals[1], stats))
         other_half = lax.ppermute(half, "tile", [(0, 1), (1, 0)])
-        stats = run(half, stats)
-        stats = run(other_half, stats)
+        stats = run(jnp.concatenate([half, other_half], axis=0), stats)
         total = (arrivals[0].shape[0] + 2 * half.shape[0]) // block_rows
     else:
         for piece in arrivals:

time: 54.6 us -> 50.5 us (0.925)
  the two profiles are of different devices: /device:TPU:0 before, /device:TPU:11 now
where the time goes in v10:
time: 50.5 us; the launch traced here: 50.1 us
  Pallas kernels  17 us (34%)
  starting transfers between devices  11.7 us (23%)
  local copies, waits for them, and re-layouts  6.96 us (14%)
  other arithmetic  5.04 us (10%)
  waiting for transfers between devices  3.7 us (7%)
  matrix products  3.52 us (7%)
  between operations  2.19 us (4%)
    pallas_call x2, Pallas kernels, correlate(): pl.pallas_call(functools.partial(correlate_kernel, scaling=scaling), grid...  17 us
    ppermute x3, starting transfers between devices, swap(): lax.ppermute(payload, 'orient', [(a, b) for a, b in pairs] + [(b, a) for...  5.95 us
    ppermute x1, starting transfers between devices, extended(): lax.ppermute(lax.slice_in_dim(block, 0, width, axis=dim), axis, backward)  4.38 us
    dot_general x6, matrix products, matmul(): return jnp.dot(left, right, preferred_element_type=jnp.float32)  3.52 us
    ppermute x3, waiting for transfers between devices, swap(): lax.ppermute(payload, 'orient', [(a, b) for a, b in pairs] + [(b, a) for...  2.92 us
    transpose x1, local copies, waits for them, and re-layouts, body(): col_sin = row_sin.T  1.81 us
    select_n x1, other arithmetic, body(): square_out = jnp.where(row_mask, squares / orient_count, 0.0)  1.66 us
    convert_element_type x2, other arithmetic, run(): piece_ids = piece[:, box_size, 0].astype(jnp.int32)  1.3 us
  transfers between devices with their start and end apart: 6, of which 3 were waited for; matrix products, arithmetic and copies ran while one was open for 21% of the time, Pallas kernels for 17%

profile of v10, /device:TPU:11, one launch (start us, length us, event | category | flops | bytes accessed | tf_op | source)
XLA Modules:
  0.0 50.1 jit_solution(16454476148076834778)
XLA Ops:
  0.7 0.9 %broadcast_select_fusion.2 = (bf16[96,128]{1,0:T(8,128)(2,1)S(1)}, bf16[96,128]{1,0:T(8,128)(2,1)S(1)}) fusion(pred[]{:T(512)S(6)} %eq.11, bf16[128,128]{1,0:T(8,128)(2,1)} %param.7), kind=kLoop, calls=%fused_computation.23 | loop fusion | flops 24576 | bytes 98305 | tf_op jit(solution)/shard_map/jit(_where)/select_n | solution.py:79
  2.3 0.9 %pad_bitcast_fusion = bf16[200,192]{1,0:T(8,128)(2,1)S(1)} fusion(bf16[1,192,192]{2,1,0:T(8,128)(2,1)} %param.8, bf16[]{:T(256)} %bitcast.1), kind=kLoop, calls=%fused_computation.16 | loop fusion | bytes 150530 | tf_op jit(solution)/shard_map/reshape | solution.py:206
  3.5 1.2 %fusion.9 = (bf16[96,320]{0,1:T(8,128)(2,1)S(1)}, bf16[96,320]{0,1:T(8,128)(2,1)S(1)}, bf16[96,320]{0,1:T(8,128)(2,1)S(1)}, bf16[96,320]{0,1:T(8,128)(2,1)S(1)}) fusion(bf16[320,320]{0,1:T(8,128)(2,1)} %constant.45.clone, bf16[320,320]{0,1:T(8,128)(2,1)} %constant.44.clone), kind=kLoop, calls=%fused_computation.39 | loop fusion | bytes 491520 | tf_op jit(solution)/shard_map/slice | solution.py:195
  4.7 1.8 %slice_bitcast_fusion = (bf16[320,128]{1,0:T(8,128)(2,1)}, bf16[128,320]{0,1:T(8,128)(2,1)S(1)}, bf16[128,320]{0,1:T(8,128)(2,1)S(1)}, bf16[320,128]{1,0:T(8,128)(2,1)}) fusion(bf16[320,320]{0,1:T(8,128)(2,1)} %constant.45.clone, bf16[320,320]{0,1:T(8,128)(2,1)} %constant.44.clone), kind=kLoop, calls=%fused_computation.35 | loop fusion | bytes 491520 | tf_op jit(solution)/shard_map/transpose | solution.py:201
  6.9 0.8 %collective-permute-done = bf16[264,192]{1,0:T(8,128)(2,1)S(1)} collective-permute-done((bf16[264,192]{1,0:T(8,128)(2,1)S(1)}, bf16[264,192]{1,0:T(8,128)(2,1)S(1)}, u32[]{:S(2)}, u32[]{:S(2)}) %collective-permute-start) | collective-permute-done | bytes 101408 | tf_op jit(solution)/shard_map/ppermute | solution.py:62
  7.8 1.5 %collective-permute-start.1 = (bf16[464,192]{1,0:T(8,128)(2,1)S(1)}, bf16[464,192]{1,0:T(8,128)(2,1)S(1)}, u32[]{:S(2)}, u32[]{:S(2)}) collective-permute-start(bf16[464,192]{1,0:T(8,128)(2,1)S(1)} %pad_maximum_fusion.4), channel_id=1, source_target_pairs={{2,4},{6,8},{10,12},{0,14},{4,2},{8,6},{12,10},{14,0},{3,5},{7,9},... | collective-permute-start | bytes 534536 | tf_op jit(solution)/shard_map/ppermute | solution.py:62
  9.3 0.8 %copy.19.cos_rows_ref = bf16[192,320]{1,0:T(8,128)(2,1)} copy(bf16[192,320]{0,1:T(8,128)(2,1)S(1)} %get-tuple-element.38) | data formatting | bytes 245760 | tf_op jit(solution)/shard_map/concatenate | solution.py:194
  10.1 0.8 %copy.20.sin_rows_ref = bf16[192,320]{1,0:T(8,128)(2,1)} copy(bf16[192,320]{0,1:T(8,128)(2,1)S(1)} %get-tuple-element.40) | data formatting | bytes 245760 | tf_op jit(solution)/shard_map/concatenate | solution.py:195
  10.8 0.8 %copy.21.rows_ref = bf16[256,320]{1,0:T(8,128)(2,1)} copy(bf16[256,320]{0,1:T(8,128)(2,1)S(1)} %pad_maximum_fusion.7) | data formatting | bytes 327680 | tf_op jit(solution)/shard_map/concatenate | solution.py:226
  11.6 0.8 %pad_maximum_fusion.2.cols_ref = bf16[640,192]{1,0:T(8,128)(2,1)} fusion(bf16[320,192]{1,0:T(8,128)(2,1)S(1)} %get-tuple-element.39, bf16[320,192]{1,0:T(8,128)(2,1)S(1)} %get-tuple-element.37), kind=kLoop, calls=%fused_computation.9 | loop fusion | flops 491520 | bytes 491520 | tf_op jit(solution)/shard_map/concatenate | solution.py:225
  12.4 2.1 %collective-permute-done.1 = bf16[464,192]{1,0:T(8,128)(2,1)S(1)} collective-permute-done((bf16[464,192]{1,0:T(8,128)(2,1)S(1)}, bf16[464,192]{1,0:T(8,128)(2,1)S(1)}, u32[]{:S(2)}, u32[]{:S(2)}) %collective-permute-start.1) | collective-permute-done | bytes 178208 | tf_op jit(solution)/shard_map/ppermute | solution.py:62
  14.9 1.3 %collective-permute-start.3 = (bf16[320,96]{1,0:T(8,128)(2,1)S(1)}, bf16[320,96]{1,0:T(8,128)(2,1)S(1)}, u32[]{:S(2)}, u32[]{:S(2)}) collective-permute-start(bf16[320,96]{1,0:T(8,128)(2,1)S(1)} %get-tuple-element.41), channel_id=1, source_target_pairs={{0,1},{2,3},{4,5},{6,7},{8,9},{10,11},{12,13},{14,15},{16,17},{18,... | collective-permute-start | bytes 184328 | tf_op jit(solution)/shard_map/ppermute | solution.py:22
  16.2 4.4 %collective-permute-start.4 = (bf16[320,96]{1,0:T(8,128)(2,1)S(1)}, bf16[320,96]{1,0:T(8,128)(2,1)S(1)}, u32[]{:S(2)}, u32[]{:S(2)}) collective-permute-start(bf16[320,96]{1,0:T(8,128)(2,1)S(1)} %get-tuple-element.42), channel_id=1, source_target_pairs={{1,0},{3,2},{5,4},{7,6},{9,8},{11,10},{13,12},{15,14},{17,16},{19,... | collective-permute-start | bytes 184328 | tf_op jit(solution)/shard_map/ppermute | solution.py:25
  20.7 4.2 %collective-permute-start.2 = (bf16[400,192]{1,0:T(8,128)(2,1)S(1)}, bf16[400,192]{1,0:T(8,128)(2,1)S(1)}, u32[]{:S(2)}, u32[]{:S(2)}) collective-permute-start(bf16[400,192]{1,0:T(8,128)(2,1)S(1)} %constant_dynamic-slice_fusion), channel_id=1, source_target_pairs={{0,8},{14,6},{2,10},{4,12},{8,0},{6,14},{10,2},{12,4},{1,9},{15,7}... | collective-permute-start | bytes 460808 | tf_op jit(solution)/shard_map/ppermute | solution.py:62
  24.9 0.6 %fusion.4.ids_ref = s32[4]{0:T(128)} fusion(bf16[4,200,192]{2,1,0:T(8,128)(2,1)S(1)} %bitcast.24), kind=kLoop, calls=%fused_computation.30 | loop fusion | flops 4 | bytes 24 | tf_op jit(solution)/shard_map/convert_element_type | solution.py:235
  25.5 0.4 fusion
  26.3 0.4 convolution_convert_fusion
  27.0 1.0 %fusion.2.spec_i_ref = bf16[320,320]{1,0:T(8,128)(2,1)} fusion(f32[320,320]{1,0:T(8,128)S(1)} %fusion.13, bf16[320,320]{0,1:T(8,128)(2,1)S(1)} %copy-done.1, bf16[320,320]{1,0:T(8,128)(2,1)S(1)} %convolution_convert_fusion), kind=kOutput, calls=%fused_computation.6 | convolution fusion | flops 65740800 | bytes 1024000 | tf_op jit(solution)/shard_map/dot_general | solution.py:41
  28.0 1.0 %fusion.1.spec_r_ref = bf16[320,320]{1,0:T(8,128)(2,1)} fusion(f32[320,320]{1,0:T(8,128)S(1)} %fusion.12, bf16[320,320]{0,1:T(8,128)(2,1)S(1)} %copy-done.1, bf16[320,320]{1,0:T(8,128)(2,1)S(1)} %fusion), kind=kOutput, calls=%fused_computation.5 | convolution fusion | flops 65740800 | bytes 1024000 | tf_op jit(solution)/shard_map/dot_general | solution.py:41
  29.1 8.5 %shard_map.94 = (f32[128,128]{1,0:T(8,128)}, f32[128,128]{1,0:T(8,128)}, f32[128,128]{1,0:T(8,128)}) custom-call(s32[4]{0:T(128)} %fusion.4.ids_ref, bf16[4,200,192]{2,1,0:T(8,128)(2,1)} %bitcast.25, f32[8,320,320]{2,1,0:T(8,128)} %ctf_ref.3, bf16[320,320]{1,0:T(8,128)(2,1)} %fusion.1.spec_r_ref, bf16[320,320]{1,0:T(8,128)(2,1)} %fusion.2.spec_i_ref, ...), custom_call_target="tpu_custom_call" | custom-call | tf_op jit(solution)/shard_map/pallas_call | solution.py:172
  38.3 0.8 %collective-permute-done.5 = bf16[400,192]{1,0:T(8,128)(2,1)S(1)} collective-permute-done((bf16[400,192]{1,0:T(8,128)(2,1)S(1)}, bf16[400,192]{1,0:T(8,128)(2,1)S(1)}, u32[]{:S(2)}, u32[]{:S(2)}) %collective-permute-start.5) | collective-permute-done | bytes 153632 | tf_op jit(solution)/shard_map/ppermute | solution.py:241
  39.1 0.7 %fusion.3.ids_ref = s32[4]{0:T(128)} fusion(bf16[4,200,192]{2,1,0:T(8,128)(2,1)S(1)} %bitcast.26), kind=kLoop, calls=%fused_computation.28 | loop fusion | flops 4 | bytes 24 | tf_op jit(solution)/shard_map/convert_element_type | solution.py:235
  39.9 8.5 %shard_map.95 = (f32[128,128]{1,0:T(8,128)}, f32[128,128]{1,0:T(8,128)}, f32[128,128]{1,0:T(8,128)}) custom-call(s32[4]{0:T(128)} %fusion.3.ids_ref, bf16[4,200,192]{2,1,0:T(8,128)(2,1)} %bitcast.27, f32[8,320,320]{2,1,0:T(8,128)} %ctf_ref.3, bf16[320,320]{1,0:T(8,128)(2,1)} %fusion.1.spec_r_ref, ...), custom_call_target="tpu_custom_call", output_to_operand_aliasing={{0}: (11, {}), {1}: (12, {}), {2}: (13, {})} | custom-call | tf_op jit(solution)/shard_map/pallas_call | solution.py:172
  48.4 1.7 %multiply_select_fusion = (f32[128,128]{1,0:T(8,128)}, f32[128,128]{1,0:T(8,128)}, f32[128,128]{1,0:T(8,128)}) fusion(f32[128,128]{1,0:T(8,128)} %get-tuple-element.26, pred[128]{0:T(512)(128)(4,1)S(1)} %iota_compare_fusion, f32[128,128]{1,0:T(8,128)} %get-tuple-element.25, f32[128,128]{1,0:T(8,128)} %get-tuple-element.24), kind=kLoop, calls=%fused_computation.17 | loop fusion | flops 81920 | bytes 393344 | tf_op jit(solution)/shard_map/jit(_where)/select_n | solution.py:254
  (37 shorter events, 2.2 us)
Async XLA Ops:
  0.6 14.0 %copy-start.4 = (bf16[128,128]{1,0:T(8,128)(2,1)S(1)}, bf16[128,128]{1,0:T(8,128)(2,1)}, u32[]{:S(2)}) copy-start(bf16[128,128]{1,0:T(8,128)(2,1)} %param.7) | copy-start | bytes 98308
  0.7 24.9 %copy-start.1 = (bf16[320,320]{0,1:T(8,128)(2,1)S(1)}, bf16[320,320]{0,1:T(8,128)(2,1)}, u32[]{:S(2)}) copy-start(bf16[320,320]{0,1:T(8,128)(2,1)} %constant.45.clone) | copy-start | bytes 614404
  3.2 4.5 %collective-permute-start = (bf16[264,192]{1,0:T(8,128)(2,1)S(1)}, bf16[264,192]{1,0:T(8,128)(2,1)S(1)}, u32[]{:S(2)}, u32[]{:S(2)}) collective-permute-start(bf16[264,192]{1,0:T(8,128)(2,1)S(1)} %pad_maximum_fusion.8), channel_id=1, source_target_pairs={{0,2},{4,6},{8,10},{12,14},{2,0},{6,4},{10,8},{14,12},{1,3},{5,7},... | collective-permute-start | bytes 304136 | tf_op jit(solution)/shard_map/ppermute | solution.py:62
  4.7 21.2 %copy-start.2 = (bf16[320,320]{0,1:T(8,128)(2,1)S(1)}, bf16[320,320]{0,1:T(8,128)(2,1)}, u32[]{:S(2)}) copy-start(bf16[320,320]{0,1:T(8,128)(2,1)} %constant.44.clone) | copy-start | bytes 614404
  7.8 6.7 %collective-permute-start.1 = (bf16[464,192]{1,0:T(8,128)(2,1)S(1)}, bf16[464,192]{1,0:T(8,128)(2,1)S(1)}, u32[]{:S(2)}, u32[]{:S(2)}) collective-permute-start(bf16[464,192]{1,0:T(8,128)(2,1)S(1)} %pad_maximum_fusion.4), channel_id=1, source_target_pairs={{2,4},{6,8},{10,12},{0,14},{4,2},{8,6},{12,10},{14,0},{3,5},{7,9},... | collective-permute-start | bytes 534536 | tf_op jit(solution)/shard_map/ppermute | solution.py:62
  14.9 10.6 %collective-permute-start.3 = (bf16[320,96]{1,0:T(8,128)(2,1)S(1)}, bf16[320,96]{1,0:T(8,128)(2,1)S(1)}, u32[]{:S(2)}, u32[]{:S(2)}) collective-permute-start(bf16[320,96]{1,0:T(8,128)(2,1)S(1)} %get-tuple-element.41), channel_id=1, source_target_pairs={{0,1},{2,3},{4,5},{6,7},{8,9},{10,11},{12,13},{14,15},{16,17},{18,... | collective-permute-start | bytes 184328 | tf_op jit(solution)/shard_map/ppermute | solution.py:22
  16.2 9.4 %collective-permute-start.4 = (bf16[320,96]{1,0:T(8,128)(2,1)S(1)}, bf16[320,96]{1,0:T(8,128)(2,1)S(1)}, u32[]{:S(2)}, u32[]{:S(2)}) collective-permute-start(bf16[320,96]{1,0:T(8,128)(2,1)S(1)} %get-tuple-element.42), channel_id=1, source_target_pairs={{1,0},{3,2},{5,4},{7,6},{9,8},{11,10},{13,12},{15,14},{17,16},{19,... | collective-permute-start | bytes 184328 | tf_op jit(solution)/shard_map/ppermute | solution.py:25
  20.6 8.4 %copy-start = (bf16[800,192]{1,0:T(8,128)(2,1)}, bf16[800,192]{1,0:T(8,128)(2,1)S(1)}, u32[]{:S(2)}) copy-start(bf16[800,192]{1,0:T(8,128)(2,1)S(1)} %pad_maximum_fusion) | copy-start | bytes 921604
  20.7 16.9 %collective-permute-start.2 = (bf16[400,192]{1,0:T(8,128)(2,1)S(1)}, bf16[400,192]{1,0:T(8,128)(2,1)S(1)}, u32[]{:S(2)}, u32[]{:S(2)}) collective-permute-start(bf16[400,192]{1,0:T(8,128)(2,1)S(1)} %constant_dynamic-slice_fusion), channel_id=1, source_target_pairs={{0,8},{14,6},{2,10},{4,12},{8,0},{6,14},{10,2},{12,4},{1,9},{15,7}... | collective-permute-start | bytes 460808 | tf_op jit(solution)/shard_map/ppermute | solution.py:62
  37.5 1.5 %collective-permute-start.5 = (bf16[400,192]{1,0:T(8,128)(2,1)S(1)}, bf16[400,192]{1,0:T(8,128)(2,1)S(1)}, u32[]{:S(2)}, u32[]{:S(2)}) collective-permute-start(bf16[400,192]{1,0:T(8,128)(2,1)S(1)} %collective-permute-done.2), channel_id=1, source_target_pairs={{0,1},{1,0},{2,3},{3,2},{4,5},{5,4},{6,7},{7,6},{8,9},{9,8},{10,11... | collective-permute-start | bytes 460808 | tf_op jit(solution)/shard_map/ppermute | solution.py:241
  39.1 0.8 %copy-start.3 = (bf16[800,192]{1,0:T(8,128)(2,1)}, bf16[800,192]{1,0:T(8,128)(2,1)S(1)}, u32[]{:S(2)}) copy-start(bf16[800,192]{1,0:T(8,128)(2,1)S(1)} %pad_maximum_fusion.1) | copy-start | bytes 921604

commit v11 on v10

--- a/solution.py
+++ b/solution.py
@@ -94,8 +94,8 @@
     return arrivals, jnp.concatenate([top, tile, bottom], axis=0)
 
 
-def correlate_kernel(ids_ref, tmpl_ref, ctf_ref, spec_r_ref, spec_i_ref, cos_rows_ref, sin_rows_ref,
-                     cols_ref, rows_ref, col_cos_ref, col_sin_ref, *refs, scaling):
+def correlate_kernel(ids_ref, live_ref, tmpl_ref, ctf_ref, spec_r_ref, spec_i_ref, cos_rows_ref, sin_rows_ref,
+                     cols_ref, rows_ref, col_cos_ref, col_sin_ref, *refs, scaling, total, block):
     if len(refs) == 6:
         prev_peak_ref, prev_sum_ref, prev_sq_ref, peak_ref, sum_ref, sq_ref = refs
     else:
@@ -148,34 +148,43 @@
         sum_ref[...] = sum_ref[...] + corr
         sq_ref[...] = sq_ref[...] + corr * corr
 
-
-def correlate(ids, all_templates, ctf, spec_real, spec_imag, tables, scaling, previous):
+    if total:
+        @pl.when(o == pl.num_programs(0) - 1)
+        def _():
+            rows_at = lax.broadcasted_iota(jnp.int32, peak_ref.shape, 0)
+            live = rows_at < block * live_ref[0]
+            peak_ref[...] = jnp.where(live, peak_ref[...], 0.0)
+            sum_ref[...] = jnp.where(live, sum_ref[...] / total, 0.0)
+            sq_ref[...] = jnp.where(live, sq_ref[...] / total, 0.0)
+
+
+def correlate(ids, live, all_templates, ctf, spec_real, spec_imag, tables, scaling, previous, total):
     count = all_templates.shape[0]
     box = all_templates.shape[2]
     n = ctf.shape[1]
     tile = tables[4].shape[1]
-    full = lambda shape: pl.BlockSpec(shape, lambda o, ids: (0,) * len(shape))
+    full = lambda shape: pl.BlockSpec(shape, lambda o, ids, live: (0,) * len(shape))
     in_specs = [
-        pl.BlockSpec((1, box, box), lambda o, ids: (o, 0, 0)),
-        pl.BlockSpec((1, n, n), lambda o, ids: (ids[o], 0, 0)),
+        pl.BlockSpec((1, box, box), lambda o, ids, live: (o, 0, 0)),
+        pl.BlockSpec((1, n, n), lambda o, ids, live: (ids[o], 0, 0)),
         full((n, n)),
         full((n, n)),
     ] + [full(t.shape) for t in tables] + [full((tile, tile))] * len(previous)
     out_block = full((tile, tile))
     grid_spec = pltpu.PrefetchScalarGridSpec(
-        num_scalar_prefetch=1,
+        num_scalar_prefetch=2,
         grid=(count,),
         in_specs=in_specs,
         out_specs=[out_block, out_block, out_block],
     )
     out_shape = [jax.ShapeDtypeStruct((tile, tile), jnp.float32)] * 3
     return pl.pallas_call(
-        functools.partial(correlate_kernel, scaling=scaling),
+        functools.partial(correlate_kernel, scaling=scaling, total=total, block=RB),
         grid_spec=grid_spec,
         out_shape=out_shape,
         compiler_params=pltpu.CompilerParams(dimension_semantics=("arbitrary",)),
-        input_output_aliases={5 + len(tables) + i: i for i in range(len(previous))},
-    )(ids, all_templates, ctf, spec_real, spec_imag, *tables, *previous)
+        input_output_aliases={6 + len(tables) + i: i for i in range(len(previous))},
+    )(ids, live, all_templates, ctf, spec_real, spec_imag, *tables, *previous)
 
 
 def body(micrograph, templates, defocus, ctf, usable):
@@ -208,7 +217,13 @@
     split_last = split_last and local_count == 1 and (margin * tile_width) % box_size == 0
     if split_last:
         arrivals, row_padded = exchange_with_rows(packed, micrograph, margin)
-        padded = extended(row_padded, (("tile", 1),), margin)
+        core = lax.axis_index("tile")
+        edge = jnp.where(core == 0, row_padded[:, tile_width - margin :], row_padded[:, :margin])
+        got = lax.ppermute(edge, "tile", [(0, 1), (1, 0)])
+        zero = jnp.zeros_like(got)
+        padded = jnp.concatenate(
+            [jnp.where(core == 0, zero, got), row_padded, jnp.where(core == 0, got, zero)], axis=1
+        )
     else:
         arrivals = exchange_rounds(packed)
         padded = extended(micrograph, (("orient", 0), ("tile", 1)), margin)
@@ -229,30 +244,24 @@
     )
     shape = (tile_width, tile_width)
     stats = ()
-    def run(piece, stats):
+    live = usable.reshape(-1)[:1]
+
+    def run(piece, stats, total=0):
         count = piece.shape[0] // block_rows
         piece = piece.reshape(count, block_rows, box_size)
         piece_ids = piece[:, box_size, 0].astype(jnp.int32)
-        return correlate(piece_ids, piece, ctf, spec_real, spec_imag, tables, scaling, stats)
+        return correlate(piece_ids, live, piece, ctf, spec_real, spec_imag, tables, scaling, stats, total)
 
     if split_last:
         stats = run(arrivals[0], stats)
         half, stats = lax.optimization_barrier((arrivals[1], stats))
         other_half = lax.ppermute(half, "tile", [(0, 1), (1, 0)])
-        stats = run(jnp.concatenate([half, other_half], axis=0), stats)
         total = (arrivals[0].shape[0] + 2 * half.shape[0]) // block_rows
+        stats = run(jnp.concatenate([half, other_half], axis=0), stats, float(total))
     else:
-        for piece in arrivals:
-            stats = run(piece, stats)
-    peak_map, sum_map, squares = stats
-
-    live = usable[0, 0]
-    row_mask = (jnp.arange(tile_width, dtype=jnp.int32) < RB * live)[:, None]
-    orient_count = float(total)
-    peak_out = jnp.where(row_mask, peak_map, 0.0)
-    mean_out = jnp.where(row_mask, sum_map / orient_count, 0.0)
-    square_out = jnp.where(row_mask, squares / orient_count, 0.0)
-    return (peak_out, mean_out, square_out)
+        for last, piece in enumerate(arrivals, 1 - len(arrivals)):
+            stats = run(piece, stats, 0 if last else float(total))
+    return stats
 
 
 def solution(mesh):

time: 50.5 us -> 45.7 us (0.905)
  the two profiles are of different devices: /device:TPU:11 before, /device:TPU:15 now
where the time goes in v11:
time: 45.7 us; the launch traced here: 45.4 us
  Pallas kernels  17 us (37%)
  starting transfers between devices  8.85 us (19%)
  local copies, waits for them, and re-layouts  6.86 us (15%)
  other arithmetic  3.58 us (8%)
  matrix products  3.51 us (8%)
  waiting for transfers between devices  3.38 us (7%)
  between operations  2.19 us (5%)
    pallas_call x2, Pallas kernels, correlate(): pl.pallas_call(functools.partial(correlate_kernel, scaling=scaling, total...  17 us
    ppermute x3, starting transfers between devices, swap(): lax.ppermute(payload, 'orient', [(a, b) for a, b in pairs] + [(b, a) for...  5.97 us
    dot_general x6, matrix products, matmul(): return jnp.dot(left, right, preferred_element_type=jnp.float32)  3.51 us
    ppermute x1, starting transfers between devices, body(): got = lax.ppermute(edge, 'tile', [(0, 1), (1, 0)])  2.53 us
    ppermute x3, waiting for transfers between devices, swap(): lax.ppermute(payload, 'orient', [(a, b) for a, b in pairs] + [(b, a) for...  2.21 us
    transpose x1, local copies, waits for them, and re-layouts, body(): col_sin = row_sin.T  1.83 us
    convert_element_type x2, other arithmetic, run(): piece_ids = piece[:, box_size, 0].astype(jnp.int32)  1.42 us
    slice x1, local copies, waits for them, and re-layouts, body(): sin_full[low:]  1.19 us
  transfers between devices with their start and end apart: 5, of which 3 were waited for; matrix products, arithmetic and copies ran while one was open for 24% of the time, Pallas kernels for 19%

profile of v11, /device:TPU:15, one launch (start us, length us, event | category | flops | bytes accessed | tf_op | source)
XLA Modules:
  0.0 45.4 jit_solution(12321705786512321188)
XLA Ops:
  0.7 0.8 %broadcast_select_fusion.3 = (bf16[96,128]{1,0:T(8,128)(2,1)S(1)}, bf16[96,128]{1,0:T(8,128)(2,1)S(1)}) fusion(pred[]{:T(512)S(6)} %eq.16, bf16[128,128]{1,0:T(8,128)(2,1)} %param.7), kind=kLoop, calls=%fused_computation.23 | loop fusion | flops 24576 | bytes 98305 | tf_op jit(solution)/shard_map/jit(_where)/select_n | solution.py:79
  2.2 1.0 %pad_bitcast_fusion = bf16[200,192]{1,0:T(8,128)(2,1)S(1)} fusion(bf16[1,192,192]{2,1,0:T(8,128)(2,1)} %param.8, bf16[]{:T(256)} %bitcast), kind=kLoop, calls=%fused_computation.16 | loop fusion | bytes 150530 | tf_op jit(solution)/shard_map/reshape | solution.py:215
  3.6 1.2 %fusion.9 = (bf16[96,320]{0,1:T(8,128)(2,1)S(1)}, bf16[96,320]{0,1:T(8,128)(2,1)S(1)}, bf16[96,320]{0,1:T(8,128)(2,1)S(1)}, bf16[96,320]{0,1:T(8,128)(2,1)S(1)}) fusion(bf16[320,320]{0,1:T(8,128)(2,1)} %constant.37.clone, bf16[320,320]{0,1:T(8,128)(2,1)} %constant.36.clone), kind=kLoop, calls=%fused_computation.38 | loop fusion | bytes 491520 | tf_op jit(solution)/shard_map/slice | solution.py:204
  4.8 1.8 %slice_bitcast_fusion = (bf16[320,128]{1,0:T(8,128)(2,1)}, bf16[128,320]{0,1:T(8,128)(2,1)S(1)}, bf16[128,320]{0,1:T(8,128)(2,1)S(1)}, bf16[320,128]{1,0:T(8,128)(2,1)}) fusion(bf16[320,320]{0,1:T(8,128)(2,1)} %constant.37.clone, bf16[320,320]{0,1:T(8,128)(2,1)} %constant.36.clone), kind=kLoop, calls=%fused_computation.34 | loop fusion | bytes 491520 | tf_op jit(solution)/shard_map/transpose | solution.py:210
  6.9 0.8 %collective-permute-done = bf16[264,192]{1,0:T(8,128)(2,1)S(1)} collective-permute-done((bf16[264,192]{1,0:T(8,128)(2,1)S(1)}, bf16[264,192]{1,0:T(8,128)(2,1)S(1)}, u32[]{:S(2)}, u32[]{:S(2)}) %collective-permute-start) | collective-permute-done | bytes 101408 | tf_op jit(solution)/shard_map/ppermute | solution.py:62
  7.8 1.5 %collective-permute-start.1 = (bf16[464,192]{1,0:T(8,128)(2,1)S(1)}, bf16[464,192]{1,0:T(8,128)(2,1)S(1)}, u32[]{:S(2)}, u32[]{:S(2)}) collective-permute-start(bf16[464,192]{1,0:T(8,128)(2,1)S(1)} %pad_maximum_fusion.4), channel_id=1, source_target_pairs={{2,4},{6,8},{10,12},{0,14},{4,2},{8,6},{12,10},{14,0},{3,5},{7,9},... | collective-permute-start | bytes 534536 | tf_op jit(solution)/shard_map/ppermute | solution.py:62
  9.3 0.8 %copy.19.cos_rows_ref = bf16[192,320]{1,0:T(8,128)(2,1)} copy(bf16[192,320]{0,1:T(8,128)(2,1)S(1)} %get-tuple-element.32) | data formatting | bytes 245760 | tf_op jit(solution)/shard_map/concatenate | solution.py:203
  10.1 0.8 %copy.20.sin_rows_ref = bf16[192,320]{1,0:T(8,128)(2,1)} copy(bf16[192,320]{0,1:T(8,128)(2,1)S(1)} %get-tuple-element.34) | data formatting | bytes 245760 | tf_op jit(solution)/shard_map/concatenate | solution.py:204
  10.9 0.8 %copy.21.rows_ref = bf16[256,320]{1,0:T(8,128)(2,1)} copy(bf16[256,320]{0,1:T(8,128)(2,1)S(1)} %pad_maximum_fusion.7) | data formatting | bytes 327680 | tf_op jit(solution)/shard_map/concatenate | solution.py:241
  12.4 0.8 %pad_maximum_fusion.2.cols_ref = bf16[640,192]{1,0:T(8,128)(2,1)} fusion(bf16[320,192]{1,0:T(8,128)(2,1)S(1)} %get-tuple-element.33, bf16[320,192]{1,0:T(8,128)(2,1)S(1)} %get-tuple-element.31), kind=kLoop, calls=%fused_computation.9 | loop fusion | flops 491520 | bytes 491520 | tf_op jit(solution)/shard_map/concatenate | solution.py:240
  13.1 1.4 %collective-permute-done.1 = bf16[464,192]{1,0:T(8,128)(2,1)S(1)} collective-permute-done((bf16[464,192]{1,0:T(8,128)(2,1)S(1)}, bf16[464,192]{1,0:T(8,128)(2,1)S(1)}, u32[]{:S(2)}, u32[]{:S(2)}) %collective-permute-start.1) | collective-permute-done | bytes 178208 | tf_op jit(solution)/shard_map/ppermute | solution.py:62
  14.9 2.5 %collective-permute-start.3 = (bf16[320,96]{1,0:T(8,128)(2,1)S(1)}, bf16[320,96]{1,0:T(8,128)(2,1)S(1)}, u32[]{:S(2)}, u32[]{:S(2)}) collective-permute-start(bf16[320,96]{1,0:T(8,128)(2,1)S(1)} %slice_select_fusion), channel_id=1, source_target_pairs={{0,1},{1,0},{2,3},{3,2},{4,5},{5,4},{6,7},{7,6},{8,9},{9,8},{10,11... | collective-permute-start | bytes 184328 | tf_op jit(solution)/shard_map/ppermute | solution.py:222
  17.5 4.2 %collective-permute-start.2 = (bf16[400,192]{1,0:T(8,128)(2,1)S(1)}, bf16[400,192]{1,0:T(8,128)(2,1)S(1)}, u32[]{:S(2)}, u32[]{:S(2)}) collective-permute-start(bf16[400,192]{1,0:T(8,128)(2,1)S(1)} %constant_dynamic-slice_fusion), channel_id=1, source_target_pairs={{0,8},{14,6},{2,10},{4,12},{8,0},{6,14},{10,2},{12,4},{1,9},{15,7}... | collective-permute-start | bytes 460808 | tf_op jit(solution)/shard_map/ppermute | solution.py:62
  21.7 0.7 %fusion.4.ids_ref = s32[4]{0:T(128)} fusion(bf16[4,200,192]{2,1,0:T(8,128)(2,1)S(1)} %bitcast.26), kind=kLoop, calls=%fused_computation.30 | loop fusion | flops 4 | bytes 24 | tf_op jit(solution)/shard_map/convert_element_type | solution.py:252
  22.5 0.4 fusion
  22.9 0.4 convolution_convert_fusion
  23.2 0.3 fusion.12
  23.9 1.0 %fusion.2.spec_i_ref = bf16[320,320]{1,0:T(8,128)(2,1)} fusion(f32[320,320]{1,0:T(8,128)S(1)} %fusion.12, bf16[320,320]{0,1:T(8,128)(2,1)S(1)} %copy-done.1, bf16[320,320]{1,0:T(8,128)(2,1)S(1)} %convolution_convert_fusion), kind=kOutput, calls=%fused_computation.6 | convolution fusion | flops 65740800 | bytes 1024000 | tf_op jit(solution)/shard_map/dot_general | solution.py:41
  25.0 1.0 %fusion.1.spec_r_ref = bf16[320,320]{1,0:T(8,128)(2,1)} fusion(f32[320,320]{1,0:T(8,128)S(1)} %fusion.11, bf16[320,320]{0,1:T(8,128)(2,1)S(1)} %copy-done.1, bf16[320,320]{1,0:T(8,128)(2,1)S(1)} %fusion), kind=kOutput, calls=%fused_computation.5 | convolution fusion | flops 65740800 | bytes 1024000 | tf_op jit(solution)/shard_map/dot_general | solution.py:41
  26.0 8.5 %shard_map.94 = (f32[128,128]{1,0:T(8,128)}, f32[128,128]{1,0:T(8,128)}, f32[128,128]{1,0:T(8,128)}) custom-call(s32[4]{0:T(128)} %fusion.4.ids_ref, s32[1]{0:T(128)} %bitcast.24.live_ref, bf16[4,200,192]{2,1,0:T(8,128)(2,1)} %bitcast.27, f32[8,320,320]{2,1,0:T(8,128)} %ctf_ref.3, bf16[320,320]{1,0:T(8,128)(2,1)} %fusion.1.spec_r_ref, ...), custom_call_target="tpu_custom_call" | custom-call | tf_op jit(solution)/shard_map/pallas_call | solution.py:181
  34.5 0.4 collective-permute-start.4
  34.8 1.2 %collective-permute-done.4 = bf16[400,192]{1,0:T(8,128)(2,1)S(1)} collective-permute-done((bf16[400,192]{1,0:T(8,128)(2,1)S(1)}, bf16[400,192]{1,0:T(8,128)(2,1)S(1)}, u32[]{:S(2)}, u32[]{:S(2)}) %collective-permute-start.4) | collective-permute-done | bytes 153632 | tf_op jit(solution)/shard_map/ppermute | solution.py:258
  36.1 0.7 %fusion.3.ids_ref = s32[4]{0:T(128)} fusion(bf16[4,200,192]{2,1,0:T(8,128)(2,1)S(1)} %bitcast.28), kind=kLoop, calls=%fused_computation.28 | loop fusion | flops 4 | bytes 24 | tf_op jit(solution)/shard_map/convert_element_type | solution.py:252
  36.8 8.6 %shard_map.95 = (f32[128,128]{1,0:T(8,128)}, f32[128,128]{1,0:T(8,128)}, f32[128,128]{1,0:T(8,128)}) custom-call(s32[4]{0:T(128)} %fusion.3.ids_ref, s32[1]{0:T(128)} %bitcast.25.live_ref, bf16[4,200,192]{2,1,0:T(8,128)(2,1)} %bitcast.29, f32[8,320,320]{2,1,0:T(8,128)} %ctf_ref.3, ...), custom_call_target="tpu_custom_call", output_to_operand_aliasing={{0}: (12, {}), {1}: (13, {}), {2}: (14, {})} | custom-call | tf_op jit(solution)/shard_map/pallas_call | solution.py:181
  (34 shorter events, 1.7 us)
Async XLA Ops:
  0.6 14.0 %copy-start.4 = (bf16[128,128]{1,0:T(8,128)(2,1)S(1)}, bf16[128,128]{1,0:T(8,128)(2,1)}, u32[]{:S(2)}) copy-start(bf16[128,128]{1,0:T(8,128)(2,1)} %param.7) | copy-start | bytes 98308
  2.2 20.2 %copy-start.1 = (bf16[320,320]{0,1:T(8,128)(2,1)S(1)}, bf16[320,320]{0,1:T(8,128)(2,1)}, u32[]{:S(2)}) copy-start(bf16[320,320]{0,1:T(8,128)(2,1)} %constant.37.clone) | copy-start | bytes 614404
  3.2 4.5 %collective-permute-start = (bf16[264,192]{1,0:T(8,128)(2,1)S(1)}, bf16[264,192]{1,0:T(8,128)(2,1)S(1)}, u32[]{:S(2)}, u32[]{:S(2)}) collective-permute-start(bf16[264,192]{1,0:T(8,128)(2,1)S(1)} %pad_maximum_fusion.8), channel_id=1, source_target_pairs={{0,2},{4,6},{8,10},{12,14},{2,0},{6,4},{10,8},{14,12},{1,3},{5,7},... | collective-permute-start | bytes 304136 | tf_op jit(solution)/shard_map/ppermute | solution.py:62
  4.7 18.1 %copy-start.2 = (bf16[320,320]{0,1:T(8,128)(2,1)S(1)}, bf16[320,320]{0,1:T(8,128)(2,1)}, u32[]{:S(2)}) copy-start(bf16[320,320]{0,1:T(8,128)(2,1)} %constant.36.clone) | copy-start | bytes 614404
  7.8 6.7 %collective-permute-start.1 = (bf16[464,192]{1,0:T(8,128)(2,1)S(1)}, bf16[464,192]{1,0:T(8,128)(2,1)S(1)}, u32[]{:S(2)}, u32[]{:S(2)}) collective-permute-start(bf16[464,192]{1,0:T(8,128)(2,1)S(1)} %pad_maximum_fusion.4), channel_id=1, source_target_pairs={{2,4},{6,8},{10,12},{0,14},{4,2},{8,6},{12,10},{14,0},{3,5},{7,9},... | collective-permute-start | bytes 534536 | tf_op jit(solution)/shard_map/ppermute | solution.py:62
  14.9 7.6 %collective-permute-start.3 = (bf16[320,96]{1,0:T(8,128)(2,1)S(1)}, bf16[320,96]{1,0:T(8,128)(2,1)S(1)}, u32[]{:S(2)}, u32[]{:S(2)}) collective-permute-start(bf16[320,96]{1,0:T(8,128)(2,1)S(1)} %slice_select_fusion), channel_id=1, source_target_pairs={{0,1},{1,0},{2,3},{3,2},{4,5},{5,4},{6,7},{7,6},{8,9},{9,8},{10,11... | collective-permute-start | bytes 184328 | tf_op jit(solution)/shard_map/ppermute | solution.py:222
  17.5 8.5 %copy-start = (bf16[800,192]{1,0:T(8,128)(2,1)}, bf16[800,192]{1,0:T(8,128)(2,1)S(1)}, u32[]{:S(2)}) copy-start(bf16[800,192]{1,0:T(8,128)(2,1)S(1)} %pad_maximum_fusion) | copy-start | bytes 921604
  17.5 16.9 %collective-permute-start.2 = (bf16[400,192]{1,0:T(8,128)(2,1)S(1)}, bf16[400,192]{1,0:T(8,128)(2,1)S(1)}, u32[]{:S(2)}, u32[]{:S(2)}) collective-permute-start(bf16[400,192]{1,0:T(8,128)(2,1)S(1)} %constant_dynamic-slice_fusion), channel_id=1, source_target_pairs={{0,8},{14,6},{2,10},{4,12},{8,0},{6,14},{10,2},{12,4},{1,9},{15,7}... | collective-permute-start | bytes 460808 | tf_op jit(solution)/shard_map/ppermute | solution.py:62
  34.5 1.5 %collective-permute-start.4 = (bf16[400,192]{1,0:T(8,128)(2,1)S(1)}, bf16[400,192]{1,0:T(8,128)(2,1)S(1)}, u32[]{:S(2)}, u32[]{:S(2)}) collective-permute-start(bf16[400,192]{1,0:T(8,128)(2,1)S(1)} %collective-permute-done.2), channel_id=1, source_target_pairs={{0,1},{1,0},{2,3},{3,2},{4,5},{5,4},{6,7},{7,6},{8,9},{9,8},{10,11... | collective-permute-start | bytes 460808 | tf_op jit(solution)/shard_map/ppermute | solution.py:258
  36.1 0.8 %copy-start.3 = (bf16[800,192]{1,0:T(8,128)(2,1)}, bf16[800,192]{1,0:T(8,128)(2,1)S(1)}, u32[]{:S(2)}) copy-start(bf16[800,192]{1,0:T(8,128)(2,1)S(1)} %pad_maximum_fusion.1) | copy-start | bytes 921604

commit v12 on v11

--- a/solution.py
+++ b/solution.py
@@ -78,16 +78,15 @@
 
     first, rows_one = send(block, jnp.where(odd, high_rows, low_rows), [(2 * i, 2 * i + 1) for i in range(size // 2)])
     held = jnp.concatenate([block, first], axis=0)
+    core = lax.axis_index("tile")
+    share = block.shape[0]
+    mine = lax.dynamic_slice_in_dim(held, core * share, share, 0)
     second_pairs = [(2 * i + 1, 2 * i + 2) for i in range(size // 2 - 1)] + [(0, size - 1)]
-    second, rows_two = send(held, jnp.where(odd, low_rows, high_rows), second_pairs)
-    held = jnp.concatenate([held, second], axis=0)
+    second, rows_two = send(mine, jnp.where(odd, low_rows, high_rows), second_pairs)
     third_pairs = [(0, size // 2), (size - 1, size // 2 - 1), (1, size // 2 + 1), (2, size // 2 + 2)]
-    cores = lax.axis_size("tile")
-    share = held.shape[0] // cores
-    core = lax.axis_index("tile")
-    mine = lax.dynamic_slice_in_dim(held, core * share, share, 0)
-    third = swap(mine, third_pairs)
-    arrivals = [held, third]
+    third = swap(jnp.concatenate([mine, second], axis=0), third_pairs)
+    second_other = lax.ppermute(second, "tile", [(0, 1), (1, 0)])
+    arrivals = [jnp.concatenate([held, second, second_other], axis=0), third]
     zero = jnp.zeros_like(rows_one)
     top = jnp.where(odd, rows_one, jnp.where(index == 0, zero, rows_two))
     bottom = jnp.where(odd, jnp.where(index == size - 1, zero, rows_two), rows_one)

time: 45.7 us -> 46.7 us (1.022)
  the two profiles are of different devices: /device:TPU:15 before, /device:TPU:0 now
where the time goes in v12:
time: 46.7 us; the launch traced here: 46.4 us
  Pallas kernels  17 us (36%)
  starting transfers between devices  8.2 us (18%)
  local copies, waits for them, and re-layouts  6.78 us (15%)
  waiting for transfers between devices  4.85 us (10%)
  other arithmetic  3.81 us (8%)
  matrix products  3.51 us (8%)
  between operations  2.2 us (5%)
    pallas_call x2, Pallas kernels, correlate(): pl.pallas_call(functools.partial(correlate_kernel, scaling=scaling, total...  17 us
    ppermute x3, starting transfers between devices, swap(): lax.ppermute(payload, 'orient', [(a, b) for a, b in pairs] + [(b, a) for...  7.5 us
    dot_general x6, matrix products, matmul(): return jnp.dot(left, right, preferred_element_type=jnp.float32)  3.51 us
    ppermute x3, waiting for transfers between devices, swap(): lax.ppermute(payload, 'orient', [(a, b) for a, b in pairs] + [(b, a) for...  3.41 us
    transpose x1, local copies, waits for them, and re-layouts, body(): col_sin = row_sin.T  1.78 us
    ppermute x1, waiting for transfers between devices, body(): other_half = lax.ppermute(half, 'tile', [(0, 1), (1, 0)])  1.44 us
    convert_element_type x2, other arithmetic, run(): piece_ids = piece[:, box_size, 0].astype(jnp.int32)  1.41 us
    slice x1, local copies, waits for them, and re-layouts, body(): sin_full[low:]  1.19 us
  transfers between devices with their start and end apart: 6, of which 2 were waited for; matrix products, arithmetic and copies ran while one was open for 23% of the time, Pallas kernels for 18%

profile of v12, /device:TPU:0, one launch (start us, length us, event | category | flops | bytes accessed | tf_op | source)
XLA Modules:
  0.0 46.4 jit_solution(11861651461550039705)
XLA Ops:
  0.7 0.8 %broadcast_select_fusion.3 = (bf16[96,128]{1,0:T(8,128)(2,1)S(1)}, bf16[96,128]{1,0:T(8,128)(2,1)S(1)}) fusion(pred[]{:T(512)S(6)} %eq.16, bf16[128,128]{1,0:T(8,128)(2,1)} %param.7), kind=kLoop, calls=%fused_computation.27 | loop fusion | flops 24576 | bytes 98305 | tf_op jit(solution)/shard_map/jit(_where)/select_n | solution.py:79
  2.2 0.9 %pad_bitcast_fusion = bf16[200,192]{1,0:T(8,128)(2,1)S(1)} fusion(bf16[1,192,192]{2,1,0:T(8,128)(2,1)} %param.8, bf16[]{:T(256)} %bitcast), kind=kLoop, calls=%fused_computation.20 | loop fusion | bytes 150530 | tf_op jit(solution)/shard_map/reshape | solution.py:214
  3.2 3.0 %collective-permute-start = (bf16[264,192]{1,0:T(8,128)(2,1)S(1)}, bf16[264,192]{1,0:T(8,128)(2,1)S(1)}, u32[]{:S(2)}, u32[]{:S(2)}) collective-permute-start(bf16[264,192]{1,0:T(8,128)(2,1)S(1)} %pad_maximum_fusion.8), channel_id=1, source_target_pairs={{0,2},{4,6},{8,10},{12,14},{2,0},{6,4},{10,8},{14,12},{1,3},{5,7},... | collective-permute-start | bytes 304136 | tf_op jit(solution)/shard_map/ppermute | solution.py:62
  6.2 1.2 %fusion.10 = (bf16[96,320]{0,1:T(8,128)(2,1)S(1)}, bf16[96,320]{0,1:T(8,128)(2,1)S(1)}, bf16[96,320]{0,1:T(8,128)(2,1)S(1)}, bf16[96,320]{0,1:T(8,128)(2,1)S(1)}) fusion(bf16[320,320]{0,1:T(8,128)(2,1)} %constant.37.clone, bf16[320,320]{0,1:T(8,128)(2,1)} %constant.36.clone), kind=kLoop, calls=%fused_computation.41 | loop fusion | bytes 491520 | tf_op jit(solution)/shard_map/slice | solution.py:203
  7.4 1.8 %slice_bitcast_fusion = (bf16[320,128]{1,0:T(8,128)(2,1)}, bf16[128,320]{0,1:T(8,128)(2,1)S(1)}, bf16[128,320]{0,1:T(8,128)(2,1)S(1)}, bf16[320,128]{1,0:T(8,128)(2,1)}) fusion(bf16[320,320]{0,1:T(8,128)(2,1)} %constant.37.clone, bf16[320,320]{0,1:T(8,128)(2,1)} %constant.36.clone), kind=kLoop, calls=%fused_computation.37 | loop fusion | bytes 491520 | tf_op jit(solution)/shard_map/transpose | solution.py:209
  9.4 0.8 %copy.19.cos_rows_ref = bf16[192,320]{1,0:T(8,128)(2,1)} copy(bf16[192,320]{0,1:T(8,128)(2,1)S(1)} %get-tuple-element.32) | data formatting | bytes 245760 | tf_op jit(solution)/shard_map/concatenate | solution.py:202
  10.3 0.8 %copy.20.sin_rows_ref = bf16[192,320]{1,0:T(8,128)(2,1)} copy(bf16[192,320]{0,1:T(8,128)(2,1)S(1)} %get-tuple-element.34) | data formatting | bytes 245760 | tf_op jit(solution)/shard_map/concatenate | solution.py:203
  11.1 0.8 %copy.21.rows_ref = bf16[256,320]{1,0:T(8,128)(2,1)} copy(bf16[256,320]{0,1:T(8,128)(2,1)S(1)} %pad_maximum_fusion.7) | data formatting | bytes 327680 | tf_op jit(solution)/shard_map/concatenate | solution.py:240
  12.9 3.6 %collective-permute-start.1 = (bf16[264,192]{1,0:T(8,128)(2,1)S(1)}, bf16[264,192]{1,0:T(8,128)(2,1)S(1)}, u32[]{:S(2)}, u32[]{:S(2)}) collective-permute-start(bf16[264,192]{1,0:T(8,128)(2,1)S(1)} %pad_maximum_fusion.9), channel_id=1, source_target_pairs={{2,4},{6,8},{10,12},{0,14},{4,2},{8,6},{12,10},{14,0},{3,5},{7,9},... | collective-permute-start | bytes 304136 | tf_op jit(solution)/shard_map/ppermute | solution.py:62
  16.5 0.8 %pad_maximum_fusion.2.cols_ref = bf16[640,192]{1,0:T(8,128)(2,1)} fusion(bf16[320,192]{1,0:T(8,128)(2,1)S(1)} %get-tuple-element.33, bf16[320,192]{1,0:T(8,128)(2,1)S(1)} %get-tuple-element.31), kind=kLoop, calls=%fused_computation.9 | loop fusion | flops 491520 | bytes 491520 | tf_op jit(solution)/shard_map/concatenate | solution.py:239
  17.3 3.4 %collective-permute-done.1 = bf16[264,192]{1,0:T(8,128)(2,1)S(1)} collective-permute-done((bf16[264,192]{1,0:T(8,128)(2,1)S(1)}, bf16[264,192]{1,0:T(8,128)(2,1)S(1)}, u32[]{:S(2)}, u32[]{:S(2)}) %collective-permute-start.1) | collective-permute-done | bytes 101408 | tf_op jit(solution)/shard_map/ppermute | solution.py:62
  21.1 0.6 %collective-permute-start.3 = (bf16[200,192]{1,0:T(8,128)(2,1)S(1)}, bf16[200,192]{1,0:T(8,128)(2,1)S(1)}, u32[]{:S(2)}, u32[]{:S(2)}) collective-permute-start(bf16[200,192]{1,0:T(8,128)(2,1)S(1)} %slice.65), channel_id=1, source_target_pairs={{0,1},{1,0},{2,3},{3,2},{4,5},{5,4},{6,7},{7,6},{8,9},{9,8},{10,11... | collective-permute-start | bytes 230408 | tf_op jit(solution)/shard_map/ppermute | solution.py:88
  21.7 0.9 %collective-permute-start.2 = (bf16[400,192]{1,0:T(8,128)(2,1)S(1)}, bf16[400,192]{1,0:T(8,128)(2,1)S(1)}, u32[]{:S(2)}, u32[]{:S(2)}) collective-permute-start(bf16[400,192]{1,0:T(8,128)(2,1)S(1)} %pad_maximum_fusion.4), channel_id=1, source_target_pairs={{0,8},{14,6},{2,10},{4,12},{8,0},{6,14},{10,2},{12,4},{1,9},{15,7}... | collective-permute-start | bytes 460808 | tf_op jit(solution)/shard_map/ppermute | solution.py:62
  22.6 0.4 fusion
  23.0 0.4 convolution_convert_fusion
  23.4 0.3 fusion.13
  23.7 0.3 fusion.12
  24.1 1.1 %fusion.2.spec_i_ref = bf16[320,320]{1,0:T(8,128)(2,1)} fusion(f32[320,320]{1,0:T(8,128)S(1)} %fusion.13, bf16[320,320]{0,1:T(8,128)(2,1)S(1)} %copy-done, bf16[320,320]{1,0:T(8,128)(2,1)S(1)} %convolution_convert_fusion), kind=kOutput, calls=%fused_computation.6 | convolution fusion | flops 65740800 | bytes 1024000 | tf_op jit(solution)/shard_map/dot_general | solution.py:41
  25.1 1.0 %fusion.1.spec_r_ref = bf16[320,320]{1,0:T(8,128)(2,1)} fusion(f32[320,320]{1,0:T(8,128)S(1)} %fusion.12, bf16[320,320]{0,1:T(8,128)(2,1)S(1)} %copy-done, bf16[320,320]{1,0:T(8,128)(2,1)S(1)} %fusion), kind=kOutput, calls=%fused_computation.5 | convolution fusion | flops 65740800 | bytes 1024000 | tf_op jit(solution)/shard_map/dot_general | solution.py:41
  26.3 0.7 %fusion.5.ids_ref = s32[4]{0:T(128)} fusion(bf16[4,200,192]{2,1,0:T(8,128)(2,1)S(1)} %bitcast.28), kind=kLoop, calls=%fused_computation.34 | loop fusion | flops 4 | bytes 24 | tf_op jit(solution)/shard_map/convert_element_type | solution.py:251
  27.0 8.5 %shard_map.94 = (f32[128,128]{1,0:T(8,128)}, f32[128,128]{1,0:T(8,128)}, f32[128,128]{1,0:T(8,128)}) custom-call(s32[4]{0:T(128)} %fusion.5.ids_ref, s32[1]{0:T(128)} %bitcast.24.live_ref, bf16[4,200,192]{2,1,0:T(8,128)(2,1)} %bitcast.29, f32[8,320,320]{2,1,0:T(8,128)} %ctf_ref.3, bf16[320,320]{1,0:T(8,128)(2,1)} %fusion.1.spec_r_ref, ...), custom_call_target="tpu_custom_call" | custom-call | tf_op jit(solution)/shard_map/pallas_call | solution.py:180
  35.5 1.4 %collective-permute-done.5 = bf16[400,192]{1,0:T(8,128)(2,1)S(1)} collective-permute-done((bf16[400,192]{1,0:T(8,128)(2,1)S(1)}, bf16[400,192]{1,0:T(8,128)(2,1)S(1)}, u32[]{:S(2)}, u32[]{:S(2)}) %collective-permute-start.5) | collective-permute-done | bytes 153632 | tf_op jit(solution)/shard_map/ppermute | solution.py:257
  37.1 0.7 %fusion.4.ids_ref = s32[4]{0:T(128)} fusion(bf16[4,200,192]{2,1,0:T(8,128)(2,1)S(1)} %bitcast.26), kind=kLoop, calls=%fused_computation.32 | loop fusion | flops 4 | bytes 24 | tf_op jit(solution)/shard_map/convert_element_type | solution.py:251
  37.8 8.6 %shard_map.95 = (f32[128,128]{1,0:T(8,128)}, f32[128,128]{1,0:T(8,128)}, f32[128,128]{1,0:T(8,128)}) custom-call(s32[4]{0:T(128)} %fusion.4.ids_ref, s32[1]{0:T(128)} %bitcast.25.live_ref, bf16[4,200,192]{2,1,0:T(8,128)(2,1)} %bitcast.27, f32[8,320,320]{2,1,0:T(8,128)} %ctf_ref.3, ...), custom_call_target="tpu_custom_call", output_to_operand_aliasing={{0}: (12, {}), {1}: (13, {}), {2}: (14, {})} | custom-call | tf_op jit(solution)/shard_map/pallas_call | solution.py:180
  (37 shorter events, 1.5 us)
Async XLA Ops:
  0.6 22.0 %copy-start = (bf16[320,320]{0,1:T(8,128)(2,1)S(1)}, bf16[320,320]{0,1:T(8,128)(2,1)}, u32[]{:S(2)}) copy-start(bf16[320,320]{0,1:T(8,128)(2,1)} %constant.37.clone) | copy-start | bytes 614404
  0.6 20.2 %copy-start.4 = (bf16[128,128]{1,0:T(8,128)(2,1)S(1)}, bf16[128,128]{1,0:T(8,128)(2,1)}, u32[]{:S(2)}) copy-start(bf16[128,128]{1,0:T(8,128)(2,1)} %param.7) | copy-start | bytes 98308
  3.2 19.9 %copy-start.1 = (bf16[320,320]{0,1:T(8,128)(2,1)S(1)}, bf16[320,320]{0,1:T(8,128)(2,1)}, u32[]{:S(2)}) copy-start(bf16[320,320]{0,1:T(8,128)(2,1)} %constant.36.clone) | copy-start | bytes 614404
  3.2 9.4 %collective-permute-start = (bf16[264,192]{1,0:T(8,128)(2,1)S(1)}, bf16[264,192]{1,0:T(8,128)(2,1)S(1)}, u32[]{:S(2)}, u32[]{:S(2)}) collective-permute-start(bf16[264,192]{1,0:T(8,128)(2,1)S(1)} %pad_maximum_fusion.8), channel_id=1, source_target_pairs={{0,2},{4,6},{8,10},{12,14},{2,0},{6,4},{10,8},{14,12},{1,3},{5,7},... | collective-permute-start | bytes 304136 | tf_op jit(solution)/shard_map/ppermute | solution.py:62
  12.9 7.8 %collective-permute-start.1 = (bf16[264,192]{1,0:T(8,128)(2,1)S(1)}, bf16[264,192]{1,0:T(8,128)(2,1)S(1)}, u32[]{:S(2)}, u32[]{:S(2)}) collective-permute-start(bf16[264,192]{1,0:T(8,128)(2,1)S(1)} %pad_maximum_fusion.9), channel_id=1, source_target_pairs={{2,4},{6,8},{10,12},{0,14},{4,2},{8,6},{12,10},{14,0},{3,5},{7,9},... | collective-permute-start | bytes 304136 | tf_op jit(solution)/shard_map/ppermute | solution.py:62
  21.1 1.5 %collective-permute-start.4 = (bf16[320,96]{1,0:T(8,128)(2,1)S(1)}, bf16[320,96]{1,0:T(8,128)(2,1)S(1)}, u32[]{:S(2)}, u32[]{:S(2)}) collective-permute-start(bf16[320,96]{1,0:T(8,128)(2,1)S(1)} %slice_select_fusion), channel_id=1, source_target_pairs={{0,1},{1,0},{2,3},{3,2},{4,5},{5,4},{6,7},{7,6},{8,9},{9,8},{10,11... | collective-permute-start | bytes 184328 | tf_op jit(solution)/shard_map/ppermute | solution.py:221
  21.1 5.0 %collective-permute-start.3 = (bf16[200,192]{1,0:T(8,128)(2,1)S(1)}, bf16[200,192]{1,0:T(8,128)(2,1)S(1)}, u32[]{:S(2)}, u32[]{:S(2)}) collective-permute-start(bf16[200,192]{1,0:T(8,128)(2,1)S(1)} %slice.65), channel_id=1, source_target_pairs={{0,1},{1,0},{2,3},{3,2},{4,5},{5,4},{6,7},{7,6},{8,9},{9,8},{10,11... | collective-permute-start | bytes 230408 | tf_op jit(solution)/shard_map/ppermute | solution.py:88
  21.7 13.7 %collective-permute-start.2 = (bf16[400,192]{1,0:T(8,128)(2,1)S(1)}, bf16[400,192]{1,0:T(8,128)(2,1)S(1)}, u32[]{:S(2)}, u32[]{:S(2)}) collective-permute-start(bf16[400,192]{1,0:T(8,128)(2,1)S(1)} %pad_maximum_fusion.4), channel_id=1, source_target_pairs={{0,8},{14,6},{2,10},{4,12},{8,0},{6,14},{10,2},{12,4},{1,9},{15,7}... | collective-permute-start | bytes 460808 | tf_op jit(solution)/shard_map/ppermute | solution.py:62
  26.3 0.8 %copy-start.3 = (bf16[800,192]{1,0:T(8,128)(2,1)}, bf16[800,192]{1,0:T(8,128)(2,1)S(1)}, u32[]{:S(2)}) copy-start(bf16[800,192]{1,0:T(8,128)(2,1)S(1)} %pad_maximum_fusion) | copy-start | bytes 921604
  35.5 1.5 %collective-permute-start.5 = (bf16[400,192]{1,0:T(8,128)(2,1)S(1)}, bf16[400,192]{1,0:T(8,128)(2,1)S(1)}, u32[]{:S(2)}, u32[]{:S(2)}) collective-permute-start(bf16[400,192]{1,0:T(8,128)(2,1)S(1)} %collective-permute-done.2), channel_id=1, source_target_pairs={{0,1},{1,0},{2,3},{3,2},{4,5},{5,4},{6,7},{7,6},{8,9},{9,8},{10,11... | collective-permute-start | bytes 460808 | tf_op jit(solution)/shard_map/ppermute | solution.py:257
  37.1 0.8 %copy-start.2 = (bf16[800,192]{1,0:T(8,128)(2,1)}, bf16[800,192]{1,0:T(8,128)(2,1)S(1)}, u32[]{:S(2)}) copy-start(bf16[800,192]{1,0:T(8,128)(2,1)S(1)} %pad_maximum_fusion.1) | copy-start | bytes 921604

commit v13 on v12

--- a/solution.py
+++ b/solution.py
@@ -66,23 +66,24 @@
     size = lax.axis_size("orient")
     index = lax.axis_index("orient")
     odd = index % 2 == 1
-    low_rows = tile[tile.shape[0] - width :]
-    high_rows = tile[:width]
     lanes = block.shape[1]
-    carried = width * tile.shape[1] // lanes
+
+    def edge_rows(bottom):
+        start = jnp.where(bottom, tile.shape[0] - width, 0)
+        return lax.dynamic_slice_in_dim(tile, start, width, 0)
 
     def send(held, rows, pairs):
-        payload = jnp.concatenate([held, rows.reshape(carried, lanes)], axis=0)
-        got = swap(payload, pairs)
-        return got[: held.shape[0]], got[held.shape[0] :].reshape(width, tile.shape[1])
-
-    first, rows_one = send(block, jnp.where(odd, high_rows, low_rows), [(2 * i, 2 * i + 1) for i in range(size // 2)])
+        padded_rows = jnp.pad(rows, ((0, 0), (0, lanes - rows.shape[1])))
+        got = swap(jnp.concatenate([held, padded_rows], axis=0), pairs)
+        return got[: held.shape[0]], got[held.shape[0] :, : tile.shape[1]]
+
+    first, rows_one = send(block, edge_rows(jnp.logical_not(odd)), [(2 * i, 2 * i + 1) for i in range(size // 2)])
     held = jnp.concatenate([block, first], axis=0)
     core = lax.axis_index("tile")
     share = block.shape[0]
     mine = lax.dynamic_slice_in_dim(held, core * share, share, 0)
     second_pairs = [(2 * i + 1, 2 * i + 2) for i in range(size // 2 - 1)] + [(0, size - 1)]
-    second, rows_two = send(mine, jnp.where(odd, low_rows, high_rows), second_pairs)
+    second, rows_two = send(mine, edge_rows(odd), second_pairs)
     third_pairs = [(0, size // 2), (size - 1, size // 2 - 1), (1, size // 2 + 1), (2, size // 2 + 2)]
     third = swap(jnp.concatenate([mine, second], axis=0), third_pairs)
     second_other = lax.ppermute(second, "tile", [(0, 1), (1, 0)])
@@ -213,7 +214,7 @@
     block_rows = box_size + 8
     packed = jnp.concatenate([templates, id_rows], axis=1).reshape(local_count * block_rows, box_size)
     split_last = lax.axis_size("orient") == 8 and lax.axis_size("tile") == 2
-    split_last = split_last and local_count == 1 and (margin * tile_width) % box_size == 0
+    split_last = split_last and local_count == 1 and tile_width <= box_size
     if split_last:
         arrivals, row_padded = exchange_with_rows(packed, micrograph, margin)
         core = lax.axis_index("tile")

time: 46.7 us -> 46.7 us (level)
  other arithmetic: 3.81 us -> 2.98 us
    select_n x2 -> x1, other arithmetic: 0.84 us -> 0.01 us  [exchange_with_rows(): top = jnp.where(odd, rows_one, jnp.where(index == 0, zero, rows_two))]
    dynamic_slice x0 -> x1, local copies, waits for them, and re-layouts: none -> 0.83 us  [edge_rows(): return lax.dynamic_slice_in_dim(tile, start, width, 0)]
where the time goes in v13:
time: 46.7 us; the launch traced here: 46.4 us
  Pallas kernels  17 us (36%)
  starting transfers between devices  8.2 us (18%)
  local copies, waits for them, and re-layouts  7.23 us (15%)
  waiting for transfers between devices  5.2 us (11%)
  matrix products  3.53 us (8%)
  other arithmetic  2.98 us (6%)
  between operations  2.2 us (5%)
    pallas_call x2, Pallas kernels, correlate(): pl.pallas_call(functools.partial(correlate_kernel, scaling=scaling, total...  17 us
    ppermute x3, starting transfers between devices, swap(): lax.ppermute(payload, 'orient', [(a, b) for a, b in pairs] + [(b, a) for...  7.5 us
    ppermute x3, waiting for transfers between devices, swap(): lax.ppermute(payload, 'orient', [(a, b) for a, b in pairs] + [(b, a) for...  3.76 us
    dot_general x6, matrix products, matmul(): return jnp.dot(left, right, preferred_element_type=jnp.float32)  3.53 us
    transpose x1, local copies, waits for them, and re-layouts, body(): col_sin = row_sin.T  1.78 us
    ppermute x1, waiting for transfers between devices, body(): other_half = lax.ppermute(half, 'tile', [(0, 1), (1, 0)])  1.44 us
    convert_element_type x2, other arithmetic, run(): piece_ids = piece[:, box_size, 0].astype(jnp.int32)  1.41 us
    slice x1, local copies, waits for them, and re-layouts, body(): sin_full[low:]  1.23 us
  transfers between devices with their start and end apart: 6, of which 2 were waited for; matrix products, arithmetic and copies ran while one was open for 23% of the time, Pallas kernels for 18%

profile of v13, /device:TPU:0, one launch (start us, length us, event | category | flops | bytes accessed | tf_op | source)
XLA Modules:
  0.0 46.4 jit_solution(14657067855244651399)
XLA Ops:
  1.4 0.9 %pad_bitcast_fusion = bf16[200,192]{1,0:T(8,128)(2,1)S(1)} fusion(bf16[1,192,192]{2,1,0:T(8,128)(2,1)} %param.8, bf16[]{:T(256)} %bitcast), kind=kLoop, calls=%fused_computation.23 | loop fusion | bytes 150530 | tf_op jit(solution)/shard_map/reshape | solution.py:215
  2.3 0.8 %constant_dynamic-slice_fusion.1 = (bf16[96,128]{1,0:T(8,128)(2,1)S(1)}, bf16[96,128]{1,0:T(8,128)(2,1)S(1)}) fusion(bf16[128,128]{1,0:T(8,128)(2,1)} %param.7, s32[]{:T(128)S(6)} %select_n.60, s32[]{:T(128)S(6)} %select_n.62), kind=kLoop, calls=%fused_computation.35 | loop fusion | bytes 98312 | tf_op jit(solution)/shard_map/dynamic_slice | solution.py:73
  3.1 3.0 %collective-permute-start = (bf16[296,192]{1,0:T(8,128)(2,1)S(1)}, bf16[296,192]{1,0:T(8,128)(2,1)S(1)}, u32[]{:S(2)}, u32[]{:S(2)}) collective-permute-start(bf16[296,192]{1,0:T(8,128)(2,1)S(1)} %fusion.5), channel_id=1, source_target_pairs={{0,2},{4,6},{8,10},{12,14},{2,0},{6,4},{10,8},{14,12},{1,3},{5,7},... | collective-permute-start | bytes 341000 | tf_op jit(solution)/shard_map/ppermute | solution.py:62
  6.1 1.2 %fusion.12 = (bf16[96,320]{0,1:T(8,128)(2,1)S(1)}, bf16[96,320]{0,1:T(8,128)(2,1)S(1)}, bf16[96,320]{0,1:T(8,128)(2,1)S(1)}, bf16[96,320]{0,1:T(8,128)(2,1)S(1)}) fusion(bf16[320,320]{0,1:T(8,128)(2,1)} %constant.43.clone, bf16[320,320]{0,1:T(8,128)(2,1)} %constant.42.clone), kind=kLoop, calls=%fused_computation.40 | loop fusion | bytes 491520 | tf_op jit(solution)/shard_map/slice | solution.py:204
  7.4 1.8 %slice_bitcast_fusion = (bf16[320,128]{1,0:T(8,128)(2,1)}, bf16[128,320]{0,1:T(8,128)(2,1)S(1)}, bf16[128,320]{0,1:T(8,128)(2,1)S(1)}, bf16[320,128]{1,0:T(8,128)(2,1)}) fusion(bf16[320,320]{0,1:T(8,128)(2,1)} %constant.43.clone, bf16[320,320]{0,1:T(8,128)(2,1)} %constant.42.clone), kind=kLoop, calls=%fused_computation.36 | loop fusion | bytes 491520 | tf_op jit(solution)/shard_map/transpose | solution.py:210
  9.3 0.8 %copy.19.cos_rows_ref = bf16[192,320]{1,0:T(8,128)(2,1)} copy(bf16[192,320]{0,1:T(8,128)(2,1)S(1)} %get-tuple-element.32) | data formatting | bytes 245760 | tf_op jit(solution)/shard_map/concatenate | solution.py:203
  10.2 0.8 %copy.20.sin_rows_ref = bf16[192,320]{1,0:T(8,128)(2,1)} copy(bf16[192,320]{0,1:T(8,128)(2,1)S(1)} %get-tuple-element.34) | data formatting | bytes 245760 | tf_op jit(solution)/shard_map/concatenate | solution.py:204
  11.0 0.8 %copy.21.rows_ref = bf16[256,320]{1,0:T(8,128)(2,1)} copy(bf16[256,320]{0,1:T(8,128)(2,1)S(1)} %pad_maximum_fusion.7) | data formatting | bytes 327680 | tf_op jit(solution)/shard_map/concatenate | solution.py:241
  12.7 3.6 %collective-permute-start.1 = (bf16[296,192]{1,0:T(8,128)(2,1)S(1)}, bf16[296,192]{1,0:T(8,128)(2,1)S(1)}, u32[]{:S(2)}, u32[]{:S(2)}) collective-permute-start(bf16[296,192]{1,0:T(8,128)(2,1)S(1)} %fusion.6), channel_id=1, source_target_pairs={{2,4},{6,8},{10,12},{0,14},{4,2},{8,6},{12,10},{14,0},{3,5},{7,9},... | collective-permute-start | bytes 341000 | tf_op jit(solution)/shard_map/ppermute | solution.py:62
  16.4 0.8 %pad_maximum_fusion.2.cols_ref = bf16[640,192]{1,0:T(8,128)(2,1)} fusion(bf16[320,192]{1,0:T(8,128)(2,1)S(1)} %get-tuple-element.33, bf16[320,192]{1,0:T(8,128)(2,1)S(1)} %get-tuple-element.31), kind=kLoop, calls=%fused_computation.9 | loop fusion | flops 491520 | bytes 491520 | tf_op jit(solution)/shard_map/concatenate | solution.py:240
  17.1 3.8 %collective-permute-done.1 = bf16[296,192]{1,0:T(8,128)(2,1)S(1)} collective-permute-done((bf16[296,192]{1,0:T(8,128)(2,1)S(1)}, bf16[296,192]{1,0:T(8,128)(2,1)S(1)}, u32[]{:S(2)}, u32[]{:S(2)}) %collective-permute-start.1) | collective-permute-done | bytes 113696 | tf_op jit(solution)/shard_map/ppermute | solution.py:62
  21.1 0.6 %collective-permute-start.3 = (bf16[200,192]{1,0:T(8,128)(2,1)S(1)}, bf16[200,192]{1,0:T(8,128)(2,1)S(1)}, u32[]{:S(2)}, u32[]{:S(2)}) collective-permute-start(bf16[200,192]{1,0:T(8,128)(2,1)S(1)} %slice.57), channel_id=1, source_target_pairs={{0,1},{1,0},{2,3},{3,2},{4,5},{5,4},{6,7},{7,6},{8,9},{9,8},{10,11... | collective-permute-start | bytes 230408 | tf_op jit(solution)/shard_map/ppermute | solution.py:89
  21.7 0.9 %collective-permute-start.2 = (bf16[400,192]{1,0:T(8,128)(2,1)S(1)}, bf16[400,192]{1,0:T(8,128)(2,1)S(1)}, u32[]{:S(2)}, u32[]{:S(2)}) collective-permute-start(bf16[400,192]{1,0:T(8,128)(2,1)S(1)} %pad_maximum_fusion.4), channel_id=1, source_target_pairs={{0,8},{14,6},{2,10},{4,12},{8,0},{6,14},{10,2},{12,4},{1,9},{15,7}... | collective-permute-start | bytes 460808 | tf_op jit(solution)/shard_map/ppermute | solution.py:62
  22.6 0.4 fusion
  23.0 0.4 convolution_convert_fusion
  23.4 0.3 fusion.15
  23.7 0.3 fusion.14
  24.1 1.1 %fusion.2.spec_i_ref = bf16[320,320]{1,0:T(8,128)(2,1)} fusion(f32[320,320]{1,0:T(8,128)S(1)} %fusion.15, bf16[320,320]{0,1:T(8,128)(2,1)S(1)} %copy-done, bf16[320,320]{1,0:T(8,128)(2,1)S(1)} %convolution_convert_fusion), kind=kOutput, calls=%fused_computation.6 | convolution fusion | flops 65740800 | bytes 1024000 | tf_op jit(solution)/shard_map/dot_general | solution.py:41
  25.1 1.0 %fusion.1.spec_r_ref = bf16[320,320]{1,0:T(8,128)(2,1)} fusion(f32[320,320]{1,0:T(8,128)S(1)} %fusion.14, bf16[320,320]{0,1:T(8,128)(2,1)S(1)} %copy-done, bf16[320,320]{1,0:T(8,128)(2,1)S(1)} %fusion), kind=kOutput, calls=%fused_computation.5 | convolution fusion | flops 65740800 | bytes 1024000 | tf_op jit(solution)/shard_map/dot_general | solution.py:41
  26.3 0.7 %fusion.9.ids_ref = s32[4]{0:T(128)} fusion(bf16[4,200,192]{2,1,0:T(8,128)(2,1)S(1)} %bitcast.28), kind=kLoop, calls=%fused_computation.33 | loop fusion | flops 4 | bytes 24 | tf_op jit(solution)/shard_map/convert_element_type | solution.py:252
  27.0 8.5 %shard_map.94 = (f32[128,128]{1,0:T(8,128)}, f32[128,128]{1,0:T(8,128)}, f32[128,128]{1,0:T(8,128)}) custom-call(s32[4]{0:T(128)} %fusion.9.ids_ref, s32[1]{0:T(128)} %bitcast.24.live_ref, bf16[4,200,192]{2,1,0:T(8,128)(2,1)} %bitcast.29, f32[8,320,320]{2,1,0:T(8,128)} %ctf_ref.3, bf16[320,320]{1,0:T(8,128)(2,1)} %fusion.1.spec_r_ref, ...), custom_call_target="tpu_custom_call" | custom-call | tf_op jit(solution)/shard_map/pallas_call | solution.py:181
  35.5 1.4 %collective-permute-done.5 = bf16[400,192]{1,0:T(8,128)(2,1)S(1)} collective-permute-done((bf16[400,192]{1,0:T(8,128)(2,1)S(1)}, bf16[400,192]{1,0:T(8,128)(2,1)S(1)}, u32[]{:S(2)}, u32[]{:S(2)}) %collective-permute-start.5) | collective-permute-done | bytes 153632 | tf_op jit(solution)/shard_map/ppermute | solution.py:258
  37.0 0.7 %fusion.8.ids_ref = s32[4]{0:T(128)} fusion(bf16[4,200,192]{2,1,0:T(8,128)(2,1)S(1)} %bitcast.26), kind=kLoop, calls=%fused_computation.31 | loop fusion | flops 4 | bytes 24 | tf_op jit(solution)/shard_map/convert_element_type | solution.py:252
  37.8 8.6 %shard_map.95 = (f32[128,128]{1,0:T(8,128)}, f32[128,128]{1,0:T(8,128)}, f32[128,128]{1,0:T(8,128)}) custom-call(s32[4]{0:T(128)} %fusion.8.ids_ref, s32[1]{0:T(128)} %bitcast.25.live_ref, bf16[4,200,192]{2,1,0:T(8,128)(2,1)} %bitcast.27, f32[8,320,320]{2,1,0:T(8,128)} %ctf_ref.3, ...), custom_call_target="tpu_custom_call", output_to_operand_aliasing={{0}: (12, {}), {1}: (13, {}), {2}: (14, {})} | custom-call | tf_op jit(solution)/shard_map/pallas_call | solution.py:181
  (31 shorter events, 1.1 us)
Async XLA Ops:
  0.6 22.0 %copy-start = (bf16[320,320]{0,1:T(8,128)(2,1)S(1)}, bf16[320,320]{0,1:T(8,128)(2,1)}, u32[]{:S(2)}) copy-start(bf16[320,320]{0,1:T(8,128)(2,1)} %constant.43.clone) | copy-start | bytes 614404
  0.6 20.3 %copy-start.4 = (bf16[128,128]{1,0:T(8,128)(2,1)S(1)}, bf16[128,128]{1,0:T(8,128)(2,1)}, u32[]{:S(2)}) copy-start(bf16[128,128]{1,0:T(8,128)(2,1)} %param.7) | copy-start | bytes 98308
  3.1 9.3 %collective-permute-start = (bf16[296,192]{1,0:T(8,128)(2,1)S(1)}, bf16[296,192]{1,0:T(8,128)(2,1)S(1)}, u32[]{:S(2)}, u32[]{:S(2)}) collective-permute-start(bf16[296,192]{1,0:T(8,128)(2,1)S(1)} %fusion.5), channel_id=1, source_target_pairs={{0,2},{4,6},{8,10},{12,14},{2,0},{6,4},{10,8},{14,12},{1,3},{5,7},... | collective-permute-start | bytes 341000 | tf_op jit(solution)/shard_map/ppermute | solution.py:62
  6.1 16.9 %copy-start.1 = (bf16[320,320]{0,1:T(8,128)(2,1)S(1)}, bf16[320,320]{0,1:T(8,128)(2,1)}, u32[]{:S(2)}) copy-start(bf16[320,320]{0,1:T(8,128)(2,1)} %constant.42.clone) | copy-start | bytes 614404
  12.7 8.2 %collective-permute-start.1 = (bf16[296,192]{1,0:T(8,128)(2,1)S(1)}, bf16[296,192]{1,0:T(8,128)(2,1)S(1)}, u32[]{:S(2)}, u32[]{:S(2)}) collective-permute-start(bf16[296,192]{1,0:T(8,128)(2,1)S(1)} %fusion.6), channel_id=1, source_target_pairs={{2,4},{6,8},{10,12},{0,14},{4,2},{8,6},{12,10},{14,0},{3,5},{7,9},... | collective-permute-start | bytes 341000 | tf_op jit(solution)/shard_map/ppermute | solution.py:62
  21.0 1.5 %collective-permute-start.4 = (bf16[320,96]{1,0:T(8,128)(2,1)S(1)}, bf16[320,96]{1,0:T(8,128)(2,1)S(1)}, u32[]{:S(2)}, u32[]{:S(2)}) collective-permute-start(bf16[320,96]{1,0:T(8,128)(2,1)S(1)} %slice_select_fusion), channel_id=1, source_target_pairs={{0,1},{1,0},{2,3},{3,2},{4,5},{5,4},{6,7},{7,6},{8,9},{9,8},{10,11... | collective-permute-start | bytes 184328 | tf_op jit(solution)/shard_map/ppermute | solution.py:222
  21.1 5.1 %collective-permute-start.3 = (bf16[200,192]{1,0:T(8,128)(2,1)S(1)}, bf16[200,192]{1,0:T(8,128)(2,1)S(1)}, u32[]{:S(2)}, u32[]{:S(2)}) collective-permute-start(bf16[200,192]{1,0:T(8,128)(2,1)S(1)} %slice.57), channel_id=1, source_target_pairs={{0,1},{1,0},{2,3},{3,2},{4,5},{5,4},{6,7},{7,6},{8,9},{9,8},{10,11... | collective-permute-start | bytes 230408 | tf_op jit(solution)/shard_map/ppermute | solution.py:89
  21.7 13.7 %collective-permute-start.2 = (bf16[400,192]{1,0:T(8,128)(2,1)S(1)}, bf16[400,192]{1,0:T(8,128)(2,1)S(1)}, u32[]{:S(2)}, u32[]{:S(2)}) collective-permute-start(bf16[400,192]{1,0:T(8,128)(2,1)S(1)} %pad_maximum_fusion.4), channel_id=1, source_target_pairs={{0,8},{14,6},{2,10},{4,12},{8,0},{6,14},{10,2},{12,4},{1,9},{15,7}... | collective-permute-start | bytes 460808 | tf_op jit(solution)/shard_map/ppermute | solution.py:62
  26.2 0.8 %copy-start.3 = (bf16[800,192]{1,0:T(8,128)(2,1)}, bf16[800,192]{1,0:T(8,128)(2,1)S(1)}, u32[]{:S(2)}) copy-start(bf16[800,192]{1,0:T(8,128)(2,1)S(1)} %pad_maximum_fusion) | copy-start | bytes 921604
  35.5 1.5 %collective-permute-start.5 = (bf16[400,192]{1,0:T(8,128)(2,1)S(1)}, bf16[400,192]{1,0:T(8,128)(2,1)S(1)}, u32[]{:S(2)}, u32[]{:S(2)}) collective-permute-start(bf16[400,192]{1,0:T(8,128)(2,1)S(1)} %collective-permute-done.2), channel_id=1, source_target_pairs={{0,1},{1,0},{2,3},{3,2},{4,5},{5,4},{6,7},{7,6},{8,9},{9,8},{10,11... | collective-permute-start | bytes 460808 | tf_op jit(solution)/shard_map/ppermute | solution.py:258
  37.0 0.8 %copy-start.2 = (bf16[800,192]{1,0:T(8,128)(2,1)}, bf16[800,192]{1,0:T(8,128)(2,1)S(1)}, u32[]{:S(2)}) copy-start(bf16[800,192]{1,0:T(8,128)(2,1)S(1)} %pad_maximum_fusion.1) | copy-start | bytes 921604

commit v14 on v13

--- a/solution.py
+++ b/solution.py
@@ -62,22 +62,25 @@
     return lax.ppermute(payload, "orient", [(a, b) for a, b in pairs] + [(b, a) for a, b in pairs])
 
 
-def exchange_with_rows(block, tile, width):
+def exchange_with_rows(parts, tile, width):
     size = lax.axis_size("orient")
     index = lax.axis_index("orient")
     odd = index % 2 == 1
-    lanes = block.shape[1]
+    lanes = parts[0].shape[1]
+    block = jnp.concatenate(parts, axis=0)
 
     def edge_rows(bottom):
         start = jnp.where(bottom, tile.shape[0] - width, 0)
         return lax.dynamic_slice_in_dim(tile, start, width, 0)
 
     def send(held, rows, pairs):
+        held = held if isinstance(held, list) else [held]
         padded_rows = jnp.pad(rows, ((0, 0), (0, lanes - rows.shape[1])))
-        got = swap(jnp.concatenate([held, padded_rows], axis=0), pairs)
-        return got[: held.shape[0]], got[held.shape[0] :, : tile.shape[1]]
-
-    first, rows_one = send(block, edge_rows(jnp.logical_not(odd)), [(2 * i, 2 * i + 1) for i in range(size // 2)])
+        got = swap(jnp.concatenate(held + [padded_rows], axis=0), pairs)
+        count = sum(piece.shape[0] for piece in held)
+        return got[:count], got[count:, : tile.shape[1]]
+
+    first, rows_one = send(list(parts), edge_rows(jnp.logical_not(odd)), [(2 * i, 2 * i + 1) for i in range(size // 2)])
     held = jnp.concatenate([block, first], axis=0)
     core = lax.axis_index("tile")
     share = block.shape[0]
@@ -216,7 +219,7 @@
     split_last = lax.axis_size("orient") == 8 and lax.axis_size("tile") == 2
     split_last = split_last and local_count == 1 and tile_width <= box_size
     if split_last:
-        arrivals, row_padded = exchange_with_rows(packed, micrograph, margin)
+        arrivals, row_padded = exchange_with_rows([templates[0], id_rows[0]], micrograph, margin)
         core = lax.axis_index("tile")
         edge = jnp.where(core == 0, row_padded[:, tile_width - margin :], row_padded[:, :margin])
         got = lax.ppermute(edge, "tile", [(0, 1), (1, 0)])

time: 46.7 us -> 47.7 us (1.021)
  other arithmetic: 2.98 us -> 3.82 us
    unnamed x10 -> x16, local copies, waits for them, and re-layouts: 0.1 us -> 1.08 us
    reshape x1 -> x0, local copies, waits for them, and re-layouts: 0.91 us -> none  [body(): jnp.concatenate([templates, id_rows], axis=1)]
    concatenate x3 -> x2, other arithmetic: 0.11 us -> 0.93 us  [send(): got = swap(jnp.concatenate(held + [padded_rows], axis=0), pairs)]
  transfers between devices with their start and end apart: 6 -> 6, of which waited for: 2 -> 2; matrix products, arithmetic and copies ran while one was open for 23% -> 25% of each run, Pallas kernels for 18% -> 18%
where the time goes in v14:
time: 47.7 us; the launch traced here: 47.3 us
  Pallas kernels  17 us (36%)
  starting transfers between devices  8.2 us (17%)
  local copies, waits for them, and re-layouts  7.28 us (15%)
  waiting for transfers between devices  5.2 us (11%)
  other arithmetic  3.82 us (8%)
  matrix products  3.53 us (7%)
  between operations  2.28 us (5%)
    pallas_call x2, Pallas kernels, correlate(): pl.pallas_call(functools.partial(correlate_kernel, scaling=scaling, total...  17 us
    ppermute x3, starting transfers between devices, swap(): lax.ppermute(payload, 'orient', [(a, b) for a, b in pairs] + [(b, a) for...  7.5 us
    ppermute x3, waiting for transfers between devices, swap(): lax.ppermute(payload, 'orient', [(a, b) for a, b in pairs] + [(b, a) for...  3.75 us
    dot_general x6, matrix products, matmul(): return jnp.dot(left, right, preferred_element_type=jnp.float32)  3.53 us
    transpose x1, local copies, waits for them, and re-layouts, body(): col_sin = row_sin.T  1.77 us
    ppermute x1, waiting for transfers between devices, body(): other_half = lax.ppermute(half, 'tile', [(0, 1), (1, 0)])  1.44 us
    convert_element_type x2, other arithmetic, run(): piece_ids = piece[:, box_size, 0].astype(jnp.int32)  1.38 us
    slice x1, local copies, waits for them, and re-layouts, body(): sin_full[low:]  1.23 us
  transfers between devices with their start and end apart: 6, of which 2 were waited for; matrix products, arithmetic and copies ran while one was open for 25% of the time, Pallas kernels for 18%

profile of v14, /device:TPU:0, one launch (start us, length us, event | category | flops | bytes accessed | tf_op | source)
XLA Modules:
  0.0 47.3 jit_solution(14343109741086005408)
XLA Ops:
  1.4 0.8 %constant_dynamic-slice_fusion.1 = (bf16[96,128]{1,0:T(8,128)(2,1)S(1)}, bf16[96,128]{1,0:T(8,128)(2,1)S(1)}) fusion(bf16[128,128]{1,0:T(8,128)(2,1)} %param.7, s32[]{:T(128)S(6)} %select_n.60, s32[]{:T(128)S(6)} %select_n.62), kind=kLoop, calls=%fused_computation.40 | loop fusion | bytes 98312 | tf_op jit(solution)/shard_map/dynamic_slice | solution.py:74
  2.2 0.9 %fusion.5 = bf16[296,192]{1,0:T(8,128)(2,1)S(1)} fusion(bf16[96,128]{1,0:T(8,128)(2,1)S(1)} %get-tuple-element.41, bf16[8,192]{1,0:T(8,128)(2,1)S(1)} %squeeze.9, bf16[192,192]{1,0:T(8,128)(2,1)} %bitcast.28), kind=kLoop, calls=%fused_computation.20 | loop fusion | flops 454656 | bytes 215040 | tf_op jit(solution)/shard_map/concatenate | solution.py:79
  3.1 3.0 %collective-permute-start = (bf16[296,192]{1,0:T(8,128)(2,1)S(1)}, bf16[296,192]{1,0:T(8,128)(2,1)S(1)}, u32[]{:S(2)}, u32[]{:S(2)}) collective-permute-start(bf16[296,192]{1,0:T(8,128)(2,1)S(1)} %fusion.5), channel_id=1, source_target_pairs={{0,2},{4,6},{8,10},{12,14},{2,0},{6,4},{10,8},{14,12},{1,3},{5,7},... | collective-permute-start | bytes 341000 | tf_op jit(solution)/shard_map/ppermute | solution.py:62
  6.2 0.9 %constant_dynamic-update-slice_fusion.4 = bf16[800,192]{1,0:T(8,128)(2,1)S(1)} fusion(bf16[1,192,192]{2,1,0:T(8,128)(2,1)} %param.8), kind=kLoop, calls=%fused_computation.34 | loop fusion | bytes 172032
  7.1 1.2 %fusion.13 = (bf16[96,320]{0,1:T(8,128)(2,1)S(1)}, bf16[96,320]{0,1:T(8,128)(2,1)S(1)}, bf16[96,320]{0,1:T(8,128)(2,1)S(1)}, bf16[96,320]{0,1:T(8,128)(2,1)S(1)}) fusion(bf16[320,320]{0,1:T(8,128)(2,1)} %constant.43.clone, bf16[320,320]{0,1:T(8,128)(2,1)} %constant.42.clone), kind=kLoop, calls=%fused_computation.45 | loop fusion | bytes 491520 | tf_op jit(solution)/shard_map/slice | solution.py:207
  8.3 1.8 %slice_bitcast_fusion = (bf16[320,128]{1,0:T(8,128)(2,1)}, bf16[128,320]{0,1:T(8,128)(2,1)S(1)}, bf16[128,320]{0,1:T(8,128)(2,1)S(1)}, bf16[320,128]{1,0:T(8,128)(2,1)}) fusion(bf16[320,320]{0,1:T(8,128)(2,1)} %constant.43.clone, bf16[320,320]{0,1:T(8,128)(2,1)} %constant.42.clone), kind=kLoop, calls=%fused_computation.41 | loop fusion | bytes 491520 | tf_op jit(solution)/shard_map/transpose | solution.py:213
  10.3 0.8 %copy.19.cos_rows_ref = bf16[192,320]{1,0:T(8,128)(2,1)} copy(bf16[192,320]{0,1:T(8,128)(2,1)S(1)} %get-tuple-element.32) | data formatting | bytes 245760 | tf_op jit(solution)/shard_map/concatenate | solution.py:206
  11.1 0.8 %copy.20.sin_rows_ref = bf16[192,320]{1,0:T(8,128)(2,1)} copy(bf16[192,320]{0,1:T(8,128)(2,1)S(1)} %get-tuple-element.34) | data formatting | bytes 245760 | tf_op jit(solution)/shard_map/concatenate | solution.py:207
  11.9 0.8 %copy.21.rows_ref = bf16[256,320]{1,0:T(8,128)(2,1)} copy(bf16[256,320]{0,1:T(8,128)(2,1)S(1)} %pad_maximum_fusion.6) | data formatting | bytes 327680 | tf_op jit(solution)/shard_map/concatenate | solution.py:244
  13.7 3.6 %collective-permute-start.1 = (bf16[296,192]{1,0:T(8,128)(2,1)S(1)}, bf16[296,192]{1,0:T(8,128)(2,1)S(1)}, u32[]{:S(2)}, u32[]{:S(2)}) collective-permute-start(bf16[296,192]{1,0:T(8,128)(2,1)S(1)} %fusion.6), channel_id=1, source_target_pairs={{2,4},{6,8},{10,12},{0,14},{4,2},{8,6},{12,10},{14,0},{3,5},{7,9},... | collective-permute-start | bytes 341000 | tf_op jit(solution)/shard_map/ppermute | solution.py:62
  17.4 0.8 %pad_maximum_fusion.1.cols_ref = bf16[640,192]{1,0:T(8,128)(2,1)} fusion(bf16[320,192]{1,0:T(8,128)(2,1)S(1)} %get-tuple-element.33, bf16[320,192]{1,0:T(8,128)(2,1)S(1)} %get-tuple-element.31), kind=kLoop, calls=%fused_computation.8 | loop fusion | flops 491520 | bytes 491520 | tf_op jit(solution)/shard_map/concatenate | solution.py:243
  18.1 3.7 %collective-permute-done.1 = bf16[296,192]{1,0:T(8,128)(2,1)S(1)} collective-permute-done((bf16[296,192]{1,0:T(8,128)(2,1)S(1)}, bf16[296,192]{1,0:T(8,128)(2,1)S(1)}, u32[]{:S(2)}, u32[]{:S(2)}) %collective-permute-start.1) | collective-permute-done | bytes 113696 | tf_op jit(solution)/shard_map/ppermute | solution.py:62
  22.1 0.6 %collective-permute-start.3 = (bf16[200,192]{1,0:T(8,128)(2,1)S(1)}, bf16[200,192]{1,0:T(8,128)(2,1)S(1)}, u32[]{:S(2)}, u32[]{:S(2)}) collective-permute-start(bf16[200,192]{1,0:T(8,128)(2,1)S(1)} %get-tuple-element.36), channel_id=1, source_target_pairs={{0,1},{1,0},{2,3},{3,2},{4,5},{5,4},{6,7},{7,6},{8,9},{9,8},{10,11... | collective-permute-start | bytes 230408 | tf_op jit(solution)/shard_map/ppermute | solution.py:92
  22.7 0.9 %collective-permute-start.2 = (bf16[400,192]{1,0:T(8,128)(2,1)S(1)}, bf16[400,192]{1,0:T(8,128)(2,1)S(1)}, u32[]{:S(2)}, u32[]{:S(2)}) collective-permute-start(bf16[400,192]{1,0:T(8,128)(2,1)S(1)} %pad_maximum_fusion.3), channel_id=1, source_target_pairs={{0,8},{14,6},{2,10},{4,12},{8,0},{6,14},{10,2},{12,4},{1,9},{15,7}... | collective-permute-start | bytes 460808 | tf_op jit(solution)/shard_map/ppermute | solution.py:62
  23.6 0.4 fusion
  24.0 0.4 convolution_convert_fusion
  24.4 0.3 fusion.16
  25.1 1.0 %fusion.2.spec_i_ref = bf16[320,320]{1,0:T(8,128)(2,1)} fusion(f32[320,320]{1,0:T(8,128)S(1)} %fusion.16, bf16[320,320]{0,1:T(8,128)(2,1)S(1)} %copy-done, bf16[320,320]{1,0:T(8,128)(2,1)S(1)} %convolution_convert_fusion), kind=kOutput, calls=%fused_computation.6 | convolution fusion | flops 65740800 | bytes 1024000 | tf_op jit(solution)/shard_map/dot_general | solution.py:41
  26.1 1.1 %fusion.1.spec_r_ref = bf16[320,320]{1,0:T(8,128)(2,1)} fusion(f32[320,320]{1,0:T(8,128)S(1)} %fusion.15, bf16[320,320]{0,1:T(8,128)(2,1)S(1)} %copy-done, bf16[320,320]{1,0:T(8,128)(2,1)S(1)} %fusion), kind=kOutput, calls=%fused_computation.5 | convolution fusion | flops 65740800 | bytes 1024000 | tf_op jit(solution)/shard_map/dot_general | solution.py:41
  27.2 0.7 %fusion.10.ids_ref = s32[4]{0:T(128)} fusion(bf16[4,200,192]{2,1,0:T(8,128)(2,1)S(1)} %bitcast.30), kind=kLoop, calls=%fused_computation.38 | loop fusion | flops 4 | bytes 24 | tf_op jit(solution)/shard_map/convert_element_type | solution.py:255
  27.9 8.4 %shard_map.94 = (f32[128,128]{1,0:T(8,128)}, f32[128,128]{1,0:T(8,128)}, f32[128,128]{1,0:T(8,128)}) custom-call(s32[4]{0:T(128)} %fusion.10.ids_ref, s32[1]{0:T(128)} %bitcast.24.live_ref, bf16[4,200,192]{2,1,0:T(8,128)(2,1)} %bitcast.31, f32[8,320,320]{2,1,0:T(8,128)} %ctf_ref.3, bf16[320,320]{1,0:T(8,128)(2,1)} %fusion.1.spec_r_ref, ...), custom_call_target="tpu_custom_call" | custom-call | tf_op jit(solution)/shard_map/pallas_call | solution.py:184
  36.5 1.4 %collective-permute-done.5 = bf16[400,192]{1,0:T(8,128)(2,1)S(1)} collective-permute-done((bf16[400,192]{1,0:T(8,128)(2,1)S(1)}, bf16[400,192]{1,0:T(8,128)(2,1)S(1)}, u32[]{:S(2)}, u32[]{:S(2)}) %collective-permute-start.5) | collective-permute-done | bytes 153632 | tf_op jit(solution)/shard_map/ppermute | solution.py:261
  38.0 0.7 %fusion.9.ids_ref = s32[4]{0:T(128)} fusion(bf16[4,200,192]{2,1,0:T(8,128)(2,1)S(1)} %bitcast.26), kind=kLoop, calls=%fused_computation.36 | loop fusion | flops 4 | bytes 24 | tf_op jit(solution)/shard_map/convert_element_type | solution.py:255
  38.7 8.6 %shard_map.95 = (f32[128,128]{1,0:T(8,128)}, f32[128,128]{1,0:T(8,128)}, f32[128,128]{1,0:T(8,128)}) custom-call(s32[4]{0:T(128)} %fusion.9.ids_ref, s32[1]{0:T(128)} %bitcast.25.live_ref, bf16[4,200,192]{2,1,0:T(8,128)(2,1)} %bitcast.27, f32[8,320,320]{2,1,0:T(8,128)} %ctf_ref.3, ...), custom_call_target="tpu_custom_call", output_to_operand_aliasing={{0}: (12, {}), {1}: (13, {}), {2}: (14, {})} | custom-call | tf_op jit(solution)/shard_map/pallas_call | solution.py:184
  (35 shorter events, 1.4 us)
Async XLA Ops:
  0.6 23.0 %copy-start = (bf16[320,320]{0,1:T(8,128)(2,1)S(1)}, bf16[320,320]{0,1:T(8,128)(2,1)}, u32[]{:S(2)}) copy-start(bf16[320,320]{0,1:T(8,128)(2,1)} %constant.43.clone) | copy-start | bytes 614404
  0.6 21.2 %copy-start.5 = (bf16[128,128]{1,0:T(8,128)(2,1)S(1)}, bf16[128,128]{1,0:T(8,128)(2,1)}, u32[]{:S(2)}) copy-start(bf16[128,128]{1,0:T(8,128)(2,1)} %param.7) | copy-start | bytes 98308
  0.7 12.8 %copy-start.3 = (bf16[1,192,192]{2,1,0:T(8,128)(2,1)S(1)}, bf16[1,192,192]{2,1,0:T(8,128)(2,1)}, u32[]{:S(2)}) copy-start(bf16[1,192,192]{2,1,0:T(8,128)(2,1)} %param.8) | copy-start | bytes 221188
  3.1 10.2 %collective-permute-start = (bf16[296,192]{1,0:T(8,128)(2,1)S(1)}, bf16[296,192]{1,0:T(8,128)(2,1)S(1)}, u32[]{:S(2)}, u32[]{:S(2)}) collective-permute-start(bf16[296,192]{1,0:T(8,128)(2,1)S(1)} %fusion.5), channel_id=1, source_target_pairs={{0,2},{4,6},{8,10},{12,14},{2,0},{6,4},{10,8},{14,12},{1,3},{5,7},... | collective-permute-start | bytes 341000 | tf_op jit(solution)/shard_map/ppermute | solution.py:62
  7.0 16.9 %copy-start.1 = (bf16[320,320]{0,1:T(8,128)(2,1)S(1)}, bf16[320,320]{0,1:T(8,128)(2,1)}, u32[]{:S(2)}) copy-start(bf16[320,320]{0,1:T(8,128)(2,1)} %constant.42.clone) | copy-start | bytes 614404
  13.7 8.2 %collective-permute-start.1 = (bf16[296,192]{1,0:T(8,128)(2,1)S(1)}, bf16[296,192]{1,0:T(8,128)(2,1)S(1)}, u32[]{:S(2)}, u32[]{:S(2)}) collective-permute-start(bf16[296,192]{1,0:T(8,128)(2,1)S(1)} %fusion.6), channel_id=1, source_target_pairs={{2,4},{6,8},{10,12},{0,14},{4,2},{8,6},{12,10},{14,0},{3,5},{7,9},... | collective-permute-start | bytes 341000 | tf_op jit(solution)/shard_map/ppermute | solution.py:62
  22.0 1.6 %collective-permute-start.4 = (bf16[320,96]{1,0:T(8,128)(2,1)S(1)}, bf16[320,96]{1,0:T(8,128)(2,1)S(1)}, u32[]{:S(2)}, u32[]{:S(2)}) collective-permute-start(bf16[320,96]{1,0:T(8,128)(2,1)S(1)} %slice_select_fusion), channel_id=1, source_target_pairs={{0,1},{1,0},{2,3},{3,2},{4,5},{5,4},{6,7},{7,6},{8,9},{9,8},{10,11... | collective-permute-start | bytes 184328 | tf_op jit(solution)/shard_map/ppermute | solution.py:225
  22.1 5.1 %collective-permute-start.3 = (bf16[200,192]{1,0:T(8,128)(2,1)S(1)}, bf16[200,192]{1,0:T(8,128)(2,1)S(1)}, u32[]{:S(2)}, u32[]{:S(2)}) collective-permute-start(bf16[200,192]{1,0:T(8,128)(2,1)S(1)} %get-tuple-element.36), channel_id=1, source_target_pairs={{0,1},{1,0},{2,3},{3,2},{4,5},{5,4},{6,7},{7,6},{8,9},{9,8},{10,11... | collective-permute-start | bytes 230408 | tf_op jit(solution)/shard_map/ppermute | solution.py:92
  22.7 13.7 %collective-permute-start.2 = (bf16[400,192]{1,0:T(8,128)(2,1)S(1)}, bf16[400,192]{1,0:T(8,128)(2,1)S(1)}, u32[]{:S(2)}, u32[]{:S(2)}) collective-permute-start(bf16[400,192]{1,0:T(8,128)(2,1)S(1)} %pad_maximum_fusion.3), channel_id=1, source_target_pairs={{0,8},{14,6},{2,10},{4,12},{8,0},{6,14},{10,2},{12,4},{1,9},{15,7}... | collective-permute-start | bytes 460808 | tf_op jit(solution)/shard_map/ppermute | solution.py:62
  27.2 0.8 %copy-start.4 = (bf16[800,192]{1,0:T(8,128)(2,1)}, bf16[800,192]{1,0:T(8,128)(2,1)S(1)}, u32[]{:S(2)}) copy-start(bf16[800,192]{1,0:T(8,128)(2,1)S(1)} %constant_dynamic-update-slice_fusion) | copy-start | bytes 921604
  36.4 1.5 %collective-permute-start.5 = (bf16[400,192]{1,0:T(8,128)(2,1)S(1)}, bf16[400,192]{1,0:T(8,128)(2,1)S(1)}, u32[]{:S(2)}, u32[]{:S(2)}) collective-permute-start(bf16[400,192]{1,0:T(8,128)(2,1)S(1)} %collective-permute-done.2), channel_id=1, source_target_pairs={{0,1},{1,0},{2,3},{3,2},{4,5},{5,4},{6,7},{7,6},{8,9},{9,8},{10,11... | collective-permute-start | bytes 460808 | tf_op jit(solution)/shard_map/ppermute | solution.py:261
  38.0 0.8 %copy-start.2 = (bf16[800,192]{1,0:T(8,128)(2,1)}, bf16[800,192]{1,0:T(8,128)(2,1)S(1)}, u32[]{:S(2)}) copy-start(bf16[800,192]{1,0:T(8,128)(2,1)S(1)} %pad_maximum_fusion) | copy-start | bytes 921604

commit v15 on v11

--- a/solution.py
+++ b/solution.py
@@ -94,8 +94,8 @@
     return arrivals, jnp.concatenate([top, tile, bottom], axis=0)
 
 
-def correlate_kernel(ids_ref, live_ref, tmpl_ref, ctf_ref, spec_r_ref, spec_i_ref, cos_rows_ref, sin_rows_ref,
-                     cols_ref, rows_ref, col_cos_ref, col_sin_ref, *refs, scaling, total, block):
+def correlate_kernel(ids_ref, live_ref, tmpl_ref, other_ref, ctf_ref, spec_r_ref, spec_i_ref, cos_rows_ref,
+                     sin_rows_ref, cols_ref, rows_ref, col_cos_ref, col_sin_ref, *refs, scaling, total, block, first):
     if len(refs) == 6:
         prev_peak_ref, prev_sum_ref, prev_sq_ref, peak_ref, sum_ref, sq_ref = refs
     else:
@@ -107,7 +107,7 @@
     def mm(a, b):
         return jnp.dot(a, b, preferred_element_type=f32)
 
-    template = tmpl_ref[0]
+    template = jnp.where(o < first, tmpl_ref[0], other_ref[0])
     part_real = mm(template, cos_rows_ref[...]).astype(bf16)
     part_imag = (-mm(template, sin_rows_ref[...])).astype(bf16)
     cols = cols_ref[...]
@@ -158,14 +158,20 @@
             sq_ref[...] = jnp.where(live, sq_ref[...] / total, 0.0)
 
 
-def correlate(ids, live, all_templates, ctf, spec_real, spec_imag, tables, scaling, previous, total):
-    count = all_templates.shape[0]
-    box = all_templates.shape[2]
+def correlate(ids, live, pieces, ctf, spec_real, spec_imag, tables, scaling, previous, total):
+    pieces = list(pieces)
+    first = pieces[0].shape[0]
+    count = sum(piece.shape[0] for piece in pieces)
+    if len(pieces) == 1:
+        pieces.append(pieces[0])
+    last_other = pieces[1].shape[0] - 1
+    box = pieces[0].shape[2]
     n = ctf.shape[1]
     tile = tables[4].shape[1]
     full = lambda shape: pl.BlockSpec(shape, lambda o, ids, live: (0,) * len(shape))
     in_specs = [
-        pl.BlockSpec((1, box, box), lambda o, ids, live: (o, 0, 0)),
+        pl.BlockSpec((1, box, box), lambda o, ids, live: (jnp.minimum(o, first - 1), 0, 0)),
+        pl.BlockSpec((1, box, box), lambda o, ids, live: (jnp.clip(o - first, 0, last_other), 0, 0)),
         pl.BlockSpec((1, n, n), lambda o, ids, live: (ids[o], 0, 0)),
         full((n, n)),
         full((n, n)),
@@ -178,13 +184,14 @@
         out_specs=[out_block, out_block, out_block],
     )
     out_shape = [jax.ShapeDtypeStruct((tile, tile), jnp.float32)] * 3
+    kernel = functools.partial(correlate_kernel, scaling=scaling, total=total, block=RB, first=first)
     return pl.pallas_call(
-        functools.partial(correlate_kernel, scaling=scaling, total=total, block=RB),
+        kernel,
         grid_spec=grid_spec,
         out_shape=out_shape,
         compiler_params=pltpu.CompilerParams(dimension_semantics=("arbitrary",)),
-        input_output_aliases={6 + len(tables) + i: i for i in range(len(previous))},
-    )(ids, live, all_templates, ctf, spec_real, spec_imag, *tables, *previous)
+        input_output_aliases={7 + len(tables) + i: i for i in range(len(previous))},
+    )(ids, live, pieces[0], pieces[1], ctf, spec_real, spec_imag, *tables, *previous)
 
 
 def body(micrograph, templates, defocus, ctf, usable):
@@ -246,21 +253,20 @@
     stats = ()
     live = usable.reshape(-1)[:1]
 
-    def run(piece, stats, total=0):
-        count = piece.shape[0] // block_rows
-        piece = piece.reshape(count, block_rows, box_size)
-        piece_ids = piece[:, box_size, 0].astype(jnp.int32)
-        return correlate(piece_ids, live, piece, ctf, spec_real, spec_imag, tables, scaling, stats, total)
+    def run(pieces, stats, total=0):
+        pieces = [piece.reshape(piece.shape[0] // block_rows, block_rows, box_size) for piece in pieces]
+        piece_ids = jnp.concatenate([piece[:, box_size, 0] for piece in pieces]).astype(jnp.int32)
+        return correlate(piece_ids, live, pieces, ctf, spec_real, spec_imag, tables, scaling, stats, total)
 
     if split_last:
-        stats = run(arrivals[0], stats)
+        stats = run([arrivals[0]], stats)
         half, stats = lax.optimization_barrier((arrivals[1], stats))
         other_half = lax.ppermute(half, "tile", [(0, 1), (1, 0)])
         total = (arrivals[0].shape[0] + 2 * half.shape[0]) // block_rows
-        stats = run(jnp.concatenate([half, other_half], axis=0), stats, float(total))
+        stats = run([half, other_half], stats, float(total))
     else:
         for last, piece in enumerate(arrivals, 1 - len(arrivals)):
-            stats = run(piece, stats, 0 if last else float(total))
+            stats = run([piece], stats, 0 if last else float(total))
     return stats
 
 

time: 45.7 us -> 45.8 us (level)
  the two profiles are of different devices: /device:TPU:15 before, /device:TPU:11 now
where the time goes in v15:
time: 45.8 us; the launch traced here: 45.4 us
  Pallas kernels  17.2 us (38%)
  starting transfers between devices  8.85 us (19%)
  local copies, waits for them, and re-layouts  7.02 us (15%)
  matrix products  3.51 us (8%)
  other arithmetic  3.37 us (7%)
  waiting for transfers between devices  3.29 us (7%)
  between operations  2.19 us (5%)
    pallas_call x2, Pallas kernels, correlate(): pl.pallas_call(kernel, grid_spec=grid_spec, out_shape=out_shape, compiler...  17.2 us
    ppermute x3, starting transfers between devices, swap(): lax.ppermute(payload, 'orient', [(a, b) for a, b in pairs] + [(b, a) for...  5.96 us
    dot_general x6, matrix products, matmul(): return jnp.dot(left, right, preferred_element_type=jnp.float32)  3.51 us
    ppermute x1, starting transfers between devices, body(): got = lax.ppermute(edge, 'tile', [(0, 1), (1, 0)])  2.53 us
    ppermute x3, waiting for transfers between devices, swap(): lax.ppermute(payload, 'orient', [(a, b) for a, b in pairs] + [(b, a) for...  2.23 us
    transpose x1, local copies, waits for them, and re-layouts, body(): col_sin = row_sin.T  1.82 us
    convert_element_type x2, other arithmetic, run(): jnp.concatenate([piece[:, box_size, 0] for piece in pieces])  1.27 us
    slice x1, local copies, waits for them, and re-layouts, body(): sin_full[low:]  1.19 us
  transfers between devices with their start and end apart: 5, of which 3 were waited for; matrix products, arithmetic and copies ran while one was open for 24% of the time, Pallas kernels for 19%

profile of v15, /device:TPU:11, one launch (start us, length us, event | category | flops | bytes accessed | tf_op | source)
XLA Modules:
  0.0 45.4 jit_solution(2691448449506690810)
XLA Ops:
  0.7 0.8 %broadcast_select_fusion.3 = (bf16[96,128]{1,0:T(8,128)(2,1)S(1)}, bf16[96,128]{1,0:T(8,128)(2,1)S(1)}) fusion(pred[]{:T(512)S(6)} %eq.16, bf16[128,128]{1,0:T(8,128)(2,1)} %param.7), kind=kLoop, calls=%fused_computation.22 | loop fusion | flops 24576 | bytes 98305 | tf_op jit(solution)/shard_map/jit(_where)/select_n | solution.py:79
  2.2 1.0 %pad_bitcast_fusion = bf16[200,192]{1,0:T(8,128)(2,1)S(1)} fusion(bf16[1,192,192]{2,1,0:T(8,128)(2,1)} %param.8, bf16[]{:T(256)} %bitcast), kind=kLoop, calls=%fused_computation.15 | loop fusion | bytes 150530 | tf_op jit(solution)/shard_map/reshape | solution.py:222
  3.6 1.2 %fusion.8 = (bf16[96,320]{0,1:T(8,128)(2,1)S(1)}, bf16[96,320]{0,1:T(8,128)(2,1)S(1)}, bf16[96,320]{0,1:T(8,128)(2,1)S(1)}, bf16[96,320]{0,1:T(8,128)(2,1)S(1)}) fusion(bf16[320,320]{0,1:T(8,128)(2,1)} %constant.37.clone, bf16[320,320]{0,1:T(8,128)(2,1)} %constant.36.clone), kind=kLoop, calls=%fused_computation.38 | loop fusion | bytes 491520 | tf_op jit(solution)/shard_map/slice | solution.py:211
  4.8 1.8 %slice_bitcast_fusion = (bf16[320,128]{1,0:T(8,128)(2,1)}, bf16[128,320]{0,1:T(8,128)(2,1)S(1)}, bf16[128,320]{0,1:T(8,128)(2,1)S(1)}, bf16[320,128]{1,0:T(8,128)(2,1)}) fusion(bf16[320,320]{0,1:T(8,128)(2,1)} %constant.37.clone, bf16[320,320]{0,1:T(8,128)(2,1)} %constant.36.clone), kind=kLoop, calls=%fused_computation.34 | loop fusion | bytes 491520 | tf_op jit(solution)/shard_map/transpose | solution.py:217
  6.9 0.8 %collective-permute-done = bf16[264,192]{1,0:T(8,128)(2,1)S(1)} collective-permute-done((bf16[264,192]{1,0:T(8,128)(2,1)S(1)}, bf16[264,192]{1,0:T(8,128)(2,1)S(1)}, u32[]{:S(2)}, u32[]{:S(2)}) %collective-permute-start) | collective-permute-done | bytes 101408 | tf_op jit(solution)/shard_map/ppermute | solution.py:62
  7.8 1.5 %collective-permute-start.1 = (bf16[464,192]{1,0:T(8,128)(2,1)S(1)}, bf16[464,192]{1,0:T(8,128)(2,1)S(1)}, u32[]{:S(2)}, u32[]{:S(2)}) collective-permute-start(bf16[464,192]{1,0:T(8,128)(2,1)S(1)} %pad_maximum_fusion.3), channel_id=1, source_target_pairs={{2,4},{6,8},{10,12},{0,14},{4,2},{8,6},{12,10},{14,0},{3,5},{7,9},... | collective-permute-start | bytes 534536 | tf_op jit(solution)/shard_map/ppermute | solution.py:62
  9.3 0.8 %copy.19.cos_rows_ref = bf16[192,320]{1,0:T(8,128)(2,1)} copy(bf16[192,320]{0,1:T(8,128)(2,1)S(1)} %get-tuple-element.32) | data formatting | bytes 245760 | tf_op jit(solution)/shard_map/concatenate | solution.py:210
  10.1 0.8 %copy.20.sin_rows_ref = bf16[192,320]{1,0:T(8,128)(2,1)} copy(bf16[192,320]{0,1:T(8,128)(2,1)S(1)} %get-tuple-element.34) | data formatting | bytes 245760 | tf_op jit(solution)/shard_map/concatenate | solution.py:211
  10.9 0.8 %copy.21.rows_ref = bf16[256,320]{1,0:T(8,128)(2,1)} copy(bf16[256,320]{0,1:T(8,128)(2,1)S(1)} %pad_maximum_fusion.6) | data formatting | bytes 327680 | tf_op jit(solution)/shard_map/concatenate | solution.py:248
  12.3 0.8 %pad_maximum_fusion.1.cols_ref = bf16[640,192]{1,0:T(8,128)(2,1)} fusion(bf16[320,192]{1,0:T(8,128)(2,1)S(1)} %get-tuple-element.33, bf16[320,192]{1,0:T(8,128)(2,1)S(1)} %get-tuple-element.31), kind=kLoop, calls=%fused_computation.8 | loop fusion | flops 491520 | bytes 491520 | tf_op jit(solution)/shard_map/concatenate | solution.py:247
  13.1 1.4 %collective-permute-done.1 = bf16[464,192]{1,0:T(8,128)(2,1)S(1)} collective-permute-done((bf16[464,192]{1,0:T(8,128)(2,1)S(1)}, bf16[464,192]{1,0:T(8,128)(2,1)S(1)}, u32[]{:S(2)}, u32[]{:S(2)}) %collective-permute-start.1) | collective-permute-done | bytes 178208 | tf_op jit(solution)/shard_map/ppermute | solution.py:62
  14.9 2.5 %collective-permute-start.3 = (bf16[320,96]{1,0:T(8,128)(2,1)S(1)}, bf16[320,96]{1,0:T(8,128)(2,1)S(1)}, u32[]{:S(2)}, u32[]{:S(2)}) collective-permute-start(bf16[320,96]{1,0:T(8,128)(2,1)S(1)} %slice_select_fusion), channel_id=1, source_target_pairs={{0,1},{1,0},{2,3},{3,2},{4,5},{5,4},{6,7},{7,6},{8,9},{9,8},{10,11... | collective-permute-start | bytes 184328 | tf_op jit(solution)/shard_map/ppermute | solution.py:229
  17.5 4.2 %collective-permute-start.2 = (bf16[400,192]{1,0:T(8,128)(2,1)S(1)}, bf16[400,192]{1,0:T(8,128)(2,1)S(1)}, u32[]{:S(2)}, u32[]{:S(2)}) collective-permute-start(bf16[400,192]{1,0:T(8,128)(2,1)S(1)} %constant_dynamic-slice_fusion), channel_id=1, source_target_pairs={{0,8},{14,6},{2,10},{4,12},{8,0},{6,14},{10,2},{12,4},{1,9},{15,7}... | collective-permute-start | bytes 460808 | tf_op jit(solution)/shard_map/ppermute | solution.py:62
  21.7 0.7 %fusion.3.ids_ref = s32[4]{0:T(128)} fusion(bf16[4,200,192]{2,1,0:T(8,128)(2,1)S(1)} %bitcast.27), kind=kLoop, calls=%fused_computation.27 | loop fusion | flops 4 | bytes 24 | tf_op jit(solution)/shard_map/convert_element_type | solution.py:258
  22.4 0.4 fusion
  22.8 0.4 convolution_convert_fusion
  23.2 0.3 fusion.11
  23.9 1.0 %fusion.2.spec_i_ref = bf16[320,320]{1,0:T(8,128)(2,1)} fusion(f32[320,320]{1,0:T(8,128)S(1)} %fusion.11, bf16[320,320]{0,1:T(8,128)(2,1)S(1)} %copy-done.1, bf16[320,320]{1,0:T(8,128)(2,1)S(1)} %convolution_convert_fusion), kind=kOutput, calls=%fused_computation.6 | convolution fusion | flops 65740800 | bytes 1024000 | tf_op jit(solution)/shard_map/dot_general | solution.py:41
  24.9 1.0 %fusion.1.spec_r_ref = bf16[320,320]{1,0:T(8,128)(2,1)} fusion(f32[320,320]{1,0:T(8,128)S(1)} %fusion.10, bf16[320,320]{0,1:T(8,128)(2,1)S(1)} %copy-done.1, bf16[320,320]{1,0:T(8,128)(2,1)S(1)} %fusion), kind=kOutput, calls=%fused_computation.5 | convolution fusion | flops 65740800 | bytes 1024000 | tf_op jit(solution)/shard_map/dot_general | solution.py:41
  26.0 8.5 %shard_map.94 = (f32[128,128]{1,0:T(8,128)}, f32[128,128]{1,0:T(8,128)}, f32[128,128]{1,0:T(8,128)}) custom-call(s32[4]{0:T(128)} %fusion.3.ids_ref, s32[1]{0:T(128)} %bitcast.25.live_ref, bf16[4,200,192]{2,1,0:T(8,128)(2,1)} %bitcast.28, bf16[4,200,192]{2,1,0:T(8,128)(2,1)} %bitcast.29, f32[8,320,320]{2,1,0:T(8,128)} %ctf_ref.3, ...), custom_call_target="tpu_custom_call" | custom-call | tf_op jit(solution)/shard_map/pallas_call | solution.py:188
  34.5 0.4 collective-permute-start.4
  35.0 1.1 %collective-permute-done.4 = bf16[400,192]{1,0:T(8,128)(2,1)S(1)} collective-permute-done((bf16[400,192]{1,0:T(8,128)(2,1)S(1)}, bf16[400,192]{1,0:T(8,128)(2,1)S(1)}, u32[]{:S(2)}, u32[]{:S(2)}) %collective-permute-start.4) | collective-permute-done | bytes 153632 | tf_op jit(solution)/shard_map/ppermute | solution.py:264
  36.2 0.6 %maximum_convert_fusion.ids_ref = s32[4]{0:T(128)} fusion(bf16[2]{0:T(256)(128)(2,1)S(1)} %slice_reduce_fusion, bf16[2]{0:T(256)(128)(2,1)S(1)} %slice_reduce_fusion.1), kind=kLoop, calls=%fused_computation.30 | loop fusion | flops 16 | bytes 24 | tf_op jit(solution)/shard_map/convert_element_type | solution.py:258
  36.8 8.7 %shard_map.95 = (f32[128,128]{1,0:T(8,128)}, f32[128,128]{1,0:T(8,128)}, f32[128,128]{1,0:T(8,128)}) custom-call(s32[4]{0:T(128)} %maximum_convert_fusion.ids_ref, s32[1]{0:T(128)} %bitcast.26.live_ref, bf16[2,200,192]{2,1,0:T(8,128)(2,1)} %bitcast.31, bf16[2,200,192]{2,1,0:T(8,128)(2,1)} %bitcast.33, ...), custom_call_target="tpu_custom_call", output_to_operand_aliasing={{0}: (13, {}), {1}: (14, {}), {2}: (15, {})} | custom-call | tf_op jit(solution)/shard_map/pallas_call | solution.py:188
  (37 shorter events, 1.9 us)
Async XLA Ops:
  0.6 14.0 %copy-start.3 = (bf16[128,128]{1,0:T(8,128)(2,1)S(1)}, bf16[128,128]{1,0:T(8,128)(2,1)}, u32[]{:S(2)}) copy-start(bf16[128,128]{1,0:T(8,128)(2,1)} %param.7) | copy-start | bytes 98308
  2.2 20.2 %copy-start.1 = (bf16[320,320]{0,1:T(8,128)(2,1)S(1)}, bf16[320,320]{0,1:T(8,128)(2,1)}, u32[]{:S(2)}) copy-start(bf16[320,320]{0,1:T(8,128)(2,1)} %constant.37.clone) | copy-start | bytes 614404
  3.2 4.5 %collective-permute-start = (bf16[264,192]{1,0:T(8,128)(2,1)S(1)}, bf16[264,192]{1,0:T(8,128)(2,1)S(1)}, u32[]{:S(2)}, u32[]{:S(2)}) collective-permute-start(bf16[264,192]{1,0:T(8,128)(2,1)S(1)} %pad_maximum_fusion.7), channel_id=1, source_target_pairs={{0,2},{4,6},{8,10},{12,14},{2,0},{6,4},{10,8},{14,12},{1,3},{5,7},... | collective-permute-start | bytes 304136 | tf_op jit(solution)/shard_map/ppermute | solution.py:62
  4.7 18.1 %copy-start.2 = (bf16[320,320]{0,1:T(8,128)(2,1)S(1)}, bf16[320,320]{0,1:T(8,128)(2,1)}, u32[]{:S(2)}) copy-start(bf16[320,320]{0,1:T(8,128)(2,1)} %constant.36.clone) | copy-start | bytes 614404
  7.8 6.7 %collective-permute-start.1 = (bf16[464,192]{1,0:T(8,128)(2,1)S(1)}, bf16[464,192]{1,0:T(8,128)(2,1)S(1)}, u32[]{:S(2)}, u32[]{:S(2)}) collective-permute-start(bf16[464,192]{1,0:T(8,128)(2,1)S(1)} %pad_maximum_fusion.3), channel_id=1, source_target_pairs={{2,4},{6,8},{10,12},{0,14},{4,2},{8,6},{12,10},{14,0},{3,5},{7,9},... | collective-permute-start | bytes 534536 | tf_op jit(solution)/shard_map/ppermute | solution.py:62
  14.9 7.5 %collective-permute-start.3 = (bf16[320,96]{1,0:T(8,128)(2,1)S(1)}, bf16[320,96]{1,0:T(8,128)(2,1)S(1)}, u32[]{:S(2)}, u32[]{:S(2)}) collective-permute-start(bf16[320,96]{1,0:T(8,128)(2,1)S(1)} %slice_select_fusion), channel_id=1, source_target_pairs={{0,1},{1,0},{2,3},{3,2},{4,5},{5,4},{6,7},{7,6},{8,9},{9,8},{10,11... | collective-permute-start | bytes 184328 | tf_op jit(solution)/shard_map/ppermute | solution.py:229
  17.5 8.5 %copy-start = (bf16[800,192]{1,0:T(8,128)(2,1)}, bf16[800,192]{1,0:T(8,128)(2,1)S(1)}, u32[]{:S(2)}) copy-start(bf16[800,192]{1,0:T(8,128)(2,1)S(1)} %pad_maximum_fusion) | copy-start | bytes 921604
  17.5 17.0 %collective-permute-start.2 = (bf16[400,192]{1,0:T(8,128)(2,1)S(1)}, bf16[400,192]{1,0:T(8,128)(2,1)S(1)}, u32[]{:S(2)}, u32[]{:S(2)}) collective-permute-start(bf16[400,192]{1,0:T(8,128)(2,1)S(1)} %constant_dynamic-slice_fusion), channel_id=1, source_target_pairs={{0,8},{14,6},{2,10},{4,12},{8,0},{6,14},{10,2},{12,4},{1,9},{15,7}... | collective-permute-start | bytes 460808 | tf_op jit(solution)/shard_map/ppermute | solution.py:62
  34.5 2.2 %copy-start.4 = (bf16[400,192]{1,0:T(8,128)(2,1)}, bf16[400,192]{1,0:T(8,128)(2,1)S(1)}, u32[]{:S(2)}) copy-start(bf16[400,192]{1,0:T(8,128)(2,1)S(1)} %collective-permute-done.2) | copy-start | bytes 460804
  34.5 1.5 %collective-permute-start.4 = (bf16[400,192]{1,0:T(8,128)(2,1)S(1)}, bf16[400,192]{1,0:T(8,128)(2,1)S(1)}, u32[]{:S(2)}, u32[]{:S(2)}) collective-permute-start(bf16[400,192]{1,0:T(8,128)(2,1)S(1)} %collective-permute-done.2), channel_id=1, source_target_pairs={{0,1},{1,0},{2,3},{3,2},{4,5},{5,4},{6,7},{7,6},{8,9},{9,8},{10,11... | collective-permute-start | bytes 460808 | tf_op jit(solution)/shard_map/ppermute | solution.py:264
  36.1 0.7 %copy-start.5 = (bf16[400,192]{1,0:T(8,128)(2,1)}, bf16[400,192]{1,0:T(8,128)(2,1)S(1)}, u32[]{:S(2)}) copy-start(bf16[400,192]{1,0:T(8,128)(2,1)S(1)} %collective-permute-done.4) | copy-start | bytes 460804

commit v16 on v15

--- a/solution.py
+++ b/solution.py
@@ -94,8 +94,12 @@
     return arrivals, jnp.concatenate([top, tile, bottom], axis=0)
 
 
-def correlate_kernel(ids_ref, live_ref, tmpl_ref, other_ref, ctf_ref, spec_r_ref, spec_i_ref, cos_rows_ref,
-                     sin_rows_ref, cols_ref, rows_ref, col_cos_ref, col_sin_ref, *refs, scaling, total, block, first):
+def correlate_kernel(ids_ref, live_ref, tmpl_ref, other_ref, *refs, scaling, total, block, first, group):
+    ctf_refs = refs[:group]
+    (spec_r_ref, spec_i_ref, cos_rows_ref, sin_rows_ref, cols_ref, rows_ref, col_cos_ref, col_sin_ref) = refs[
+        group : group + 8
+    ]
+    refs = refs[group + 8 :]
     if len(refs) == 6:
         prev_peak_ref, prev_sum_ref, prev_sq_ref, peak_ref, sum_ref, sq_ref = refs
     else:
@@ -107,46 +111,56 @@
     def mm(a, b):
         return jnp.dot(a, b, preferred_element_type=f32)
 
-    template = jnp.where(o < first, tmpl_ref[0], other_ref[0])
-    part_real = mm(template, cos_rows_ref[...]).astype(bf16)
-    part_imag = (-mm(template, sin_rows_ref[...])).astype(bf16)
-    cols = cols_ref[...]
-    n = cols.shape[0] // 2
-    from_real = mm(cols, part_real)
-    from_imag = mm(cols, part_imag)
-    full_real = from_real[:n] + from_imag[n:]
-    full_imag = from_imag[:n] - from_real[n:]
-    weight = ctf_ref[0]
-    w_real = (full_real * weight).astype(bf16).astype(f32)
-    w_imag = (full_imag * weight).astype(bf16).astype(f32)
-    spec_real = spec_r_ref[...].astype(f32)
-    spec_imag = spec_i_ref[...].astype(f32)
-    prod_real = (spec_real * w_real + spec_imag * w_imag).astype(bf16)
-    prod_imag = (spec_imag * w_real - spec_real * w_imag).astype(bf16)
-    rows = rows_ref[...]
-    tile = rows.shape[0] // 2
-    left_from_real = mm(rows, prod_real)
-    left_from_imag = mm(rows, prod_imag)
-    left_real = (left_from_real[:tile] - left_from_imag[tile:]).astype(bf16)
-    left_imag = (left_from_imag[:tile] + left_from_real[tile:]).astype(bf16)
-    corr = (mm(left_real, col_cos_ref[...]) - mm(left_imag, col_sin_ref[...])) * scaling
+    def one(g):
+        template = jnp.where(o < first, tmpl_ref[g], other_ref[g])
+        part_real = mm(template, cos_rows_ref[...]).astype(bf16)
+        part_imag = (-mm(template, sin_rows_ref[...])).astype(bf16)
+        cols = cols_ref[...]
+        n = cols.shape[0] // 2
+        from_real = mm(cols, part_real)
+        from_imag = mm(cols, part_imag)
+        full_real = from_real[:n] + from_imag[n:]
+        full_imag = from_imag[:n] - from_real[n:]
+        weight = ctf_refs[g][0]
+        w_real = (full_real * weight).astype(bf16).astype(f32)
+        w_imag = (full_imag * weight).astype(bf16).astype(f32)
+        spec_real = spec_r_ref[...].astype(f32)
+        spec_imag = spec_i_ref[...].astype(f32)
+        prod_real = (spec_real * w_real + spec_imag * w_imag).astype(bf16)
+        prod_imag = (spec_imag * w_real - spec_real * w_imag).astype(bf16)
+        rows = rows_ref[...]
+        tile = rows.shape[0] // 2
+        left_from_real = mm(rows, prod_real)
+        left_from_imag = mm(rows, prod_imag)
+        left_real = (left_from_real[:tile] - left_from_imag[tile:]).astype(bf16)
+        left_imag = (left_from_imag[:tile] + left_from_real[tile:]).astype(bf16)
+        return (mm(left_real, col_cos_ref[...]) - mm(left_imag, col_sin_ref[...])) * scaling
+
+    corrs = [one(g) for g in range(group)]
+    step_peak = corrs[0]
+    step_sum = corrs[0]
+    step_sq = corrs[0] * corrs[0]
+    for corr in corrs[1:]:
+        step_peak = jnp.maximum(step_peak, corr)
+        step_sum = step_sum + corr
+        step_sq = step_sq + corr * corr
 
     @pl.when(o == 0)
     def _():
         if len(refs) == 6:
-            peak_ref[...] = jnp.maximum(prev_peak_ref[...], corr)
-            sum_ref[...] = prev_sum_ref[...] + corr
-            sq_ref[...] = prev_sq_ref[...] + corr * corr
+            peak_ref[...] = jnp.maximum(prev_peak_ref[...], step_peak)
+            sum_ref[...] = prev_sum_ref[...] + step_sum
+            sq_ref[...] = prev_sq_ref[...] + step_sq
         else:
-            peak_ref[...] = corr
-            sum_ref[...] = corr
-            sq_ref[...] = corr * corr
+            peak_ref[...] = step_peak
+            sum_ref[...] = step_sum
+            sq_ref[...] = step_sq
 
     @pl.when(o > 0)
     def _():
-        peak_ref[...] = jnp.maximum(peak_ref[...], corr)
-        sum_ref[...] = sum_ref[...] + corr
-        sq_ref[...] = sq_ref[...] + corr * corr
+        peak_ref[...] = jnp.maximum(peak_ref[...], step_peak)
+        sum_ref[...] = sum_ref[...] + step_sum
+        sq_ref[...] = sq_ref[...] + step_sq
 
     if total:
         @pl.when(o == pl.num_programs(0) - 1)
@@ -160,38 +174,49 @@
 
 def correlate(ids, live, pieces, ctf, spec_real, spec_imag, tables, scaling, previous, total):
     pieces = list(pieces)
-    first = pieces[0].shape[0]
-    count = sum(piece.shape[0] for piece in pieces)
+    group = 2 if all(piece.shape[0] % 2 == 0 for piece in pieces) else 1
+    first = pieces[0].shape[0] // group
+    steps = sum(piece.shape[0] for piece in pieces) // group
     if len(pieces) == 1:
         pieces.append(pieces[0])
-    last_other = pieces[1].shape[0] - 1
+    last_other = pieces[1].shape[0] // group - 1
     box = pieces[0].shape[2]
     n = ctf.shape[1]
     tile = tables[4].shape[1]
     full = lambda shape: pl.BlockSpec(shape, lambda o, ids, live: (0,) * len(shape))
-    in_specs = [
-        pl.BlockSpec((1, box, box), lambda o, ids, live: (jnp.minimum(o, first - 1), 0, 0)),
-        pl.BlockSpec((1, box, box), lambda o, ids, live: (jnp.clip(o - first, 0, last_other), 0, 0)),
-        pl.BlockSpec((1, n, n), lambda o, ids, live: (ids[o], 0, 0)),
-        full((n, n)),
-        full((n, n)),
-    ] + [full(t.shape) for t in tables] + [full((tile, tile))] * len(previous)
+
+    def plane(g):
+        return pl.BlockSpec((1, n, n), lambda o, ids, live: (ids[o * group + g], 0, 0))
+
+    in_specs = (
+        [
+            pl.BlockSpec((group, box, box), lambda o, ids, live: (jnp.minimum(o, first - 1), 0, 0)),
+            pl.BlockSpec((group, box, box), lambda o, ids, live: (jnp.clip(o - first, 0, last_other), 0, 0)),
+        ]
+        + [plane(g) for g in range(group)]
+        + [full((n, n)), full((n, n))]
+        + [full(t.shape) for t in tables]
+        + [full((tile, tile))] * len(previous)
+    )
     out_block = full((tile, tile))
     grid_spec = pltpu.PrefetchScalarGridSpec(
         num_scalar_prefetch=2,
-        grid=(count,),
+        grid=(steps,),
         in_specs=in_specs,
         out_specs=[out_block, out_block, out_block],
     )
     out_shape = [jax.ShapeDtypeStruct((tile, tile), jnp.float32)] * 3
-    kernel = functools.partial(correlate_kernel, scaling=scaling, total=total, block=RB, first=first)
+    kernel = functools.partial(
+        correlate_kernel, scaling=scaling, total=total, block=RB, first=first, group=group
+    )
+    base = 4 + group + 2 + len(tables)
     return pl.pallas_call(
         kernel,
         grid_spec=grid_spec,
         out_shape=out_shape,
         compiler_params=pltpu.CompilerParams(dimension_semantics=("arbitrary",)),
-        input_output_aliases={7 + len(tables) + i: i for i in range(len(previous))},
-    )(ids, live, pieces[0], pieces[1], ctf, spec_real, spec_imag, *tables, *previous)
+        input_output_aliases={base + i: i for i in range(len(previous))},
+    )(ids, live, pieces[0], pieces[1], *([ctf] * group), spec_real, spec_imag, *tables, *previous)
 
 
 def body(micrograph, templates, defocus, ctf, usable):

time: 45.8 us -> 44.9 us (0.980)
  Pallas kernels: 17.2 us -> 16.4 us
    pallas_call x2, Pallas kernels: 17.2 us -> 16.4 us  [correlate(): pl.pallas_call(kernel, grid_spec=grid_spec, out_shape=out_shape, compiler...]
  transfers between devices with their start and end apart: 5 -> 5, of which waited for: 3 -> 3; matrix products, arithmetic and copies ran while one was open for 24% -> 24% of each run, Pallas kernels for 19% -> 18%
where the time goes in v16:
time: 44.9 us; the launch traced here: 44.6 us
  Pallas kernels  16.4 us (37%)
  starting transfers between devices  8.85 us (20%)
  local copies, waits for them, and re-layouts  7.02 us (16%)
  matrix products  3.51 us (8%)
  other arithmetic  3.37 us (8%)
  waiting for transfers between devices  3.29 us (7%)
  between operations  2.19 us (5%)
    pallas_call x2, Pallas kernels, correlate(): pl.pallas_call(kernel, grid_spec=grid_spec, out_shape=out_shape, compiler...  16.4 us
    ppermute x3, starting transfers between devices, swap(): lax.ppermute(payload, 'orient', [(a, b) for a, b in pairs] + [(b, a) for...  5.96 us
    dot_general x6, matrix products, matmul(): return jnp.dot(left, right, preferred_element_type=jnp.float32)  3.51 us
    ppermute x1, starting transfers between devices, body(): got = lax.ppermute(edge, 'tile', [(0, 1), (1, 0)])  2.53 us
    ppermute x3, waiting for transfers between devices, swap(): lax.ppermute(payload, 'orient', [(a, b) for a, b in pairs] + [(b, a) for...  2.23 us
    transpose x1, local copies, waits for them, and re-layouts, body(): col_sin = row_sin.T  1.82 us
    convert_element_type x2, other arithmetic, run(): jnp.concatenate([piece[:, box_size, 0] for piece in pieces])  1.27 us
    slice x1, local copies, waits for them, and re-layouts, body(): sin_full[low:]  1.19 us
  transfers between devices with their start and end apart: 5, of which 3 were waited for; matrix products, arithmetic and copies ran while one was open for 24% of the time, Pallas kernels for 18%

profile of v16, /device:TPU:11, one launch (start us, length us, event | category | flops | bytes accessed | tf_op | source)
XLA Modules:
  0.0 44.6 jit_solution(6735054021497264539)
XLA Ops:
  0.7 0.8 %broadcast_select_fusion.3 = (bf16[96,128]{1,0:T(8,128)(2,1)S(1)}, bf16[96,128]{1,0:T(8,128)(2,1)S(1)}) fusion(pred[]{:T(512)S(6)} %eq.16, bf16[128,128]{1,0:T(8,128)(2,1)} %param.7), kind=kLoop, calls=%fused_computation.22 | loop fusion | flops 24576 | bytes 98305 | tf_op jit(solution)/shard_map/jit(_where)/select_n | solution.py:79
  2.2 1.0 %pad_bitcast_fusion = bf16[200,192]{1,0:T(8,128)(2,1)S(1)} fusion(bf16[1,192,192]{2,1,0:T(8,128)(2,1)} %param.8, bf16[]{:T(256)} %bitcast), kind=kLoop, calls=%fused_computation.15 | loop fusion | bytes 150530 | tf_op jit(solution)/shard_map/reshape | solution.py:247
  3.6 1.2 %fusion.8 = (bf16[96,320]{0,1:T(8,128)(2,1)S(1)}, bf16[96,320]{0,1:T(8,128)(2,1)S(1)}, bf16[96,320]{0,1:T(8,128)(2,1)S(1)}, bf16[96,320]{0,1:T(8,128)(2,1)S(1)}) fusion(bf16[320,320]{0,1:T(8,128)(2,1)} %constant.37.clone, bf16[320,320]{0,1:T(8,128)(2,1)} %constant.36.clone), kind=kLoop, calls=%fused_computation.38 | loop fusion | bytes 491520 | tf_op jit(solution)/shard_map/slice | solution.py:236
  4.8 1.8 %slice_bitcast_fusion = (bf16[320,128]{1,0:T(8,128)(2,1)}, bf16[128,320]{0,1:T(8,128)(2,1)S(1)}, bf16[128,320]{0,1:T(8,128)(2,1)S(1)}, bf16[320,128]{1,0:T(8,128)(2,1)}) fusion(bf16[320,320]{0,1:T(8,128)(2,1)} %constant.37.clone, bf16[320,320]{0,1:T(8,128)(2,1)} %constant.36.clone), kind=kLoop, calls=%fused_computation.34 | loop fusion | bytes 491520 | tf_op jit(solution)/shard_map/transpose | solution.py:242
  6.9 0.8 %collective-permute-done = bf16[264,192]{1,0:T(8,128)(2,1)S(1)} collective-permute-done((bf16[264,192]{1,0:T(8,128)(2,1)S(1)}, bf16[264,192]{1,0:T(8,128)(2,1)S(1)}, u32[]{:S(2)}, u32[]{:S(2)}) %collective-permute-start) | collective-permute-done | bytes 101408 | tf_op jit(solution)/shard_map/ppermute | solution.py:62
  7.8 1.5 %collective-permute-start.1 = (bf16[464,192]{1,0:T(8,128)(2,1)S(1)}, bf16[464,192]{1,0:T(8,128)(2,1)S(1)}, u32[]{:S(2)}, u32[]{:S(2)}) collective-permute-start(bf16[464,192]{1,0:T(8,128)(2,1)S(1)} %pad_maximum_fusion.3), channel_id=1, source_target_pairs={{2,4},{6,8},{10,12},{0,14},{4,2},{8,6},{12,10},{14,0},{3,5},{7,9},... | collective-permute-start | bytes 534536 | tf_op jit(solution)/shard_map/ppermute | solution.py:62
  9.3 0.8 %copy.19.refs_4_ = bf16[192,320]{1,0:T(8,128)(2,1)} copy(bf16[192,320]{0,1:T(8,128)(2,1)S(1)} %get-tuple-element.32) | data formatting | bytes 245760 | tf_op jit(solution)/shard_map/concatenate | solution.py:235
  10.1 0.8 %copy.20.refs_5_ = bf16[192,320]{1,0:T(8,128)(2,1)} copy(bf16[192,320]{0,1:T(8,128)(2,1)S(1)} %get-tuple-element.34) | data formatting | bytes 245760 | tf_op jit(solution)/shard_map/concatenate | solution.py:236
  10.9 0.8 %copy.21.refs_7_ = bf16[256,320]{1,0:T(8,128)(2,1)} copy(bf16[256,320]{0,1:T(8,128)(2,1)S(1)} %pad_maximum_fusion.6) | data formatting | bytes 327680 | tf_op jit(solution)/shard_map/concatenate | solution.py:273
  12.3 0.8 %pad_maximum_fusion.1.refs_6_ = bf16[640,192]{1,0:T(8,128)(2,1)} fusion(bf16[320,192]{1,0:T(8,128)(2,1)S(1)} %get-tuple-element.33, bf16[320,192]{1,0:T(8,128)(2,1)S(1)} %get-tuple-element.31), kind=kLoop, calls=%fused_computation.8 | loop fusion | flops 491520 | bytes 491520 | tf_op jit(solution)/shard_map/concatenate | solution.py:272
  13.1 1.4 %collective-permute-done.1 = bf16[464,192]{1,0:T(8,128)(2,1)S(1)} collective-permute-done((bf16[464,192]{1,0:T(8,128)(2,1)S(1)}, bf16[464,192]{1,0:T(8,128)(2,1)S(1)}, u32[]{:S(2)}, u32[]{:S(2)}) %collective-permute-start.1) | collective-permute-done | bytes 178208 | tf_op jit(solution)/shard_map/ppermute | solution.py:62
  14.9 2.5 %collective-permute-start.3 = (bf16[320,96]{1,0:T(8,128)(2,1)S(1)}, bf16[320,96]{1,0:T(8,128)(2,1)S(1)}, u32[]{:S(2)}, u32[]{:S(2)}) collective-permute-start(bf16[320,96]{1,0:T(8,128)(2,1)S(1)} %slice_select_fusion), channel_id=1, source_target_pairs={{0,1},{1,0},{2,3},{3,2},{4,5},{5,4},{6,7},{7,6},{8,9},{9,8},{10,11... | collective-permute-start | bytes 184328 | tf_op jit(solution)/shard_map/ppermute | solution.py:254
  17.5 4.2 %collective-permute-start.2 = (bf16[400,192]{1,0:T(8,128)(2,1)S(1)}, bf16[400,192]{1,0:T(8,128)(2,1)S(1)}, u32[]{:S(2)}, u32[]{:S(2)}) collective-permute-start(bf16[400,192]{1,0:T(8,128)(2,1)S(1)} %constant_dynamic-slice_fusion), channel_id=1, source_target_pairs={{0,8},{14,6},{2,10},{4,12},{8,0},{6,14},{10,2},{12,4},{1,9},{15,7}... | collective-permute-start | bytes 460808 | tf_op jit(solution)/shard_map/ppermute | solution.py:62
  21.7 0.7 %fusion.3.ids_ref = s32[4]{0:T(128)} fusion(bf16[4,200,192]{2,1,0:T(8,128)(2,1)S(1)} %bitcast.27), kind=kLoop, calls=%fused_computation.27 | loop fusion | flops 4 | bytes 24 | tf_op jit(solution)/shard_map/convert_element_type | solution.py:283
  22.4 0.4 fusion
  22.8 0.4 convolution_convert_fusion
  23.2 0.3 fusion.11
  23.9 1.0 %fusion.2.refs_3_ = bf16[320,320]{1,0:T(8,128)(2,1)} fusion(f32[320,320]{1,0:T(8,128)S(1)} %fusion.11, bf16[320,320]{0,1:T(8,128)(2,1)S(1)} %copy-done.1, bf16[320,320]{1,0:T(8,128)(2,1)S(1)} %convolution_convert_fusion), kind=kOutput, calls=%fused_computation.6 | convolution fusion | flops 65740800 | bytes 1024000 | tf_op jit(solution)/shard_map/dot_general | solution.py:41
  24.9 1.0 %fusion.1.refs_2_ = bf16[320,320]{1,0:T(8,128)(2,1)} fusion(f32[320,320]{1,0:T(8,128)S(1)} %fusion.10, bf16[320,320]{0,1:T(8,128)(2,1)S(1)} %copy-done.1, bf16[320,320]{1,0:T(8,128)(2,1)S(1)} %fusion), kind=kOutput, calls=%fused_computation.5 | convolution fusion | flops 65740800 | bytes 1024000 | tf_op jit(solution)/shard_map/dot_general | solution.py:41
  26.0 8.1 %shard_map.94 = (f32[128,128]{1,0:T(8,128)}, f32[128,128]{1,0:T(8,128)}, f32[128,128]{1,0:T(8,128)}) custom-call(s32[4]{0:T(128)} %fusion.3.ids_ref, s32[1]{0:T(128)} %bitcast.25.live_ref, bf16[4,200,192]{2,1,0:T(8,128)(2,1)} %bitcast.28, bf16[4,200,192]{2,1,0:T(8,128)(2,1)} %bitcast.29, f32[8,320,320]{2,1,0:T(8,128)} %refs_1_.3, f32[8,320,320]{2,1,0:T(8,128)} %refs_1_.3, ...), custom_call_target="tpu_custom_call" | custom-call | tf_op jit(solution)/shard_map/pallas_call | solution.py:213
  34.1 0.4 collective-permute-start.4
  34.6 1.1 %collective-permute-done.4 = bf16[400,192]{1,0:T(8,128)(2,1)S(1)} collective-permute-done((bf16[400,192]{1,0:T(8,128)(2,1)S(1)}, bf16[400,192]{1,0:T(8,128)(2,1)S(1)}, u32[]{:S(2)}, u32[]{:S(2)}) %collective-permute-start.4) | collective-permute-done | bytes 153632 | tf_op jit(solution)/shard_map/ppermute | solution.py:289
  35.8 0.6 %maximum_convert_fusion.ids_ref = s32[4]{0:T(128)} fusion(bf16[2]{0:T(256)(128)(2,1)S(1)} %slice_reduce_fusion, bf16[2]{0:T(256)(128)(2,1)S(1)} %slice_reduce_fusion.1), kind=kLoop, calls=%fused_computation.30 | loop fusion | flops 16 | bytes 24 | tf_op jit(solution)/shard_map/convert_element_type | solution.py:283
  36.4 8.2 %shard_map.95 = (f32[128,128]{1,0:T(8,128)}, f32[128,128]{1,0:T(8,128)}, f32[128,128]{1,0:T(8,128)}) custom-call(s32[4]{0:T(128)} %maximum_convert_fusion.ids_ref, s32[1]{0:T(128)} %bitcast.26.live_ref, bf16[2,200,192]{2,1,0:T(8,128)(2,1)} %bitcast.31, bf16[2,200,192]{2,1,0:T(8,128)(2,1)} %bitcast.33, ...), custom_call_target="tpu_custom_call", output_to_operand_aliasing={{0}: (14, {}), {1}: (15, {}), {2}: (16, {})} | custom-call | tf_op jit(solution)/shard_map/pallas_call | solution.py:213
  (37 shorter events, 1.9 us)
Async XLA Ops:
  0.6 14.0 %copy-start.5 = (bf16[128,128]{1,0:T(8,128)(2,1)S(1)}, bf16[128,128]{1,0:T(8,128)(2,1)}, u32[]{:S(2)}) copy-start(bf16[128,128]{1,0:T(8,128)(2,1)} %param.7) | copy-start | bytes 98308
  2.2 20.2 %copy-start.1 = (bf16[320,320]{0,1:T(8,128)(2,1)S(1)}, bf16[320,320]{0,1:T(8,128)(2,1)}, u32[]{:S(2)}) copy-start(bf16[320,320]{0,1:T(8,128)(2,1)} %constant.37.clone) | copy-start | bytes 614404
  3.2 4.5 %collective-permute-start = (bf16[264,192]{1,0:T(8,128)(2,1)S(1)}, bf16[264,192]{1,0:T(8,128)(2,1)S(1)}, u32[]{:S(2)}, u32[]{:S(2)}) collective-permute-start(bf16[264,192]{1,0:T(8,128)(2,1)S(1)} %pad_maximum_fusion.7), channel_id=1, source_target_pairs={{0,2},{4,6},{8,10},{12,14},{2,0},{6,4},{10,8},{14,12},{1,3},{5,7},... | collective-permute-start | bytes 304136 | tf_op jit(solution)/shard_map/ppermute | solution.py:62
  4.7 18.1 %copy-start.2 = (bf16[320,320]{0,1:T(8,128)(2,1)S(1)}, bf16[320,320]{0,1:T(8,128)(2,1)}, u32[]{:S(2)}) copy-start(bf16[320,320]{0,1:T(8,128)(2,1)} %constant.36.clone) | copy-start | bytes 614404
  7.8 6.7 %collective-permute-start.1 = (bf16[464,192]{1,0:T(8,128)(2,1)S(1)}, bf16[464,192]{1,0:T(8,128)(2,1)S(1)}, u32[]{:S(2)}, u32[]{:S(2)}) collective-permute-start(bf16[464,192]{1,0:T(8,128)(2,1)S(1)} %pad_maximum_fusion.3), channel_id=1, source_target_pairs={{2,4},{6,8},{10,12},{0,14},{4,2},{8,6},{12,10},{14,0},{3,5},{7,9},... | collective-permute-start | bytes 534536 | tf_op jit(solution)/shard_map/ppermute | solution.py:62
  14.9 7.5 %collective-permute-start.3 = (bf16[320,96]{1,0:T(8,128)(2,1)S(1)}, bf16[320,96]{1,0:T(8,128)(2,1)S(1)}, u32[]{:S(2)}, u32[]{:S(2)}) collective-permute-start(bf16[320,96]{1,0:T(8,128)(2,1)S(1)} %slice_select_fusion), channel_id=1, source_target_pairs={{0,1},{1,0},{2,3},{3,2},{4,5},{5,4},{6,7},{7,6},{8,9},{9,8},{10,11... | collective-permute-start | bytes 184328 | tf_op jit(solution)/shard_map/ppermute | solution.py:254
  17.5 8.5 %copy-start = (bf16[800,192]{1,0:T(8,128)(2,1)}, bf16[800,192]{1,0:T(8,128)(2,1)S(1)}, u32[]{:S(2)}) copy-start(bf16[800,192]{1,0:T(8,128)(2,1)S(1)} %pad_maximum_fusion) | copy-start | bytes 921604
  17.5 16.6 %collective-permute-start.2 = (bf16[400,192]{1,0:T(8,128)(2,1)S(1)}, bf16[400,192]{1,0:T(8,128)(2,1)S(1)}, u32[]{:S(2)}, u32[]{:S(2)}) collective-permute-start(bf16[400,192]{1,0:T(8,128)(2,1)S(1)} %constant_dynamic-slice_fusion), channel_id=1, source_target_pairs={{0,8},{14,6},{2,10},{4,12},{8,0},{6,14},{10,2},{12,4},{1,9},{15,7}... | collective-permute-start | bytes 460808 | tf_op jit(solution)/shard_map/ppermute | solution.py:62
  34.1 2.2 %copy-start.3 = (bf16[400,192]{1,0:T(8,128)(2,1)}, bf16[400,192]{1,0:T(8,128)(2,1)S(1)}, u32[]{:S(2)}) copy-start(bf16[400,192]{1,0:T(8,128)(2,1)S(1)} %collective-permute-done.2) | copy-start | bytes 460804
  34.1 1.5 %collective-permute-start.4 = (bf16[400,192]{1,0:T(8,128)(2,1)S(1)}, bf16[400,192]{1,0:T(8,128)(2,1)S(1)}, u32[]{:S(2)}, u32[]{:S(2)}) collective-permute-start(bf16[400,192]{1,0:T(8,128)(2,1)S(1)} %collective-permute-done.2), channel_id=1, source_target_pairs={{0,1},{1,0},{2,3},{3,2},{4,5},{5,4},{6,7},{7,6},{8,9},{9,8},{10,11... | collective-permute-start | bytes 460808 | tf_op jit(solution)/shard_map/ppermute | solution.py:289
  35.6 0.7 %copy-start.4 = (bf16[400,192]{1,0:T(8,128)(2,1)}, bf16[400,192]{1,0:T(8,128)(2,1)S(1)}, u32[]{:S(2)}) copy-start(bf16[400,192]{1,0:T(8,128)(2,1)S(1)} %collective-permute-done.4) | copy-start | bytes 460804

commit v17 on v16

--- a/solution.py
+++ b/solution.py
@@ -174,7 +174,7 @@
 
 def correlate(ids, live, pieces, ctf, spec_real, spec_imag, tables, scaling, previous, total):
     pieces = list(pieces)
-    group = 2 if all(piece.shape[0] % 2 == 0 for piece in pieces) else 1
+    group = next(g for g in (4, 2, 1) if all(piece.shape[0] % g == 0 for piece in pieces))
     first = pieces[0].shape[0] // group
     steps = sum(piece.shape[0] for piece in pieces) // group
     if len(pieces) == 1:

time: 44.9 us -> 44.8 us (level)
  the two profiles are of different devices: /device:TPU:11 before, /device:TPU:15 now
where the time goes in v17:
time: 44.8 us; the launch traced here: 44.5 us
  Pallas kernels  16.3 us (36%)
  starting transfers between devices  8.85 us (20%)
  local copies, waits for them, and re-layouts  7.02 us (16%)
  matrix products  3.51 us (8%)
  other arithmetic  3.37 us (8%)
  waiting for transfers between devices  3.29 us (7%)
  between operations  2.18 us (5%)
    pallas_call x2, Pallas kernels, correlate(): pl.pallas_call(kernel, grid_spec=grid_spec, out_shape=out_shape, compiler...  16.3 us
    ppermute x3, starting transfers between devices, swap(): lax.ppermute(payload, 'orient', [(a, b) for a, b in pairs] + [(b, a) for...  5.96 us
    dot_general x6, matrix products, matmul(): return jnp.dot(left, right, preferred_element_type=jnp.float32)  3.51 us
    ppermute x1, starting transfers between devices, body(): got = lax.ppermute(edge, 'tile', [(0, 1), (1, 0)])  2.53 us
    ppermute x3, waiting for transfers between devices, swap(): lax.ppermute(payload, 'orient', [(a, b) for a, b in pairs] + [(b, a) for...  2.23 us
    transpose x1, local copies, waits for them, and re-layouts, body(): col_sin = row_sin.T  1.82 us
    convert_element_type x2, other arithmetic, run(): jnp.concatenate([piece[:, box_size, 0] for piece in pieces])  1.27 us
    slice x1, local copies, waits for them, and re-layouts, body(): sin_full[low:]  1.19 us
  transfers between devices with their start and end apart: 5, of which 3 were waited for; matrix products, arithmetic and copies ran while one was open for 24% of the time, Pallas kernels for 18%

profile of v17, /device:TPU:15, one launch (start us, length us, event | category | flops | bytes accessed | tf_op | source)
XLA Modules:
  0.0 44.5 jit_solution(14854483527168320840)
XLA Ops:
  0.7 0.8 %broadcast_select_fusion.3 = (bf16[96,128]{1,0:T(8,128)(2,1)S(1)}, bf16[96,128]{1,0:T(8,128)(2,1)S(1)}) fusion(pred[]{:T(512)S(6)} %eq.16, bf16[128,128]{1,0:T(8,128)(2,1)} %param.7), kind=kLoop, calls=%fused_computation.22 | loop fusion | flops 24576 | bytes 98305 | tf_op jit(solution)/shard_map/jit(_where)/select_n | solution.py:79
  2.2 1.0 %pad_bitcast_fusion = bf16[200,192]{1,0:T(8,128)(2,1)S(1)} fusion(bf16[1,192,192]{2,1,0:T(8,128)(2,1)} %param.8, bf16[]{:T(256)} %bitcast), kind=kLoop, calls=%fused_computation.15 | loop fusion | bytes 150530 | tf_op jit(solution)/shard_map/reshape | solution.py:247
  3.6 1.2 %fusion.8 = (bf16[96,320]{0,1:T(8,128)(2,1)S(1)}, bf16[96,320]{0,1:T(8,128)(2,1)S(1)}, bf16[96,320]{0,1:T(8,128)(2,1)S(1)}, bf16[96,320]{0,1:T(8,128)(2,1)S(1)}) fusion(bf16[320,320]{0,1:T(8,128)(2,1)} %constant.37.clone, bf16[320,320]{0,1:T(8,128)(2,1)} %constant.36.clone), kind=kLoop, calls=%fused_computation.38 | loop fusion | bytes 491520 | tf_op jit(solution)/shard_map/slice | solution.py:236
  4.8 1.8 %slice_bitcast_fusion = (bf16[320,128]{1,0:T(8,128)(2,1)}, bf16[128,320]{0,1:T(8,128)(2,1)S(1)}, bf16[128,320]{0,1:T(8,128)(2,1)S(1)}, bf16[320,128]{1,0:T(8,128)(2,1)}) fusion(bf16[320,320]{0,1:T(8,128)(2,1)} %constant.37.clone, bf16[320,320]{0,1:T(8,128)(2,1)} %constant.36.clone), kind=kLoop, calls=%fused_computation.34 | loop fusion | bytes 491520 | tf_op jit(solution)/shard_map/transpose | solution.py:242
  6.9 0.8 %collective-permute-done = bf16[264,192]{1,0:T(8,128)(2,1)S(1)} collective-permute-done((bf16[264,192]{1,0:T(8,128)(2,1)S(1)}, bf16[264,192]{1,0:T(8,128)(2,1)S(1)}, u32[]{:S(2)}, u32[]{:S(2)}) %collective-permute-start) | collective-permute-done | bytes 101408 | tf_op jit(solution)/shard_map/ppermute | solution.py:62
  7.8 1.5 %collective-permute-start.1 = (bf16[464,192]{1,0:T(8,128)(2,1)S(1)}, bf16[464,192]{1,0:T(8,128)(2,1)S(1)}, u32[]{:S(2)}, u32[]{:S(2)}) collective-permute-start(bf16[464,192]{1,0:T(8,128)(2,1)S(1)} %pad_maximum_fusion.3), channel_id=1, source_target_pairs={{2,4},{6,8},{10,12},{0,14},{4,2},{8,6},{12,10},{14,0},{3,5},{7,9},... | collective-permute-start | bytes 534536 | tf_op jit(solution)/shard_map/ppermute | solution.py:62
  9.3 0.8 %copy.19.refs_6_.refs_4_ = bf16[192,320]{1,0:T(8,128)(2,1)} copy(bf16[192,320]{0,1:T(8,128)(2,1)S(1)} %get-tuple-element.32) | data formatting | bytes 245760 | tf_op jit(solution)/shard_map/concatenate | solution.py:235
  10.1 0.8 %copy.20.refs_7_.refs_5_ = bf16[192,320]{1,0:T(8,128)(2,1)} copy(bf16[192,320]{0,1:T(8,128)(2,1)S(1)} %get-tuple-element.34) | data formatting | bytes 245760 | tf_op jit(solution)/shard_map/concatenate | solution.py:236
  10.9 0.8 %copy.21.refs_9_.refs_7_ = bf16[256,320]{1,0:T(8,128)(2,1)} copy(bf16[256,320]{0,1:T(8,128)(2,1)S(1)} %pad_maximum_fusion.6) | data formatting | bytes 327680 | tf_op jit(solution)/shard_map/concatenate | solution.py:273
  12.3 0.8 %pad_maximum_fusion.1.refs_8_.refs_6_ = bf16[640,192]{1,0:T(8,128)(2,1)} fusion(bf16[320,192]{1,0:T(8,128)(2,1)S(1)} %get-tuple-element.33, bf16[320,192]{1,0:T(8,128)(2,1)S(1)} %get-tuple-element.31), kind=kLoop, calls=%fused_computation.8 | loop fusion | flops 491520 | bytes 491520 | tf_op jit(solution)/shard_map/concatenate | solution.py:272
  13.1 1.4 %collective-permute-done.1 = bf16[464,192]{1,0:T(8,128)(2,1)S(1)} collective-permute-done((bf16[464,192]{1,0:T(8,128)(2,1)S(1)}, bf16[464,192]{1,0:T(8,128)(2,1)S(1)}, u32[]{:S(2)}, u32[]{:S(2)}) %collective-permute-start.1) | collective-permute-done | bytes 178208 | tf_op jit(solution)/shard_map/ppermute | solution.py:62
  14.9 2.5 %collective-permute-start.3 = (bf16[320,96]{1,0:T(8,128)(2,1)S(1)}, bf16[320,96]{1,0:T(8,128)(2,1)S(1)}, u32[]{:S(2)}, u32[]{:S(2)}) collective-permute-start(bf16[320,96]{1,0:T(8,128)(2,1)S(1)} %slice_select_fusion), channel_id=1, source_target_pairs={{0,1},{1,0},{2,3},{3,2},{4,5},{5,4},{6,7},{7,6},{8,9},{9,8},{10,11... | collective-permute-start | bytes 184328 | tf_op jit(solution)/shard_map/ppermute | solution.py:254
  17.5 4.2 %collective-permute-start.2 = (bf16[400,192]{1,0:T(8,128)(2,1)S(1)}, bf16[400,192]{1,0:T(8,128)(2,1)S(1)}, u32[]{:S(2)}, u32[]{:S(2)}) collective-permute-start(bf16[400,192]{1,0:T(8,128)(2,1)S(1)} %constant_dynamic-slice_fusion), channel_id=1, source_target_pairs={{0,8},{14,6},{2,10},{4,12},{8,0},{6,14},{10,2},{12,4},{1,9},{15,7}... | collective-permute-start | bytes 460808 | tf_op jit(solution)/shard_map/ppermute | solution.py:62
  21.7 0.7 %fusion.3.ids_ref = s32[4]{0:T(128)} fusion(bf16[4,200,192]{2,1,0:T(8,128)(2,1)S(1)} %bitcast.27), kind=kLoop, calls=%fused_computation.27 | loop fusion | flops 4 | bytes 24 | tf_op jit(solution)/shard_map/convert_element_type | solution.py:283
  22.4 0.4 fusion
  22.8 0.4 convolution_convert_fusion
  23.5 0.3 fusion.10
  23.9 1.0 %fusion.2.refs_5_.refs_3_ = bf16[320,320]{1,0:T(8,128)(2,1)} fusion(f32[320,320]{1,0:T(8,128)S(1)} %fusion.11, bf16[320,320]{0,1:T(8,128)(2,1)S(1)} %copy-done.1, bf16[320,320]{1,0:T(8,128)(2,1)S(1)} %convolution_convert_fusion), kind=kOutput, calls=%fused_computation.6 | convolution fusion | flops 65740800 | bytes 1024000 | tf_op jit(solution)/shard_map/dot_general | solution.py:41
  24.9 1.0 %fusion.1.refs_4_.refs_2_ = bf16[320,320]{1,0:T(8,128)(2,1)} fusion(f32[320,320]{1,0:T(8,128)S(1)} %fusion.10, bf16[320,320]{0,1:T(8,128)(2,1)S(1)} %copy-done.1, bf16[320,320]{1,0:T(8,128)(2,1)S(1)} %fusion), kind=kOutput, calls=%fused_computation.5 | convolution fusion | flops 65740800 | bytes 1024000 | tf_op jit(solution)/shard_map/dot_general | solution.py:41
  26.0 8.0 %shard_map.94 = (f32[128,128]{1,0:T(8,128)}, f32[128,128]{1,0:T(8,128)}, f32[128,128]{1,0:T(8,128)}) custom-call(s32[4]{0:T(128)} %fusion.3.ids_ref, s32[1]{0:T(128)} %bitcast.25.live_ref, bf16[4,200,192]{2,1,0:T(8,128)(2,1)} %bitcast.28, bf16[4,200,192]{2,1,0:T(8,128)(2,1)} %bitcast.29, f32[8,320,320]{2,1,0:T(8,128)} %refs_1_.3, f32[8,320,320]{2,1,0:T(8,128)} %refs_1_.3, ...), custom_call_target="tpu_custom_call" | custom-call | tf_op jit(solution)/shard_map/pallas_call | solution.py:213
  34.0 0.4 collective-permute-start.4
  34.5 1.1 %collective-permute-done.4 = bf16[400,192]{1,0:T(8,128)(2,1)S(1)} collective-permute-done((bf16[400,192]{1,0:T(8,128)(2,1)S(1)}, bf16[400,192]{1,0:T(8,128)(2,1)S(1)}, u32[]{:S(2)}, u32[]{:S(2)}) %collective-permute-start.4) | collective-permute-done | bytes 153632 | tf_op jit(solution)/shard_map/ppermute | solution.py:289
  35.7 0.6 %maximum_convert_fusion.ids_ref = s32[4]{0:T(128)} fusion(bf16[2]{0:T(256)(128)(2,1)S(1)} %slice_reduce_fusion, bf16[2]{0:T(256)(128)(2,1)S(1)} %slice_reduce_fusion.1), kind=kLoop, calls=%fused_computation.30 | loop fusion | flops 16 | bytes 24 | tf_op jit(solution)/shard_map/convert_element_type | solution.py:283
  36.3 8.2 %shard_map.95 = (f32[128,128]{1,0:T(8,128)}, f32[128,128]{1,0:T(8,128)}, f32[128,128]{1,0:T(8,128)}) custom-call(s32[4]{0:T(128)} %maximum_convert_fusion.ids_ref, s32[1]{0:T(128)} %bitcast.26.live_ref, bf16[2,200,192]{2,1,0:T(8,128)(2,1)} %bitcast.31, bf16[2,200,192]{2,1,0:T(8,128)(2,1)} %bitcast.33, ...), custom_call_target="tpu_custom_call", output_to_operand_aliasing={{0}: (14, {}), {1}: (15, {}), {2}: (16, {})} | custom-call | tf_op jit(solution)/shard_map/pallas_call | solution.py:213
  (37 shorter events, 1.8 us)
Async XLA Ops:
  0.6 14.0 %copy-start.5 = (bf16[128,128]{1,0:T(8,128)(2,1)S(1)}, bf16[128,128]{1,0:T(8,128)(2,1)}, u32[]{:S(2)}) copy-start(bf16[128,128]{1,0:T(8,128)(2,1)} %param.7) | copy-start | bytes 98308
  2.2 20.2 %copy-start.1 = (bf16[320,320]{0,1:T(8,128)(2,1)S(1)}, bf16[320,320]{0,1:T(8,128)(2,1)}, u32[]{:S(2)}) copy-start(bf16[320,320]{0,1:T(8,128)(2,1)} %constant.37.clone) | copy-start | bytes 614404
  3.2 4.5 %collective-permute-start = (bf16[264,192]{1,0:T(8,128)(2,1)S(1)}, bf16[264,192]{1,0:T(8,128)(2,1)S(1)}, u32[]{:S(2)}, u32[]{:S(2)}) collective-permute-start(bf16[264,192]{1,0:T(8,128)(2,1)S(1)} %pad_maximum_fusion.7), channel_id=1, source_target_pairs={{0,2},{4,6},{8,10},{12,14},{2,0},{6,4},{10,8},{14,12},{1,3},{5,7},... | collective-permute-start | bytes 304136 | tf_op jit(solution)/shard_map/ppermute | solution.py:62
  4.7 18.1 %copy-start.2 = (bf16[320,320]{0,1:T(8,128)(2,1)S(1)}, bf16[320,320]{0,1:T(8,128)(2,1)}, u32[]{:S(2)}) copy-start(bf16[320,320]{0,1:T(8,128)(2,1)} %constant.36.clone) | copy-start | bytes 614404
  7.8 6.7 %collective-permute-start.1 = (bf16[464,192]{1,0:T(8,128)(2,1)S(1)}, bf16[464,192]{1,0:T(8,128)(2,1)S(1)}, u32[]{:S(2)}, u32[]{:S(2)}) collective-permute-start(bf16[464,192]{1,0:T(8,128)(2,1)S(1)} %pad_maximum_fusion.3), channel_id=1, source_target_pairs={{2,4},{6,8},{10,12},{0,14},{4,2},{8,6},{12,10},{14,0},{3,5},{7,9},... | collective-permute-start | bytes 534536 | tf_op jit(solution)/shard_map/ppermute | solution.py:62
  14.9 7.5 %collective-permute-start.3 = (bf16[320,96]{1,0:T(8,128)(2,1)S(1)}, bf16[320,96]{1,0:T(8,128)(2,1)S(1)}, u32[]{:S(2)}, u32[]{:S(2)}) collective-permute-start(bf16[320,96]{1,0:T(8,128)(2,1)S(1)} %slice_select_fusion), channel_id=1, source_target_pairs={{0,1},{1,0},{2,3},{3,2},{4,5},{5,4},{6,7},{7,6},{8,9},{9,8},{10,11... | collective-permute-start | bytes 184328 | tf_op jit(solution)/shard_map/ppermute | solution.py:254
  17.5 8.5 %copy-start = (bf16[800,192]{1,0:T(8,128)(2,1)}, bf16[800,192]{1,0:T(8,128)(2,1)S(1)}, u32[]{:S(2)}) copy-start(bf16[800,192]{1,0:T(8,128)(2,1)S(1)} %pad_maximum_fusion) | copy-start | bytes 921604
  17.5 16.5 %collective-permute-start.2 = (bf16[400,192]{1,0:T(8,128)(2,1)S(1)}, bf16[400,192]{1,0:T(8,128)(2,1)S(1)}, u32[]{:S(2)}, u32[]{:S(2)}) collective-permute-start(bf16[400,192]{1,0:T(8,128)(2,1)S(1)} %constant_dynamic-slice_fusion), channel_id=1, source_target_pairs={{0,8},{14,6},{2,10},{4,12},{8,0},{6,14},{10,2},{12,4},{1,9},{15,7}... | collective-permute-start | bytes 460808 | tf_op jit(solution)/shard_map/ppermute | solution.py:62
  34.0 2.2 %copy-start.3 = (bf16[400,192]{1,0:T(8,128)(2,1)}, bf16[400,192]{1,0:T(8,128)(2,1)S(1)}, u32[]{:S(2)}) copy-start(bf16[400,192]{1,0:T(8,128)(2,1)S(1)} %collective-permute-done.2) | copy-start | bytes 460804
  34.0 1.5 %collective-permute-start.4 = (bf16[400,192]{1,0:T(8,128)(2,1)S(1)}, bf16[400,192]{1,0:T(8,128)(2,1)S(1)}, u32[]{:S(2)}, u32[]{:S(2)}) collective-permute-start(bf16[400,192]{1,0:T(8,128)(2,1)S(1)} %collective-permute-done.2), channel_id=1, source_target_pairs={{0,1},{1,0},{2,3},{3,2},{4,5},{5,4},{6,7},{7,6},{8,9},{9,8},{10,11... | collective-permute-start | bytes 460808 | tf_op jit(solution)/shard_map/ppermute | solution.py:289
  35.5 0.7 %copy-start.4 = (bf16[400,192]{1,0:T(8,128)(2,1)}, bf16[400,192]{1,0:T(8,128)(2,1)S(1)}, u32[]{:S(2)}) copy-start(bf16[400,192]{1,0:T(8,128)(2,1)S(1)} %collective-permute-done.4) | copy-start | bytes 460804

commit v18 on v16

--- a/solution.py
+++ b/solution.py
@@ -94,22 +94,41 @@
     return arrivals, jnp.concatenate([top, tile, bottom], axis=0)
 
 
-def correlate_kernel(ids_ref, live_ref, tmpl_ref, other_ref, *refs, scaling, total, block, first, group):
+def correlate_kernel(ids_ref, live_ref, tmpl_ref, other_ref, *refs, scaling, total, block, first, group, from_half):
+    bf16 = jnp.bfloat16
+    f32 = jnp.float32
+    o = pl.program_id(0)
+
+    def mm(a, b):
+        return jnp.dot(a, b, preferred_element_type=f32)
+
     ctf_refs = refs[:group]
-    (spec_r_ref, spec_i_ref, cos_rows_ref, sin_rows_ref, cols_ref, rows_ref, col_cos_ref, col_sin_ref) = refs[
-        group : group + 8
-    ]
-    refs = refs[group + 8 :]
+    refs = refs[group:]
+    if from_half:
+        half_r_ref, half_i_ref, cos_ref, sin_ref = refs[:4]
+        refs = refs[4:]
+    else:
+        spec_r_ref, spec_i_ref = refs[:2]
+        refs = refs[2:]
+    (cos_rows_ref, sin_rows_ref, cols_ref, rows_ref, col_cos_ref, col_sin_ref) = refs[:6]
+    refs = refs[6:]
+    if from_half:
+        spec_r_ref, spec_i_ref = refs[-2:]
+        refs = refs[:-2]
+
+        @pl.when(o == 0)
+        def _():
+            cos = cos_ref[...]
+            sin = sin_ref[...]
+            half_real = half_r_ref[...]
+            half_imag = half_i_ref[...]
+            spec_r_ref[...] = (mm(cos, half_real) + mm(sin, half_imag)).astype(bf16)
+            spec_i_ref[...] = (mm(cos, half_imag) - mm(sin, half_real)).astype(bf16)
+
     if len(refs) == 6:
         prev_peak_ref, prev_sum_ref, prev_sq_ref, peak_ref, sum_ref, sq_ref = refs
     else:
         peak_ref, sum_ref, sq_ref = refs
-    bf16 = jnp.bfloat16
-    f32 = jnp.float32
-    o = pl.program_id(0)
-
-    def mm(a, b):
-        return jnp.dot(a, b, preferred_element_type=f32)
 
     def one(g):
         template = jnp.where(o < first, tmpl_ref[g], other_ref[g])
@@ -172,7 +191,7 @@
             sq_ref[...] = jnp.where(live, sq_ref[...] / total, 0.0)
 
 
-def correlate(ids, live, pieces, ctf, spec_real, spec_imag, tables, scaling, previous, total):
+def correlate(ids, live, pieces, ctf, spectrum, tables, scaling, previous, total, from_half=False):
     pieces = list(pieces)
     group = 2 if all(piece.shape[0] % 2 == 0 for piece in pieces) else 1
     first = pieces[0].shape[0] // group
@@ -194,29 +213,33 @@
             pl.BlockSpec((group, box, box), lambda o, ids, live: (jnp.clip(o - first, 0, last_other), 0, 0)),
         ]
         + [plane(g) for g in range(group)]
-        + [full((n, n)), full((n, n))]
+        + [full((n, n))] * len(spectrum)
         + [full(t.shape) for t in tables]
         + [full((tile, tile))] * len(previous)
     )
     out_block = full((tile, tile))
+    out_specs = [out_block, out_block, out_block]
+    out_shape = [jax.ShapeDtypeStruct((tile, tile), jnp.float32)] * 3
+    if from_half:
+        out_specs += [full((n, n)), full((n, n))]
+        out_shape += [jax.ShapeDtypeStruct((n, n), jnp.bfloat16)] * 2
     grid_spec = pltpu.PrefetchScalarGridSpec(
         num_scalar_prefetch=2,
         grid=(steps,),
         in_specs=in_specs,
-        out_specs=[out_block, out_block, out_block],
-    )
-    out_shape = [jax.ShapeDtypeStruct((tile, tile), jnp.float32)] * 3
+        out_specs=out_specs,
+    )
     kernel = functools.partial(
-        correlate_kernel, scaling=scaling, total=total, block=RB, first=first, group=group
-    )
-    base = 4 + group + 2 + len(tables)
+        correlate_kernel, scaling=scaling, total=total, block=RB, first=first, group=group, from_half=from_half
+    )
+    base = 4 + group + len(spectrum) + len(tables)
     return pl.pallas_call(
         kernel,
         grid_spec=grid_spec,
         out_shape=out_shape,
         compiler_params=pltpu.CompilerParams(dimension_semantics=("arbitrary",)),
         input_output_aliases={base + i: i for i in range(len(previous))},
-    )(ids, live, pieces[0], pieces[1], *([ctf] * group), spec_real, spec_imag, *tables, *previous)
+    )(ids, live, pieces[0], pieces[1], *([ctf] * group), *spectrum, *tables, *previous)
 
 
 def body(micrograph, templates, defocus, ctf, usable):
@@ -263,8 +286,6 @@
 
     half_real = matmul(padded, cos_full).astype(bf16)
     half_imag = (-matmul(padded, sin_full)).astype(bf16)
-    spec_real = (matmul(cos_full, half_real) + matmul(sin_full, half_imag)).astype(bf16)
-    spec_imag = (matmul(cos_full, half_imag) - matmul(sin_full, half_real)).astype(bf16)
 
     tables = (
         cos_rows,
@@ -278,10 +299,16 @@
     stats = ()
     live = usable.reshape(-1)[:1]
 
+    spectrum = [half_real, half_imag, cos_full, sin_full]
+
     def run(pieces, stats, total=0):
         pieces = [piece.reshape(piece.shape[0] // block_rows, block_rows, box_size) for piece in pieces]
         piece_ids = jnp.concatenate([piece[:, box_size, 0] for piece in pieces]).astype(jnp.int32)
-        return correlate(piece_ids, live, pieces, ctf, spec_real, spec_imag, tables, scaling, stats, total)
+        from_half = len(spectrum) == 4
+        outs = correlate(piece_ids, live, pieces, ctf, spectrum, tables, scaling, stats, total, from_half)
+        if from_half:
+            spectrum[:] = outs[3:]
+        return tuple(outs[:3])
 
     if split_last:
         stats = run([arrivals[0]], stats)

time: 44.9 us -> 44.7 us (level)
  the two profiles are of different devices: /device:TPU:11 before, /device:TPU:0 now
where the time goes in v18:
time: 44.7 us; the launch traced here: 43.9 us
  Pallas kernels  17.4 us (39%)
  local copies, waits for them, and re-layouts  8.68 us (19%)
  starting transfers between devices  8.36 us (19%)
  other arithmetic  3.51 us (8%)
  matrix products  2.17 us (5%)
  between operations  2.15 us (5%)
  waiting for transfers between devices  1.63 us (4%)
    pallas_call x2, Pallas kernels, correlate(): pl.pallas_call(kernel, grid_spec=grid_spec, out_shape=out_shape, compiler...  17.4 us
    ppermute x3, starting transfers between devices, swap(): lax.ppermute(payload, 'orient', [(a, b) for a, b in pairs] + [(b, a) for...  8.01 us
    dot_general x2, matrix products, matmul(): return jnp.dot(left, right, preferred_element_type=jnp.float32)  2.17 us
    transpose x1, local copies, waits for them, and re-layouts, body(): col_sin = row_sin.T  1.78 us
    optimization_barrier x2, local copies, waits for them, and re-layouts, body(): lax.optimization_barrier((jnp.asarray(cos_np), jnp.asarray(sin_np)))  1.74 us
    convert_element_type x2, other arithmetic, run(): jnp.concatenate([piece[:, box_size, 0] for piece in pieces])  1.41 us
    slice x1, local copies, waits for them, and re-layouts, body(): sin_full[low:]  1.19 us
    ppermute x1, waiting for transfers between devices, body(): other_half = lax.ppermute(half, 'tile', [(0, 1), (1, 0)])  1.14 us
  transfers between devices with their start and end apart: 5, of which 3 were waited for; matrix products, arithmetic and copies ran while one was open for 26% of the time, Pallas kernels for 21%

profile of v18, /device:TPU:0, one launch (start us, length us, event | category | flops | bytes accessed | tf_op | source)
XLA Modules:
  0.0 43.9 jit_solution(6412024471749035554)
XLA Ops:
  0.7 0.8 %broadcast_select_fusion.3 = (bf16[96,128]{1,0:T(8,128)(2,1)S(1)}, bf16[96,128]{1,0:T(8,128)(2,1)S(1)}) fusion(pred[]{:T(512)S(6)} %eq.16, bf16[128,128]{1,0:T(8,128)(2,1)} %param.7), kind=kLoop, calls=%fused_computation.18 | loop fusion | flops 24576 | bytes 98305 | tf_op jit(solution)/shard_map/jit(_where)/select_n | solution.py:79
  2.3 0.9 %pad_bitcast_fusion = bf16[200,192]{1,0:T(8,128)(2,1)S(1)} fusion(bf16[1,192,192]{2,1,0:T(8,128)(2,1)} %param.8, bf16[]{:T(256)} %bitcast), kind=kLoop, calls=%fused_computation.11 | loop fusion | bytes 150530 | tf_op jit(solution)/shard_map/reshape | solution.py:270
  3.2 3.0 %collective-permute-start = (bf16[264,192]{1,0:T(8,128)(2,1)S(1)}, bf16[264,192]{1,0:T(8,128)(2,1)S(1)}, u32[]{:S(2)}, u32[]{:S(2)}) collective-permute-start(bf16[264,192]{1,0:T(8,128)(2,1)S(1)} %pad_maximum_fusion.7), channel_id=1, source_target_pairs={{0,2},{4,6},{8,10},{12,14},{2,0},{6,4},{10,8},{14,12},{1,3},{5,7},... | collective-permute-start | bytes 304136 | tf_op jit(solution)/shard_map/ppermute | solution.py:62
  6.2 1.2 %fusion.6 = (bf16[96,320]{0,1:T(8,128)(2,1)S(1)}, bf16[96,320]{0,1:T(8,128)(2,1)S(1)}, bf16[96,320]{0,1:T(8,128)(2,1)S(1)}, bf16[96,320]{0,1:T(8,128)(2,1)S(1)}) fusion(bf16[320,320]{0,1:T(8,128)(2,1)} %constant.37.clone, bf16[320,320]{0,1:T(8,128)(2,1)} %constant.36.clone), kind=kLoop, calls=%fused_computation.34 | loop fusion | bytes 491520 | tf_op jit(solution)/shard_map/slice | solution.py:259
  7.4 1.8 %slice_bitcast_fusion = (bf16[320,128]{1,0:T(8,128)(2,1)}, bf16[128,320]{0,1:T(8,128)(2,1)S(1)}, bf16[128,320]{0,1:T(8,128)(2,1)S(1)}, bf16[320,128]{1,0:T(8,128)(2,1)}) fusion(bf16[320,320]{0,1:T(8,128)(2,1)} %constant.37.clone, bf16[320,320]{0,1:T(8,128)(2,1)} %constant.36.clone), kind=kLoop, calls=%fused_computation.30 | loop fusion | bytes 491520 | tf_op jit(solution)/shard_map/transpose | solution.py:265
  9.4 0.1 fusion.4
  9.5 0.3 collective-permute-done
  9.9 4.8 %collective-permute-start.1 = (bf16[464,192]{1,0:T(8,128)(2,1)S(1)}, bf16[464,192]{1,0:T(8,128)(2,1)S(1)}, u32[]{:S(2)}, u32[]{:S(2)}) collective-permute-start(bf16[464,192]{1,0:T(8,128)(2,1)S(1)} %pad_maximum_fusion.3), channel_id=1, source_target_pairs={{2,4},{6,8},{10,12},{0,14},{4,2},{8,6},{12,10},{14,0},{3,5},{7,9},... | collective-permute-start | bytes 534536 | tf_op jit(solution)/shard_map/ppermute | solution.py:62
  14.7 0.9 %copy.21.refs_4_ = bf16[320,320]{1,0:T(8,128)(2,1)} copy(bf16[320,320]{0,1:T(8,128)(2,1)S(1)} %copy-done.1) | data formatting | bytes 409600 | tf_op jit(solution)/shard_map/optimization_barrier | solution.py:256
  15.6 0.9 %copy.22.refs_5_ = bf16[320,320]{1,0:T(8,128)(2,1)} copy(bf16[320,320]{0,1:T(8,128)(2,1)S(1)} %copy-done.2) | data formatting | bytes 409600 | tf_op jit(solution)/shard_map/optimization_barrier | solution.py:256
  16.5 0.8 %copy.23.refs_6_.refs_4_ = bf16[192,320]{1,0:T(8,128)(2,1)} copy(bf16[192,320]{0,1:T(8,128)(2,1)S(1)} %get-tuple-element.36) | data formatting | bytes 245760 | tf_op jit(solution)/shard_map/concatenate | solution.py:258
  17.2 0.8 %copy.24.refs_7_.refs_5_ = bf16[192,320]{1,0:T(8,128)(2,1)} copy(bf16[192,320]{0,1:T(8,128)(2,1)S(1)} %get-tuple-element.38) | data formatting | bytes 245760 | tf_op jit(solution)/shard_map/concatenate | solution.py:259
  18.0 0.8 %copy.25.refs_9_.refs_7_ = bf16[256,320]{1,0:T(8,128)(2,1)} copy(bf16[256,320]{0,1:T(8,128)(2,1)S(1)} %pad_maximum_fusion.6) | data formatting | bytes 327680 | tf_op jit(solution)/shard_map/concatenate | solution.py:294
  19.5 0.8 %pad_maximum_fusion.1.refs_8_.refs_6_ = bf16[640,192]{1,0:T(8,128)(2,1)} fusion(bf16[320,192]{1,0:T(8,128)(2,1)S(1)} %get-tuple-element.37, bf16[320,192]{1,0:T(8,128)(2,1)S(1)} %get-tuple-element.35), kind=kLoop, calls=%fused_computation.4 | loop fusion | flops 491520 | bytes 491520 | tf_op jit(solution)/shard_map/concatenate | solution.py:293
  20.9 0.2 collective-permute-start.2
  21.0 0.8 %fusion.1.ids_ref = s32[4]{0:T(128)} fusion(bf16[4,200,192]{2,1,0:T(8,128)(2,1)S(1)} %bitcast.19), kind=kLoop, calls=%fused_computation.23 | loop fusion | flops 4 | bytes 24 | tf_op jit(solution)/shard_map/convert_element_type | solution.py:306
  21.8 0.2 collective-permute-done.3
  22.0 1.1 %fusion.refs_3_ = bf16[320,320]{1,0:T(8,128)(2,1)} fusion(bf16[320,320]{0,1:T(8,128)(2,1)S(1)} %copy-done.2, bf16[320,96]{1,0:T(8,128)(2,1)S(1)} %get-tuple-element.40, bf16[320,128]{1,0:T(8,128)(2,1)S(1)} %constant_dynamic-update-slice_fusion, bf16[320,96]{1,0:T(8,128)(2,1)S(1)} %get-tuple-element.39), kind=kOutput, calls=%fused_computation.1 | convolution fusion | flops 66355200 | bytes 614400 | tf_op jit(solution)/shard_map/dot_general | solution.py:41
  23.1 1.1 %convolution_convert_fusion.refs_2_ = bf16[320,320]{1,0:T(8,128)(2,1)} fusion(bf16[320,320]{0,1:T(8,128)(2,1)S(1)} %copy-done.1, bf16[320,96]{1,0:T(8,128)(2,1)S(1)} %get-tuple-element.40, bf16[320,128]{1,0:T(8,128)(2,1)S(1)} %constant_dynamic-update-slice_fusion, bf16[320,96]{1,0:T(8,128)(2,1)S(1)} %get-tuple-element.39), kind=kOutput, calls=%fused_computation.2 | convolution fusion | flops 66252800 | bytes 614400 | tf_op jit(solution)/shard_map/dot_general | solution.py:41
  24.2 9.2 %shard_map.94 = (f32[128,128]{1,0:T(8,128)}, f32[128,128]{1,0:T(8,128)}, f32[128,128]{1,0:T(8,128)}, bf16[320,320]{1,0:T(8,128)(2,1)}, bf16[320,320]{1,0:T(8,128)(2,1)}) custom-call(s32[4]{0:T(128)} %fusion.1.ids_ref, s32[1]{0:T(128)} %bitcast.17.live_ref, bf16[4,200,192]{2,1,0:T(8,128)(2,1)} %bitcast.20, bf16[4,200,192]{2,1,0:T(8,128)(2,1)} %bitcast.21, ...), custom_call_target="tpu_custom_call" | custom-call | tf_op jit(solution)/shard_map/pallas_call | solution.py:236
  33.4 0.3 collective-permute-start.4
  33.8 1.1 %collective-permute-done.4 = bf16[400,192]{1,0:T(8,128)(2,1)S(1)} collective-permute-done((bf16[400,192]{1,0:T(8,128)(2,1)S(1)}, bf16[400,192]{1,0:T(8,128)(2,1)S(1)}, u32[]{:S(2)}, u32[]{:S(2)}) %collective-permute-start.4) | collective-permute-done | bytes 153632 | tf_op jit(solution)/shard_map/ppermute | solution.py:316
  35.0 0.7 %maximum_convert_fusion.ids_ref = s32[4]{0:T(128)} fusion(bf16[2]{0:T(256)(128)(2,1)S(1)} %slice_reduce_fusion, bf16[2]{0:T(256)(128)(2,1)S(1)} %slice_reduce_fusion.1), kind=kLoop, calls=%fused_computation.26 | loop fusion | flops 16 | bytes 24 | tf_op jit(solution)/shard_map/convert_element_type | solution.py:306
  35.7 8.2 %shard_map.95 = (f32[128,128]{1,0:T(8,128)}, f32[128,128]{1,0:T(8,128)}, f32[128,128]{1,0:T(8,128)}) custom-call(s32[4]{0:T(128)} %maximum_convert_fusion.ids_ref, s32[1]{0:T(128)} %bitcast.18.live_ref, bf16[2,200,192]{2,1,0:T(8,128)(2,1)} %bitcast.23, bf16[2,200,192]{2,1,0:T(8,128)(2,1)} %bitcast.25, ...), custom_call_target="tpu_custom_call", output_to_operand_aliasing={{0}: (14, {}), {1}: (15, {}), {2}: (16, {})} | custom-call | tf_op jit(solution)/shard_map/pallas_call | solution.py:236
  (35 shorter events, 1.2 us)
Async XLA Ops:
  0.6 14.1 %copy-start.1 = (bf16[320,320]{0,1:T(8,128)(2,1)S(1)}, bf16[320,320]{0,1:T(8,128)(2,1)}, u32[]{:S(2)}) copy-start(bf16[320,320]{0,1:T(8,128)(2,1)} %constant.36.clone) | copy-start | bytes 614404
  0.6 15.0 %copy-start.2 = (bf16[320,320]{0,1:T(8,128)(2,1)S(1)}, bf16[320,320]{0,1:T(8,128)(2,1)}, u32[]{:S(2)}) copy-start(bf16[320,320]{0,1:T(8,128)(2,1)} %constant.37.clone) | copy-start | bytes 614404
  0.7 19.8 %copy-start.5 = (bf16[128,128]{1,0:T(8,128)(2,1)S(1)}, bf16[128,128]{1,0:T(8,128)(2,1)}, u32[]{:S(2)}) copy-start(bf16[128,128]{1,0:T(8,128)(2,1)} %param.7) | copy-start | bytes 98308
  3.2 6.6 %collective-permute-start = (bf16[264,192]{1,0:T(8,128)(2,1)S(1)}, bf16[264,192]{1,0:T(8,128)(2,1)S(1)}, u32[]{:S(2)}, u32[]{:S(2)}) collective-permute-start(bf16[264,192]{1,0:T(8,128)(2,1)S(1)} %pad_maximum_fusion.7), channel_id=1, source_target_pairs={{0,2},{4,6},{8,10},{12,14},{2,0},{6,4},{10,8},{14,12},{1,3},{5,7},... | collective-permute-start | bytes 304136 | tf_op jit(solution)/shard_map/ppermute | solution.py:62
  9.9 10.4 %collective-permute-start.1 = (bf16[464,192]{1,0:T(8,128)(2,1)S(1)}, bf16[464,192]{1,0:T(8,128)(2,1)S(1)}, u32[]{:S(2)}, u32[]{:S(2)}) collective-permute-start(bf16[464,192]{1,0:T(8,128)(2,1)S(1)} %pad_maximum_fusion.3), channel_id=1, source_target_pairs={{2,4},{6,8},{10,12},{0,14},{4,2},{8,6},{12,10},{14,0},{3,5},{7,9},... | collective-permute-start | bytes 534536 | tf_op jit(solution)/shard_map/ppermute | solution.py:62
  20.7 1.3 %collective-permute-start.3 = (bf16[320,96]{1,0:T(8,128)(2,1)S(1)}, bf16[320,96]{1,0:T(8,128)(2,1)S(1)}, u32[]{:S(2)}, u32[]{:S(2)}) collective-permute-start(bf16[320,96]{1,0:T(8,128)(2,1)S(1)} %slice_select_fusion), channel_id=1, source_target_pairs={{0,1},{1,0},{2,3},{3,2},{4,5},{5,4},{6,7},{7,6},{8,9},{9,8},{10,11... | collective-permute-start | bytes 184328 | tf_op jit(solution)/shard_map/ppermute | solution.py:277
  20.8 3.4 %copy-start = (bf16[800,192]{1,0:T(8,128)(2,1)}, bf16[800,192]{1,0:T(8,128)(2,1)S(1)}, u32[]{:S(2)}) copy-start(bf16[800,192]{1,0:T(8,128)(2,1)S(1)} %pad_maximum_fusion) | copy-start | bytes 921604
  20.9 12.5 %collective-permute-start.2 = (bf16[400,192]{1,0:T(8,128)(2,1)S(1)}, bf16[400,192]{1,0:T(8,128)(2,1)S(1)}, u32[]{:S(2)}, u32[]{:S(2)}) collective-permute-start(bf16[400,192]{1,0:T(8,128)(2,1)S(1)} %constant_dynamic-slice_fusion), channel_id=1, source_target_pairs={{0,8},{14,6},{2,10},{4,12},{8,0},{6,14},{10,2},{12,4},{1,9},{15,7}... | collective-permute-start | bytes 460808 | tf_op jit(solution)/shard_map/ppermute | solution.py:62
  33.4 2.3 %copy-start.3 = (bf16[400,192]{1,0:T(8,128)(2,1)}, bf16[400,192]{1,0:T(8,128)(2,1)S(1)}, u32[]{:S(2)}) copy-start(bf16[400,192]{1,0:T(8,128)(2,1)S(1)} %collective-permute-done.2) | copy-start | bytes 460804
  33.4 1.5 %collective-permute-start.4 = (bf16[400,192]{1,0:T(8,128)(2,1)S(1)}, bf16[400,192]{1,0:T(8,128)(2,1)S(1)}, u32[]{:S(2)}, u32[]{:S(2)}) collective-permute-start(bf16[400,192]{1,0:T(8,128)(2,1)S(1)} %collective-permute-done.2), channel_id=1, source_target_pairs={{0,1},{1,0},{2,3},{3,2},{4,5},{5,4},{6,7},{7,6},{8,9},{9,8},{10,11... | collective-permute-start | bytes 460808 | tf_op jit(solution)/shard_map/ppermute | solution.py:316
  34.9 0.8 %copy-start.4 = (bf16[400,192]{1,0:T(8,128)(2,1)}, bf16[400,192]{1,0:T(8,128)(2,1)S(1)}, u32[]{:S(2)}) copy-start(bf16[400,192]{1,0:T(8,128)(2,1)S(1)} %collective-permute-done.4) | copy-start | bytes 460804

commit v19 on v18

--- a/solution.py
+++ b/solution.py
@@ -105,8 +105,8 @@
     ctf_refs = refs[:group]
     refs = refs[group:]
     if from_half:
-        half_r_ref, half_i_ref, cos_ref, sin_ref = refs[:4]
-        refs = refs[4:]
+        padded_ref, cos_ref, sin_ref = refs[:3]
+        refs = refs[3:]
     else:
         spec_r_ref, spec_i_ref = refs[:2]
         refs = refs[2:]
@@ -120,8 +120,9 @@
         def _():
             cos = cos_ref[...]
             sin = sin_ref[...]
-            half_real = half_r_ref[...]
-            half_imag = half_i_ref[...]
+            padded = padded_ref[...]
+            half_real = mm(padded, cos).astype(bf16)
+            half_imag = (-mm(padded, sin)).astype(bf16)
             spec_r_ref[...] = (mm(cos, half_real) + mm(sin, half_imag)).astype(bf16)
             spec_i_ref[...] = (mm(cos, half_imag) - mm(sin, half_real)).astype(bf16)
 
@@ -284,8 +285,6 @@
         padded = extended(micrograph, (("orient", 0), ("tile", 1)), margin)
     total = sum(piece.shape[0] for piece in arrivals) // block_rows
 
-    half_real = matmul(padded, cos_full).astype(bf16)
-    half_imag = (-matmul(padded, sin_full)).astype(bf16)
 
     tables = (
         cos_rows,
@@ -299,12 +298,12 @@
     stats = ()
     live = usable.reshape(-1)[:1]
 
-    spectrum = [half_real, half_imag, cos_full, sin_full]
+    spectrum = [padded, cos_full, sin_full]
 
     def run(pieces, stats, total=0):
         pieces = [piece.reshape(piece.shape[0] // block_rows, block_rows, box_size) for piece in pieces]
         piece_ids = jnp.concatenate([piece[:, box_size, 0] for piece in pieces]).astype(jnp.int32)
-        from_half = len(spectrum) == 4
+        from_half = len(spectrum) == 3
         outs = correlate(piece_ids, live, pieces, ctf, spectrum, tables, scaling, stats, total, from_half)
         if from_half:
             spectrum[:] = outs[3:]

time: 44.7 us -> 43.6 us (0.975)
  matrix products: 2.17 us -> 0 us
  other arithmetic: 3.51 us -> 4.31 us
    dot_general x2 -> x0, matrix products: 2.17 us -> none  [matmul(): return jnp.dot(left, right, preferred_element_type=jnp.float32)]
    concatenate x0 -> x1, other arithmetic: none -> 0.85 us  [body(): jnp.concatenate([jnp.where(core == 0, zero, got), row_padded, jnp.where(c...]
  transfers between devices with their start and end apart: 5 -> 5, of which waited for: 3 -> 3; matrix products, arithmetic and copies ran while one was open for 26% -> 23% of each run, Pallas kernels for 21% -> 22%
where the time goes in v19:
time: 43.6 us; the launch traced here: 43 us
  Pallas kernels  17.8 us (41%)
  local copies, waits for them, and re-layouts  8.69 us (20%)
  starting transfers between devices  8.3 us (19%)
  other arithmetic  4.31 us (10%)
  between operations  2.15 us (5%)
  waiting for transfers between devices  1.73 us (4%)
    pallas_call x2, Pallas kernels, correlate(): pl.pallas_call(kernel, grid_spec=grid_spec, out_shape=out_shape, compiler...  17.8 us
    ppermute x3, starting transfers between devices, swap(): lax.ppermute(payload, 'orient', [(a, b) for a, b in pairs] + [(b, a) for...  8 us
    transpose x1, local copies, waits for them, and re-layouts, body(): col_sin = row_sin.T  1.78 us
    optimization_barrier x2, local copies, waits for them, and re-layouts, body(): lax.optimization_barrier((jnp.asarray(cos_np), jnp.asarray(sin_np)))  1.73 us
    convert_element_type x2, other arithmetic, run(): jnp.concatenate([piece[:, box_size, 0] for piece in pieces])  1.37 us
    slice x1, local copies, waits for them, and re-layouts, body(): sin_full[low:]  1.19 us
    ppermute x1, waiting for transfers between devices, body(): other_half = lax.ppermute(half, 'tile', [(0, 1), (1, 0)])  1.19 us
    reshape x1, local copies, waits for them, and re-layouts, body(): jnp.concatenate([templates, id_rows], axis=1)  0.91 us
  transfers between devices with their start and end apart: 5, of which 3 were waited for; matrix products, arithmetic and copies ran while one was open for 23% of the time, Pallas kernels for 22%

profile of v19, /device:TPU:0, one launch (start us, length us, event | category | flops | bytes accessed | tf_op | source)
XLA Modules:
  0.0 43.0 jit_solution(10937229467743325117)
XLA Ops:
  0.7 0.8 %broadcast_select_fusion.3 = (bf16[96,128]{1,0:T(8,128)(2,1)S(1)}, bf16[96,128]{1,0:T(8,128)(2,1)S(1)}) fusion(pred[]{:T(512)S(6)} %eq.16, bf16[128,128]{1,0:T(8,128)(2,1)} %param.7), kind=kLoop, calls=%fused_computation.15 | loop fusion | flops 24576 | bytes 98305 | tf_op jit(solution)/shard_map/jit(_where)/select_n | solution.py:79
  2.3 0.9 %pad_bitcast_fusion = bf16[200,192]{1,0:T(8,128)(2,1)S(1)} fusion(bf16[1,192,192]{2,1,0:T(8,128)(2,1)} %param.8, bf16[]{:T(256)} %bitcast), kind=kLoop, calls=%fused_computation.8 | loop fusion | bytes 150530 | tf_op jit(solution)/shard_map/reshape | solution.py:271
  3.2 3.0 %collective-permute-start = (bf16[264,192]{1,0:T(8,128)(2,1)S(1)}, bf16[264,192]{1,0:T(8,128)(2,1)S(1)}, u32[]{:S(2)}, u32[]{:S(2)}) collective-permute-start(bf16[264,192]{1,0:T(8,128)(2,1)S(1)} %pad_maximum_fusion.7), channel_id=1, source_target_pairs={{0,2},{4,6},{8,10},{12,14},{2,0},{6,4},{10,8},{14,12},{1,3},{5,7},... | collective-permute-start | bytes 304136 | tf_op jit(solution)/shard_map/ppermute | solution.py:62
  6.2 1.2 %fusion.3 = (bf16[96,320]{0,1:T(8,128)(2,1)S(1)}, bf16[96,320]{0,1:T(8,128)(2,1)S(1)}, bf16[96,320]{0,1:T(8,128)(2,1)S(1)}, bf16[96,320]{0,1:T(8,128)(2,1)S(1)}) fusion(bf16[320,320]{0,1:T(8,128)(2,1)} %constant.37.clone, bf16[320,320]{0,1:T(8,128)(2,1)} %constant.36.clone), kind=kLoop, calls=%fused_computation.29 | loop fusion | bytes 491520 | tf_op jit(solution)/shard_map/slice | solution.py:260
  7.4 1.8 %slice_bitcast_fusion = (bf16[320,128]{1,0:T(8,128)(2,1)}, bf16[128,320]{0,1:T(8,128)(2,1)S(1)}, bf16[128,320]{0,1:T(8,128)(2,1)S(1)}, bf16[320,128]{1,0:T(8,128)(2,1)}) fusion(bf16[320,320]{0,1:T(8,128)(2,1)} %constant.37.clone, bf16[320,320]{0,1:T(8,128)(2,1)} %constant.36.clone), kind=kLoop, calls=%fused_computation.25 | loop fusion | bytes 491520 | tf_op jit(solution)/shard_map/transpose | solution.py:266
  9.3 0.1 fusion.2
  9.4 0.1 fusion.1
  9.5 0.3 collective-permute-done
  9.9 4.8 %collective-permute-start.1 = (bf16[464,192]{1,0:T(8,128)(2,1)S(1)}, bf16[464,192]{1,0:T(8,128)(2,1)S(1)}, u32[]{:S(2)}, u32[]{:S(2)}) collective-permute-start(bf16[464,192]{1,0:T(8,128)(2,1)S(1)} %pad_maximum_fusion.3), channel_id=1, source_target_pairs={{2,4},{6,8},{10,12},{0,14},{4,2},{8,6},{12,10},{14,0},{3,5},{7,9},... | collective-permute-start | bytes 534536 | tf_op jit(solution)/shard_map/ppermute | solution.py:62
  14.7 0.9 %copy.21.refs_3_ = bf16[320,320]{1,0:T(8,128)(2,1)} copy(bf16[320,320]{0,1:T(8,128)(2,1)S(1)} %copy-done.2) | data formatting | bytes 409600 | tf_op jit(solution)/shard_map/optimization_barrier | solution.py:257
  15.6 0.9 %copy.22.refs_4_ = bf16[320,320]{1,0:T(8,128)(2,1)} copy(bf16[320,320]{0,1:T(8,128)(2,1)S(1)} %copy-done.1) | data formatting | bytes 409600 | tf_op jit(solution)/shard_map/optimization_barrier | solution.py:257
  16.5 0.8 %copy.23.refs_5_.refs_4_ = bf16[192,320]{1,0:T(8,128)(2,1)} copy(bf16[192,320]{0,1:T(8,128)(2,1)S(1)} %get-tuple-element.36) | data formatting | bytes 245760 | tf_op jit(solution)/shard_map/concatenate | solution.py:259
  17.2 0.8 %copy.24.refs_6_.refs_5_ = bf16[192,320]{1,0:T(8,128)(2,1)} copy(bf16[192,320]{0,1:T(8,128)(2,1)S(1)} %get-tuple-element.38) | data formatting | bytes 245760 | tf_op jit(solution)/shard_map/concatenate | solution.py:260
  18.0 0.8 %copy.25.refs_8_.refs_7_ = bf16[256,320]{1,0:T(8,128)(2,1)} copy(bf16[256,320]{0,1:T(8,128)(2,1)S(1)} %pad_maximum_fusion.6) | data formatting | bytes 327680 | tf_op jit(solution)/shard_map/concatenate | solution.py:293
  19.5 0.8 %pad_maximum_fusion.1.refs_7_.refs_6_ = bf16[640,192]{1,0:T(8,128)(2,1)} fusion(bf16[320,192]{1,0:T(8,128)(2,1)S(1)} %get-tuple-element.37, bf16[320,192]{1,0:T(8,128)(2,1)S(1)} %get-tuple-element.35), kind=kLoop, calls=%fused_computation.1 | loop fusion | flops 491520 | bytes 491520 | tf_op jit(solution)/shard_map/concatenate | solution.py:292
  20.9 0.2 collective-permute-start.2
  21.0 0.7 %fusion.ids_ref = s32[4]{0:T(128)} fusion(bf16[4,200,192]{2,1,0:T(8,128)(2,1)S(1)} %bitcast.17), kind=kLoop, calls=%fused_computation.20 | loop fusion | flops 4 | bytes 24 | tf_op jit(solution)/shard_map/convert_element_type | solution.py:305
  21.8 0.3 collective-permute-done.3
  22.0 0.8 %pad_maximum_fusion.2.refs_2_ = bf16[320,320]{1,0:T(8,128)(2,1)} fusion(bf16[320,96]{1,0:T(8,128)(2,1)S(1)} %get-tuple-element.40, bf16[320,128]{1,0:T(8,128)(2,1)S(1)} %constant_dynamic-update-slice_fusion, bf16[320,96]{1,0:T(8,128)(2,1)S(1)} %get-tuple-element.39), kind=kLoop, calls=%fused_computation.2 | loop fusion | flops 614400 | bytes 409600 | tf_op jit(solution)/shard_map/concatenate | solution.py:280
  22.9 9.6 %shard_map.94 = (f32[128,128]{1,0:T(8,128)}, f32[128,128]{1,0:T(8,128)}, f32[128,128]{1,0:T(8,128)}, bf16[320,320]{1,0:T(8,128)(2,1)}, bf16[320,320]{1,0:T(8,128)(2,1)}) custom-call(s32[4]{0:T(128)} %fusion.ids_ref, s32[1]{0:T(128)} %bitcast.15.live_ref, bf16[4,200,192]{2,1,0:T(8,128)(2,1)} %bitcast.18, bf16[4,200,192]{2,1,0:T(8,128)(2,1)} %bitcast.19, ...), custom_call_target="tpu_custom_call" | custom-call | tf_op jit(solution)/shard_map/pallas_call | solution.py:237
  32.5 0.2 collective-permute-start.4
  32.8 1.2 %collective-permute-done.4 = bf16[400,192]{1,0:T(8,128)(2,1)S(1)} collective-permute-done((bf16[400,192]{1,0:T(8,128)(2,1)S(1)}, bf16[400,192]{1,0:T(8,128)(2,1)S(1)}, u32[]{:S(2)}, u32[]{:S(2)}) %collective-permute-start.4) | collective-permute-done | bytes 153632 | tf_op jit(solution)/shard_map/ppermute | solution.py:315
  34.1 0.7 %maximum_convert_fusion.ids_ref = s32[4]{0:T(128)} fusion(bf16[2]{0:T(256)(128)(2,1)S(1)} %slice_reduce_fusion, bf16[2]{0:T(256)(128)(2,1)S(1)} %slice_reduce_fusion.1), kind=kLoop, calls=%fused_computation.23 | loop fusion | flops 16 | bytes 24 | tf_op jit(solution)/shard_map/convert_element_type | solution.py:305
  34.7 8.2 %shard_map.95 = (f32[128,128]{1,0:T(8,128)}, f32[128,128]{1,0:T(8,128)}, f32[128,128]{1,0:T(8,128)}) custom-call(s32[4]{0:T(128)} %maximum_convert_fusion.ids_ref, s32[1]{0:T(128)} %bitcast.16.live_ref, bf16[2,200,192]{2,1,0:T(8,128)(2,1)} %bitcast.21, bf16[2,200,192]{2,1,0:T(8,128)(2,1)} %bitcast.23, ...), custom_call_target="tpu_custom_call", output_to_operand_aliasing={{0}: (14, {}), {1}: (15, {}), {2}: (16, {})} | custom-call | tf_op jit(solution)/shard_map/pallas_call | solution.py:237
  (34 shorter events, 1.0 us)
Async XLA Ops:
  0.6 14.1 %copy-start.2 = (bf16[320,320]{0,1:T(8,128)(2,1)S(1)}, bf16[320,320]{0,1:T(8,128)(2,1)}, u32[]{:S(2)}) copy-start(bf16[320,320]{0,1:T(8,128)(2,1)} %constant.36.clone) | copy-start | bytes 614404
  0.6 15.0 %copy-start.1 = (bf16[320,320]{0,1:T(8,128)(2,1)S(1)}, bf16[320,320]{0,1:T(8,128)(2,1)}, u32[]{:S(2)}) copy-start(bf16[320,320]{0,1:T(8,128)(2,1)} %constant.37.clone) | copy-start | bytes 614404
  0.7 19.8 %copy-start.5 = (bf16[128,128]{1,0:T(8,128)(2,1)S(1)}, bf16[128,128]{1,0:T(8,128)(2,1)}, u32[]{:S(2)}) copy-start(bf16[128,128]{1,0:T(8,128)(2,1)} %param.7) | copy-start | bytes 98308
  3.2 6.6 %collective-permute-start = (bf16[264,192]{1,0:T(8,128)(2,1)S(1)}, bf16[264,192]{1,0:T(8,128)(2,1)S(1)}, u32[]{:S(2)}, u32[]{:S(2)}) collective-permute-start(bf16[264,192]{1,0:T(8,128)(2,1)S(1)} %pad_maximum_fusion.7), channel_id=1, source_target_pairs={{0,2},{4,6},{8,10},{12,14},{2,0},{6,4},{10,8},{14,12},{1,3},{5,7},... | collective-permute-start | bytes 304136 | tf_op jit(solution)/shard_map/ppermute | solution.py:62
  9.9 10.4 %collective-permute-start.1 = (bf16[464,192]{1,0:T(8,128)(2,1)S(1)}, bf16[464,192]{1,0:T(8,128)(2,1)S(1)}, u32[]{:S(2)}, u32[]{:S(2)}) collective-permute-start(bf16[464,192]{1,0:T(8,128)(2,1)S(1)} %pad_maximum_fusion.3), channel_id=1, source_target_pairs={{2,4},{6,8},{10,12},{0,14},{4,2},{8,6},{12,10},{14,0},{3,5},{7,9},... | collective-permute-start | bytes 534536 | tf_op jit(solution)/shard_map/ppermute | solution.py:62
  20.7 1.3 %collective-permute-start.3 = (bf16[320,96]{1,0:T(8,128)(2,1)S(1)}, bf16[320,96]{1,0:T(8,128)(2,1)S(1)}, u32[]{:S(2)}, u32[]{:S(2)}) collective-permute-start(bf16[320,96]{1,0:T(8,128)(2,1)S(1)} %slice_select_fusion), channel_id=1, source_target_pairs={{0,1},{1,0},{2,3},{3,2},{4,5},{5,4},{6,7},{7,6},{8,9},{9,8},{10,11... | collective-permute-start | bytes 184328 | tf_op jit(solution)/shard_map/ppermute | solution.py:278
  20.9 2.0 %copy-start = (bf16[800,192]{1,0:T(8,128)(2,1)}, bf16[800,192]{1,0:T(8,128)(2,1)S(1)}, u32[]{:S(2)}) copy-start(bf16[800,192]{1,0:T(8,128)(2,1)S(1)} %pad_maximum_fusion) | copy-start | bytes 921604
  20.9 11.6 %collective-permute-start.2 = (bf16[400,192]{1,0:T(8,128)(2,1)S(1)}, bf16[400,192]{1,0:T(8,128)(2,1)S(1)}, u32[]{:S(2)}, u32[]{:S(2)}) collective-permute-start(bf16[400,192]{1,0:T(8,128)(2,1)S(1)} %constant_dynamic-slice_fusion), channel_id=1, source_target_pairs={{0,8},{14,6},{2,10},{4,12},{8,0},{6,14},{10,2},{12,4},{1,9},{15,7}... | collective-permute-start | bytes 460808 | tf_op jit(solution)/shard_map/ppermute | solution.py:62
  32.5 2.3 %copy-start.3 = (bf16[400,192]{1,0:T(8,128)(2,1)}, bf16[400,192]{1,0:T(8,128)(2,1)S(1)}, u32[]{:S(2)}) copy-start(bf16[400,192]{1,0:T(8,128)(2,1)S(1)} %collective-permute-done.2) | copy-start | bytes 460804
  32.5 1.5 %collective-permute-start.4 = (bf16[400,192]{1,0:T(8,128)(2,1)S(1)}, bf16[400,192]{1,0:T(8,128)(2,1)S(1)}, u32[]{:S(2)}, u32[]{:S(2)}) collective-permute-start(bf16[400,192]{1,0:T(8,128)(2,1)S(1)} %collective-permute-done.2), channel_id=1, source_target_pairs={{0,1},{1,0},{2,3},{3,2},{4,5},{5,4},{6,7},{7,6},{8,9},{9,8},{10,11... | collective-permute-start | bytes 460808 | tf_op jit(solution)/shard_map/ppermute | solution.py:315
  34.0 0.8 %copy-start.4 = (bf16[400,192]{1,0:T(8,128)(2,1)}, bf16[400,192]{1,0:T(8,128)(2,1)S(1)}, u32[]{:S(2)}) copy-start(bf16[400,192]{1,0:T(8,128)(2,1)S(1)} %collective-permute-done.4) | copy-start | bytes 460804

commit v20 on v19

--- a/solution.py
+++ b/solution.py
@@ -94,7 +94,7 @@
     return arrivals, jnp.concatenate([top, tile, bottom], axis=0)
 
 
-def correlate_kernel(ids_ref, live_ref, tmpl_ref, other_ref, *refs, scaling, total, block, first, group, from_half):
+def correlate_kernel(ids_ref, other_ids_ref, live_ref, tmpl_ref, other_ref, *refs, scaling, total, block, first, group, from_half):
     bf16 = jnp.bfloat16
     f32 = jnp.float32
     o = pl.program_id(0)
@@ -203,15 +203,22 @@
     box = pieces[0].shape[2]
     n = ctf.shape[1]
     tile = tables[4].shape[1]
-    full = lambda shape: pl.BlockSpec(shape, lambda o, ids, live: (0,) * len(shape))
+    full = lambda shape: pl.BlockSpec(shape, lambda o, ids, other_ids, live: (0,) * len(shape))
 
     def plane(g):
-        return pl.BlockSpec((1, n, n), lambda o, ids, live: (ids[o * group + g], 0, 0))
+        def pick(o, ids, other_ids, live):
+            mine = ids[jnp.minimum(o, first - 1) * group + g]
+            other = other_ids[jnp.clip(o - first, 0, last_other) * group + g]
+            return (jnp.where(o < first, mine, other), 0, 0)
+
+        return pl.BlockSpec((1, n, n), pick)
 
     in_specs = (
         [
-            pl.BlockSpec((group, box, box), lambda o, ids, live: (jnp.minimum(o, first - 1), 0, 0)),
-            pl.BlockSpec((group, box, box), lambda o, ids, live: (jnp.clip(o - first, 0, last_other), 0, 0)),
+            pl.BlockSpec((group, box, box), lambda o, ids, other_ids, live: (jnp.minimum(o, first - 1), 0, 0)),
+            pl.BlockSpec(
+                (group, box, box), lambda o, ids, other_ids, live: (jnp.clip(o - first, 0, last_other), 0, 0)
+            ),
         ]
         + [plane(g) for g in range(group)]
         + [full((n, n))] * len(spectrum)
@@ -225,7 +232,7 @@
         out_specs += [full((n, n)), full((n, n))]
         out_shape += [jax.ShapeDtypeStruct((n, n), jnp.bfloat16)] * 2
     grid_spec = pltpu.PrefetchScalarGridSpec(
-        num_scalar_prefetch=2,
+        num_scalar_prefetch=3,
         grid=(steps,),
         in_specs=in_specs,
         out_specs=out_specs,
@@ -233,14 +240,14 @@
     kernel = functools.partial(
         correlate_kernel, scaling=scaling, total=total, block=RB, first=first, group=group, from_half=from_half
     )
-    base = 4 + group + len(spectrum) + len(tables)
+    base = 5 + group + len(spectrum) + len(tables)
     return pl.pallas_call(
         kernel,
         grid_spec=grid_spec,
         out_shape=out_shape,
         compiler_params=pltpu.CompilerParams(dimension_semantics=("arbitrary",)),
         input_output_aliases={base + i: i for i in range(len(previous))},
-    )(ids, live, pieces[0], pieces[1], *([ctf] * group), *spectrum, *tables, *previous)
+    )(ids[0], ids[-1], live, pieces[0], pieces[1], *([ctf] * group), *spectrum, *tables, *previous)
 
 
 def body(micrograph, templates, defocus, ctf, usable):
@@ -302,7 +309,7 @@
 
     def run(pieces, stats, total=0):
         pieces = [piece.reshape(piece.shape[0] // block_rows, block_rows, box_size) for piece in pieces]
-        piece_ids = jnp.concatenate([piece[:, box_size, 0] for piece in pieces]).astype(jnp.int32)
+        piece_ids = [piece[:, box_size, 0].astype(jnp.int32) for piece in pieces]
         from_half = len(spectrum) == 3
         outs = correlate(piece_ids, live, pieces, ctf, spectrum, tables, scaling, stats, total, from_half)
         if from_half:

time: 43.6 us -> 43.5 us (level)
  other arithmetic: 4.31 us -> 5.02 us
  waiting for transfers between devices: 1.73 us -> 1.12 us
    convert_element_type x2 -> x3, other arithmetic: 1.37 us -> 2.07 us  [run(): piece_ids = [piece[:, box_size, 0].astype(jnp.int32) for piece in pieces]]
    ppermute x1, waiting for transfers between devices: 1.19 us -> 0.57 us  [body(): other_half = lax.ppermute(half, 'tile', [(0, 1), (1, 0)])]
  transfers between devices with their start and end apart: 5 -> 5, of which waited for: 3 -> 3; matrix products, arithmetic and copies ran while one was open for 23% -> 25% of each run, Pallas kernels for 22% -> 22%
where the time goes in v20:
time: 43.5 us; the launch traced here: 42.9 us
  Pallas kernels  17.8 us (41%)
  local copies, waits for them, and re-layouts  8.51 us (20%)
  starting transfers between devices  8.31 us (19%)
  other arithmetic  5.02 us (12%)
  between operations  2.15 us (5%)
  waiting for transfers between devices  1.12 us (3%)
    pallas_call x2, Pallas kernels, correlate(): pl.pallas_call(kernel, grid_spec=grid_spec, out_shape=out_shape, compiler...  17.8 us
    ppermute x3, starting transfers between devices, swap(): lax.ppermute(payload, 'orient', [(a, b) for a, b in pairs] + [(b, a) for...  8 us
    convert_element_type x3, other arithmetic, run(): piece_ids = [piece[:, box_size, 0].astype(jnp.int32) for piece in pieces]  2.07 us
    transpose x1, local copies, waits for them, and re-layouts, body(): col_sin = row_sin.T  1.78 us
    optimization_barrier x2, local copies, waits for them, and re-layouts, body(): lax.optimization_barrier((jnp.asarray(cos_np), jnp.asarray(sin_np)))  1.73 us
    slice x1, local copies, waits for them, and re-layouts, body(): sin_full[low:]  1.19 us
    reshape x1, local copies, waits for them, and re-layouts, body(): jnp.concatenate([templates, id_rows], axis=1)  0.91 us
  transfers between devices with their start and end apart: 5, of which 3 were waited for; matrix products, arithmetic and copies ran while one was open for 25% of the time, Pallas kernels for 22%

profile of v20, /device:TPU:0, one launch (start us, length us, event | category | flops | bytes accessed | tf_op | source)
XLA Modules:
  0.0 42.9 jit_solution(15551616236122026888)
XLA Ops:
  0.7 0.8 %broadcast_select_fusion.3 = (bf16[96,128]{1,0:T(8,128)(2,1)S(1)}, bf16[96,128]{1,0:T(8,128)(2,1)S(1)}) fusion(pred[]{:T(512)S(6)} %eq.16, bf16[128,128]{1,0:T(8,128)(2,1)} %param.7), kind=kLoop, calls=%fused_computation.15 | loop fusion | flops 24576 | bytes 98305 | tf_op jit(solution)/shard_map/jit(_where)/select_n | solution.py:79
  2.3 0.9 %pad_bitcast_fusion = bf16[200,192]{1,0:T(8,128)(2,1)S(1)} fusion(bf16[1,192,192]{2,1,0:T(8,128)(2,1)} %param.8, bf16[]{:T(256)} %bitcast), kind=kLoop, calls=%fused_computation.8 | loop fusion | bytes 150530 | tf_op jit(solution)/shard_map/reshape | solution.py:278
  3.2 3.0 %collective-permute-start = (bf16[264,192]{1,0:T(8,128)(2,1)S(1)}, bf16[264,192]{1,0:T(8,128)(2,1)S(1)}, u32[]{:S(2)}, u32[]{:S(2)}) collective-permute-start(bf16[264,192]{1,0:T(8,128)(2,1)S(1)} %pad_maximum_fusion.7), channel_id=1, source_target_pairs={{0,2},{4,6},{8,10},{12,14},{2,0},{6,4},{10,8},{14,12},{1,3},{5,7},... | collective-permute-start | bytes 304136 | tf_op jit(solution)/shard_map/ppermute | solution.py:62
  6.2 1.2 %fusion.5 = (bf16[96,320]{0,1:T(8,128)(2,1)S(1)}, bf16[96,320]{0,1:T(8,128)(2,1)S(1)}, bf16[96,320]{0,1:T(8,128)(2,1)S(1)}, bf16[96,320]{0,1:T(8,128)(2,1)S(1)}) fusion(bf16[320,320]{0,1:T(8,128)(2,1)} %constant.37.clone, bf16[320,320]{0,1:T(8,128)(2,1)} %constant.36.clone), kind=kLoop, calls=%fused_computation.30 | loop fusion | bytes 491520 | tf_op jit(solution)/shard_map/slice | solution.py:267
  7.4 1.8 %slice_bitcast_fusion = (bf16[320,128]{1,0:T(8,128)(2,1)}, bf16[128,320]{0,1:T(8,128)(2,1)S(1)}, bf16[128,320]{0,1:T(8,128)(2,1)S(1)}, bf16[320,128]{1,0:T(8,128)(2,1)}) fusion(bf16[320,320]{0,1:T(8,128)(2,1)} %constant.37.clone, bf16[320,320]{0,1:T(8,128)(2,1)} %constant.36.clone), kind=kLoop, calls=%fused_computation.26 | loop fusion | bytes 491520 | tf_op jit(solution)/shard_map/transpose | solution.py:273
  9.4 0.1 fusion.3
  9.5 0.3 collective-permute-done
  9.9 4.8 %collective-permute-start.1 = (bf16[464,192]{1,0:T(8,128)(2,1)S(1)}, bf16[464,192]{1,0:T(8,128)(2,1)S(1)}, u32[]{:S(2)}, u32[]{:S(2)}) collective-permute-start(bf16[464,192]{1,0:T(8,128)(2,1)S(1)} %pad_maximum_fusion.3), channel_id=1, source_target_pairs={{2,4},{6,8},{10,12},{0,14},{4,2},{8,6},{12,10},{14,0},{3,5},{7,9},... | collective-permute-start | bytes 534536 | tf_op jit(solution)/shard_map/ppermute | solution.py:62
  14.7 0.9 %copy.21.refs_3_ = bf16[320,320]{1,0:T(8,128)(2,1)} copy(bf16[320,320]{0,1:T(8,128)(2,1)S(1)} %copy-done.2) | data formatting | bytes 409600 | tf_op jit(solution)/shard_map/optimization_barrier | solution.py:264
  15.6 0.9 %copy.22.refs_4_ = bf16[320,320]{1,0:T(8,128)(2,1)} copy(bf16[320,320]{0,1:T(8,128)(2,1)S(1)} %copy-done.1) | data formatting | bytes 409600 | tf_op jit(solution)/shard_map/optimization_barrier | solution.py:264
  16.5 0.8 %copy.23.refs_5_.refs_4_ = bf16[192,320]{1,0:T(8,128)(2,1)} copy(bf16[192,320]{0,1:T(8,128)(2,1)S(1)} %get-tuple-element.36) | data formatting | bytes 245760 | tf_op jit(solution)/shard_map/concatenate | solution.py:266
  17.2 0.8 %copy.24.refs_6_.refs_5_ = bf16[192,320]{1,0:T(8,128)(2,1)} copy(bf16[192,320]{0,1:T(8,128)(2,1)S(1)} %get-tuple-element.38) | data formatting | bytes 245760 | tf_op jit(solution)/shard_map/concatenate | solution.py:267
  18.0 0.8 %copy.25.refs_8_.refs_7_ = bf16[256,320]{1,0:T(8,128)(2,1)} copy(bf16[256,320]{0,1:T(8,128)(2,1)S(1)} %pad_maximum_fusion.6) | data formatting | bytes 327680 | tf_op jit(solution)/shard_map/concatenate | solution.py:300
  19.5 0.8 %pad_maximum_fusion.1.refs_7_.refs_6_ = bf16[640,192]{1,0:T(8,128)(2,1)} fusion(bf16[320,192]{1,0:T(8,128)(2,1)S(1)} %get-tuple-element.37, bf16[320,192]{1,0:T(8,128)(2,1)S(1)} %get-tuple-element.35), kind=kLoop, calls=%fused_computation.1 | loop fusion | flops 491520 | bytes 491520 | tf_op jit(solution)/shard_map/concatenate | solution.py:299
  20.9 0.2 collective-permute-start.2
  21.0 0.7 %fusion.ids_ref.other_ids_ref = s32[4]{0:T(128)} fusion(bf16[4,200,192]{2,1,0:T(8,128)(2,1)S(1)} %bitcast.17), kind=kLoop, calls=%fused_computation.20 | loop fusion | flops 4 | bytes 24 | tf_op jit(solution)/shard_map/convert_element_type | solution.py:312
  21.8 0.3 collective-permute-done.3
  22.0 0.8 %pad_maximum_fusion.2.refs_2_ = bf16[320,320]{1,0:T(8,128)(2,1)} fusion(bf16[320,96]{1,0:T(8,128)(2,1)S(1)} %get-tuple-element.40, bf16[320,128]{1,0:T(8,128)(2,1)S(1)} %constant_dynamic-update-slice_fusion, bf16[320,96]{1,0:T(8,128)(2,1)S(1)} %get-tuple-element.39), kind=kLoop, calls=%fused_computation.2 | loop fusion | flops 614400 | bytes 409600 | tf_op jit(solution)/shard_map/concatenate | solution.py:287
  22.9 9.6 %shard_map.94 = (f32[128,128]{1,0:T(8,128)}, f32[128,128]{1,0:T(8,128)}, f32[128,128]{1,0:T(8,128)}, bf16[320,320]{1,0:T(8,128)(2,1)}, bf16[320,320]{1,0:T(8,128)(2,1)}) custom-call(s32[4]{0:T(128)} %fusion.ids_ref.other_ids_ref, s32[4]{0:T(128)} %fusion.ids_ref.other_ids_ref, s32[1]{0:T(128)} %bitcast.15.live_ref, bf16[4,200,192]{2,1,0:T(8,128)(2,1)} %bitcast.18, ...), custom_call_target="tpu_custom_call" | custom-call | tf_op jit(solution)/shard_map/pallas_call | solution.py:244
  32.5 0.2 collective-permute-start.4
  32.7 0.7 %fusion.2.ids_ref = s32[2]{0:T(128)} fusion(bf16[2,200,192]{2,1,0:T(8,128)(2,1)S(1)} %bitcast.20), kind=kLoop, calls=%fused_computation.24 | loop fusion | flops 2 | bytes 12 | tf_op jit(solution)/shard_map/convert_element_type | solution.py:312
  33.4 0.6 %collective-permute-done.4 = bf16[400,192]{1,0:T(8,128)(2,1)S(1)} collective-permute-done((bf16[400,192]{1,0:T(8,128)(2,1)S(1)}, bf16[400,192]{1,0:T(8,128)(2,1)S(1)}, u32[]{:S(2)}, u32[]{:S(2)}) %collective-permute-start.4) | collective-permute-done | bytes 153632 | tf_op jit(solution)/shard_map/ppermute | solution.py:322
  34.0 0.7 %fusion.1.other_ids_ref = s32[2]{0:T(128)} fusion(bf16[2,200,192]{2,1,0:T(8,128)(2,1)S(1)} %bitcast.22), kind=kLoop, calls=%fused_computation.22 | loop fusion | flops 2 | bytes 12 | tf_op jit(solution)/shard_map/convert_element_type | solution.py:312
  34.7 8.2 %shard_map.95 = (f32[128,128]{1,0:T(8,128)}, f32[128,128]{1,0:T(8,128)}, f32[128,128]{1,0:T(8,128)}) custom-call(s32[2]{0:T(128)} %fusion.2.ids_ref, s32[2]{0:T(128)} %fusion.1.other_ids_ref, s32[1]{0:T(128)} %bitcast.16.live_ref, bf16[2,200,192]{2,1,0:T(8,128)(2,1)} %bitcast.21, ...), custom_call_target="tpu_custom_call", output_to_operand_aliasing={{0}: (15, {}), {1}: (16, {}), {2}: (17, {})} | custom-call | tf_op jit(solution)/shard_map/pallas_call | solution.py:244
  (33 shorter events, 1.0 us)
Async XLA Ops:
  0.6 14.1 %copy-start.2 = (bf16[320,320]{0,1:T(8,128)(2,1)S(1)}, bf16[320,320]{0,1:T(8,128)(2,1)}, u32[]{:S(2)}) copy-start(bf16[320,320]{0,1:T(8,128)(2,1)} %constant.36.clone) | copy-start | bytes 614404
  0.6 15.0 %copy-start.1 = (bf16[320,320]{0,1:T(8,128)(2,1)S(1)}, bf16[320,320]{0,1:T(8,128)(2,1)}, u32[]{:S(2)}) copy-start(bf16[320,320]{0,1:T(8,128)(2,1)} %constant.37.clone) | copy-start | bytes 614404
  0.7 19.8 %copy-start.3 = (bf16[128,128]{1,0:T(8,128)(2,1)S(1)}, bf16[128,128]{1,0:T(8,128)(2,1)}, u32[]{:S(2)}) copy-start(bf16[128,128]{1,0:T(8,128)(2,1)} %param.7) | copy-start | bytes 98308
  3.2 6.6 %collective-permute-start = (bf16[264,192]{1,0:T(8,128)(2,1)S(1)}, bf16[264,192]{1,0:T(8,128)(2,1)S(1)}, u32[]{:S(2)}, u32[]{:S(2)}) collective-permute-start(bf16[264,192]{1,0:T(8,128)(2,1)S(1)} %pad_maximum_fusion.7), channel_id=1, source_target_pairs={{0,2},{4,6},{8,10},{12,14},{2,0},{6,4},{10,8},{14,12},{1,3},{5,7},... | collective-permute-start | bytes 304136 | tf_op jit(solution)/shard_map/ppermute | solution.py:62
  9.9 10.4 %collective-permute-start.1 = (bf16[464,192]{1,0:T(8,128)(2,1)S(1)}, bf16[464,192]{1,0:T(8,128)(2,1)S(1)}, u32[]{:S(2)}, u32[]{:S(2)}) collective-permute-start(bf16[464,192]{1,0:T(8,128)(2,1)S(1)} %pad_maximum_fusion.3), channel_id=1, source_target_pairs={{2,4},{6,8},{10,12},{0,14},{4,2},{8,6},{12,10},{14,0},{3,5},{7,9},... | collective-permute-start | bytes 534536 | tf_op jit(solution)/shard_map/ppermute | solution.py:62
  20.7 1.3 %collective-permute-start.3 = (bf16[320,96]{1,0:T(8,128)(2,1)S(1)}, bf16[320,96]{1,0:T(8,128)(2,1)S(1)}, u32[]{:S(2)}, u32[]{:S(2)}) collective-permute-start(bf16[320,96]{1,0:T(8,128)(2,1)S(1)} %slice_select_fusion), channel_id=1, source_target_pairs={{0,1},{1,0},{2,3},{3,2},{4,5},{5,4},{6,7},{7,6},{8,9},{9,8},{10,11... | collective-permute-start | bytes 184328 | tf_op jit(solution)/shard_map/ppermute | solution.py:285
  20.9 2.0 %copy-start = (bf16[800,192]{1,0:T(8,128)(2,1)}, bf16[800,192]{1,0:T(8,128)(2,1)S(1)}, u32[]{:S(2)}) copy-start(bf16[800,192]{1,0:T(8,128)(2,1)S(1)} %pad_maximum_fusion) | copy-start | bytes 921604
  20.9 11.6 %collective-permute-start.2 = (bf16[400,192]{1,0:T(8,128)(2,1)S(1)}, bf16[400,192]{1,0:T(8,128)(2,1)S(1)}, u32[]{:S(2)}, u32[]{:S(2)}) collective-permute-start(bf16[400,192]{1,0:T(8,128)(2,1)S(1)} %constant_dynamic-slice_fusion), channel_id=1, source_target_pairs={{0,8},{14,6},{2,10},{4,12},{8,0},{6,14},{10,2},{12,4},{1,9},{15,7}... | collective-permute-start | bytes 460808 | tf_op jit(solution)/shard_map/ppermute | solution.py:62
  32.5 2.2 %copy-start.4 = (bf16[400,192]{1,0:T(8,128)(2,1)}, bf16[400,192]{1,0:T(8,128)(2,1)S(1)}, u32[]{:S(2)}) copy-start(bf16[400,192]{1,0:T(8,128)(2,1)S(1)} %collective-permute-done.2) | copy-start | bytes 460804
  32.5 1.5 %collective-permute-start.4 = (bf16[400,192]{1,0:T(8,128)(2,1)S(1)}, bf16[400,192]{1,0:T(8,128)(2,1)S(1)}, u32[]{:S(2)}, u32[]{:S(2)}) collective-permute-start(bf16[400,192]{1,0:T(8,128)(2,1)S(1)} %collective-permute-done.2), channel_id=1, source_target_pairs={{0,1},{1,0},{2,3},{3,2},{4,5},{5,4},{6,7},{7,6},{8,9},{9,8},{10,11... | collective-permute-start | bytes 460808 | tf_op jit(solution)/shard_map/ppermute | solution.py:322
  34.0 0.7 %copy-start.5 = (bf16[400,192]{1,0:T(8,128)(2,1)}, bf16[400,192]{1,0:T(8,128)(2,1)S(1)}, u32[]{:S(2)}) copy-start(bf16[400,192]{1,0:T(8,128)(2,1)S(1)} %collective-permute-done.4) | copy-start | bytes 460804

commit v21 on v19

--- a/solution.py
+++ b/solution.py
@@ -131,12 +131,21 @@
     else:
         peak_ref, sum_ref, sq_ref = refs
 
+    cos_rows = cos_rows_ref[...]
+    sin_rows = sin_rows_ref[...]
+    cols = cols_ref[...]
+    rows = rows_ref[...]
+    col_cos = col_cos_ref[...]
+    col_sin = col_sin_ref[...]
+    spec_real = spec_r_ref[...].astype(f32)
+    spec_imag = spec_i_ref[...].astype(f32)
+    n = cols.shape[0] // 2
+    tile = rows.shape[0] // 2
+
     def one(g):
         template = jnp.where(o < first, tmpl_ref[g], other_ref[g])
-        part_real = mm(template, cos_rows_ref[...]).astype(bf16)
-        part_imag = (-mm(template, sin_rows_ref[...])).astype(bf16)
-        cols = cols_ref[...]
-        n = cols.shape[0] // 2
+        part_real = mm(template, cos_rows).astype(bf16)
+        part_imag = (-mm(template, sin_rows)).astype(bf16)
         from_real = mm(cols, part_real)
         from_imag = mm(cols, part_imag)
         full_real = from_real[:n] + from_imag[n:]
@@ -144,17 +153,13 @@
         weight = ctf_refs[g][0]
         w_real = (full_real * weight).astype(bf16).astype(f32)
         w_imag = (full_imag * weight).astype(bf16).astype(f32)
-        spec_real = spec_r_ref[...].astype(f32)
-        spec_imag = spec_i_ref[...].astype(f32)
         prod_real = (spec_real * w_real + spec_imag * w_imag).astype(bf16)
         prod_imag = (spec_imag * w_real - spec_real * w_imag).astype(bf16)
-        rows = rows_ref[...]
-        tile = rows.shape[0] // 2
         left_from_real = mm(rows, prod_real)
         left_from_imag = mm(rows, prod_imag)
         left_real = (left_from_real[:tile] - left_from_imag[tile:]).astype(bf16)
         left_imag = (left_from_imag[:tile] + left_from_real[tile:]).astype(bf16)
-        return (mm(left_real, col_cos_ref[...]) - mm(left_imag, col_sin_ref[...])) * scaling
+        return (mm(left_real, col_cos) - mm(left_imag, col_sin)) * scaling
 
     corrs = [one(g) for g in range(group)]
     step_peak = corrs[0]

time: 43.6 us -> 43.7 us (level)
  no operation moved by 1% of the time
where the time goes in v21:
time: 43.7 us; the launch traced here: 43 us
  Pallas kernels  17.8 us (41%)
  local copies, waits for them, and re-layouts  8.69 us (20%)
  starting transfers between devices  8.3 us (19%)
  other arithmetic  4.31 us (10%)
  between operations  2.15 us (5%)
  waiting for transfers between devices  1.73 us (4%)
    pallas_call x2, Pallas kernels, correlate(): pl.pallas_call(kernel, grid_spec=grid_spec, out_shape=out_shape, compiler...  17.8 us
    ppermute x3, starting transfers between devices, swap(): lax.ppermute(payload, 'orient', [(a, b) for a, b in pairs] + [(b, a) for...  8 us
    transpose x1, local copies, waits for them, and re-layouts, body(): col_sin = row_sin.T  1.78 us
    optimization_barrier x2, local copies, waits for them, and re-layouts, body(): lax.optimization_barrier((jnp.asarray(cos_np), jnp.asarray(sin_np)))  1.73 us
    convert_element_type x2, other arithmetic, run(): jnp.concatenate([piece[:, box_size, 0] for piece in pieces])  1.37 us
    slice x1, local copies, waits for them, and re-layouts, body(): sin_full[low:]  1.19 us
    ppermute x1, waiting for transfers between devices, body(): other_half = lax.ppermute(half, 'tile', [(0, 1), (1, 0)])  1.19 us
    reshape x1, local copies, waits for them, and re-layouts, body(): jnp.concatenate([templates, id_rows], axis=1)  0.91 us
  transfers between devices with their start and end apart: 5, of which 3 were waited for; matrix products, arithmetic and copies ran while one was open for 23% of the time, Pallas kernels for 22%

profile of v21, /device:TPU:0, one launch (start us, length us, event | category | flops | bytes accessed | tf_op | source)
XLA Modules:
  0.0 43.0 jit_solution(13154385348471629284)
XLA Ops:
  0.7 0.8 %broadcast_select_fusion.3 = (bf16[96,128]{1,0:T(8,128)(2,1)S(1)}, bf16[96,128]{1,0:T(8,128)(2,1)S(1)}) fusion(pred[]{:T(512)S(6)} %eq.16, bf16[128,128]{1,0:T(8,128)(2,1)} %param.7), kind=kLoop, calls=%fused_computation.15 | loop fusion | flops 24576 | bytes 98305 | tf_op jit(solution)/shard_map/jit(_where)/select_n | solution.py:79
  2.3 0.9 %pad_bitcast_fusion = bf16[200,192]{1,0:T(8,128)(2,1)S(1)} fusion(bf16[1,192,192]{2,1,0:T(8,128)(2,1)} %param.8, bf16[]{:T(256)} %bitcast), kind=kLoop, calls=%fused_computation.8 | loop fusion | bytes 150530 | tf_op jit(solution)/shard_map/reshape | solution.py:276
  3.2 3.0 %collective-permute-start = (bf16[264,192]{1,0:T(8,128)(2,1)S(1)}, bf16[264,192]{1,0:T(8,128)(2,1)S(1)}, u32[]{:S(2)}, u32[]{:S(2)}) collective-permute-start(bf16[264,192]{1,0:T(8,128)(2,1)S(1)} %pad_maximum_fusion.7), channel_id=1, source_target_pairs={{0,2},{4,6},{8,10},{12,14},{2,0},{6,4},{10,8},{14,12},{1,3},{5,7},... | collective-permute-start | bytes 304136 | tf_op jit(solution)/shard_map/ppermute | solution.py:62
  6.2 1.2 %fusion.3 = (bf16[96,320]{0,1:T(8,128)(2,1)S(1)}, bf16[96,320]{0,1:T(8,128)(2,1)S(1)}, bf16[96,320]{0,1:T(8,128)(2,1)S(1)}, bf16[96,320]{0,1:T(8,128)(2,1)S(1)}) fusion(bf16[320,320]{0,1:T(8,128)(2,1)} %constant.37.clone, bf16[320,320]{0,1:T(8,128)(2,1)} %constant.36.clone), kind=kLoop, calls=%fused_computation.29 | loop fusion | bytes 491520 | tf_op jit(solution)/shard_map/slice | solution.py:265
  7.4 1.8 %slice_bitcast_fusion = (bf16[320,128]{1,0:T(8,128)(2,1)}, bf16[128,320]{0,1:T(8,128)(2,1)S(1)}, bf16[128,320]{0,1:T(8,128)(2,1)S(1)}, bf16[320,128]{1,0:T(8,128)(2,1)}) fusion(bf16[320,320]{0,1:T(8,128)(2,1)} %constant.37.clone, bf16[320,320]{0,1:T(8,128)(2,1)} %constant.36.clone), kind=kLoop, calls=%fused_computation.25 | loop fusion | bytes 491520 | tf_op jit(solution)/shard_map/transpose | solution.py:271
  9.3 0.1 fusion.2
  9.4 0.1 fusion.1
  9.5 0.3 collective-permute-done
  9.9 4.8 %collective-permute-start.1 = (bf16[464,192]{1,0:T(8,128)(2,1)S(1)}, bf16[464,192]{1,0:T(8,128)(2,1)S(1)}, u32[]{:S(2)}, u32[]{:S(2)}) collective-permute-start(bf16[464,192]{1,0:T(8,128)(2,1)S(1)} %pad_maximum_fusion.3), channel_id=1, source_target_pairs={{2,4},{6,8},{10,12},{0,14},{4,2},{8,6},{12,10},{14,0},{3,5},{7,9},... | collective-permute-start | bytes 534536 | tf_op jit(solution)/shard_map/ppermute | solution.py:62
  14.7 0.9 %copy.21.refs_3_ = bf16[320,320]{1,0:T(8,128)(2,1)} copy(bf16[320,320]{0,1:T(8,128)(2,1)S(1)} %copy-done.2) | data formatting | bytes 409600 | tf_op jit(solution)/shard_map/optimization_barrier | solution.py:262
  15.6 0.9 %copy.22.refs_4_ = bf16[320,320]{1,0:T(8,128)(2,1)} copy(bf16[320,320]{0,1:T(8,128)(2,1)S(1)} %copy-done.1) | data formatting | bytes 409600 | tf_op jit(solution)/shard_map/optimization_barrier | solution.py:262
  16.5 0.8 %copy.23.refs_5_.refs_4_ = bf16[192,320]{1,0:T(8,128)(2,1)} copy(bf16[192,320]{0,1:T(8,128)(2,1)S(1)} %get-tuple-element.36) | data formatting | bytes 245760 | tf_op jit(solution)/shard_map/concatenate | solution.py:264
  17.2 0.8 %copy.24.refs_6_.refs_5_ = bf16[192,320]{1,0:T(8,128)(2,1)} copy(bf16[192,320]{0,1:T(8,128)(2,1)S(1)} %get-tuple-element.38) | data formatting | bytes 245760 | tf_op jit(solution)/shard_map/concatenate | solution.py:265
  18.0 0.8 %copy.25.refs_8_.refs_7_ = bf16[256,320]{1,0:T(8,128)(2,1)} copy(bf16[256,320]{0,1:T(8,128)(2,1)S(1)} %pad_maximum_fusion.6) | data formatting | bytes 327680 | tf_op jit(solution)/shard_map/concatenate | solution.py:298
  19.5 0.8 %pad_maximum_fusion.1.refs_7_.refs_6_ = bf16[640,192]{1,0:T(8,128)(2,1)} fusion(bf16[320,192]{1,0:T(8,128)(2,1)S(1)} %get-tuple-element.37, bf16[320,192]{1,0:T(8,128)(2,1)S(1)} %get-tuple-element.35), kind=kLoop, calls=%fused_computation.1 | loop fusion | flops 491520 | bytes 491520 | tf_op jit(solution)/shard_map/concatenate | solution.py:297
  20.9 0.2 collective-permute-start.2
  21.0 0.7 %fusion.ids_ref = s32[4]{0:T(128)} fusion(bf16[4,200,192]{2,1,0:T(8,128)(2,1)S(1)} %bitcast.17), kind=kLoop, calls=%fused_computation.20 | loop fusion | flops 4 | bytes 24 | tf_op jit(solution)/shard_map/convert_element_type | solution.py:310
  21.8 0.3 collective-permute-done.3
  22.0 0.8 %pad_maximum_fusion.2.refs_2_ = bf16[320,320]{1,0:T(8,128)(2,1)} fusion(bf16[320,96]{1,0:T(8,128)(2,1)S(1)} %get-tuple-element.40, bf16[320,128]{1,0:T(8,128)(2,1)S(1)} %constant_dynamic-update-slice_fusion, bf16[320,96]{1,0:T(8,128)(2,1)S(1)} %get-tuple-element.39), kind=kLoop, calls=%fused_computation.2 | loop fusion | flops 614400 | bytes 409600 | tf_op jit(solution)/shard_map/concatenate | solution.py:285
  22.9 9.6 %shard_map.94 = (f32[128,128]{1,0:T(8,128)}, f32[128,128]{1,0:T(8,128)}, f32[128,128]{1,0:T(8,128)}, bf16[320,320]{1,0:T(8,128)(2,1)}, bf16[320,320]{1,0:T(8,128)(2,1)}) custom-call(s32[4]{0:T(128)} %fusion.ids_ref, s32[1]{0:T(128)} %bitcast.15.live_ref, bf16[4,200,192]{2,1,0:T(8,128)(2,1)} %bitcast.18, bf16[4,200,192]{2,1,0:T(8,128)(2,1)} %bitcast.19, ...), custom_call_target="tpu_custom_call" | custom-call | tf_op jit(solution)/shard_map/pallas_call | solution.py:242
  32.5 0.2 collective-permute-start.4
  32.8 1.2 %collective-permute-done.4 = bf16[400,192]{1,0:T(8,128)(2,1)S(1)} collective-permute-done((bf16[400,192]{1,0:T(8,128)(2,1)S(1)}, bf16[400,192]{1,0:T(8,128)(2,1)S(1)}, u32[]{:S(2)}, u32[]{:S(2)}) %collective-permute-start.4) | collective-permute-done | bytes 153632 | tf_op jit(solution)/shard_map/ppermute | solution.py:320
  34.1 0.7 %maximum_convert_fusion.ids_ref = s32[4]{0:T(128)} fusion(bf16[2]{0:T(256)(128)(2,1)S(1)} %slice_reduce_fusion, bf16[2]{0:T(256)(128)(2,1)S(1)} %slice_reduce_fusion.1), kind=kLoop, calls=%fused_computation.23 | loop fusion | flops 16 | bytes 24 | tf_op jit(solution)/shard_map/convert_element_type | solution.py:310
  34.8 8.2 %shard_map.95 = (f32[128,128]{1,0:T(8,128)}, f32[128,128]{1,0:T(8,128)}, f32[128,128]{1,0:T(8,128)}) custom-call(s32[4]{0:T(128)} %maximum_convert_fusion.ids_ref, s32[1]{0:T(128)} %bitcast.16.live_ref, bf16[2,200,192]{2,1,0:T(8,128)(2,1)} %bitcast.21, bf16[2,200,192]{2,1,0:T(8,128)(2,1)} %bitcast.23, ...), custom_call_target="tpu_custom_call", output_to_operand_aliasing={{0}: (14, {}), {1}: (15, {}), {2}: (16, {})} | custom-call | tf_op jit(solution)/shard_map/pallas_call | solution.py:242
  (34 shorter events, 1.0 us)
Async XLA Ops:
  0.6 14.1 %copy-start.2 = (bf16[320,320]{0,1:T(8,128)(2,1)S(1)}, bf16[320,320]{0,1:T(8,128)(2,1)}, u32[]{:S(2)}) copy-start(bf16[320,320]{0,1:T(8,128)(2,1)} %constant.36.clone) | copy-start | bytes 614404
  0.6 15.0 %copy-start.1 = (bf16[320,320]{0,1:T(8,128)(2,1)S(1)}, bf16[320,320]{0,1:T(8,128)(2,1)}, u32[]{:S(2)}) copy-start(bf16[320,320]{0,1:T(8,128)(2,1)} %constant.37.clone) | copy-start | bytes 614404
  0.7 19.8 %copy-start.5 = (bf16[128,128]{1,0:T(8,128)(2,1)S(1)}, bf16[128,128]{1,0:T(8,128)(2,1)}, u32[]{:S(2)}) copy-start(bf16[128,128]{1,0:T(8,128)(2,1)} %param.7) | copy-start | bytes 98308
  3.2 6.6 %collective-permute-start = (bf16[264,192]{1,0:T(8,128)(2,1)S(1)}, bf16[264,192]{1,0:T(8,128)(2,1)S(1)}, u32[]{:S(2)}, u32[]{:S(2)}) collective-permute-start(bf16[264,192]{1,0:T(8,128)(2,1)S(1)} %pad_maximum_fusion.7), channel_id=1, source_target_pairs={{0,2},{4,6},{8,10},{12,14},{2,0},{6,4},{10,8},{14,12},{1,3},{5,7},... | collective-permute-start | bytes 304136 | tf_op jit(solution)/shard_map/ppermute | solution.py:62
  9.9 10.4 %collective-permute-start.1 = (bf16[464,192]{1,0:T(8,128)(2,1)S(1)}, bf16[464,192]{1,0:T(8,128)(2,1)S(1)}, u32[]{:S(2)}, u32[]{:S(2)}) collective-permute-start(bf16[464,192]{1,0:T(8,128)(2,1)S(1)} %pad_maximum_fusion.3), channel_id=1, source_target_pairs={{2,4},{6,8},{10,12},{0,14},{4,2},{8,6},{12,10},{14,0},{3,5},{7,9},... | collective-permute-start | bytes 534536 | tf_op jit(solution)/shard_map/ppermute | solution.py:62
  20.7 1.3 %collective-permute-start.3 = (bf16[320,96]{1,0:T(8,128)(2,1)S(1)}, bf16[320,96]{1,0:T(8,128)(2,1)S(1)}, u32[]{:S(2)}, u32[]{:S(2)}) collective-permute-start(bf16[320,96]{1,0:T(8,128)(2,1)S(1)} %slice_select_fusion), channel_id=1, source_target_pairs={{0,1},{1,0},{2,3},{3,2},{4,5},{5,4},{6,7},{7,6},{8,9},{9,8},{10,11... | collective-permute-start | bytes 184328 | tf_op jit(solution)/shard_map/ppermute | solution.py:283
  20.9 2.0 %copy-start = (bf16[800,192]{1,0:T(8,128)(2,1)}, bf16[800,192]{1,0:T(8,128)(2,1)S(1)}, u32[]{:S(2)}) copy-start(bf16[800,192]{1,0:T(8,128)(2,1)S(1)} %pad_maximum_fusion) | copy-start | bytes 921604
  20.9 11.6 %collective-permute-start.2 = (bf16[400,192]{1,0:T(8,128)(2,1)S(1)}, bf16[400,192]{1,0:T(8,128)(2,1)S(1)}, u32[]{:S(2)}, u32[]{:S(2)}) collective-permute-start(bf16[400,192]{1,0:T(8,128)(2,1)S(1)} %constant_dynamic-slice_fusion), channel_id=1, source_target_pairs={{0,8},{14,6},{2,10},{4,12},{8,0},{6,14},{10,2},{12,4},{1,9},{15,7}... | collective-permute-start | bytes 460808 | tf_op jit(solution)/shard_map/ppermute | solution.py:62
  32.5 2.3 %copy-start.3 = (bf16[400,192]{1,0:T(8,128)(2,1)}, bf16[400,192]{1,0:T(8,128)(2,1)S(1)}, u32[]{:S(2)}) copy-start(bf16[400,192]{1,0:T(8,128)(2,1)S(1)} %collective-permute-done.2) | copy-start | bytes 460804
  32.5 1.5 %collective-permute-start.4 = (bf16[400,192]{1,0:T(8,128)(2,1)S(1)}, bf16[400,192]{1,0:T(8,128)(2,1)S(1)}, u32[]{:S(2)}, u32[]{:S(2)}) collective-permute-start(bf16[400,192]{1,0:T(8,128)(2,1)S(1)} %collective-permute-done.2), channel_id=1, source_target_pairs={{0,1},{1,0},{2,3},{3,2},{4,5},{5,4},{6,7},{7,6},{8,9},{9,8},{10,11... | collective-permute-start | bytes 460808 | tf_op jit(solution)/shard_map/ppermute | solution.py:320
  34.0 0.8 %copy-start.4 = (bf16[400,192]{1,0:T(8,128)(2,1)}, bf16[400,192]{1,0:T(8,128)(2,1)S(1)}, u32[]{:S(2)}) copy-start(bf16[400,192]{1,0:T(8,128)(2,1)S(1)} %collective-permute-done.4) | copy-start | bytes 460804

commit v22 on v19

--- a/solution.py
+++ b/solution.py
@@ -66,20 +66,21 @@
     size = lax.axis_size("orient")
     index = lax.axis_index("orient")
     odd = index % 2 == 1
-    low_rows = tile[tile.shape[0] - width :]
-    high_rows = tile[:width]
     lanes = block.shape[1]
-    carried = width * tile.shape[1] // lanes
+
+    def edge_rows(bottom):
+        start = jnp.where(bottom, tile.shape[0] - width, 0)
+        return lax.dynamic_slice_in_dim(tile, start, width, 0)
 
     def send(held, rows, pairs):
-        payload = jnp.concatenate([held, rows.reshape(carried, lanes)], axis=0)
-        got = swap(payload, pairs)
-        return got[: held.shape[0]], got[held.shape[0] :].reshape(width, tile.shape[1])
-
-    first, rows_one = send(block, jnp.where(odd, high_rows, low_rows), [(2 * i, 2 * i + 1) for i in range(size // 2)])
+        padded_rows = jnp.pad(rows, ((0, 0), (0, lanes - rows.shape[1])))
+        got = swap(jnp.concatenate([held, padded_rows], axis=0), pairs)
+        return got[: held.shape[0]], got[held.shape[0] :, : tile.shape[1]]
+
+    first, rows_one = send(block, edge_rows(jnp.logical_not(odd)), [(2 * i, 2 * i + 1) for i in range(size // 2)])
     held = jnp.concatenate([block, first], axis=0)
     second_pairs = [(2 * i + 1, 2 * i + 2) for i in range(size // 2 - 1)] + [(0, size - 1)]
-    second, rows_two = send(held, jnp.where(odd, low_rows, high_rows), second_pairs)
+    second, rows_two = send(held, edge_rows(odd), second_pairs)
     held = jnp.concatenate([held, second], axis=0)
     third_pairs = [(0, size // 2), (size - 1, size // 2 - 1), (1, size // 2 + 1), (2, size // 2 + 2)]
     cores = lax.axis_size("tile")
@@ -270,7 +271,7 @@
     block_rows = box_size + 8
     packed = jnp.concatenate([templates, id_rows], axis=1).reshape(local_count * block_rows, box_size)
     split_last = lax.axis_size("orient") == 8 and lax.axis_size("tile") == 2
-    split_last = split_last and local_count == 1 and (margin * tile_width) % box_size == 0
+    split_last = split_last and local_count == 1 and tile_width <= box_size
     if split_last:
         arrivals, row_padded = exchange_with_rows(packed, micrograph, margin)
         core = lax.axis_index("tile")

time: 43.6 us -> 48.2 us (1.11)
  waiting for transfers between devices: 1.73 us -> 5.58 us
  local copies, waits for them, and re-layouts: 8.69 us -> 11 us
  other arithmetic: 4.31 us -> 3.49 us
    ppermute x3, waiting for transfers between devices: 0.28 us -> 4.42 us  [swap(): lax.ppermute(payload, 'orient', [(a, b) for a, b in pairs] + [(b, a) for...]
    optimization_barrier x2, local copies, waits for them, and re-layouts: 1.73 us -> 3.59 us  [body(): lax.optimization_barrier((jnp.asarray(cos_np), jnp.asarray(sin_np)))]
    select_n x2 -> x1, other arithmetic: 0.84 us -> 0.01 us  [exchange_with_rows(): top = jnp.where(odd, rows_one, jnp.where(index == 0, zero, rows_two))]
    dynamic_slice x0 -> x1, local copies, waits for them, and re-layouts: none -> 0.83 us  [edge_rows(): return lax.dynamic_slice_in_dim(tile, start, width, 0)]
    ppermute x3, starting transfers between devices: 8 us -> 7.5 us  [swap(): lax.ppermute(payload, 'orient', [(a, b) for a, b in pairs] + [(b, a) for...]
  transfers between devices with their start and end apart: 5 -> 5, of which waited for: 3 -> 2; matrix products, arithmetic and copies ran while one was open for 23% -> 25% of each run, Pallas kernels for 22% -> 20%
where the time goes in v22:
time: 48.2 us; the launch traced here: 47.8 us
  Pallas kernels  17.8 us (37%)
  local copies, waits for them, and re-layouts  11 us (23%)
  starting transfers between devices  7.83 us (16%)
  waiting for transfers between devices  5.58 us (12%)
  other arithmetic  3.49 us (7%)
  between operations  2.1 us (4%)
    pallas_call x2, Pallas kernels, correlate(): pl.pallas_call(kernel, grid_spec=grid_spec, out_shape=out_shape, compiler...  17.8 us
    ppermute x3, starting transfers between devices, swap(): lax.ppermute(payload, 'orient', [(a, b) for a, b in pairs] + [(b, a) for...  7.5 us
    ppermute x3, waiting for transfers between devices, swap(): lax.ppermute(payload, 'orient', [(a, b) for a, b in pairs] + [(b, a) for...  4.42 us
    optimization_barrier x2, local copies, waits for them, and re-layouts, body(): lax.optimization_barrier((jnp.asarray(cos_np), jnp.asarray(sin_np)))  3.59 us
    transpose x1, local copies, waits for them, and re-layouts, body(): col_sin = row_sin.T  1.77 us
    convert_element_type x2, other arithmetic, run(): jnp.concatenate([piece[:, box_size, 0] for piece in pieces])  1.37 us
    slice x1, local copies, waits for them, and re-layouts, body(): sin_full[low:]  1.19 us
    ppermute x1, waiting for transfers between devices, body(): other_half = lax.ppermute(half, 'tile', [(0, 1), (1, 0)])  1.15 us
  transfers between devices with their start and end apart: 5, of which 2 were waited for; matrix products, arithmetic and copies ran while one was open for 25% of the time, Pallas kernels for 20%

profile of v22, /device:TPU:0, one launch (start us, length us, event | category | flops | bytes accessed | tf_op | source)
XLA Modules:
  0.0 47.8 jit_solution(8054584237533902281)
XLA Ops:
  1.3 0.9 %pad_bitcast_fusion = bf16[200,192]{1,0:T(8,128)(2,1)S(1)} fusion(bf16[1,192,192]{2,1,0:T(8,128)(2,1)} %param.8, bf16[]{:T(256)} %bitcast), kind=kLoop, calls=%fused_computation.12 | loop fusion | bytes 150530 | tf_op jit(solution)/shard_map/reshape | solution.py:272
  2.2 0.8 %constant_dynamic-slice_fusion.2 = (bf16[96,128]{1,0:T(8,128)(2,1)S(1)}, bf16[96,128]{1,0:T(8,128)(2,1)S(1)}) fusion(bf16[128,128]{1,0:T(8,128)(2,1)} %param.7, s32[]{:T(128)S(6)} %select_n.60, s32[]{:T(128)S(6)} %select_n.61), kind=kLoop, calls=%fused_computation.25 | loop fusion | bytes 98312 | tf_op jit(solution)/shard_map/dynamic_slice | solution.py:73
  3.1 3.0 %collective-permute-start = (bf16[296,192]{1,0:T(8,128)(2,1)S(1)}, bf16[296,192]{1,0:T(8,128)(2,1)S(1)}, u32[]{:S(2)}, u32[]{:S(2)}) collective-permute-start(bf16[296,192]{1,0:T(8,128)(2,1)S(1)} %fusion.3), channel_id=1, source_target_pairs={{0,2},{4,6},{8,10},{12,14},{2,0},{6,4},{10,8},{14,12},{1,3},{5,7},... | collective-permute-start | bytes 341000 | tf_op jit(solution)/shard_map/ppermute | solution.py:62
  6.1 1.2 %fusion.7 = (bf16[96,320]{0,1:T(8,128)(2,1)S(1)}, bf16[96,320]{0,1:T(8,128)(2,1)S(1)}, bf16[96,320]{0,1:T(8,128)(2,1)S(1)}, bf16[96,320]{0,1:T(8,128)(2,1)S(1)}) fusion(bf16[320,320]{0,1:T(8,128)(2,1)} %constant.43.clone, bf16[320,320]{0,1:T(8,128)(2,1)} %constant.42.clone), kind=kLoop, calls=%fused_computation.31 | loop fusion | bytes 491520 | tf_op jit(solution)/shard_map/slice | solution.py:261
  7.3 1.8 %slice_bitcast_fusion = (bf16[320,128]{1,0:T(8,128)(2,1)}, bf16[128,320]{0,1:T(8,128)(2,1)S(1)}, bf16[128,320]{0,1:T(8,128)(2,1)S(1)}, bf16[320,128]{1,0:T(8,128)(2,1)}) fusion(bf16[320,320]{0,1:T(8,128)(2,1)} %constant.43.clone, bf16[320,320]{0,1:T(8,128)(2,1)} %constant.42.clone), kind=kLoop, calls=%fused_computation.27 | loop fusion | bytes 491520 | tf_op jit(solution)/shard_map/transpose | solution.py:267
  9.0 1.8 %copy.21.refs_3_ = bf16[320,320]{1,0:T(8,128)(2,1)} copy(bf16[320,320]{0,1:T(8,128)(2,1)} %constant.42.clone) | data formatting | bytes 409600 | tf_op jit(solution)/shard_map/optimization_barrier | solution.py:258
  10.8 1.8 %copy.22.refs_4_ = bf16[320,320]{1,0:T(8,128)(2,1)} copy(bf16[320,320]{0,1:T(8,128)(2,1)} %constant.43.clone) | data formatting | bytes 409600 | tf_op jit(solution)/shard_map/optimization_barrier | solution.py:258
  12.6 0.1 fusion.6
  12.8 0.8 %copy.23.refs_5_.refs_4_ = bf16[192,320]{1,0:T(8,128)(2,1)} copy(bf16[192,320]{0,1:T(8,128)(2,1)S(1)} %get-tuple-element.36) | data formatting | bytes 245760 | tf_op jit(solution)/shard_map/concatenate | solution.py:260
  13.5 0.1 fusion.5
  13.7 0.8 %copy.24.refs_6_.refs_5_ = bf16[192,320]{1,0:T(8,128)(2,1)} copy(bf16[192,320]{0,1:T(8,128)(2,1)S(1)} %get-tuple-element.38) | data formatting | bytes 245760 | tf_op jit(solution)/shard_map/concatenate | solution.py:261
  14.5 3.6 %collective-permute-start.1 = (bf16[496,192]{1,0:T(8,128)(2,1)S(1)}, bf16[496,192]{1,0:T(8,128)(2,1)S(1)}, u32[]{:S(2)}, u32[]{:S(2)}) collective-permute-start(bf16[496,192]{1,0:T(8,128)(2,1)S(1)} %fusion.2), channel_id=1, source_target_pairs={{2,4},{6,8},{10,12},{0,14},{4,2},{8,6},{12,10},{14,0},{3,5},{7,9},... | collective-permute-start | bytes 571400 | tf_op jit(solution)/shard_map/ppermute | solution.py:62
  18.2 0.8 %copy.25.refs_8_.refs_7_ = bf16[256,320]{1,0:T(8,128)(2,1)} copy(bf16[256,320]{0,1:T(8,128)(2,1)S(1)} %pad_maximum_fusion.5) | data formatting | bytes 327680 | tf_op jit(solution)/shard_map/concatenate | solution.py:294
  19.7 0.8 %pad_maximum_fusion.1.refs_7_.refs_6_ = bf16[640,192]{1,0:T(8,128)(2,1)} fusion(bf16[320,192]{1,0:T(8,128)(2,1)S(1)} %get-tuple-element.37, bf16[320,192]{1,0:T(8,128)(2,1)S(1)} %get-tuple-element.35), kind=kLoop, calls=%fused_computation.3 | loop fusion | flops 491520 | bytes 491520 | tf_op jit(solution)/shard_map/concatenate | solution.py:293
  20.4 4.4 %collective-permute-done.1 = bf16[496,192]{1,0:T(8,128)(2,1)S(1)} collective-permute-done((bf16[496,192]{1,0:T(8,128)(2,1)S(1)}, bf16[496,192]{1,0:T(8,128)(2,1)S(1)}, u32[]{:S(2)}, u32[]{:S(2)}) %collective-permute-start.1) | collective-permute-done | bytes 190496 | tf_op jit(solution)/shard_map/ppermute | solution.py:62
  25.2 0.9 %collective-permute-start.2 = (bf16[400,192]{1,0:T(8,128)(2,1)S(1)}, bf16[400,192]{1,0:T(8,128)(2,1)S(1)}, u32[]{:S(2)}, u32[]{:S(2)}) collective-permute-start(bf16[400,192]{1,0:T(8,128)(2,1)S(1)} %constant_dynamic-slice_fusion), channel_id=1, source_target_pairs={{0,8},{14,6},{2,10},{4,12},{8,0},{6,14},{10,2},{12,4},{1,9},{15,7}... | collective-permute-start | bytes 460808 | tf_op jit(solution)/shard_map/ppermute | solution.py:62
  26.1 0.8 %fusion.4.ids_ref = s32[4]{0:T(128)} fusion(bf16[4,200,192]{2,1,0:T(8,128)(2,1)S(1)} %bitcast.17), kind=kLoop, calls=%fused_computation.20 | loop fusion | flops 4 | bytes 24 | tf_op jit(solution)/shard_map/convert_element_type | solution.py:306
  26.8 0.9 %pad_maximum_fusion.2.refs_2_ = bf16[320,320]{1,0:T(8,128)(2,1)} fusion(bf16[320,96]{1,0:T(8,128)(2,1)S(1)} %get-tuple-element.40, bf16[96,128]{1,0:T(8,128)(2,1)S(1)} %get-tuple-element.26, bf16[128,128]{1,0:T(8,128)(2,1)S(1)} %copy-done.1, bf16[96,128]{1,0:T(8,128)(2,1)S(1)} %get-tuple-element.25, bf16[320,96]{1,0:T(8,128)(2,1)S(1)} %get-tuple-element.39), kind=kLoop, calls=%fused_computation.7 | loop fusion | flops 1024000 | bytes 409600 | tf_op jit(solution)/shard_map/concatenate | solution.py:281
  27.7 9.6 %shard_map.94 = (f32[128,128]{1,0:T(8,128)}, f32[128,128]{1,0:T(8,128)}, f32[128,128]{1,0:T(8,128)}, bf16[320,320]{1,0:T(8,128)(2,1)}, bf16[320,320]{1,0:T(8,128)(2,1)}) custom-call(s32[4]{0:T(128)} %fusion.4.ids_ref, s32[1]{0:T(128)} %bitcast.15.live_ref, bf16[4,200,192]{2,1,0:T(8,128)(2,1)} %bitcast.18, bf16[4,200,192]{2,1,0:T(8,128)(2,1)} %bitcast.19, ...), custom_call_target="tpu_custom_call" | custom-call | tf_op jit(solution)/shard_map/pallas_call | solution.py:238
  37.3 0.3 collective-permute-start.4
  37.6 0.1 slice_reduce_fusion.1
  37.7 1.2 %collective-permute-done.4 = bf16[400,192]{1,0:T(8,128)(2,1)S(1)} collective-permute-done((bf16[400,192]{1,0:T(8,128)(2,1)S(1)}, bf16[400,192]{1,0:T(8,128)(2,1)S(1)}, u32[]{:S(2)}, u32[]{:S(2)}) %collective-permute-start.4) | collective-permute-done | bytes 153632 | tf_op jit(solution)/shard_map/ppermute | solution.py:316
  38.9 0.6 %maximum_convert_fusion.ids_ref = s32[4]{0:T(128)} fusion(bf16[2]{0:T(256)(128)(2,1)S(1)} %slice_reduce_fusion, bf16[2]{0:T(256)(128)(2,1)S(1)} %slice_reduce_fusion.1), kind=kLoop, calls=%fused_computation.26 | loop fusion | flops 16 | bytes 24 | tf_op jit(solution)/shard_map/convert_element_type | solution.py:306
  39.5 8.2 %shard_map.95 = (f32[128,128]{1,0:T(8,128)}, f32[128,128]{1,0:T(8,128)}, f32[128,128]{1,0:T(8,128)}) custom-call(s32[4]{0:T(128)} %maximum_convert_fusion.ids_ref, s32[1]{0:T(128)} %bitcast.16.live_ref, bf16[2,200,192]{2,1,0:T(8,128)(2,1)} %bitcast.21, bf16[2,200,192]{2,1,0:T(8,128)(2,1)} %bitcast.23, ...), custom_call_target="tpu_custom_call", output_to_operand_aliasing={{0}: (14, {}), {1}: (15, {}), {2}: (16, {})} | custom-call | tf_op jit(solution)/shard_map/pallas_call | solution.py:238
  (24 shorter events, 0.5 us)
Async XLA Ops:
  0.6 24.2 %copy-start.1 = (bf16[128,128]{1,0:T(8,128)(2,1)S(1)}, bf16[128,128]{1,0:T(8,128)(2,1)}, u32[]{:S(2)}) copy-start(bf16[128,128]{1,0:T(8,128)(2,1)} %param.7) | copy-start | bytes 98308
  3.1 11.4 %collective-permute-start = (bf16[296,192]{1,0:T(8,128)(2,1)S(1)}, bf16[296,192]{1,0:T(8,128)(2,1)S(1)}, u32[]{:S(2)}, u32[]{:S(2)}) collective-permute-start(bf16[296,192]{1,0:T(8,128)(2,1)S(1)} %fusion.3), channel_id=1, source_target_pairs={{0,2},{4,6},{8,10},{12,14},{2,0},{6,4},{10,8},{14,12},{1,3},{5,7},... | collective-permute-start | bytes 341000 | tf_op jit(solution)/shard_map/ppermute | solution.py:62
  14.5 10.4 %collective-permute-start.1 = (bf16[496,192]{1,0:T(8,128)(2,1)S(1)}, bf16[496,192]{1,0:T(8,128)(2,1)S(1)}, u32[]{:S(2)}, u32[]{:S(2)}) collective-permute-start(bf16[496,192]{1,0:T(8,128)(2,1)S(1)} %fusion.2), channel_id=1, source_target_pairs={{2,4},{6,8},{10,12},{0,14},{4,2},{8,6},{12,10},{14,0},{3,5},{7,9},... | collective-permute-start | bytes 571400 | tf_op jit(solution)/shard_map/ppermute | solution.py:62
  25.0 1.8 %collective-permute-start.3 = (bf16[320,96]{1,0:T(8,128)(2,1)S(1)}, bf16[320,96]{1,0:T(8,128)(2,1)S(1)}, u32[]{:S(2)}, u32[]{:S(2)}) collective-permute-start(bf16[320,96]{1,0:T(8,128)(2,1)S(1)} %slice_select_fusion), channel_id=1, source_target_pairs={{0,1},{1,0},{2,3},{3,2},{4,5},{5,4},{6,7},{7,6},{8,9},{9,8},{10,11... | collective-permute-start | bytes 184328 | tf_op jit(solution)/shard_map/ppermute | solution.py:279
  25.2 2.5 %copy-start = (bf16[800,192]{1,0:T(8,128)(2,1)}, bf16[800,192]{1,0:T(8,128)(2,1)S(1)}, u32[]{:S(2)}) copy-start(bf16[800,192]{1,0:T(8,128)(2,1)S(1)} %pad_maximum_fusion) | copy-start | bytes 921604
  25.2 12.1 %collective-permute-start.2 = (bf16[400,192]{1,0:T(8,128)(2,1)S(1)}, bf16[400,192]{1,0:T(8,128)(2,1)S(1)}, u32[]{:S(2)}, u32[]{:S(2)}) collective-permute-start(bf16[400,192]{1,0:T(8,128)(2,1)S(1)} %constant_dynamic-slice_fusion), channel_id=1, source_target_pairs={{0,8},{14,6},{2,10},{4,12},{8,0},{6,14},{10,2},{12,4},{1,9},{15,7}... | collective-permute-start | bytes 460808 | tf_op jit(solution)/shard_map/ppermute | solution.py:62
  37.3 2.2 %copy-start.2 = (bf16[400,192]{1,0:T(8,128)(2,1)}, bf16[400,192]{1,0:T(8,128)(2,1)S(1)}, u32[]{:S(2)}) copy-start(bf16[400,192]{1,0:T(8,128)(2,1)S(1)} %collective-permute-done.2) | copy-start | bytes 460804
  37.3 1.5 %collective-permute-start.4 = (bf16[400,192]{1,0:T(8,128)(2,1)S(1)}, bf16[400,192]{1,0:T(8,128)(2,1)S(1)}, u32[]{:S(2)}, u32[]{:S(2)}) collective-permute-start(bf16[400,192]{1,0:T(8,128)(2,1)S(1)} %collective-permute-done.2), channel_id=1, source_target_pairs={{0,1},{1,0},{2,3},{3,2},{4,5},{5,4},{6,7},{7,6},{8,9},{9,8},{10,11... | collective-permute-start | bytes 460808 | tf_op jit(solution)/shard_map/ppermute | solution.py:316
  38.8 0.7 %copy-start.3 = (bf16[400,192]{1,0:T(8,128)(2,1)}, bf16[400,192]{1,0:T(8,128)(2,1)S(1)}, u32[]{:S(2)}) copy-start(bf16[400,192]{1,0:T(8,128)(2,1)S(1)} %collective-permute-done.4) | copy-start | bytes 460804
